TPU v7x, 32 devices: a whole 2x2x4 slice. The times are simulated.
32 devices in a mesh: group: 2 (over y), section: 4 (over x, core), shard: 4 (over z).
Axes of the slice: x: 2, y: 2, z: 4, core: 2. Of those that a mesh axis runs over, the one named last changes fastest.
Arguments:
- image_tokens: bfloat16 [4, 96, 8192], P('group', 'section', 'shard'), parts along dimension 0, may hold values from -6 to 6
- keyval_weight: bfloat16 [4, 8192, 1024], P('section', 'shard'), may hold values from -0.0625 to 0.0625
- query_gain: float32 [4, 4096], P('section'), may hold values from 0.5 to 5
- key_norm_gain: float32 [4, 512], P('section'), may hold values from 0.5 to 5
- gate_logit: float32 [4, 32], P('section'), may hold values from -1.5 to 1.5
- text_queries: bfloat16 [4, 256, 4096], P('group', 'shard'), parts along dimension 0, may hold values from -6 to 6
- text_document: int32 [4, 256], P('group', 'shard'), parts along dimension 0, may hold values from 0 to 7, never falling along the last dimension, each value on 1 to 128 neighbouring positions
- image_document: int32 [4, 96], P('group'), parts along dimension 0, may hold values from 0 to 7, never falling along the last dimension, each value on 1 to 48 neighbouring positions
- cotangent: bfloat16 [4, 4, 256, 4096], P('section', 'group', 'shard'), parts along dimension 1, may hold values from -6 to 6
Outputs:
- section_states: float32 [4, 4, 256, 4096], P('section', 'group', 'shard'), parts along dimension 1
- image_grad: float32 [4, 96, 8192], P('group', 'section', 'shard'), parts along dimension 0
There are 2 independent parts, one for each index of `group`. A program takes and returns all parts, laid end to end along the dimension named above; an argument that names none is the same for every part. Nothing has to cross between parts.
Inputs may be any that keep to these rules, and one draw needn't show every extreme that they name: `text_document`: numbers never fall along a micro-batch's text tokens; every number from 0 to 7 appears in each micro-batch. `image_document`: numbers never fall along a micro-batch's image tokens; every number from 0 to 7 appears in each micro-batch.
All inputs are finite; a program needn't handle non-finite values.
Results may differ from a plain program's by a relative error of at most 0.034.
The roundings to bfloat16 on the way count: a program that leaves them out, or rounds other values in their place, can miss the bound.
Values may be sent and summed in bfloat16 or wider, within the bound.
No kernel may reach another device: no remote copies, remote signals or barrier semaphores. Data moves between devices by JAX's collectives and lax.ppermute only.
A program may use at most 128 MiB of HBM per device.

v0:
```python
import math

import jax
import jax.numpy as jnp
from jax import lax
from jax.sharding import PartitionSpec as P

epsilon = 1e-05


def from_behind(block, axis, distance):
    devices = range(lax.axis_size(axis))
    route = [(i - distance, i) for i in devices if i - distance in devices]
    return lax.ppermute(block, axis, route)


def head_normalize(input_rows, gain_row, head_count):
    shaped = input_rows.reshape(input_rows.shape[0], head_count, -1)
    factor = lax.rsqrt(jnp.mean(shaped * shaped, axis=-1, keepdims=True) + epsilon)
    return (shaped * factor * gain_row.reshape(1, head_count, -1)).reshape(input_rows.shape[0], -1)


def norm_gradient(input_rows, gain_row, incoming_gradient, head_count):
    shaped = input_rows.reshape(input_rows.shape[0], head_count, -1)
    scaled = incoming_gradient.reshape(input_rows.shape[0], head_count, -1) * gain_row.reshape(
        1, head_count, -1
    )
    factor = lax.rsqrt(jnp.mean(shaped * shaped, axis=-1, keepdims=True) + epsilon)
    inner_mean = jnp.mean(shaped * scaled, axis=-1, keepdims=True)
    result = factor * scaled - shaped * factor * factor * factor * inner_mean
    return result.reshape(input_rows.shape[0], -1)


def attend_scores(current, gain_row, key_block, same_document, head_count):
    token_count = current.shape[0]
    keyval_heads = key_block.shape[1]
    head_dim = key_block.shape[2]
    query_groups = head_count // keyval_heads
    query_matrix = head_normalize(current, gain_row, head_count).astype(jnp.bfloat16)
    query_matrix = query_matrix.reshape(token_count, keyval_heads, query_groups, head_dim)
    scores = jnp.einsum(
        "tkgd,ikd->kgti", query_matrix, key_block, preferred_element_type=jnp.float32
    ) * (1.0 / math.sqrt(head_dim))
    scores = jnp.where(same_document[None, None], scores, -jnp.inf)
    row_max = jnp.max(scores, axis=-1, keepdims=True)
    powered = jnp.exp(scores - row_max)
    exact_probs = powered / jnp.sum(powered, axis=-1, keepdims=True)
    return (query_matrix, exact_probs)


def forward_layer(current, gain_row, gate_row, key_block, value_block, same_document, head_count):
    token_count = current.shape[0]
    head_dim = value_block.shape[2]
    query_matrix, exact_probs = attend_scores(
        current, gain_row, key_block, same_document, head_count
    )
    probability = exact_probs.astype(jnp.bfloat16)
    attended = jnp.einsum(
        "kgti,ikd->tkgd", probability, value_block, preferred_element_type=jnp.float32
    )
    updated = current.reshape(token_count, head_count, head_dim)
    updated = updated + jnp.tanh(gate_row)[None, :, None] * attended.reshape(
        token_count, head_count, head_dim
    )
    return updated.reshape(token_count, -1)


def backward_layer(
    current, gain_row, key_block, value_block, same_document, upstream_rows, head_count
):
    token_count = current.shape[0]
    image_count = key_block.shape[0]
    keyval_heads = key_block.shape[1]
    head_dim = key_block.shape[2]
    query_matrix, exact_probs = attend_scores(
        current, gain_row, key_block, same_document, head_count
    )
    probability = exact_probs.astype(jnp.bfloat16)
    incoming_gradient = upstream_rows.reshape(
        token_count, keyval_heads, head_count // keyval_heads, head_dim
    )
    value_grad = jnp.einsum(
        "kgti,tkgd->ikd", probability, incoming_gradient, preferred_element_type=jnp.float32
    )
    prob_grad = jnp.einsum(
        "tkgd,ikd->kgti", incoming_gradient, value_block, preferred_element_type=jnp.float32
    )
    score_grad = exact_probs * (
        prob_grad - jnp.sum(exact_probs * prob_grad, axis=-1, keepdims=True)
    )
    score_grad = score_grad.astype(jnp.bfloat16)
    key_grad = jnp.einsum(
        "kgti,tkgd->ikd", score_grad, query_matrix, preferred_element_type=jnp.float32
    ) * (1.0 / math.sqrt(head_dim))
    return jnp.concatenate(
        [key_grad.reshape(image_count, -1), value_grad.reshape(image_count, -1)], axis=1
    )


def pick_slot(array_in, slot_index):
    return lax.dynamic_index_in_dim(array_in, slot_index, 0, keepdims=False)


def per_device(
    image_tokens,
    keyval_weight,
    query_gain,
    key_norm_gain,
    gate_logit,
    text_queries,
    text_document,
    image_document,
    cotangent,
):
    section_count = lax.axis_size("section")
    section_index = lax.axis_index("section")
    micro_count = text_queries.shape[0]
    token_count = text_queries.shape[1]
    head_count = gate_logit.shape[1]
    key_width = key_norm_gain.shape[1]
    head_dim = query_gain.shape[1] // head_count
    keyval_heads = key_width // head_dim
    weights = keyval_weight[0]
    gathered = lax.all_gather(image_tokens, "section", axis=1, tiled=True)
    image_count = gathered.shape[1]
    total_rows = micro_count * image_count
    flat_rows = gathered.reshape(total_rows, gathered.shape[2])
    unscaled_sum = lax.psum(
        jnp.dot(flat_rows, weights, preferred_element_type=jnp.float32), "shard"
    )
    key_matrix = head_normalize(unscaled_sum[:, :key_width], key_norm_gain[0], keyval_heads).astype(
        jnp.bfloat16
    )
    value_matrix = unscaled_sum[:, key_width:].astype(jnp.bfloat16)
    key_blocks = key_matrix.reshape(micro_count, image_count, keyval_heads, head_dim)
    value_blocks = value_matrix.reshape(micro_count, image_count, keyval_heads, head_dim)
    same_document = text_document[:, :, None] == image_document[:, None, :]
    start_stream = text_queries.astype(jnp.float32)
    buffers = jnp.zeros_like(start_stream)
    empty_slot = jnp.zeros((token_count, text_queries.shape[2]), jnp.float32)

    def advance(instant, loop_state):
        received, stored, results = loop_state
        offset = instant - section_index
        active = jnp.logical_and(offset >= 0, offset < micro_count)
        slot_index = jnp.clip(offset, 0, micro_count - 1)
        entering = pick_slot(start_stream, slot_index)
        current = jnp.where(section_index == 0, entering, received)

        def run_layer(operand):
            return forward_layer(
                operand,
                query_gain[0],
                gate_logit[0],
                pick_slot(key_blocks, slot_index),
                pick_slot(value_blocks, slot_index),
                pick_slot(same_document, slot_index),
                head_count,
            )

        def skip_layer(operand):
            return jnp.zeros_like(operand)

        produced = lax.cond(active, run_layer, skip_layer, current)
        stored = lax.dynamic_update_index_in_dim(
            stored, jnp.where(active, current, pick_slot(stored, slot_index)), slot_index, 0
        )
        results = lax.dynamic_update_index_in_dim(
            results, jnp.where(active, produced, pick_slot(results, slot_index)), slot_index, 0
        )
        received = from_behind(produced, "section", 1)
        return (received, stored, results)

    received, stored, results = lax.fori_loop(
        0, section_count + micro_count - 1, advance, (empty_slot, buffers, buffers)
    )
    grad_parts = []
    for micro_batch_index in range(micro_count):
        grad_parts.append(
            backward_layer(
                stored[micro_batch_index],
                query_gain[0],
                key_blocks[micro_batch_index],
                value_blocks[micro_batch_index],
                same_document[micro_batch_index],
                cotangent[0, micro_batch_index],
                head_count,
            )
        )
    grad_local = jnp.concatenate(grad_parts, axis=0)
    gradient_total = lax.psum(grad_local.astype(jnp.bfloat16), "shard").astype(jnp.float32)
    key_portion = norm_gradient(
        unscaled_sum[:, :key_width], key_norm_gain[0], gradient_total[:, :key_width], keyval_heads
    )
    raw_grad = jnp.concatenate([key_portion, gradient_total[:, key_width:]], axis=1).astype(
        jnp.bfloat16
    )
    image_part = lax.dot_general(
        raw_grad, weights, (((1,), (1,)), ((), ())), preferred_element_type=jnp.float32
    )
    image_part = image_part.reshape(micro_count, image_count, weights.shape[0])
    image_grad = lax.psum_scatter(
        image_part.astype(jnp.bfloat16), "section", scatter_dimension=1, tiled=True
    ).astype(jnp.float32)
    return (results[None], image_grad)


def solution(mesh):
    placed = (
        P("group", "section", "shard"),
        P("section", "shard", None),
        P("section", None),
        P("section", None),
        P("section", None),
        P("group", "shard", None),
        P("group", "shard"),
        P("group", None),
        P("section", "group", "shard", None),
    )
    return jax.shard_map(
        per_device,
        mesh=mesh,
        in_specs=placed,
        out_specs=(P("section", "group", "shard", None), P("group", "section", "shard")),
        check_vma=False,
    )
```

profile of v0, /device:TPU:0, one launch (start us, length us, event | category | flops | bytes accessed | tf_op | source)
XLA Modules:
  0.0 331.5 jit_solution(16020866220513936231)
XLA Ops:
  7.2 10.3 %all_gather.3 = bf16[2,96,2048]{2,1,0:T(8,128)(2,1)S(1)} all-gather(bf16[2,24,2048]{2,1,0:T(8,128)(2,1)} %param.13), channel_id=1, replica_groups=mesh['group'=2,'section'=4,'shard'=4] {'section'}, dimensions={1}, use_global_device_ids=true | all-gather | bytes 983040 | tf_op jit(solution)/shard_map/all_gather | solution.py:124
  17.5 4.1 %fusion.32 = f32[192,1024]{1,0:T(8,128)} fusion(bf16[192,2048]{1,0:T(8,128)(2,1)S(1)} %bitcast.241, bf16[1,2048,1024]{2,1,0:T(8,128)(2,1)} %param.14), kind=kOutput, calls=%fused_computation.45 | convolution fusion | flops 805306368 | bytes 5767168 | tf_op jit(solution)/shard_map/dot_general | solution.py:129
  21.7 1.6 convert_element_type.51
  25.9 40.5 %all-reduce.3.cloned.1.call-done = f32[192,1024]{1,0:T(8,128)} async-done(((f32[192,1024]{1,0:T(8,128)}), f32[192,1024]{1,0:T(8,128)}) %all-reduce.3.cloned.1.call-update) | async-done | bytes 786448 | tf_op jit(solution)/shard_map/psum | solution.py:128
  72.0 1.5 broadcast_in_dim.73
  73.5 1.5 broadcast_in_dim.73.clone
  75.1 114.1 %while.19 = (s32[]{:T(128)}, f32[64,4096]{1,0:T(8,128)S(1)}, f32[2,64,4096]{2,1,0:T(8,128)}, f32[2,64,4096]{2,1,0:T(8,128)}, s32[]{:T(128)}, /*index=5*/pred[]{:...) while((s32[]{:T(128)}, f32[64,4096]{1,0:T(8,128)S(1)}, ...), condition=%wide.region_8.9_spmd.clone, body=%wide.region_2.8_spmd.clone.sunk | while | flops 155396288 | bytes 48204588 | solution.py:174
  78.2 10.9 %conditional.3 = (f32[64,4096]{1,0:T(8,128)S(1)}) conditional(s32[]{:T(128)} %convert_element_type.85, () %tuple.71, (f32[1,32]{1,0:T(1,128)}, s32[]{:T(128)}, bf16[2,96,4,128]{3,1,2,0:T(8,128)(2,1)}, s32[2,64]{1,0:T(2,128)S(1)}, bf16[2,96,4,128]{3,1,2,0:T(8,128)(2,1)}, /*index=5*/f32[64,4096]{1,0:T(8,128)S(1)}, f32[1,4096]{1,0:T(1,128)}, ...), branch_computations={%region_3.3_spmd, %region_4.7_spmd} | conditional | flops 154609856 | bytes 23036878 | solution.py:164
  81.8 4.7 %convolution_bitcast_fusion = f32[64,4,8,128]{3,0,2,1:T(8,128)} fusion(f32[4,8,64]{2,1,0:T(8,128)S(1)} %fusion.82, f32[4,8,64,96]{3,2,1,0:T(8,128)S(1)} %fusion.6, bf16[2,96,4,128]{3,1,2,0:T(8,128)(2,1)S(1)} %copy-done.17, s32[]{:T(128)S(6)} %select_n.60), kind=kOutput, calls=%fused_computation.3 | convolution fusion | flops 50923616 | bytes 3260420 | tf_op jit(solution)/shard_map/while/body/eval_jaxpr/cond/branch_1_fun/kgti,ikd->tkgd/dot_general | solution.py:58
  86.5 1.8 copy.83
  96.0 10.9 %conditional.3 = (f32[64,4096]{1,0:T(8,128)S(1)}) conditional(s32[]{:T(128)} %convert_element_type.85, () %tuple.71, (f32[1,32]{1,0:T(1,128)}, s32[]{:T(128)}, bf16[2,96,4,128]{3,1,2,0:T(8,128)(2,1)}, s32[2,64]{1,0:T(2,128)S(1)}, bf16[2,96,4,128]{3,1,2,0:T(8,128)(2,1)}, /*index=5*/f32[64,4096]{1,0:T(8,128)S(1)}, f32[1,4096]{1,0:T(1,128)}, ...), branch_computations={%region_3.3_spmd, %region_4.7_spmd} | conditional | flops 154609856 | bytes 23036878 | solution.py:164
  99.7 4.7 %convolution_bitcast_fusion = f32[64,4,8,128]{3,0,2,1:T(8,128)} fusion(f32[4,8,64]{2,1,0:T(8,128)S(1)} %fusion.82, f32[4,8,64,96]{3,2,1,0:T(8,128)S(1)} %fusion.6, bf16[2,96,4,128]{3,1,2,0:T(8,128)(2,1)S(1)} %copy-done.17, s32[]{:T(128)S(6)} %select_n.60), kind=kOutput, calls=%fused_computation.3 | convolution fusion | flops 50923616 | bytes 3260420 | tf_op jit(solution)/shard_map/while/body/eval_jaxpr/cond/branch_1_fun/kgti,ikd->tkgd/dot_general | solution.py:58
  104.3 1.8 copy.83
  107.0 2.6 collective-permute-start
  115.1 22.1 %collective-permute-start = (f32[64,4096]{1,0:T(8,128)S(1)}, f32[64,4096]{1,0:T(8,128)S(1)}, u32[]{:S(2)}, u32[]{:S(2)}) collective-permute-start(f32[64,4096]{1,0:T(8,128)S(1)} %get-tuple-element.551), channel_id=1, source_target_pairs={{0,4},{4,8},{8,12},{1,5},{5,9},{9,13},{2,6},{6,10},{10,14},{3,7},{... | collective-permute-start | bytes 3145736 | tf_op jit(solution)/shard_map/while/body/eval_jaxpr/ppermute | solution.py:14
  142.8 13.7 %collective-permute-start = (f32[64,4096]{1,0:T(8,128)S(1)}, f32[64,4096]{1,0:T(8,128)S(1)}, u32[]{:S(2)}, u32[]{:S(2)}) collective-permute-start(f32[64,4096]{1,0:T(8,128)S(1)} %get-tuple-element.551), channel_id=1, source_target_pairs={{0,4},{4,8},{8,12},{1,5},{5,9},{9,13},{2,6},{6,10},{10,14},{3,7},{... | collective-permute-start | bytes 3145736 | tf_op jit(solution)/shard_map/while/body/eval_jaxpr/ppermute | solution.py:14
  162.1 24.6 %collective-permute-start = (f32[64,4096]{1,0:T(8,128)S(1)}, f32[64,4096]{1,0:T(8,128)S(1)}, u32[]{:S(2)}, u32[]{:S(2)}) collective-permute-start(f32[64,4096]{1,0:T(8,128)S(1)} %get-tuple-element.551), channel_id=1, source_target_pairs={{0,4},{4,8},{8,12},{1,5},{5,9},{9,13},{2,6},{6,10},{10,14},{3,7},{... | collective-permute-start | bytes 3145736 | tf_op jit(solution)/shard_map/while/body/eval_jaxpr/ppermute | solution.py:14
  189.1 3.2 multiply_bitcast_fusion.2
  193.9 1.5 fusion.44
  195.4 2.0 fusion.90
  203.3 1.6 squeeze.54
  204.9 1.7 fusion.42
  207.6 1.9 fusion.89
  209.5 1.6 squeeze.55
  211.1 5.7 %fusion.52 = bf16[4,12,8,128]{3,2,1,0:T(8,128)(2,1)} fusion(bf16[64,4,8,128]{3,2,1,0:T(8,128)(2,1)} %bitcast.251, f32[4,8,64]{2,1,0:T(8,128)} %get-tuple-element.412, f32[4,8,64,96]{3,2,1,0:T(8,128)S(1)} %fusion.44), kind=kOutput, calls=%fused_computation.71 | convolution fusion | flops 50972768 | bytes 1417216 | tf_op jit(solution)/shard_map/kgti,tkgd->ikd/dot_general | solution.py:82
  216.7 3.4 %multiply_reduce_fusion.1 = (f32[4,8,64]{2,1,0:T(8,128)}, f32[4,8,64,96]{3,2,1,0:T(8,128)}) fusion(f32[4,8,64,96]{3,2,1,0:T(8,128)} %get-tuple-element.413, f32[4,8,64]{2,1,0:T(8,128)} %get-tuple-element.412, bf16[64,4,8,128]{3,2,1,0:T(8,128)(2,1)} %bitcast.252, bf16[96,4,128,1]{2,1,0,3:T(4,128)(2,1)} %bitcast.257), kind=kOutput, calls=%fused_computation.84 | convolution fusion | flops 50919424 | bytes 2211840 | tf_op jit(solution)/shard_map/tkgd,ikd->kgti/dot_general | solution.py:85
  220.1 6.8 %fusion.53 = bf16[4,12,8,128]{3,2,1,0:T(8,128)(2,1)} fusion(f32[4,8,64,96]{3,2,1,0:T(8,128)} %get-tuple-element.415, f32[4,8,64]{2,1,0:T(8,128)} %get-tuple-element.414, f32[64,4,8,128]{3,2,1,0:T(8,128)S(1)} %bitcast.232, f32[4,8,128]{2,1,0:T(8,128)S(1)} %bitcast.246, f32[64,4,8]{0,2,1:T(8,128)} %rsqrt_bitcast_fusion.1, ...), kind=kOutput, calls=%fused_computation.72 | convolution fusion | flops 52201568 | bytes 2760704 | tf_op jit(solution)/shard_map/kgti,tkgd->ikd/dot_general | solution.py:92
  227.9 5.8 %fusion.51 = bf16[4,12,8,128]{3,2,1,0:T(8,128)(2,1)S(1)} fusion(bf16[64,4,8,128]{3,2,1,0:T(8,128)(2,1)} %bitcast.249, f32[4,8,64]{2,1,0:T(8,128)} %get-tuple-element.408, f32[4,8,64,96]{3,2,1,0:T(8,128)} %copy-done.3), kind=kOutput, calls=%fused_computation.70 | convolution fusion | flops 50972768 | bytes 1417216 | tf_op jit(solution)/shard_map/kgti,tkgd->ikd/dot_general | solution.py:82
  235.2 7.0 %fusion.54 = bf16[4,12,8,128]{3,2,1,0:T(8,128)(2,1)S(1)} fusion(f32[4,8,64,96]{3,2,1,0:T(8,128)} %get-tuple-element.411, f32[4,8,64]{2,1,0:T(8,128)S(1)} %get-tuple-element.410, f32[64,4,8,128]{3,2,1,0:T(8,128)S(1)} %bitcast.234, f32[64,4,8]{0,2,1:T(8,128)S(1)} %copy-done.19, f32[4,8,128]{2,1,0:T(8,128)S(1)} %bitcast.247, f32[4,8,64]{2,1,0:T(8,128)S(1)} %copy-done.22, ...), kind=kOutput, calls=%fused_computation.73 | convolution fusion | flops 52201568 | bytes 2760704 | tf_op jit(solution)/shard_map/kgti,tkgd->ikd/dot_general | solution.py:92
  243.1 49.1 %all-reduce.5.cloned.1.call-done = bf16[192,1024]{1,0:T(8,128)(2,1)} async-done(((bf16[192,1024]{1,0:T(8,128)(2,1)}), bf16[192,1024]{1,0:T(8,128)(2,1)}) %all-reduce.5.cloned.1.call-update) | async-done | bytes 393232 | tf_op jit(solution)/shard_map/psum | solution.py:191
  294.3 3.7 %fusion.34 = bf16[2,96,2048]{2,1,0:T(8,128)(2,1)S(1)} fusion(bf16[1,2048,1024]{2,1,0:T(8,128)(2,1)} %param.14, bf16[2,96,512]{2,1,0:T(8,128)(2,1)S(1)} %bitcast.256, bf16[2,96,512]{2,1,0:T(8,128)(2,1)S(1)} %bitcast.255), kind=kOutput, calls=%fused_computation.47 | convolution fusion | flops 806486016 | bytes 5373952 | tf_op jit(solution)/shard_map/dot_general | solution.py:198
  300.0 23.0 %reduce-scatter.4.cloned.1.call-done = bf16[24,4096]{1,0:T(8,128)(2,1)} async-done(((bf16[96,4096]{1,0:T(8,128)(2,1)}), bf16[24,4096]{1,0:T(8,128)(2,1)}) %reduce-scatter.4.cloned.1.call-update) | async-done | bytes 196624
  (184 shorter events, 63.5 us)
Async XLA Ops:
  7.2 59.2 %all-reduce.3.cloned.1.call-start = ((), (), s32[]{:S(2)}) async-start(), calls=%async_computation.1 | async-start | bytes 1572864 | tf_op jit(solution)/shard_map/psum | solution.py:128
  17.5 4.2 %copy-start.8 = (bf16[2,64,4096]{2,1,0:T(8,128)(2,1)S(1)}, bf16[2,64,4096]{2,1,0:T(8,128)(2,1)}, u32[]{:S(2)}) copy-start(bf16[2,64,4096]{2,1,0:T(8,128)(2,1)} %param.18) | copy-start | bytes 3145732
  21.6 1.7 copy-start.9
  21.6 270.6 %all-reduce.5.cloned.1.call-start = ((), (), s32[]{:S(2)}) async-start(), calls=%async_computation.2 | async-start | bytes 786432 | tf_op jit(solution)/shard_map/psum | solution.py:191
  23.3 1.9 copy-start.23
  23.3 1.9 copy-start.24
  24.3 44.7 %copy-start.20 = (f32[1,512]{1,0:T(1,128)S(1)}, f32[1,512]{1,0:T(1,128)}, u32[]{:S(2)}) copy-start(f32[1,512]{1,0:T(1,128)} %param.16) | copy-start | bytes 6148
  66.3 2.6 copy-start.1
  75.1 1.9 copy-start
  80.2 1.7 copy-start.17
  81.8 6.5 %copy-start.25 = (f32[1,32]{1,0:T(1,128)S(1)}, f32[1,32]{1,0:T(1,128)}, u32[]{:S(2)}) copy-start(f32[1,32]{1,0:T(1,128)} %get-tuple-element.242) | copy-start | bytes 388 | tf_op jit(solution)/shard_map/while/body/eval_jaxpr/cond
  89.2 3.8 %collective-permute-start = (f32[64,4096]{1,0:T(8,128)S(1)}, f32[64,4096]{1,0:T(8,128)S(1)}, u32[]{:S(2)}, u32[]{:S(2)}) collective-permute-start(f32[64,4096]{1,0:T(8,128)S(1)} %get-tuple-element.551), channel_id=1, source_target_pairs={{0,4},{4,8},{8,12},{1,5},{5,9},{9,13},{2,6},{6,10},{10,14},{3,7},{... | collective-permute-start | bytes 3145736 | tf_op jit(solution)/shard_map/while/body/eval_jaxpr/ppermute | solution.py:14
  92.9 1.9 copy-start
  98.0 1.7 copy-start.17
  99.7 6.5 %copy-start.25 = (f32[1,32]{1,0:T(1,128)S(1)}, f32[1,32]{1,0:T(1,128)}, u32[]{:S(2)}) copy-start(f32[1,32]{1,0:T(1,128)} %get-tuple-element.242) | copy-start | bytes 388 | tf_op jit(solution)/shard_map/while/body/eval_jaxpr/cond
  107.0 5.0 %collective-permute-start = (f32[64,4096]{1,0:T(8,128)S(1)}, f32[64,4096]{1,0:T(8,128)S(1)}, u32[]{:S(2)}, u32[]{:S(2)}) collective-permute-start(f32[64,4096]{1,0:T(8,128)S(1)} %get-tuple-element.551), channel_id=1, source_target_pairs={{0,4},{4,8},{8,12},{1,5},{5,9},{9,13},{2,6},{6,10},{10,14},{3,7},{... | collective-permute-start | bytes 3145736 | tf_op jit(solution)/shard_map/while/body/eval_jaxpr/ppermute | solution.py:14
  112.0 1.9 copy-start
  115.1 24.5 %collective-permute-start = (f32[64,4096]{1,0:T(8,128)S(1)}, f32[64,4096]{1,0:T(8,128)S(1)}, u32[]{:S(2)}, u32[]{:S(2)}) collective-permute-start(f32[64,4096]{1,0:T(8,128)S(1)} %get-tuple-element.551), channel_id=1, source_target_pairs={{0,4},{4,8},{8,12},{1,5},{5,9},{9,13},{2,6},{6,10},{10,14},{3,7},{... | collective-permute-start | bytes 3145736 | tf_op jit(solution)/shard_map/while/body/eval_jaxpr/ppermute | solution.py:14
  139.7 1.9 copy-start
  142.8 16.1 %collective-permute-start = (f32[64,4096]{1,0:T(8,128)S(1)}, f32[64,4096]{1,0:T(8,128)S(1)}, u32[]{:S(2)}, u32[]{:S(2)}) collective-permute-start(f32[64,4096]{1,0:T(8,128)S(1)} %get-tuple-element.551), channel_id=1, source_target_pairs={{0,4},{4,8},{8,12},{1,5},{5,9},{9,13},{2,6},{6,10},{10,14},{3,7},{... | collective-permute-start | bytes 3145736 | tf_op jit(solution)/shard_map/while/body/eval_jaxpr/ppermute | solution.py:14
  159.0 1.9 copy-start
  162.1 27.0 %collective-permute-start = (f32[64,4096]{1,0:T(8,128)S(1)}, f32[64,4096]{1,0:T(8,128)S(1)}, u32[]{:S(2)}, u32[]{:S(2)}) collective-permute-start(f32[64,4096]{1,0:T(8,128)S(1)} %get-tuple-element.551), channel_id=1, source_target_pairs={{0,4},{4,8},{8,12},{1,5},{5,9},{9,13},{2,6},{6,10},{10,14},{3,7},{... | collective-permute-start | bytes 3145736 | tf_op jit(solution)/shard_map/while/body/eval_jaxpr/ppermute | solution.py:14
  193.9 3.5 %copy-start.15 = (bf16[96,512]{1,0:T(8,128)(2,1)S(1)}, bf16[96,512]{1,0:T(8,128)(2,1)}, u32[]{:S(2)}) copy-start(bf16[96,512]{1,0:T(8,128)(2,1)} %get-tuple-element.402) | copy-start | bytes 294916
  227.9 5.8 %copy-start.10 = (f32[4,8,64,96]{3,2,1,0:T(8,128)S(1)}, f32[4,8,64,96]{3,2,1,0:T(8,128)}, u32[]{:S(2)}) copy-start(f32[4,8,64,96]{3,2,1,0:T(8,128)} %get-tuple-element.409) | copy-start | bytes 2359300
  227.9 5.8 %copy-start.14 = (bf16[8,8,32,128]{3,2,1,0:T(8,128)(2,1)S(1)}, bf16[8,8,32,128]{3,2,1,0:T(8,128)(2,1)}, u32[]{:S(2)}) copy-start(bf16[8,8,32,128]{3,2,1,0:T(8,128)(2,1)} %copy.136) | copy-start | bytes 1572868
  227.9 5.8 %copy-start.18 = (bf16[96,4,128]{2,1,0:T(4,128)(2,1)S(1)}, bf16[96,4,128]{2,1,0:T(4,128)(2,1)}, u32[]{:S(2)}) copy-start(bf16[96,4,128]{2,1,0:T(4,128)(2,1)} %squeeze.55) | copy-start | bytes 294916
  227.9 5.8 %copy-start.22 = (f32[4,8,64]{2,1,0:T(8,128)S(1)}, f32[4,8,64]{2,1,0:T(8,128)}, u32[]{:S(2)}) copy-start(f32[4,8,64]{2,1,0:T(8,128)} %get-tuple-element.408) | copy-start | bytes 24580
  242.2 51.3 %copy-start.21 = (f32[1,512]{1,0:T(1,128)S(1)}, f32[1,512]{1,0:T(1,128)}, u32[]{:S(2)}) copy-start(f32[1,512]{1,0:T(1,128)} %param.16) | copy-start | bytes 6148
  242.2 51.9 %copy-start.2 = (f32[192,1024]{1,0:T(8,128)S(1)}, f32[192,1024]{1,0:T(8,128)}, u32[]{:S(2)}) copy-start(f32[192,1024]{1,0:T(8,128)} %all-reduce.3.cloned.1.call-done) | copy-start | bytes 2359300
  242.3 51.9 %copy-start.5 = (f32[192,4,128]{2,1,0:T(4,128)S(1)}, f32[192,4,128]{2,1,0:T(4,128)}, u32[]{:S(2)}) copy-start(f32[192,4,128]{2,1,0:T(4,128)} %copy-done.4) | copy-start | bytes 1179652
  243.1 79.9 %reduce-scatter.4.cloned.1.call-start = ((), (), s32[]{:S(2)}) async-start(), calls=%async_computation.3 | async-start | bytes 983040
  292.3 1.9 copy-start.11
  (11 other events, 11.3 us)
Sparse Core Ops, SparseCore 0:
  21.8 44.5 all-reduce.2
  243.2 49.0 all-reduce.4
  300.2 22.8 reduce-scatter.3
where the time goes:
time: 333 us; the launch traced here: 331 us
  waiting for transfers between devices  113 us (34%)
  starting transfers between devices  64.4 us (19%)
  matrix products  52.8 us (16%)
  local copies, waits for them, and re-layouts  46.4 us (14%)
  other arithmetic  30.3 us (9%)
  between operations  14.1 us (4%)
  blocking collectives  10.3 us (3%)
    ppermute x5, starting transfers between devices, from_behind(): return lax.ppermute(block, axis, route)  64.3 us
    psum x1, waiting for transfers between devices, per_device(): lax.psum(grad_local.astype(jnp.bfloat16), 'shard').astype(jnp.float32)  49.1 us
    psum x1, waiting for transfers between devices, per_device(): lax.psum(jnp.dot(flat_rows, weights, preferred_element_type=jnp.float32),...  40.5 us
    unnamed x4, waiting for transfers between devices  23 us
    dot_general x2, matrix products, backward_layer(): jnp.einsum('kgti,tkgd->ikd', score_grad, query_matrix, preferred_element_...  13.9 us
    dynamic_slice x14, local copies, waits for them, and re-layouts, pick_slot(): return lax.dynamic_index_in_dim(array_in, slot_index, 0, keepdims=False)  13.7 us
    dot_general x2, matrix products, backward_layer(): jnp.einsum('kgti,tkgd->ikd', probability, incoming_gradient, preferred_el...  11.5 us
    unnamed x52, local copies, waits for them, and re-layouts  11.3 us
  transfers between devices with their start and end apart: 8, of which 3 were waited for; matrix products, arithmetic and copies ran while one was open for 5% of the time, Pallas kernels for 0%

commit v1 on v0

v1 whole, which is shorter than its diff:
```python
import math

import jax
import jax.numpy as jnp
from jax import lax
from jax.sharding import PartitionSpec as P

epsilon = 1e-05


def head_normalize(input_rows, gain_row, head_count):
    shaped = input_rows.reshape(input_rows.shape[:-1] + (head_count, -1))
    factor = lax.rsqrt(jnp.mean(shaped * shaped, axis=-1, keepdims=True) + epsilon)
    gain = gain_row.reshape((1,) * (shaped.ndim - 2) + (head_count, -1))
    return (shaped * factor * gain).reshape(input_rows.shape)


def norm_gradient(input_rows, gain_row, incoming_gradient, head_count):
    shaped = input_rows.reshape(input_rows.shape[0], head_count, -1)
    scaled = incoming_gradient.reshape(input_rows.shape[0], head_count, -1) * gain_row.reshape(
        1, head_count, -1
    )
    factor = lax.rsqrt(jnp.mean(shaped * shaped, axis=-1, keepdims=True) + epsilon)
    inner_mean = jnp.mean(shaped * scaled, axis=-1, keepdims=True)
    result = factor * scaled - shaped * factor * factor * factor * inner_mean
    return result.reshape(input_rows.shape[0], -1)


def attend_scores(current, gain_row, key_block, same_document, head_count):
    micro, token_count = current.shape[0], current.shape[1]
    keyval_heads = key_block.shape[2]
    head_dim = key_block.shape[3]
    query_groups = head_count // keyval_heads
    query_matrix = head_normalize(current, gain_row, head_count).astype(jnp.bfloat16)
    query_matrix = query_matrix.reshape(micro, token_count, keyval_heads, query_groups, head_dim)
    scores = jnp.einsum(
        "mtkgd,mikd->mkgti", query_matrix, key_block, preferred_element_type=jnp.float32
    ) * (1.0 / math.sqrt(head_dim))
    scores = jnp.where(same_document[:, None, None], scores, -jnp.inf)
    row_max = jnp.max(scores, axis=-1, keepdims=True)
    powered = jnp.exp(scores - row_max)
    exact_probs = powered / jnp.sum(powered, axis=-1, keepdims=True)
    return (query_matrix, exact_probs)


def forward_layer(current, gain_row, gate_row, key_block, value_block, same_document, head_count):
    micro, token_count = current.shape[0], current.shape[1]
    head_dim = value_block.shape[3]
    query_matrix, exact_probs = attend_scores(
        current, gain_row, key_block, same_document, head_count
    )
    probability = exact_probs.astype(jnp.bfloat16)
    attended = jnp.einsum(
        "mkgti,mikd->mtkgd", probability, value_block, preferred_element_type=jnp.float32
    )
    updated = current.reshape(micro, token_count, head_count, head_dim)
    updated = updated + jnp.tanh(gate_row)[None, None, :, None] * attended.reshape(
        micro, token_count, head_count, head_dim
    )
    return updated.reshape(current.shape)


def backward_layer(current, gain_row, key_block, value_block, same_document, upstream, head_count):
    micro, token_count = current.shape[0], current.shape[1]
    image_count = key_block.shape[1]
    keyval_heads = key_block.shape[2]
    head_dim = key_block.shape[3]
    query_matrix, exact_probs = attend_scores(
        current, gain_row, key_block, same_document, head_count
    )
    probability = exact_probs.astype(jnp.bfloat16)
    incoming_gradient = upstream.reshape(
        micro, token_count, keyval_heads, head_count // keyval_heads, head_dim
    )
    value_grad = jnp.einsum(
        "mkgti,mtkgd->mikd", probability, incoming_gradient, preferred_element_type=jnp.float32
    )
    prob_grad = jnp.einsum(
        "mtkgd,mikd->mkgti", incoming_gradient, value_block, preferred_element_type=jnp.float32
    )
    score_grad = exact_probs * (
        prob_grad - jnp.sum(exact_probs * prob_grad, axis=-1, keepdims=True)
    )
    score_grad = score_grad.astype(jnp.bfloat16)
    key_grad = jnp.einsum(
        "mkgti,mtkgd->mikd", score_grad, query_matrix, preferred_element_type=jnp.float32
    ) * (1.0 / math.sqrt(head_dim))
    return jnp.concatenate(
        [
            key_grad.reshape(micro * image_count, -1),
            value_grad.reshape(micro * image_count, -1),
        ],
        axis=1,
    )


def per_device(
    image_tokens,
    keyval_weight,
    query_gain,
    key_norm_gain,
    gate_logit,
    text_queries,
    text_document,
    image_document,
    cotangent,
):
    section_count = lax.axis_size("section")
    section_index = lax.axis_index("section")
    micro_count = text_queries.shape[0]
    head_count = gate_logit.shape[1]
    key_width = key_norm_gain.shape[1]
    head_dim = query_gain.shape[1] // head_count
    keyval_heads = key_width // head_dim
    weights = keyval_weight[0]

    layer_params = lax.all_gather(
        jnp.concatenate([query_gain, gate_logit], axis=1), "section", axis=0, tiled=True
    )
    gains_all = layer_params[:, : query_gain.shape[1]]
    gates_all = layer_params[:, query_gain.shape[1] :]

    gathered = lax.all_gather(image_tokens, "section", axis=1, tiled=True)
    image_count = gathered.shape[1]
    total_rows = micro_count * image_count
    flat_rows = gathered.reshape(total_rows, gathered.shape[2])
    partial = jnp.dot(flat_rows, weights, preferred_element_type=jnp.float32)
    raw_rows = lax.psum_scatter(partial, "shard", scatter_dimension=0, tiled=True)
    key_rows = head_normalize(raw_rows[:, :key_width], key_norm_gain[0], keyval_heads)
    keyval_rows = jnp.concatenate(
        [key_rows.astype(jnp.bfloat16), raw_rows[:, key_width:].astype(jnp.bfloat16)], axis=1
    )
    keyval_all = lax.all_gather(keyval_rows, ("section", "shard"), axis=0, tiled=True)
    keyval_all = keyval_all.reshape(
        section_count, micro_count, image_count, 2, keyval_heads, head_dim
    )

    same_document = text_document[:, :, None] == image_document[:, None, :]
    stream = text_queries.astype(jnp.float32)
    streams = [stream]
    for layer in range(section_count):
        stream = forward_layer(
            stream,
            gains_all[layer],
            gates_all[layer],
            keyval_all[layer, :, :, 0],
            keyval_all[layer, :, :, 1],
            same_document,
            head_count,
        )
        streams.append(stream)
    entering = lax.select_n(section_index, *streams[:-1])
    leaving = lax.select_n(section_index, *streams[1:])

    own = lax.dynamic_index_in_dim(keyval_all, section_index, 0, keepdims=False)
    grad_local = backward_layer(
        entering,
        query_gain[0],
        own[:, :, 0],
        own[:, :, 1],
        same_document,
        cotangent[0],
        head_count,
    )
    grad_rows = lax.psum_scatter(
        grad_local.astype(jnp.bfloat16), "shard", scatter_dimension=0, tiled=True
    ).astype(jnp.float32)
    key_portion = norm_gradient(
        raw_rows[:, :key_width], key_norm_gain[0], grad_rows[:, :key_width], keyval_heads
    )
    raw_grad_rows = jnp.concatenate([key_portion, grad_rows[:, key_width:]], axis=1).astype(
        jnp.bfloat16
    )
    raw_grad = lax.all_gather(raw_grad_rows, "shard", axis=0, tiled=True)
    image_part = lax.dot_general(
        raw_grad, weights, (((1,), (1,)), ((), ())), preferred_element_type=jnp.float32
    )
    image_part = image_part.reshape(micro_count, image_count, weights.shape[0])
    image_grad = lax.psum_scatter(
        image_part.astype(jnp.bfloat16), "section", scatter_dimension=1, tiled=True
    ).astype(jnp.float32)
    return (leaving[None], image_grad)


def solution(mesh):
    placed = (
        P("group", "section", "shard"),
        P("section", "shard", None),
        P("section", None),
        P("section", None),
        P("section", None),
        P("group", "shard", None),
        P("group", "shard"),
        P("group", None),
        P("section", "group", "shard", None),
    )
    return jax.shard_map(
        per_device,
        mesh=mesh,
        in_specs=placed,
        out_specs=(P("section", "group", "shard", None), P("group", "section", "shard")),
        check_vma=False,
    )
```

time: 333 us -> 336 us (level)
  starting transfers between devices: 64.4 us -> 0.5 us
  other arithmetic: 30.3 us -> 56.2 us
  waiting for transfers between devices: 113 us -> 90 us
  local copies, waits for them, and re-layouts: 46.4 us -> 69.1 us
  blocking collectives: 10.3 us -> 30.5 us
  matrix products: 52.8 us -> 71.6 us
    psum x2 -> x0, waiting for transfers between devices: 89.6 us -> none  [the longest x1 49.1 us: per_device(): lax.psum(grad_local.astype(jnp.bfloat16), 'shard').astype(jnp.float32)]
    ppermute x5 -> x0, starting transfers between devices: 64.3 us -> none  [from_behind(): return lax.ppermute(block, axis, route)]
    reduce_scatter x0 -> x2, waiting for transfers between devices: none -> 37.6 us  [the longest x1 19.6 us: per_device(): lax.psum_scatter(grad_local.astype(jnp.bfloat16), 'shard', scatter_dimens...]
    all_gather x0 -> x1, waiting for transfers between devices: none -> 31.2 us  [per_device(): lax.all_gather(keyval_rows, ('section', 'shard'), axis=0, tiled=True)]
    mul x5 -> x14, local copies, waits for them, and re-layouts: 1.06 us -> 23.2 us  [the longest x11 22.9 us: head_normalize(): return (shaped * factor * gain).reshape(input_rows.shape)]
    sub x2 -> x1, other arithmetic: 3.92 us -> 24.8 us  [backward_layer(): prob_grad - jnp.sum(exact_probs * prob_grad, axis=-1, keepdims=True)]
    all_gather x0 -> x2, blocking collectives: none -> 20.3 us  [the longest x1 15 us: per_device(): raw_grad = lax.all_gather(raw_grad_rows, 'shard', axis=0, tiled=True)]
    reshape x5 -> x6, local copies, waits for them, and re-layouts: 1.21 us -> 13.7 us  [the longest x4 10.9 us: forward_layer(): attended.reshape(micro, token_count, head_count, head_dim)]
  transfers between devices with their start and end apart: 8 -> 4, of which waited for: 3 -> 4; matrix products, arithmetic and copies ran while one was open for 5% -> 3% of each run, Pallas kernels for 0% -> 0%
where the time goes in v1:
time: 336 us; the launch traced here: 333 us
  waiting for transfers between devices  90 us (27%)
  matrix products  71.6 us (21%)
  local copies, waits for them, and re-layouts  69.1 us (21%)
  other arithmetic  56.2 us (17%)
  blocking collectives  30.5 us (9%)
  between operations  14.8 us (4%)
    dot_general x4, matrix products, forward_layer(): jnp.einsum('mkgti,mikd->mtkgd', probability, value_block, preferred_eleme...  38.7 us
    all_gather x1, waiting for transfers between devices, per_device(): lax.all_gather(keyval_rows, ('section', 'shard'), axis=0, tiled=True)  31.2 us
    sub x1, other arithmetic, backward_layer(): prob_grad - jnp.sum(exact_probs * prob_grad, axis=-1, keepdims=True)  24.8 us
    mul x11, local copies, waits for them, and re-layouts, head_normalize(): return (shaped * factor * gain).reshape(input_rows.shape)  22.9 us
    unnamed x5, waiting for transfers between devices  21.2 us
    reduce_scatter x1, waiting for transfers between devices, per_device(): lax.psum_scatter(grad_local.astype(jnp.bfloat16), 'shard', scatter_dimens...  19.6 us
    reduce_scatter x1, waiting for transfers between devices, per_device(): lax.psum_scatter(partial, 'shard', scatter_dimension=0, tiled=True)  18 us
    all_gather x1, blocking collectives, per_device(): raw_grad = lax.all_gather(raw_grad_rows, 'shard', axis=0, tiled=True)  15 us
  transfers between devices with their start and end apart: 4, of which 4 were waited for; matrix products, arithmetic and copies ran while one was open for 3% of the time, Pallas kernels for 0%

profile of v1, /device:TPU:0, one launch (start us, length us, event | category | flops | bytes accessed | tf_op | source)
XLA Modules:
  0.0 332.6 jit_solution(9642624859613352983)
XLA Ops:
  7.2 10.3 %all_gather.13 = bf16[2,96,2048]{2,1,0:T(8,128)(2,1)S(1)} all-gather(bf16[2,24,2048]{2,1,0:T(8,128)(2,1)} %param.9), channel_id=1, replica_groups=mesh['group'=2,'section'=4,'shard'=4] {'section'}, dimensions={1}, use_global_device_ids=true | all-gather | bytes 983040 | tf_op jit(solution)/shard_map/all_gather | solution.py:123
  17.5 4.2 %fusion.8 = f32[192,1024]{1,0:T(8,128)} fusion(bf16[192,2048]{1,0:T(8,128)(2,1)S(1)} %bitcast.381, bf16[1,2048,1024]{2,1,0:T(8,128)(2,1)} %param.10), kind=kOutput, calls=%fused_computation.8 | convolution fusion | flops 805306368 | bytes 5767168 | tf_op jit(solution)/shard_map/dot_general | solution.py:127
  21.8 5.3 %all-gather = f32[4,1,4128]{2,1,0:T(1,128)S(1)} all-gather(f32[1,1,4128]{2,1,0:T(1,128)S(1)} %maximum_bitcast_fusion), channel_id=1, replica_groups=mesh['group'=2,'section'=4,'shard'=4] {'section'}, dimensions={0}, use_global_device_ids=true | all-gather | bytes 82560 | tf_op jit(solution)/shard_map/all_gather | solution.py:117
  28.0 18.0 %reduce-scatter.6.cloned.1.call-done = f32[48,1024]{1,0:T(8,128)} async-done(((f32[192,1024]{1,0:T(8,128)}), f32[48,1024]{1,0:T(8,128)}) %reduce-scatter.6.cloned.1.call-update) | async-done | bytes 196624 | tf_op jit(solution)/shard_map/reduce_scatter | solution.py:128
  58.3 31.2 %all-gather.3.cloned.1.call-done = bf16[768,1024]{1,0:T(8,128)(2,1)} async-done(((bf16[48,1024]{1,0:T(8,128)(2,1)}), bf16[768,1024]{1,0:T(8,128)(2,1)}) %all-gather.3.cloned.1.call-update) | async-done | bytes 1572880 | tf_op jit(solution)/shard_map/all_gather | solution.py:133
  89.5 2.8 reshape.232
  96.6 8.7 %fusion.51 = f32[2,4,128,8,64]{2,4,3,1,0:T(8,128)S(1)} fusion(f32[2,4,8,64]{3,2,1,0:T(8,128)S(1)} %fusion.149, bf16[1,2,96,1,4,128]{5,4,3,2,1,0:T(4,128)(2,1)} %get-tuple-element.13, pred[2,64,96]{2,1,0:T(8,128)(4,1)S(1)} %broadcast_compare_fusion, bf16[2,64,4,8,128]{4,3,2,1,0:T(8,128)(2,1)} %bitcast.385, bf16[1,2,96,1,4,128]{5,4,3,2,1,0:T(4,128)(2,1)} %copy-done.12), kind=kOutput, calls=%fused_computation.87 | convolution fusion | flops 203296864 | bytes 3567616 | tf_op jit(solution)/shard_map/mkgti,mikd->mtkgd/dot_general | solution.py:53
  109.0 2.8 mul.355
  119.9 2.7 fusion.152
  122.7 10.0 %fusion.52 = f32[2,4,128,8,64]{2,4,3,1,0:T(8,128)} fusion(f32[2,4,8,64]{3,2,1,0:T(8,128)S(1)} %fusion.152, bf16[1,2,96,1,4,128]{5,4,3,2,1,0:T(4,128)(2,1)} %get-tuple-element.11, pred[2,64,96]{2,1,0:T(8,128)(4,1)S(1)} %copy-done.19, bf16[2,64,4,8,128]{4,3,2,1,0:T(8,128)(2,1)} %bitcast.392, bf16[1,2,96,1,4,128]{5,4,3,2,1,0:T(4,128)(2,1)} %get-tuple-element.10), kind=kOutput, calls=%fused_computation.88 | convolution fusion | flops 203296864 | bytes 3567616 | tf_op jit(solution)/shard_map/mkgti,mikd->mtkgd/dot_general | solution.py:53
  132.7 2.9 multiply_reduce_fusion.1
  137.7 2.7 mul.370
  140.4 4.2 %copy.124 = f32[2,64,4,8,128]{4,3,2,1,0:T(8,128)} copy(f32[2,64,4,8,128]{4,1,3,2,0:T(8,128)} %bitcast.363) | data formatting | bytes 4194304 | tf_op jit(solution)/shard_map/mkgti,mikd->mtkgd/transpose | solution.py:53
  144.6 2.9 reshape.238
  147.5 2.9 multiply_convert_fusion.2
  154.3 10.0 %fusion.53 = f32[2,4,128,8,64]{2,4,3,1,0:T(8,128)} fusion(f32[2,4,8,64]{3,2,1,0:T(8,128)S(1)} %fusion.155, bf16[1,2,96,1,4,128]{5,4,3,2,1,0:T(4,128)(2,1)} %get-tuple-element.9, pred[2,64,96]{2,1,0:T(8,128)(4,1)S(1)} %copy-done.20, bf16[2,64,4,8,128]{4,3,2,1,0:T(8,128)(2,1)} %bitcast.394, bf16[1,2,96,1,4,128]{5,4,3,2,1,0:T(4,128)(2,1)} %get-tuple-element.8), kind=kOutput, calls=%fused_computation.89 | convolution fusion | flops 203296864 | bytes 3567616 | tf_op jit(solution)/shard_map/mkgti,mikd->mtkgd/dot_general | solution.py:53
  164.4 3.6 %multiply_reduce_fusion = f32[2,64,32]{1,2,0:T(8,128)S(1)} fusion(f32[2,64,32,128]{3,1,2,0:T(8,128)} %bitcast.366, f32[32]{0:T(128)S(1)} %copy-done.25, f32[2,64,32,128]{3,1,2,0:T(8,128)} %get-tuple-element.5, f32[2,64,32,128]{3,1,2,0:T(8,128)} %bitcast.364, f32[32]{0:T(128)S(1)} %copy-done.23), kind=kLoop, calls=%fused_computation.33 | loop fusion | flops 3141632 | bytes 6308096 | tf_op jit(solution)/shard_map/reduce_sum | solution.py:13
  170.0 2.8 mul.385
  172.8 4.1 %copy.129 = f32[2,64,4,8,128]{4,3,2,1,0:T(8,128)} copy(f32[2,64,4,8,128]{4,1,3,2,0:T(8,128)} %bitcast.367) | data formatting | bytes 4194304 | tf_op jit(solution)/shard_map/mkgti,mikd->mtkgd/transpose | solution.py:53
  176.9 2.9 reshape.241
  179.8 3.7 %multiply_convert_fusion.1 = bf16[2,64,4096]{2,1,0:T(8,128)(2,1)S(1)} fusion(f32[2,64,4096]{2,1,0:T(8,128)} %mul.385, f32[4096]{0:T(1024)S(1)} %bitcast.409, f32[2,64,4096]{2,1,0:T(8,128)} %reshape.241, f32[4096]{0:T(1024)S(1)} %get-tuple-element.28, f32[2,64,4096]{2,1,0:T(8,128)} %reshape.238, f32[4096]{0:T(1024)S(1)} %get-tuple-element.29, ...), kind=kLoop, calls=%fused_computation.32 | loop fusion | flops 5242880 | bytes 10551296 | tf_op jit(solution)/shard_map/convert_element_type | solution.py:34
  187.5 9.9 %convolution_bitcast_fusion = f32[2,64,4,8,128]{4,1,3,2,0:T(8,128)} fusion(f32[2,4,8,64]{3,2,1,0:T(8,128)S(1)} %fusion.158, bf16[1,2,96,1,4,128]{5,4,3,2,1,0:T(4,128)(2,1)S(1)} %get-tuple-element.7, pred[2,64,96]{2,1,0:T(8,128)(4,1)S(1)} %copy-done.20, bf16[2,64,4,8,128]{4,3,2,1,0:T(8,128)(2,1)} %bitcast.390, ...), kind=kOutput, calls=%fused_computation.55 | convolution fusion | flops 203296864 | bytes 3567616 | tf_op jit(solution)/shard_map/mkgti,mikd->mtkgd/dot_general | solution.py:53
  197.4 4.1 %copy.134 = f32[2,64,4,8,128]{4,3,2,1,0:T(8,128)} copy(f32[2,64,4,8,128]{4,1,3,2,0:T(8,128)} %convolution_bitcast_fusion) | data formatting | bytes 4194304 | tf_op jit(solution)/shard_map/mkgti,mikd->mtkgd/transpose | solution.py:53
  204.3 6.0 %fusion.146 = (f32[2,64,4096]{2,1,0:T(8,128)S(1)}, f32[2,64,4096]{2,1,0:T(8,128)}, f32[1,2,64,4096]{3,2,1,0:T(8,128)}) fusion(f32[2,64,4096]{2,1,0:T(8,128)} %reshape.241, f32[4096]{0:T(1024)S(1)} %get-tuple-element.28, f32[2,64,4096]{2,1,0:T(8,128)} %reshape.238, f32[4096]{0:T(1024)S(1)} %get-tuple-element.29, pred[]{:T(512)S(6)} %select_n.69, ...), kind=kLoop, calls=%fused_computation.168 | loop fusion | flops 8388608 | bytes 15794179 | tf_op jit(solution)/shard_map/mul | solution.py:13
  213.5 3.1 mul.396
  220.2 2.9 fusion.161
  223.6 9.8 %fusion.27 = bf16[2,96,4,128]{3,1,2,0:T(8,128)(2,1)} fusion(bf16[2,64,4,8,128]{4,3,2,1,0:T(8,128)(2,1)S(1)} %bitcast.373, f32[2,4,8,64]{3,2,1,0:T(8,128)} %get-tuple-element.25, pred[2,64,96]{2,1,0:T(8,128)(4,1)S(1)} %copy-done.20, bf16[2,64,4,8,128]{4,3,2,1,0:T(8,128)(2,1)} %bitcast.387, bf16[2,96,2,4,128]{4,1,3,0,2:T(8,128)(2,1)S(1)} %bitcast.397), kind=kOutput, calls=%fused_computation.62 | convolution fusion | flops 203395168 | bytes 2523136 | tf_op jit(solution)/shard_map/mkgti,mtkgd->mikd/dot_general | solution.py:75
  233.4 24.8 %fusion.17 = bf16[2,4,8,64,96]{4,3,2,1,0:T(8,128)(2,1)S(1)} fusion(f32[2,4,96,64,8]{2,3,4,1,0:T(8,128)S(1)} %fusion.61, f32[2,4,8,64,96]{4,3,2,1,0:T(8,128)} %get-tuple-element.26, f32[2,4,8,64]{3,2,1,0:T(8,128)} %get-tuple-element.25), kind=kOutput, calls=%fused_computation.21 | output fusion | flops 2363487 | bytes 3948544 | tf_op jit(solution)/shard_map/sub | solution.py:82
  260.4 19.6 %reduce-scatter.8.cloned.1.call-done = bf16[48,1024]{1,0:T(8,128)(2,1)} async-done(((bf16[192,1024]{1,0:T(8,128)(2,1)}), bf16[48,1024]{1,0:T(8,128)(2,1)}) %reduce-scatter.8.cloned.1.call-update) | async-done | bytes 98320 | tf_op jit(solution)/shard_map/reduce_scatter | solution.py:165
  282.0 15.0 %all_gather.15 = bf16[192,1024]{1,0:T(8,128)(2,1)S(1)} all-gather(bf16[48,1024]{1,0:T(8,128)(2,1)S(1)} %pad_maximum_fusion.2), channel_id=1, replica_groups=mesh['group'=2,'section'=4,'shard'=4] {'shard'}, dimensions={0}, use_global_device_ids=true | all-gather | bytes 491520 | tf_op jit(solution)/shard_map/all_gather | solution.py:174
  297.0 3.7 %fusion.10 = bf16[2,96,2048]{2,1,0:T(8,128)(2,1)S(1)} fusion(bf16[2,96,1024]{2,1,0:T(8,128)(2,1)S(1)} %bitcast.382, bf16[1,2048,1024]{2,1,0:T(8,128)(2,1)} %param.10), kind=kOutput, calls=%fused_computation.11 | convolution fusion | flops 805699584 | bytes 5373952 | tf_op jit(solution)/shard_map/dot_general | solution.py:175
  302.7 21.2 %reduce-scatter.10.cloned.1.call-done = bf16[24,4096]{1,0:T(8,128)(2,1)} async-done(((bf16[96,4096]{1,0:T(8,128)(2,1)}), bf16[24,4096]{1,0:T(8,128)(2,1)}) %reduce-scatter.10.cloned.1.call-update) | async-done | bytes 196624
  (140 shorter events, 59.0 us)
Async XLA Ops:
  7.2 38.9 %reduce-scatter.6.cloned.1.call-start = ((), (), s32[]{:S(2)}) async-start(), calls=%async_computation.3 | async-start | bytes 983040 | tf_op jit(solution)/shard_map/reduce_scatter | solution.py:128
  17.5 4.3 %copy-start.14 = (f32[1,4096]{1,0:T(1,128)S(1)}, f32[1,4096]{1,0:T(1,128)}, u32[]{:S(2)}) copy-start(f32[1,4096]{1,0:T(1,128)} %param.11) | copy-start | bytes 49156
  17.5 4.3 %copy-start.28 = (f32[1,32]{1,0:T(1,128)S(1)}, f32[1,32]{1,0:T(1,128)}, u32[]{:S(2)}) copy-start(f32[1,32]{1,0:T(1,128)} %param.13) | copy-start | bytes 388
  17.5 9.6 %copy-start = (bf16[2,64,4096]{2,1,0:T(8,128)(2,1)S(1)}, bf16[2,64,4096]{2,1,0:T(8,128)(2,1)}, u32[]{:S(2)}) copy-start(bf16[2,64,4096]{2,1,0:T(8,128)(2,1)} %param.14) | copy-start | bytes 3145732
  21.7 67.8 %all-gather.3.cloned.1.call-start = ((), (), s32[]{:S(2)}) async-start(), calls=%async_computation.4 | async-start | bytes 1671168 | tf_op jit(solution)/shard_map/all_gather | solution.py:133
  27.3 21.4 %copy-start.16 = (f32[1,512]{1,0:T(1,128)S(1)}, f32[1,512]{1,0:T(1,128)}, u32[]{:S(2)}) copy-start(f32[1,512]{1,0:T(1,128)} %param.12) | copy-start | bytes 6148
  47.0 3.9 %copy-start.7 = (f32[48,4,128]{2,1,0:T(4,128)}, f32[48,4,128]{2,1,0:T(4,128)S(1)}, u32[]{:S(2)}) copy-start(f32[48,4,128]{2,1,0:T(4,128)S(1)} %reshape.231) | copy-start | bytes 294916
  50.4 229.6 %reduce-scatter.8.cloned.1.call-start = ((), (), s32[]{:S(2)}) async-start(), calls=%async_computation.5 | async-start | bytes 491520 | tf_op jit(solution)/shard_map/reduce_scatter | solution.py:165
  55.5 1.3 copy-start.4
  55.5 2.5 copy-start.26
  55.5 2.5 copy-start.27
  58.0 35.9 %copy-start.21 = (f32[32]{0:T(128)}, f32[32]{0:T(128)S(1)}, u32[]{:S(2)}) copy-start(f32[32]{0:T(128)S(1)} %get-tuple-element.19) | copy-start | bytes 388
  58.0 35.9 %copy-start.24 = (f32[32]{0:T(128)}, f32[32]{0:T(128)S(1)}, u32[]{:S(2)}) copy-start(f32[32]{0:T(128)S(1)} %get-tuple-element.18) | copy-start | bytes 388
  58.1 38.5 %copy-start.18 = (pred[2,64,96]{2,1,0:T(8,128)(4,1)}, pred[2,64,96]{2,1,0:T(8,128)(4,1)S(1)}, u32[]{:S(2)}) copy-start(pred[2,64,96]{2,1,0:T(8,128)(4,1)S(1)} %broadcast_compare_fusion) | copy-start | bytes 36868
  92.3 4.3 %copy-start.2 = (bf16[4,2,96,2,4,128]{5,4,3,2,1,0:T(4,128)(2,1)}, bf16[4,2,96,2,4,128]{5,4,3,2,1,0:T(4,128)(2,1)S(1)}, u32[]{:S(2)}) copy-start(bf16[4,2,96,2,4,128]{5,4,3,2,1,0:T(4,128)(2,1)S(1)} %reshape.232) | copy-start | bytes 4718596
  93.9 2.7 copy-start.12
  114.3 2.4 copy-start.15
  118.7 1.2 copy-start.19
  122.7 10.0 %copy-start.22 = (f32[32]{0:T(128)S(1)}, f32[32]{0:T(128)}, u32[]{:S(2)}) copy-start(f32[32]{0:T(128)} %copy-done.21) | copy-start | bytes 388
  150.3 1.2 copy-start.20
  154.3 10.1 %copy-start.23 = (f32[32]{0:T(128)S(1)}, f32[32]{0:T(128)}, u32[]{:S(2)}) copy-start(f32[32]{0:T(128)} %copy-done.21) | copy-start | bytes 388
  154.3 10.1 %copy-start.25 = (f32[32]{0:T(128)S(1)}, f32[32]{0:T(128)}, u32[]{:S(2)}) copy-start(f32[32]{0:T(128)} %copy-done.24) | copy-start | bytes 388
  213.4 3.2 copy-start.1
  218.7 4.4 %copy-start.5 = (bf16[16,8,32,128]{3,2,1,0:T(8,128)(2,1)}, bf16[16,8,32,128]{3,2,1,0:T(8,128)(2,1)S(1)}, u32[]{:S(2)}) copy-start(bf16[16,8,32,128]{3,2,1,0:T(8,128)(2,1)S(1)} %copy.176) | copy-start | bytes 3145732
  220.2 2.9 copy-start.3
  233.4 24.8 %copy-start.6 = (bf16[16,8,32,128]{3,2,1,0:T(8,128)(2,1)S(1)}, bf16[16,8,32,128]{3,2,1,0:T(8,128)(2,1)}, u32[]{:S(2)}) copy-start(bf16[16,8,32,128]{3,2,1,0:T(8,128)(2,1)} %copy-done.5) | copy-start | bytes 3145732
  258.2 1.1 copy-start.13
  259.1 21.7 %copy-start.8 = (f32[48,4,128]{2,1,0:T(4,128)S(1)}, f32[48,4,128]{2,1,0:T(4,128)}, u32[]{:S(2)}) copy-start(f32[48,4,128]{2,1,0:T(4,128)} %copy-done.7) | copy-start | bytes 294916
  259.2 21.7 %copy-start.17 = (f32[1,512]{1,0:T(1,128)S(1)}, f32[1,512]{1,0:T(1,128)}, u32[]{:S(2)}) copy-start(f32[1,512]{1,0:T(1,128)} %param.12) | copy-start | bytes 6148
  259.2 22.0 %copy-start.10 = (f32[48,4,128]{2,1,0:T(4,128)S(1)}, f32[48,4,128]{2,1,0:T(4,128)}, u32[]{:S(2)}) copy-start(f32[48,4,128]{2,1,0:T(4,128)} %copy-done.9) | copy-start | bytes 294916
  259.2 22.0 %copy-start.11 = (f32[48,1024]{1,0:T(8,128)S(1)}, f32[48,1024]{1,0:T(8,128)}, u32[]{:S(2)}) copy-start(f32[48,1024]{1,0:T(8,128)} %reduce-scatter.6.cloned.1.call-done) | copy-start | bytes 589828
  260.3 63.6 %reduce-scatter.10.cloned.1.call-start = ((), (), s32[]{:S(2)}) async-start(), calls=%async_computation.6 | async-start | bytes 983040
  (1 other events, 0.6 us)
Sparse Core Ops, SparseCore 0:
  21.8 24.1 reduce-scatter.5
  50.5 38.9 all-gather.2
  260.4 19.4 reduce-scatter.7
  302.9 21.0 reduce-scatter.9

commit v2 on v1

v2 whole, which is shorter than its diff:
```python
import functools
import math

import jax
import jax.numpy as jnp
from jax import lax
from jax.experimental import pallas as pl
from jax.experimental.pallas import tpu as pltpu
from jax.sharding import PartitionSpec as P

epsilon = 1e-05


def head_normalize(input_rows, gain_row, head_count):
    shaped = input_rows.reshape(input_rows.shape[:-1] + (head_count, -1))
    factor = lax.rsqrt(jnp.mean(shaped * shaped, axis=-1, keepdims=True) + epsilon)
    gain = gain_row.reshape((1,) * (shaped.ndim - 2) + (head_count, -1))
    return (shaped * factor * gain).reshape(input_rows.shape)


def norm_gradient(input_rows, gain_row, incoming_gradient, head_count):
    shaped = input_rows.reshape(input_rows.shape[0], head_count, -1)
    scaled = incoming_gradient.reshape(input_rows.shape[0], head_count, -1) * gain_row.reshape(
        1, head_count, -1
    )
    factor = lax.rsqrt(jnp.mean(shaped * shaped, axis=-1, keepdims=True) + epsilon)
    inner_mean = jnp.mean(shaped * scaled, axis=-1, keepdims=True)
    result = factor * scaled - shaped * factor * factor * factor * inner_mean
    return result.reshape(input_rows.shape[0], -1)


def attention_kernel(
    section_ref,
    gates_ref,
    queries_ref,
    keyval_ref,
    gains_ref,
    mask_ref,
    mask_t_ref,
    cot_ref,
    out_ref,
    grad_ref,
    *,
    head_count,
    keyval_heads,
):
    token_count, query_width = out_ref.shape
    head_dim = query_width // head_count
    key_width = keyval_heads * head_dim
    groups = head_count // keyval_heads
    scale = 1.0 / math.sqrt(head_dim)
    section = section_ref[0]
    out_ref[...] = queries_ref[...].astype(jnp.float32)

    def head_cols(h):
        return pl.ds(h * head_dim, head_dim)

    def queries_of(layer, k):
        parts = []
        for g in range(groups):
            h = k * groups + g
            x = out_ref[:, head_cols(h)]
            mean_square = jnp.sum(x * x, axis=-1, keepdims=True) * (1.0 / head_dim)
            gain = gains_ref[layer, :, head_cols(h)]
            parts.append((x * lax.rsqrt(mean_square + epsilon) * gain).astype(jnp.bfloat16))
        return jnp.concatenate(parts, axis=0)

    def forward(layer):
        same = mask_ref[...] > 0.5
        for k in range(keyval_heads):
            query = queries_of(layer, k)
            key = keyval_ref[layer, :, head_cols(k)]
            value = keyval_ref[layer, :, pl.ds(key_width + k * head_dim, head_dim)]
            scores = lax.dot_general(
                query, key, (((1,), (1,)), ((), ())), preferred_element_type=jnp.float32
            ) * scale
            scores = jnp.where(same, scores, -jnp.inf)
            powered = jnp.exp(scores - jnp.max(scores, axis=-1, keepdims=True))
            probs = powered / jnp.sum(powered, axis=-1, keepdims=True)
            attended = jnp.dot(
                probs.astype(jnp.bfloat16), value, preferred_element_type=jnp.float32
            )
            for g in range(groups):
                h = k * groups + g
                rows = attended[g * token_count : (g + 1) * token_count]
                out_ref[:, head_cols(h)] = out_ref[:, head_cols(h)] + gates_ref[layer, h] * rows

    def layer_step(layer, carry):
        forward(layer)
        return carry

    lax.fori_loop(0, section, layer_step, 0)

    same_t = mask_t_ref[...] > 0.5
    for k in range(keyval_heads):
        query = queries_of(section, k)
        key = keyval_ref[section, :, head_cols(k)]
        value = keyval_ref[section, :, pl.ds(key_width + k * head_dim, head_dim)]
        scores_t = lax.dot_general(
            key, query, (((1,), (1,)), ((), ())), preferred_element_type=jnp.float32
        ) * scale
        scores_t = jnp.where(same_t, scores_t, -jnp.inf)
        powered = jnp.exp(scores_t - jnp.max(scores_t, axis=0, keepdims=True))
        probs_t = powered / jnp.sum(powered, axis=0, keepdims=True)
        upstream = jnp.concatenate(
            [cot_ref[:, head_cols(k * groups + g)] for g in range(groups)], axis=0
        )
        value_grad = jnp.dot(
            probs_t.astype(jnp.bfloat16), upstream, preferred_element_type=jnp.float32
        )
        prob_grad_t = lax.dot_general(
            value, upstream, (((1,), (1,)), ((), ())), preferred_element_type=jnp.float32
        )
        inner = jnp.sum(probs_t * prob_grad_t, axis=0, keepdims=True)
        score_grad_t = (probs_t * (prob_grad_t - inner)).astype(jnp.bfloat16)
        key_grad = jnp.dot(score_grad_t, query, preferred_element_type=jnp.float32) * scale
        grad_ref[:, head_cols(k)] = key_grad
        grad_ref[:, pl.ds(key_width + k * head_dim, head_dim)] = value_grad

    forward(section)


def attention_layers(section_index, gates, queries, keyval_all, gains, same_document, upstream):
    layer_count, micro_count, image_count, pair_width = keyval_all.shape
    token_count, query_width = queries.shape[1], queries.shape[2]
    head_count = gates.shape[1]
    head_dim = query_width // head_count
    keyval_heads = pair_width // 2 // head_dim
    groups = head_count // keyval_heads
    mask = jnp.tile(same_document.astype(jnp.float32), (1, groups, 1))
    mask_t = jnp.swapaxes(mask, 1, 2)
    smem = pl.BlockSpec(memory_space=pltpu.SMEM)
    flops = 2 * micro_count * (layer_count + 3) * head_count * token_count * image_count * head_dim * 2
    return pl.pallas_call(
        functools.partial(attention_kernel, head_count=head_count, keyval_heads=keyval_heads),
        grid=(micro_count,),
        in_specs=[
            smem,
            smem,
            pl.BlockSpec((None, token_count, query_width), lambda m: (m, 0, 0)),
            pl.BlockSpec((layer_count, None, image_count, pair_width), lambda m: (0, m, 0, 0)),
            pl.BlockSpec((layer_count, 1, query_width), lambda m: (0, 0, 0)),
            pl.BlockSpec((None, groups * token_count, image_count), lambda m: (m, 0, 0)),
            pl.BlockSpec((None, image_count, groups * token_count), lambda m: (m, 0, 0)),
            pl.BlockSpec((None, token_count, query_width), lambda m: (m, 0, 0)),
        ],
        out_specs=[
            pl.BlockSpec((None, token_count, query_width), lambda m: (m, 0, 0)),
            pl.BlockSpec((None, image_count, pair_width), lambda m: (m, 0, 0)),
        ],
        out_shape=[
            jax.ShapeDtypeStruct((micro_count, token_count, query_width), jnp.float32),
            jax.ShapeDtypeStruct((micro_count, image_count, pair_width), jnp.float32),
        ],
        compiler_params=pltpu.CompilerParams(dimension_semantics=("arbitrary",)),
        cost_estimate=pl.CostEstimate(
            flops=flops,
            transcendentals=micro_count * (layer_count + 1) * head_count * token_count * image_count,
            bytes_accessed=keyval_all.size * 2 + queries.size * 8 + upstream.size * 2,
        ),
    )(
        jnp.reshape(section_index, (1,)).astype(jnp.int32),
        gates,
        queries,
        keyval_all,
        gains.reshape(layer_count, 1, query_width),
        mask,
        mask_t,
        upstream,
    )


def per_device(
    image_tokens,
    keyval_weight,
    query_gain,
    key_norm_gain,
    gate_logit,
    text_queries,
    text_document,
    image_document,
    cotangent,
):
    section_count = lax.axis_size("section")
    section_index = lax.axis_index("section")
    micro_count = text_queries.shape[0]
    head_count = gate_logit.shape[1]
    key_width = key_norm_gain.shape[1]
    head_dim = query_gain.shape[1] // head_count
    keyval_heads = key_width // head_dim
    weights = keyval_weight[0]

    layer_params = lax.all_gather(
        jnp.concatenate([query_gain, gate_logit], axis=1), "section", axis=0, tiled=True
    )
    gains_all = layer_params[:, : query_gain.shape[1]]
    gates_all = layer_params[:, query_gain.shape[1] :]

    gathered = lax.all_gather(image_tokens, "section", axis=1, tiled=True)
    image_count = gathered.shape[1]
    total_rows = micro_count * image_count
    flat_rows = gathered.reshape(total_rows, gathered.shape[2])
    partial = jnp.dot(flat_rows, weights, preferred_element_type=jnp.float32)
    raw_rows = lax.psum_scatter(partial, "shard", scatter_dimension=0, tiled=True)
    key_rows = head_normalize(raw_rows[:, :key_width], key_norm_gain[0], keyval_heads)
    keyval_rows = jnp.concatenate(
        [key_rows.astype(jnp.bfloat16), raw_rows[:, key_width:].astype(jnp.bfloat16)], axis=1
    )
    keyval_all = lax.all_gather(keyval_rows, ("section", "shard"), axis=0, tiled=True)

    same_document = text_document[:, :, None] == image_document[:, None, :]
    leaving, grad_local = attention_layers(
        section_index,
        jnp.tanh(gates_all),
        text_queries,
        keyval_all.reshape(section_count, micro_count, image_count, 2 * key_width),
        gains_all,
        same_document,
        cotangent[0],
    )
    grad_local = grad_local.reshape(total_rows, 2 * key_width)
    grad_rows = lax.psum_scatter(
        grad_local.astype(jnp.bfloat16), "shard", scatter_dimension=0, tiled=True
    ).astype(jnp.float32)
    key_portion = norm_gradient(
        raw_rows[:, :key_width], key_norm_gain[0], grad_rows[:, :key_width], keyval_heads
    )
    raw_grad_rows = jnp.concatenate([key_portion, grad_rows[:, key_width:]], axis=1).astype(
        jnp.bfloat16
    )
    raw_grad = lax.all_gather(raw_grad_rows, "shard", axis=0, tiled=True)
    image_part = lax.dot_general(
        raw_grad, weights, (((1,), (1,)), ((), ())), preferred_element_type=jnp.float32
    )
    image_part = image_part.reshape(micro_count, image_count, weights.shape[0])
    image_grad = lax.psum_scatter(
        image_part.astype(jnp.bfloat16), "section", scatter_dimension=1, tiled=True
    ).astype(jnp.float32)
    return (leaving[None], image_grad)


def solution(mesh):
    placed = (
        P("group", "section", "shard"),
        P("section", "shard", None),
        P("section", None),
        P("section", None),
        P("section", None),
        P("group", "shard", None),
        P("group", "shard"),
        P("group", None),
        P("section", "group", "shard", None),
    )
    return jax.shard_map(
        per_device,
        mesh=mesh,
        in_specs=placed,
        out_specs=(P("section", "group", "shard", None), P("group", "section", "shard")),
        check_vma=False,
    )
```

time: 336 us -> 178 us (0.53)
  matrix products: 71.6 us -> 7.87 us
  local copies, waits for them, and re-layouts: 69.1 us -> 7.41 us
  other arithmetic: 56.2 us -> 6.35 us
  waiting for transfers between devices: 90 us -> 104 us
  Pallas kernels: 0 us -> 8.22 us
    dot_general x7 -> x0, matrix products: 49.9 us -> none  [the longest x4 38.7 us: forward_layer(): jnp.einsum('mkgti,mikd->mtkgd', probability, value_block, preferred_eleme...]
    sub x1 -> x0, other arithmetic: 24.8 us -> none  [backward_layer(): prob_grad - jnp.sum(exact_probs * prob_grad, axis=-1, keepdims=True)]
    mul x11 -> x1, local copies, waits for them, and re-layouts: 22.9 us -> 0.1 us  [head_normalize(): return (shaped * factor * gain).reshape(input_rows.shape)]
    transpose x5 -> x0, local copies, waits for them, and re-layouts: 15 us -> none  [the longest x4 14.9 us: forward_layer(): jnp.einsum('mkgti,mikd->mtkgd', probability, value_block, preferred_eleme...]
    sub x5 -> x0, matrix products: 13.8 us -> none  [attend_scores(): powered = jnp.exp(scores - row_max)]
    reshape x5 -> x1, local copies, waits for them, and re-layouts: 13.7 us -> 0.67 us  [attention_layers(): gains.reshape(layer_count, 1, query_width)]
    reduce_sum x6 -> x1, other arithmetic: 9.51 us -> 0.12 us  [head_normalize(): jnp.mean(shaped * shaped, axis=-1, keepdims=True) + epsilon]
    convert_element_type x5 -> x2, other arithmetic: 10.7 us -> 2.01 us  [the longest x1 1.93 us: per_device(): grad_local.astype(jnp.bfloat16)]
  transfers between devices with their start and end apart: 4 -> 4, of which waited for: 4 -> 4; matrix products, arithmetic and copies ran while one was open for 3% -> 1% of each run, Pallas kernels for 0% -> 0%
where the time goes in v2:
time: 178 us
  waiting for transfers between devices  104 us (58%)
  blocking collectives  30.3 us (17%)
  between operations  14 us (8%)
  Pallas kernels  8.22 us (5%)
  matrix products  7.87 us (4%)
  local copies, waits for them, and re-layouts  7.41 us (4%)
  other arithmetic  6.35 us (4%)
    all_gather x1, waiting for transfers between devices, per_device(): lax.all_gather(keyval_rows, ('section', 'shard'), axis=0, tiled=True)  31.4 us
    reduce_scatter x1, waiting for transfers between devices, per_device(): lax.psum_scatter(grad_local.astype(jnp.bfloat16), 'shard', scatter_dimens...  26.6 us
    reduce_scatter x1, waiting for transfers between devices, per_device(): lax.psum_scatter(partial, 'shard', scatter_dimension=0, tiled=True)  24.3 us
    unnamed x5, waiting for transfers between devices  21.2 us
    all_gather x1, blocking collectives, per_device(): raw_grad = lax.all_gather(raw_grad_rows, 'shard', axis=0, tiled=True)  14.8 us
    all_gather x1, blocking collectives, per_device(): gathered = lax.all_gather(image_tokens, 'section', axis=1, tiled=True)  10.3 us
    pallas_call x1, Pallas kernels, attention_layers(): pl.pallas_call(functools.partial(attention_kernel, head_count=head_count,...  8.22 us
    all_gather x1, blocking collectives, per_device(): lax.all_gather(jnp.concatenate([query_gain, gate_logit], axis=1), 'sectio...  5.25 us
  transfers between devices with their start and end apart: 4, of which 4 were waited for; matrix products, arithmetic and copies ran while one was open for 1% of the time, Pallas kernels for 0%

profile of v2, /device:TPU:0, one launch (start us, length us, event | category | flops | bytes accessed | tf_op | source)
XLA Modules:
  0.0 177.8 jit_solution(3605546235316228778)
XLA Ops:
  7.2 10.3 %all_gather.13 = bf16[2,96,2048]{2,1,0:T(8,128)(2,1)S(1)} all-gather(bf16[2,24,2048]{2,1,0:T(8,128)(2,1)} %param.9), channel_id=1, replica_groups=mesh['group'=2,'section'=4,'shard'=4] {'section'}, dimensions={1}, use_global_device_ids=true | all-gather | bytes 983040 | tf_op jit(solution)/shard_map/all_gather | solution.py:199
  17.5 4.1 %fusion.2 = f32[192,1024]{1,0:T(8,128)} fusion(bf16[192,2048]{1,0:T(8,128)(2,1)S(1)} %bitcast.46, bf16[1,2048,1024]{2,1,0:T(8,128)(2,1)} %param.10), kind=kOutput, calls=%fused_computation.2 | convolution fusion | flops 805306368 | bytes 5767168 | tf_op jit(solution)/shard_map/dot_general | solution.py:203
  21.6 0.0 all-gather.3.cloned.1.call-start
  21.7 24.3 %reduce-scatter.6.cloned.1.call-done = f32[48,1024]{1,0:T(8,128)} async-done(((f32[192,1024]{1,0:T(8,128)}), f32[48,1024]{1,0:T(8,128)}) %reduce-scatter.6.cloned.1.call-update) | async-done | bytes 196624 | tf_op jit(solution)/shard_map/reduce_scatter | solution.py:204
  46.0 0.9 slice.32
  46.9 0.1 multiply_reduce_fusion.1
  47.1 0.9 slice.47
  48.0 0.1 mul.80
  48.1 0.9 multiply_convert_fusion
  49.0 0.6 pad_maximum_fusion
  49.7 0.0 reduce-scatter.8.cloned.1.call-start
  49.8 5.3 %all-gather = f32[4,1,4128]{2,1,0:T(1,128)S(1)} all-gather(f32[1,1,4128]{2,1,0:T(1,128)S(1)} %maximum_bitcast_fusion), channel_id=1, replica_groups=mesh['group'=2,'section'=4,'shard'=4] {'section'}, dimensions={0}, use_global_device_ids=true | all-gather | bytes 82560 | tf_op jit(solution)/shard_map/all_gather | solution.py:193
  55.1 0.7 reshape.63.gains_ref
  55.7 0.1 compare_convert_fusion
  55.9 0.9 copy.13
  56.9 0.6 slice_tanh_fusion.gates_ref
  57.4 31.4 %all-gather.3.cloned.1.call-done = bf16[768,1024]{1,0:T(8,128)(2,1)} async-done(((bf16[48,1024]{1,0:T(8,128)(2,1)}), bf16[768,1024]{1,0:T(8,128)(2,1)}) %all-gather.3.cloned.1.call-update) | async-done | bytes 1572880 | tf_op jit(solution)/shard_map/all_gather | solution.py:209
  88.8 8.2 %shard_map.104 = (f32[2,64,4096]{2,1,0:T(8,128)}, f32[2,96,1024]{2,1,0:T(8,128)}) custom-call(s32[1]{0:T(128)} %bitcast.section_ref, f32[4,32]{1,0:T(4,128)} %slice_tanh_fusion.gates_ref, bf16[2,64,4096]{2,1,0:T(8,128)(2,1)} %queries_ref.1, bf16[4,2,96,1024]{3,2,1,0:T(8,128)(2,1)} %bitcast.61, f32[4,1,4096]{2,1,0:T(1,128)} %reshape.63.gains_ref, ...), custom_call_target="tpu_custom_call" | custom-call | flops 1409286144 | bytes 6815744 | tf_op jit(solution)/shard_map/pallas_call | solution.py:134
  97.0 1.9 %convert_element_type.27 = bf16[2,96,1024]{2,1,0:T(8,128)(2,1)} convert(f32[2,96,1024]{2,1,0:T(8,128)} %get-tuple-element.5) | non-fusion elementwise | flops 196608 | bytes 1179648 | tf_op jit(solution)/shard_map/convert_element_type | solution.py:223
  99.0 0.0 reduce-scatter.10.cloned.1.call-start
  99.0 26.6 %reduce-scatter.8.cloned.1.call-done = bf16[48,1024]{1,0:T(8,128)(2,1)} async-done(((bf16[192,1024]{1,0:T(8,128)(2,1)}), bf16[48,1024]{1,0:T(8,128)(2,1)}) %reduce-scatter.8.cloned.1.call-update) | async-done | bytes 98320 | tf_op jit(solution)/shard_map/reduce_scatter | solution.py:222
  125.7 0.8 slice_convert_fusion.1
  126.6 0.1 multiply_reduce_fusion
  126.7 0.1 mul.94
  126.8 0.8 fusion.9
  127.7 14.8 %all_gather.15 = bf16[192,1024]{1,0:T(8,128)(2,1)S(1)} all-gather(bf16[48,1024]{1,0:T(8,128)(2,1)S(1)} %pad_maximum_fusion.1), channel_id=1, replica_groups=mesh['group'=2,'section'=4,'shard'=4] {'shard'}, dimensions={0}, use_global_device_ids=true | all-gather | bytes 491520 | tf_op jit(solution)/shard_map/all_gather | solution.py:231
  142.5 3.7 %fusion.4 = bf16[2,96,2048]{2,1,0:T(8,128)(2,1)S(1)} fusion(bf16[2,96,1024]{2,1,0:T(8,128)(2,1)S(1)} %bitcast.50, bf16[1,2048,1024]{2,1,0:T(8,128)(2,1)} %param.10), kind=kOutput, calls=%fused_computation.4 | convolution fusion | flops 805699584 | bytes 5373952 | tf_op jit(solution)/shard_map/dot_general | solution.py:232
  146.2 0.8 copy.14
  147.0 1.2 copy.19
  148.2 21.2 %reduce-scatter.10.cloned.1.call-done = bf16[24,4096]{1,0:T(8,128)(2,1)} async-done(((bf16[96,4096]{1,0:T(8,128)(2,1)}), bf16[24,4096]{1,0:T(8,128)(2,1)}) %reduce-scatter.10.cloned.1.call-update) | async-done | bytes 196624
  169.4 1.1 reshape.69
  170.5 0.8 copy_convert_fusion
  (28 shorter events, 0.3 us)
Async XLA Ops:
  7.2 40.9 %copy-start.2 = (f32[1,512]{1,0:T(1,128)S(1)}, f32[1,512]{1,0:T(1,128)}, u32[]{:S(2)}) copy-start(f32[1,512]{1,0:T(1,128)} %param.12) | copy-start | bytes 6148
  7.2 38.8 %reduce-scatter.6.cloned.1.call-start = ((), (), s32[]{:S(2)}) async-start(), calls=%async_computation.3 | async-start | bytes 983040 | tf_op jit(solution)/shard_map/reduce_scatter | solution.py:204
  17.5 32.3 %copy-start.3 = (f32[1,4096]{1,0:T(1,128)S(1)}, f32[1,4096]{1,0:T(1,128)}, u32[]{:S(2)}) copy-start(f32[1,4096]{1,0:T(1,128)} %param.11) | copy-start | bytes 49156
  17.5 32.3 %copy-start.6 = (f32[1,32]{1,0:T(1,128)S(1)}, f32[1,32]{1,0:T(1,128)}, u32[]{:S(2)}) copy-start(f32[1,32]{1,0:T(1,128)} %param.13) | copy-start | bytes 388
  17.5 38.3 %copy-start.4 = (s32[2,96]{1,0:T(2,128)S(1)}, s32[2,96]{1,0:T(2,128)}, u32[]{:S(2)}) copy-start(s32[2,96]{1,0:T(2,128)} %param.16) | copy-start | bytes 2308
  17.5 38.3 %copy-start.5 = (s32[2,64]{1,0:T(2,128)S(1)}, s32[2,64]{1,0:T(2,128)}, u32[]{:S(2)}) copy-start(s32[2,64]{1,0:T(2,128)} %param.15) | copy-start | bytes 1540
  21.6 67.2 %all-gather.3.cloned.1.call-start = ((), (), s32[]{:S(2)}) async-start(), calls=%async_computation.4 | async-start | bytes 1671168 | tf_op jit(solution)/shard_map/all_gather | solution.py:209
  49.7 76.0 %reduce-scatter.8.cloned.1.call-start = ((), (), s32[]{:S(2)}) async-start(), calls=%async_computation.5 | async-start | bytes 491520 | tf_op jit(solution)/shard_map/reduce_scatter | solution.py:222
  55.9 32.9 %copy-start = (f32[2,8,64,96]{3,2,1,0:T(8,128)}, f32[2,8,64,96]{3,2,1,0:T(8,128)S(1)}, u32[]{:S(2)}) copy-start(f32[2,8,64,96]{3,2,1,0:T(8,128)S(1)} %tile.4) | copy-start | bytes 1179652
  55.9 70.9 %copy-start.1 = (f32[48,1024]{1,0:T(8,128)S(1)}, f32[48,1024]{1,0:T(8,128)}, u32[]{:S(2)}) copy-start(f32[48,1024]{1,0:T(8,128)} %reduce-scatter.6.cloned.1.call-done) | copy-start | bytes 589828
  99.0 70.4 %reduce-scatter.10.cloned.1.call-start = ((), (), s32[]{:S(2)}) async-start(), calls=%async_computation.6 | async-start | bytes 983040
Sparse Core Ops, SparseCore 0:
  21.8 24.1 reduce-scatter.5
  49.8 38.9 all-gather.2
  99.1 26.5 reduce-scatter.7
  148.3 21.0 reduce-scatter.9

commit v3 on v2

--- a/solution.py
+++ b/solution.py
@@ -170,6 +170,35 @@
     )
 
 
+def gather_blocks(block, axis):
+    count = lax.axis_size(axis)
+    if count > 8:
+        return lax.all_gather(block, axis, axis=0, tiled=False)
+    index = lax.axis_index(axis)
+    received = [block] + [
+        lax.ppermute(block, axis, [(i, (i + d) % count) for i in range(count)])
+        for d in range(1, count)
+    ]
+    stacked = jnp.stack(received)
+    return jnp.take(stacked, (index - jnp.arange(count)) % count, axis=0)
+
+
+def scatter_blocks(blocks, axis):
+    count = lax.axis_size(axis)
+    if count > 8:
+        return lax.psum_scatter(blocks, axis, scatter_dimension=0, tiled=True)[0].astype(
+            jnp.float32
+        )
+    index = lax.axis_index(axis)
+    total = lax.dynamic_index_in_dim(blocks, index, 0, keepdims=False).astype(jnp.float32)
+    for d in range(1, count):
+        part = lax.dynamic_index_in_dim(blocks, (index + d) % count, 0, keepdims=False)
+        total = total + lax.ppermute(
+            part, axis, [(i, (i + d) % count) for i in range(count)]
+        ).astype(jnp.float32)
+    return total
+
+
 def per_device(
     image_tokens,
     keyval_weight,
@@ -197,16 +226,20 @@
     gates_all = layer_params[:, query_gain.shape[1] :]
 
     gathered = lax.all_gather(image_tokens, "section", axis=1, tiled=True)
+    shard_count = lax.axis_size("shard")
     image_count = gathered.shape[1]
     total_rows = micro_count * image_count
     flat_rows = gathered.reshape(total_rows, gathered.shape[2])
     partial = jnp.dot(flat_rows, weights, preferred_element_type=jnp.float32)
-    raw_rows = lax.psum_scatter(partial, "shard", scatter_dimension=0, tiled=True)
+    raw_rows = scatter_blocks(
+        partial.reshape(shard_count, total_rows // shard_count, 2 * key_width), "shard"
+    )
     key_rows = head_normalize(raw_rows[:, :key_width], key_norm_gain[0], keyval_heads)
     keyval_rows = jnp.concatenate(
         [key_rows.astype(jnp.bfloat16), raw_rows[:, key_width:].astype(jnp.bfloat16)], axis=1
     )
-    keyval_all = lax.all_gather(keyval_rows, ("section", "shard"), axis=0, tiled=True)
+    keyval_own = gather_blocks(keyval_rows, "shard").reshape(total_rows, 2 * key_width)
+    keyval_all = gather_blocks(keyval_own, "section")
 
     same_document = text_document[:, :, None] == image_document[:, None, :]
     leaving, grad_local = attention_layers(
@@ -218,24 +251,32 @@
         same_document,
         cotangent[0],
     )
-    grad_local = grad_local.reshape(total_rows, 2 * key_width)
-    grad_rows = lax.psum_scatter(
-        grad_local.astype(jnp.bfloat16), "shard", scatter_dimension=0, tiled=True
-    ).astype(jnp.float32)
+    grad_rows = scatter_blocks(
+        grad_local.astype(jnp.bfloat16).reshape(
+            shard_count, total_rows // shard_count, 2 * key_width
+        ),
+        "shard",
+    )
     key_portion = norm_gradient(
         raw_rows[:, :key_width], key_norm_gain[0], grad_rows[:, :key_width], keyval_heads
     )
     raw_grad_rows = jnp.concatenate([key_portion, grad_rows[:, key_width:]], axis=1).astype(
         jnp.bfloat16
     )
-    raw_grad = lax.all_gather(raw_grad_rows, "shard", axis=0, tiled=True)
+    raw_grad = gather_blocks(raw_grad_rows, "shard").reshape(total_rows, 2 * key_width)
+    owned = image_count // section_count
+    raw_grad = (
+        raw_grad.reshape(micro_count, section_count, owned, 2 * key_width)
+        .transpose(1, 0, 2, 3)
+        .reshape(total_rows, 2 * key_width)
+    )
     image_part = lax.dot_general(
         raw_grad, weights, (((1,), (1,)), ((), ())), preferred_element_type=jnp.float32
     )
-    image_part = image_part.reshape(micro_count, image_count, weights.shape[0])
-    image_grad = lax.psum_scatter(
-        image_part.astype(jnp.bfloat16), "section", scatter_dimension=1, tiled=True
-    ).astype(jnp.float32)
+    image_part = image_part.astype(jnp.bfloat16).reshape(
+        section_count, micro_count, owned, weights.shape[0]
+    )
+    image_grad = scatter_blocks(image_part, "section")
     return (leaving[None], image_grad)
 
 

time: 178 us -> 121 us (0.68)
  waiting for transfers between devices: 104 us -> 46.1 us
  starting transfers between devices: 0.16 us -> 32 us
  blocking collectives: 30.3 us -> 15.5 us
  between operations: 14 us -> 1.05 us
  local copies, waits for them, and re-layouts: 7.41 us -> 4.57 us
    reduce_scatter x2 -> x0, waiting for transfers between devices: 50.9 us -> none  [the longest x1 26.6 us: per_device(): lax.psum_scatter(grad_local.astype(jnp.bfloat16), 'shard', scatter_dimens...]
    ppermute x0 -> x18, waiting for transfers between devices: none -> 46.1 us  [the longest x9 26.4 us: gather_blocks(): lax.ppermute(block, axis, [(i, (i + d) % count) for i in range(count)])]
    ppermute x0 -> x18, starting transfers between devices: none -> 32 us  [the longest x9 17.7 us: scatter_blocks(): lax.ppermute(part, axis, [(i, (i + d) % count) for i in range(count)])]
    all_gather x1 -> x0, waiting for transfers between devices: 31.4 us -> none  [per_device(): lax.all_gather(keyval_rows, ('section', 'shard'), axis=0, tiled=True)]
    unnamed x5 -> x0, waiting for transfers between devices: 21.2 us -> none
    all_gather x1 -> x0, blocking collectives: 14.8 us -> none  [per_device(): raw_grad = lax.all_gather(raw_grad_rows, 'shard', axis=0, tiled=True)]
    unnamed x18 -> x13, local copies, waits for them, and re-layouts: 3.08 us -> 0.05 us
    select_n x0 -> x5, other arithmetic: none -> 2.27 us  [gather_blocks(): return jnp.take(stacked, (index - jnp.arange(count)) % count, axis=0)]
  transfers between devices with their start and end apart: 4 -> 18, of which waited for: 4 -> 15; matrix products, arithmetic and copies ran while one was open for 1% -> 2% of each run, Pallas kernels for 0% -> 0%
where the time goes in v3:
time: 121 us; the launch traced here: 120 us
  waiting for transfers between devices  46.1 us (38%)
  starting transfers between devices  32 us (26%)
  blocking collectives  15.5 us (13%)
  Pallas kernels  8.2 us (7%)
  matrix products  6.93 us (6%)
  other arithmetic  5.66 us (5%)
  local copies, waits for them, and re-layouts  4.57 us (4%)
    ppermute x9, waiting for transfers between devices, gather_blocks(): lax.ppermute(block, axis, [(i, (i + d) % count) for i in range(count)])  26.4 us
    ppermute x9, waiting for transfers between devices, scatter_blocks(): lax.ppermute(part, axis, [(i, (i + d) % count) for i in range(count)])  19.7 us
    ppermute x9, starting transfers between devices, scatter_blocks(): lax.ppermute(part, axis, [(i, (i + d) % count) for i in range(count)])  17.7 us
    ppermute x9, starting transfers between devices, gather_blocks(): lax.ppermute(block, axis, [(i, (i + d) % count) for i in range(count)])  14.3 us
    all_gather x1, blocking collectives, per_device(): gathered = lax.all_gather(image_tokens, 'section', axis=1, tiled=True)  10.3 us
    pallas_call x1, Pallas kernels, attention_layers(): pl.pallas_call(functools.partial(attention_kernel, head_count=head_count,...  8.2 us
    all_gather x1, blocking collectives, per_device(): lax.all_gather(jnp.concatenate([query_gain, gate_logit], axis=1), 'sectio...  5.25 us
    dot_general x1, matrix products, per_device(): lax.dot_general(raw_grad, weights, (((1,), (1,)), ((), ())), preferred_el...  3.74 us
  transfers between devices with their start and end apart: 18, of which 15 were waited for; matrix products, arithmetic and copies ran while one was open for 2% of the time, Pallas kernels for 0%

profile of v3, /device:TPU:0, one launch (start us, length us, event | category | flops | bytes accessed | tf_op | source)
XLA Modules:
  0.0 120.1 jit_solution(7809477451900444051)
XLA Ops:
  0.7 10.3 %all_gather.7 = bf16[2,96,2048]{2,1,0:T(8,128)(2,1)S(1)} all-gather(bf16[2,24,2048]{2,1,0:T(8,128)(2,1)} %param.11), channel_id=1, replica_groups=mesh['group'=2,'section'=4,'shard'=4] {'section'}, dimensions={1}, use_global_device_ids=true | all-gather | bytes 983040 | tf_op jit(solution)/shard_map/all_gather | solution.py:228
  10.9 3.2 %fusion = f32[4,48,1024]{2,1,0:T(8,128)S(1)} fusion(bf16[4,48,2048]{2,1,0:T(8,128)(2,1)S(1)} %bitcast.93, bf16[1,2048,1024]{2,1,0:T(8,128)(2,1)} %param.12), kind=kOutput, calls=%fused_computation.3 | convolution fusion | flops 805306368 | bytes 5767168 | tf_op jit(solution)/shard_map/dot_general | solution.py:233
  14.2 1.6 %collective-permute-start = (f32[48,1024]{1,0:T(8,128)S(1)}, f32[48,1024]{1,0:T(8,128)S(1)}, u32[]{:S(2)}, u32[]{:S(2)}) collective-permute-start(f32[48,1024]{1,0:T(8,128)S(1)} %get-tuple-element.10), channel_id=1, source_target_pairs={{0,1},{1,2},{2,3},{3,0},{4,5},{5,6},{6,7},{7,4},{8,9},{9,10},{10,1... | collective-permute-start | bytes 589832 | tf_op jit(solution)/shard_map/ppermute | solution.py:196
  15.9 2.6 %collective-permute-start.1 = (f32[48,1024]{1,0:T(8,128)S(1)}, f32[48,1024]{1,0:T(8,128)S(1)}, u32[]{:S(2)}, u32[]{:S(2)}) collective-permute-start(f32[48,1024]{1,0:T(8,128)S(1)} %get-tuple-element.12), channel_id=1, source_target_pairs={{0,2},{1,3},{2,0},{3,1},{4,6},{5,7},{6,4},{7,5},{8,10},{9,11},{10,... | collective-permute-start | bytes 589832 | tf_op jit(solution)/shard_map/ppermute | solution.py:196
  18.4 1.4 %collective-permute-start.2 = (f32[48,1024]{1,0:T(8,128)S(1)}, f32[48,1024]{1,0:T(8,128)S(1)}, u32[]{:S(2)}, u32[]{:S(2)}) collective-permute-start(f32[48,1024]{1,0:T(8,128)S(1)} %get-tuple-element.11), channel_id=1, source_target_pairs={{0,3},{1,0},{2,1},{3,2},{4,7},{5,4},{6,5},{7,6},{8,11},{9,8},{10,9... | collective-permute-start | bytes 589832 | tf_op jit(solution)/shard_map/ppermute | solution.py:196
  21.0 5.3 %all-gather = f32[4,1,4128]{2,1,0:T(1,128)S(1)} all-gather(f32[1,1,4128]{2,1,0:T(1,128)S(1)} %maximum_bitcast_fusion), channel_id=1, replica_groups=mesh['group'=2,'section'=4,'shard'=4] {'section'}, dimensions={0}, use_global_device_ids=true | all-gather | bytes 82560 | tf_op jit(solution)/shard_map/all_gather | solution.py:222
  26.9 4.9 %collective-permute-done.1 = f32[48,1024]{1,0:T(8,128)S(1)} collective-permute-done((f32[48,1024]{1,0:T(8,128)S(1)}, f32[48,1024]{1,0:T(8,128)S(1)}, u32[]{:S(2)}, u32[]{:S(2)}) %collective-permute-start.1) | collective-permute-done | bytes 196640 | tf_op jit(solution)/shard_map/ppermute | solution.py:196
  32.3 4.7 %collective-permute-start.3 = (bf16[48,1024]{1,0:T(8,128)(2,1)S(1)}, bf16[48,1024]{1,0:T(8,128)(2,1)S(1)}, u32[]{:S(2)}, u32[]{:S(2)}) collective-permute-start(bf16[48,1024]{1,0:T(8,128)(2,1)S(1)} %get-tuple-element.17), channel_id=1, source_target_pairs={{0,1},{1,2},{2,3},{3,0},{4,5},{5,6},{6,7},{7,4},{8,9},{9,10},{10,1... | collective-permute-start | bytes 294920 | tf_op jit(solution)/shard_map/ppermute | solution.py:179
  37.0 1.6 %collective-permute-start.4 = (bf16[48,1024]{1,0:T(8,128)(2,1)S(1)}, bf16[48,1024]{1,0:T(8,128)(2,1)S(1)}, u32[]{:S(2)}, u32[]{:S(2)}) collective-permute-start(bf16[48,1024]{1,0:T(8,128)(2,1)S(1)} %get-tuple-element.17), channel_id=1, source_target_pairs={{0,2},{1,3},{2,0},{3,1},{4,6},{5,7},{6,4},{7,5},{8,10},{9,11},{10,... | collective-permute-start | bytes 294920 | tf_op jit(solution)/shard_map/ppermute | solution.py:179
  39.5 1.9 %collective-permute-done.3 = bf16[48,1024]{1,0:T(8,128)(2,1)S(1)} collective-permute-done((bf16[48,1024]{1,0:T(8,128)(2,1)S(1)}, bf16[48,1024]{1,0:T(8,128)(2,1)S(1)}, u32[]{:S(2)}, u32[]{:S(2)}) %collective-permute-start.3) | collective-permute-done | bytes 98336 | tf_op jit(solution)/shard_map/ppermute | solution.py:179
  41.4 3.6 %collective-permute-done.4 = bf16[48,1024]{1,0:T(8,128)(2,1)S(1)} collective-permute-done((bf16[48,1024]{1,0:T(8,128)(2,1)S(1)}, bf16[48,1024]{1,0:T(8,128)(2,1)S(1)}, u32[]{:S(2)}, u32[]{:S(2)}) %collective-permute-start.4) | collective-permute-done | bytes 98336 | tf_op jit(solution)/shard_map/ppermute | solution.py:179
  46.1 1.2 collective-permute-start.7
  47.2 1.4 %collective-permute-start.8 = (bf16[192,1024]{1,0:T(8,128)(2,1)S(1)}, bf16[192,1024]{1,0:T(8,128)(2,1)S(1)}, u32[]{:S(2)}, u32[]{:S(2)}) collective-permute-start(bf16[192,1024]{1,0:T(8,128)(2,1)S(1)} %bitcast.100), channel_id=1, source_target_pairs={{0,12},{4,0},{8,4},{12,8},{1,13},{5,1},{9,5},{13,9},{2,14},{6,2},{... | collective-permute-start | bytes 1179656 | tf_op jit(solution)/shard_map/ppermute | solution.py:179
  49.7 7.1 %collective-permute-done.6 = bf16[192,1024]{1,0:T(8,128)(2,1)S(1)} collective-permute-done((bf16[192,1024]{1,0:T(8,128)(2,1)S(1)}, bf16[192,1024]{1,0:T(8,128)(2,1)S(1)}, u32[]{:S(2)}, u32[]{:S(2)}) %collective-permute-start.6) | collective-permute-done | bytes 393248 | tf_op jit(solution)/shard_map/ppermute | solution.py:179
  56.9 1.2 %collective-permute-done.7 = bf16[192,1024]{1,0:T(8,128)(2,1)S(1)} collective-permute-done((bf16[192,1024]{1,0:T(8,128)(2,1)S(1)}, bf16[192,1024]{1,0:T(8,128)(2,1)S(1)}, u32[]{:S(2)}, u32[]{:S(2)}) %collective-permute-start.7) | collective-permute-done | bytes 393248 | tf_op jit(solution)/shard_map/ppermute | solution.py:179
  58.1 6.4 %collective-permute-done.8 = bf16[192,1024]{1,0:T(8,128)(2,1)S(1)} collective-permute-done((bf16[192,1024]{1,0:T(8,128)(2,1)S(1)}, bf16[192,1024]{1,0:T(8,128)(2,1)S(1)}, u32[]{:S(2)}, u32[]{:S(2)}) %collective-permute-start.8) | collective-permute-done | bytes 393248 | tf_op jit(solution)/shard_map/ppermute | solution.py:179
  65.4 2.0 %broadcast_select_fusion.keyval_ref = bf16[4,2,96,1024]{3,2,1,0:T(8,128)(2,1)} fusion(bf16[4,2,96,1024]{3,2,1,0:T(8,128)(2,1)S(1)} %bitcast.92, pred[4]{0:T(512)(128)(4,1)} %compare_and_fusion.1), kind=kLoop, calls=%fused_computation.9 | loop fusion | flops 786432 | bytes 3145732 | tf_op jit(solution)/shard_map/jit(_take)/select_n | solution.py:183
  67.4 8.2 %shard_map.104 = (f32[2,64,4096]{2,1,0:T(8,128)}, f32[2,96,1024]{2,1,0:T(8,128)}) custom-call(s32[1]{0:T(128)} %bitcast.section_ref, f32[4,32]{1,0:T(4,128)} %slice_tanh_fusion.gates_ref, bf16[2,64,4096]{2,1,0:T(8,128)(2,1)} %queries_ref.1, bf16[4,2,96,1024]{3,2,1,0:T(8,128)(2,1)} %broadcast_select_fusion.keyval_ref, f32[4,1,4096]{2,1,0:T(1,128)} %reshape.164.gains_ref, ...), custom_call_target="tpu_custom_call" | custom-call | flops 1409286144 | bytes 6815744 | tf_op jit(solution)/shard_map/pallas_call | solution.py:134
  75.6 1.2 convert_element_type.57
  76.8 1.4 %collective-permute-start.10 = (bf16[48,1024]{1,0:T(8,128)(2,1)S(1)}, bf16[48,1024]{1,0:T(8,128)(2,1)S(1)}, u32[]{:S(2)}, u32[]{:S(2)}) collective-permute-start(bf16[48,1024]{1,0:T(8,128)(2,1)S(1)} %get-tuple-element.15), channel_id=1, source_target_pairs={{0,2},{1,3},{2,0},{3,1},{4,6},{5,7},{6,4},{7,5},{8,10},{9,11},{10,... | collective-permute-start | bytes 294920 | tf_op jit(solution)/shard_map/ppermute | solution.py:196
  78.2 3.4 %collective-permute-start.11 = (bf16[48,1024]{1,0:T(8,128)(2,1)S(1)}, bf16[48,1024]{1,0:T(8,128)(2,1)S(1)}, u32[]{:S(2)}, u32[]{:S(2)}) collective-permute-start(bf16[48,1024]{1,0:T(8,128)(2,1)S(1)} %get-tuple-element.14), channel_id=1, source_target_pairs={{0,3},{1,0},{2,1},{3,2},{4,7},{5,4},{6,5},{7,6},{8,11},{9,8},{10,9... | collective-permute-start | bytes 294920 | tf_op jit(solution)/shard_map/ppermute | solution.py:196
  82.4 1.6 %collective-permute-done.11 = bf16[48,1024]{1,0:T(8,128)(2,1)S(1)} collective-permute-done((bf16[48,1024]{1,0:T(8,128)(2,1)S(1)}, bf16[48,1024]{1,0:T(8,128)(2,1)S(1)}, u32[]{:S(2)}, u32[]{:S(2)}) %collective-permute-start.11) | collective-permute-done | bytes 98336 | tf_op jit(solution)/shard_map/ppermute | solution.py:196
  84.0 4.9 %collective-permute-done.9 = bf16[48,1024]{1,0:T(8,128)(2,1)S(1)} collective-permute-done((bf16[48,1024]{1,0:T(8,128)(2,1)S(1)}, bf16[48,1024]{1,0:T(8,128)(2,1)S(1)}, u32[]{:S(2)}, u32[]{:S(2)}) %collective-permute-start.9) | collective-permute-done | bytes 98336 | tf_op jit(solution)/shard_map/ppermute | solution.py:196
  89.5 1.6 %collective-permute-start.13 = (bf16[48,1024]{1,0:T(8,128)(2,1)S(1)}, bf16[48,1024]{1,0:T(8,128)(2,1)S(1)}, u32[]{:S(2)}, u32[]{:S(2)}) collective-permute-start(bf16[48,1024]{1,0:T(8,128)(2,1)S(1)} %pad_maximum_fusion.4), channel_id=1, source_target_pairs={{0,2},{1,3},{2,0},{3,1},{4,6},{5,7},{6,4},{7,5},{8,10},{9,11},{10,... | collective-permute-start | bytes 294920 | tf_op jit(solution)/shard_map/ppermute | solution.py:179
  91.1 2.9 %collective-permute-start.14 = (bf16[48,1024]{1,0:T(8,128)(2,1)S(1)}, bf16[48,1024]{1,0:T(8,128)(2,1)S(1)}, u32[]{:S(2)}, u32[]{:S(2)}) collective-permute-start(bf16[48,1024]{1,0:T(8,128)(2,1)S(1)} %pad_maximum_fusion.4), channel_id=1, source_target_pairs={{0,3},{1,0},{2,1},{3,2},{4,7},{5,4},{6,5},{7,6},{8,11},{9,8},{10,9... | collective-permute-start | bytes 294920 | tf_op jit(solution)/shard_map/ppermute | solution.py:179
  94.0 3.2 %collective-permute-done.12 = bf16[48,1024]{1,0:T(8,128)(2,1)S(1)} collective-permute-done((bf16[48,1024]{1,0:T(8,128)(2,1)S(1)}, bf16[48,1024]{1,0:T(8,128)(2,1)S(1)}, u32[]{:S(2)}, u32[]{:S(2)}) %collective-permute-start.12) | collective-permute-done | bytes 98336 | tf_op jit(solution)/shard_map/ppermute | solution.py:179
  97.1 2.7 %collective-permute-done.13 = bf16[48,1024]{1,0:T(8,128)(2,1)S(1)} collective-permute-done((bf16[48,1024]{1,0:T(8,128)(2,1)S(1)}, bf16[48,1024]{1,0:T(8,128)(2,1)S(1)}, u32[]{:S(2)}, u32[]{:S(2)}) %collective-permute-start.13) | collective-permute-done | bytes 98336 | tf_op jit(solution)/shard_map/ppermute | solution.py:179
  100.6 3.7 %fusion.4 = bf16[192,2048]{1,0:T(8,128)(2,1)S(1)} fusion(bf16[192,1024]{1,0:T(8,128)(2,1)S(1)} %bitcast.105, bf16[1,2048,1024]{2,1,0:T(8,128)(2,1)} %param.12), kind=kOutput, calls=%fused_computation.7 | convolution fusion | flops 805699584 | bytes 5373952 | tf_op jit(solution)/shard_map/dot_general | solution.py:273
  105.4 5.7 %collective-permute-start.16 = (bf16[2,24,2048]{2,1,0:T(8,128)(2,1)S(1)}, bf16[2,24,2048]{2,1,0:T(8,128)(2,1)S(1)}, u32[]{:S(2)}, u32[]{:S(2)}) collective-permute-start(bf16[2,24,2048]{2,1,0:T(8,128)(2,1)S(1)} %get-tuple-element.9), channel_id=1, source_target_pairs={{0,8},{4,12},{8,0},{12,4},{1,9},{5,13},{9,1},{13,5},{2,10},{6,14},... | collective-permute-start | bytes 589832 | tf_op jit(solution)/shard_map/ppermute | solution.py:196
  111.8 3.6 %collective-permute-done.15 = bf16[2,24,2048]{2,1,0:T(8,128)(2,1)S(1)} collective-permute-done((bf16[2,24,2048]{2,1,0:T(8,128)(2,1)S(1)}, bf16[2,24,2048]{2,1,0:T(8,128)(2,1)S(1)}, u32[]{:S(2)}, u32[]{:S(2)}) %collective-permute-start.15) | collective-permute-done | bytes 196640 | tf_op jit(solution)/shard_map/ppermute | solution.py:196
  115.4 1.3 %collective-permute-done.16 = bf16[2,24,2048]{2,1,0:T(8,128)(2,1)S(1)} collective-permute-done((bf16[2,24,2048]{2,1,0:T(8,128)(2,1)S(1)}, bf16[2,24,2048]{2,1,0:T(8,128)(2,1)S(1)}, u32[]{:S(2)}, u32[]{:S(2)}) %collective-permute-start.16) | collective-permute-done | bytes 196640 | tf_op jit(solution)/shard_map/ppermute | solution.py:196
  116.7 2.5 %collective-permute-done.17 = bf16[2,24,2048]{2,1,0:T(8,128)(2,1)S(1)} collective-permute-done((bf16[2,24,2048]{2,1,0:T(8,128)(2,1)S(1)}, bf16[2,24,2048]{2,1,0:T(8,128)(2,1)S(1)}, u32[]{:S(2)}, u32[]{:S(2)}) %collective-permute-start.17) | collective-permute-done | bytes 196640 | tf_op jit(solution)/shard_map/ppermute | solution.py:196
  (69 shorter events, 10.8 us)
Async XLA Ops:
  10.9 8.9 %copy-start.3 = (s32[2,96]{1,0:T(2,128)S(1)}, s32[2,96]{1,0:T(2,128)}, u32[]{:S(2)}) copy-start(s32[2,96]{1,0:T(2,128)} %param.18) | copy-start | bytes 2308
  10.9 8.9 %copy-start.4 = (s32[2,64]{1,0:T(2,128)S(1)}, s32[2,64]{1,0:T(2,128)}, u32[]{:S(2)}) copy-start(s32[2,64]{1,0:T(2,128)} %param.17) | copy-start | bytes 1540
  14.1 6.8 %copy-start.2 = (f32[1,4096]{1,0:T(1,128)S(1)}, f32[1,4096]{1,0:T(1,128)}, u32[]{:S(2)}) copy-start(f32[1,4096]{1,0:T(1,128)} %param.13) | copy-start | bytes 49156
  14.1 6.8 %copy-start.5 = (f32[1,32]{1,0:T(1,128)S(1)}, f32[1,32]{1,0:T(1,128)}, u32[]{:S(2)}) copy-start(f32[1,32]{1,0:T(1,128)} %param.15) | copy-start | bytes 388
  14.2 12.7 %collective-permute-start = (f32[48,1024]{1,0:T(8,128)S(1)}, f32[48,1024]{1,0:T(8,128)S(1)}, u32[]{:S(2)}, u32[]{:S(2)}) collective-permute-start(f32[48,1024]{1,0:T(8,128)S(1)} %get-tuple-element.10), channel_id=1, source_target_pairs={{0,1},{1,2},{2,3},{3,0},{4,5},{5,6},{6,7},{7,4},{8,9},{9,10},{10,1... | collective-permute-start | bytes 589832 | tf_op jit(solution)/shard_map/ppermute | solution.py:196
  15.9 16.0 %collective-permute-start.1 = (f32[48,1024]{1,0:T(8,128)S(1)}, f32[48,1024]{1,0:T(8,128)S(1)}, u32[]{:S(2)}, u32[]{:S(2)}) collective-permute-start(f32[48,1024]{1,0:T(8,128)S(1)} %get-tuple-element.12), channel_id=1, source_target_pairs={{0,2},{1,3},{2,0},{3,1},{4,6},{5,7},{6,4},{7,5},{8,10},{9,11},{10,... | collective-permute-start | bytes 589832 | tf_op jit(solution)/shard_map/ppermute | solution.py:196
  18.4 13.4 %collective-permute-start.2 = (f32[48,1024]{1,0:T(8,128)S(1)}, f32[48,1024]{1,0:T(8,128)S(1)}, u32[]{:S(2)}, u32[]{:S(2)}) collective-permute-start(f32[48,1024]{1,0:T(8,128)S(1)} %get-tuple-element.11), channel_id=1, source_target_pairs={{0,3},{1,0},{2,1},{3,2},{4,7},{5,4},{6,5},{7,6},{8,11},{9,8},{10,9... | collective-permute-start | bytes 589832 | tf_op jit(solution)/shard_map/ppermute | solution.py:196
  20.0 12.3 %copy-start = (f32[2,8,64,96]{3,2,1,0:T(8,128)}, f32[2,8,64,96]{3,2,1,0:T(8,128)S(1)}, u32[]{:S(2)}) copy-start(f32[2,8,64,96]{3,2,1,0:T(8,128)S(1)} %tile.4) | copy-start | bytes 1179652
  20.0 12.3 %copy-start.1 = (f32[1,512]{1,0:T(1,128)S(1)}, f32[1,512]{1,0:T(1,128)}, u32[]{:S(2)}) copy-start(f32[1,512]{1,0:T(1,128)} %param.14) | copy-start | bytes 6148
  32.3 9.1 %collective-permute-start.3 = (bf16[48,1024]{1,0:T(8,128)(2,1)S(1)}, bf16[48,1024]{1,0:T(8,128)(2,1)S(1)}, u32[]{:S(2)}, u32[]{:S(2)}) collective-permute-start(bf16[48,1024]{1,0:T(8,128)(2,1)S(1)} %get-tuple-element.17), channel_id=1, source_target_pairs={{0,1},{1,2},{2,3},{3,0},{4,5},{5,6},{6,7},{7,4},{8,9},{9,10},{10,1... | collective-permute-start | bytes 294920 | tf_op jit(solution)/shard_map/ppermute | solution.py:179
  37.0 8.0 %collective-permute-start.4 = (bf16[48,1024]{1,0:T(8,128)(2,1)S(1)}, bf16[48,1024]{1,0:T(8,128)(2,1)S(1)}, u32[]{:S(2)}, u32[]{:S(2)}) collective-permute-start(bf16[48,1024]{1,0:T(8,128)(2,1)S(1)} %get-tuple-element.17), channel_id=1, source_target_pairs={{0,2},{1,3},{2,0},{3,1},{4,6},{5,7},{6,4},{7,5},{8,10},{9,11},{10,... | collective-permute-start | bytes 294920 | tf_op jit(solution)/shard_map/ppermute | solution.py:179
  38.6 6.6 %collective-permute-start.5 = (bf16[48,1024]{1,0:T(8,128)(2,1)S(1)}, bf16[48,1024]{1,0:T(8,128)(2,1)S(1)}, u32[]{:S(2)}, u32[]{:S(2)}) collective-permute-start(bf16[48,1024]{1,0:T(8,128)(2,1)S(1)} %get-tuple-element.17), channel_id=1, source_target_pairs={{0,3},{1,0},{2,1},{3,2},{4,7},{5,4},{6,5},{7,6},{8,11},{9,8},{10,9... | collective-permute-start | bytes 294920 | tf_op jit(solution)/shard_map/ppermute | solution.py:179
  46.0 10.9 %collective-permute-start.6 = (bf16[192,1024]{1,0:T(8,128)(2,1)S(1)}, bf16[192,1024]{1,0:T(8,128)(2,1)S(1)}, u32[]{:S(2)}, u32[]{:S(2)}) collective-permute-start(bf16[192,1024]{1,0:T(8,128)(2,1)S(1)} %bitcast.98), channel_id=1, source_target_pairs={{0,4},{4,8},{8,12},{12,0},{1,5},{5,9},{9,13},{13,1},{2,6},{6,10},{... | collective-permute-start | bytes 1179656 | tf_op jit(solution)/shard_map/ppermute | solution.py:179
  46.1 12.0 %collective-permute-start.7 = (bf16[192,1024]{1,0:T(8,128)(2,1)S(1)}, bf16[192,1024]{1,0:T(8,128)(2,1)S(1)}, u32[]{:S(2)}, u32[]{:S(2)}) collective-permute-start(bf16[192,1024]{1,0:T(8,128)(2,1)S(1)} %bitcast.99), channel_id=1, source_target_pairs={{0,8},{4,12},{8,0},{12,4},{1,9},{5,13},{9,1},{13,5},{2,10},{6,14},... | collective-permute-start | bytes 1179656 | tf_op jit(solution)/shard_map/ppermute | solution.py:179
  47.2 17.3 %collective-permute-start.8 = (bf16[192,1024]{1,0:T(8,128)(2,1)S(1)}, bf16[192,1024]{1,0:T(8,128)(2,1)S(1)}, u32[]{:S(2)}, u32[]{:S(2)}) collective-permute-start(bf16[192,1024]{1,0:T(8,128)(2,1)S(1)} %bitcast.100), channel_id=1, source_target_pairs={{0,12},{4,0},{8,4},{12,8},{1,13},{5,1},{9,5},{13,9},{2,14},{6,2},{... | collective-permute-start | bytes 1179656 | tf_op jit(solution)/shard_map/ppermute | solution.py:179
  76.8 5.6 %collective-permute-start.10 = (bf16[48,1024]{1,0:T(8,128)(2,1)S(1)}, bf16[48,1024]{1,0:T(8,128)(2,1)S(1)}, u32[]{:S(2)}, u32[]{:S(2)}) collective-permute-start(bf16[48,1024]{1,0:T(8,128)(2,1)S(1)} %get-tuple-element.15), channel_id=1, source_target_pairs={{0,2},{1,3},{2,0},{3,1},{4,6},{5,7},{6,4},{7,5},{8,10},{9,11},{10,... | collective-permute-start | bytes 294920 | tf_op jit(solution)/shard_map/ppermute | solution.py:196
  78.2 5.8 %collective-permute-start.11 = (bf16[48,1024]{1,0:T(8,128)(2,1)S(1)}, bf16[48,1024]{1,0:T(8,128)(2,1)S(1)}, u32[]{:S(2)}, u32[]{:S(2)}) collective-permute-start(bf16[48,1024]{1,0:T(8,128)(2,1)S(1)} %get-tuple-element.14), channel_id=1, source_target_pairs={{0,3},{1,0},{2,1},{3,2},{4,7},{5,4},{6,5},{7,6},{8,11},{9,8},{10,9... | collective-permute-start | bytes 294920 | tf_op jit(solution)/shard_map/ppermute | solution.py:196
  81.6 7.4 %collective-permute-start.9 = (bf16[48,1024]{1,0:T(8,128)(2,1)S(1)}, bf16[48,1024]{1,0:T(8,128)(2,1)S(1)}, u32[]{:S(2)}, u32[]{:S(2)}) collective-permute-start(bf16[48,1024]{1,0:T(8,128)(2,1)S(1)} %get-tuple-element.13), channel_id=1, source_target_pairs={{0,1},{1,2},{2,3},{3,0},{4,5},{5,6},{6,7},{7,4},{8,9},{9,10},{10,1... | collective-permute-start | bytes 294920 | tf_op jit(solution)/shard_map/ppermute | solution.py:196
  89.4 7.7 %collective-permute-start.12 = (bf16[48,1024]{1,0:T(8,128)(2,1)S(1)}, bf16[48,1024]{1,0:T(8,128)(2,1)S(1)}, u32[]{:S(2)}, u32[]{:S(2)}) collective-permute-start(bf16[48,1024]{1,0:T(8,128)(2,1)S(1)} %pad_maximum_fusion.4), channel_id=1, source_target_pairs={{0,1},{1,2},{2,3},{3,0},{4,5},{5,6},{6,7},{7,4},{8,9},{9,10},{10,1... | collective-permute-start | bytes 294920 | tf_op jit(solution)/shard_map/ppermute | solution.py:179
  89.5 10.3 %collective-permute-start.13 = (bf16[48,1024]{1,0:T(8,128)(2,1)S(1)}, bf16[48,1024]{1,0:T(8,128)(2,1)S(1)}, u32[]{:S(2)}, u32[]{:S(2)}) collective-permute-start(bf16[48,1024]{1,0:T(8,128)(2,1)S(1)} %pad_maximum_fusion.4), channel_id=1, source_target_pairs={{0,2},{1,3},{2,0},{3,1},{4,6},{5,7},{6,4},{7,5},{8,10},{9,11},{10,... | collective-permute-start | bytes 294920 | tf_op jit(solution)/shard_map/ppermute | solution.py:179
  91.1 8.7 %collective-permute-start.14 = (bf16[48,1024]{1,0:T(8,128)(2,1)S(1)}, bf16[48,1024]{1,0:T(8,128)(2,1)S(1)}, u32[]{:S(2)}, u32[]{:S(2)}) collective-permute-start(bf16[48,1024]{1,0:T(8,128)(2,1)S(1)} %pad_maximum_fusion.4), channel_id=1, source_target_pairs={{0,3},{1,0},{2,1},{3,2},{4,7},{5,4},{6,5},{7,6},{8,11},{9,8},{10,9... | collective-permute-start | bytes 294920 | tf_op jit(solution)/shard_map/ppermute | solution.py:179
  104.4 11.0 %collective-permute-start.15 = (bf16[2,24,2048]{2,1,0:T(8,128)(2,1)S(1)}, bf16[2,24,2048]{2,1,0:T(8,128)(2,1)S(1)}, u32[]{:S(2)}, u32[]{:S(2)}) collective-permute-start(bf16[2,24,2048]{2,1,0:T(8,128)(2,1)S(1)} %get-tuple-element.7), channel_id=1, source_target_pairs={{0,4},{4,8},{8,12},{12,0},{1,5},{5,9},{9,13},{13,1},{2,6},{6,10},{... | collective-permute-start | bytes 589832 | tf_op jit(solution)/shard_map/ppermute | solution.py:196
  105.4 11.4 %collective-permute-start.16 = (bf16[2,24,2048]{2,1,0:T(8,128)(2,1)S(1)}, bf16[2,24,2048]{2,1,0:T(8,128)(2,1)S(1)}, u32[]{:S(2)}, u32[]{:S(2)}) collective-permute-start(bf16[2,24,2048]{2,1,0:T(8,128)(2,1)S(1)} %get-tuple-element.9), channel_id=1, source_target_pairs={{0,8},{4,12},{8,0},{12,4},{1,9},{5,13},{9,1},{13,5},{2,10},{6,14},... | collective-permute-start | bytes 589832 | tf_op jit(solution)/shard_map/ppermute | solution.py:196
  111.0 8.3 %collective-permute-start.17 = (bf16[2,24,2048]{2,1,0:T(8,128)(2,1)S(1)}, bf16[2,24,2048]{2,1,0:T(8,128)(2,1)S(1)}, u32[]{:S(2)}, u32[]{:S(2)}) collective-permute-start(bf16[2,24,2048]{2,1,0:T(8,128)(2,1)S(1)} %get-tuple-element.8), channel_id=1, source_target_pairs={{0,12},{4,0},{8,4},{12,8},{1,13},{5,1},{9,5},{13,9},{2,14},{6,2},{... | collective-permute-start | bytes 589832 | tf_op jit(solution)/shard_map/ppermute | solution.py:196

commit v4 on v3

--- a/solution.py
+++ b/solution.py
@@ -31,6 +31,7 @@
 
 def attention_kernel(
     section_ref,
+    slots_ref,
     gates_ref,
     queries_ref,
     keyval_ref,
@@ -55,22 +56,23 @@
     def head_cols(h):
         return pl.ds(h * head_dim, head_dim)
 
-    def queries_of(layer, k):
+    def queries_of(slot, k):
         parts = []
         for g in range(groups):
             h = k * groups + g
             x = out_ref[:, head_cols(h)]
             mean_square = jnp.sum(x * x, axis=-1, keepdims=True) * (1.0 / head_dim)
-            gain = gains_ref[layer, :, head_cols(h)]
+            gain = gains_ref[slot, :, head_cols(h)]
             parts.append((x * lax.rsqrt(mean_square + epsilon) * gain).astype(jnp.bfloat16))
         return jnp.concatenate(parts, axis=0)
 
     def forward(layer):
+        slot = slots_ref[layer]
         same = mask_ref[...] > 0.5
         for k in range(keyval_heads):
-            query = queries_of(layer, k)
-            key = keyval_ref[layer, :, head_cols(k)]
-            value = keyval_ref[layer, :, pl.ds(key_width + k * head_dim, head_dim)]
+            query = queries_of(slot, k)
+            key = keyval_ref[slot, :, head_cols(k)]
+            value = keyval_ref[slot, :, pl.ds(key_width + k * head_dim, head_dim)]
             scores = lax.dot_general(
                 query, key, (((1,), (1,)), ((), ())), preferred_element_type=jnp.float32
             ) * scale
@@ -83,7 +85,7 @@
             for g in range(groups):
                 h = k * groups + g
                 rows = attended[g * token_count : (g + 1) * token_count]
-                out_ref[:, head_cols(h)] = out_ref[:, head_cols(h)] + gates_ref[layer, h] * rows
+                out_ref[:, head_cols(h)] = out_ref[:, head_cols(h)] + gates_ref[slot, h] * rows
 
     def layer_step(layer, carry):
         forward(layer)
@@ -92,10 +94,11 @@
     lax.fori_loop(0, section, layer_step, 0)
 
     same_t = mask_t_ref[...] > 0.5
+    own = slots_ref[section]
     for k in range(keyval_heads):
-        query = queries_of(section, k)
-        key = keyval_ref[section, :, head_cols(k)]
-        value = keyval_ref[section, :, pl.ds(key_width + k * head_dim, head_dim)]
+        query = queries_of(own, k)
+        key = keyval_ref[own, :, head_cols(k)]
+        value = keyval_ref[own, :, pl.ds(key_width + k * head_dim, head_dim)]
         scores_t = lax.dot_general(
             key, query, (((1,), (1,)), ((), ())), preferred_element_type=jnp.float32
         ) * scale
@@ -120,7 +123,9 @@
     forward(section)
 
 
-def attention_layers(section_index, gates, queries, keyval_all, gains, same_document, upstream):
+def attention_layers(
+    section_index, layer_slots, gates, queries, keyval_all, gains, same_document, upstream
+):
     layer_count, micro_count, image_count, pair_width = keyval_all.shape
     token_count, query_width = queries.shape[1], queries.shape[2]
     head_count = gates.shape[1]
@@ -135,6 +140,7 @@
         functools.partial(attention_kernel, head_count=head_count, keyval_heads=keyval_heads),
         grid=(micro_count,),
         in_specs=[
+            smem,
             smem,
             smem,
             pl.BlockSpec((None, token_count, query_width), lambda m: (m, 0, 0)),
@@ -160,6 +166,7 @@
         ),
     )(
         jnp.reshape(section_index, (1,)).astype(jnp.int32),
+        layer_slots.astype(jnp.int32),
         gates,
         queries,
         keyval_all,
@@ -172,15 +179,25 @@
 
 def gather_blocks(block, axis):
     count = lax.axis_size(axis)
+    index = lax.axis_index(axis)
+    positions = jnp.arange(count, dtype=jnp.int32)
     if count > 8:
-        return lax.all_gather(block, axis, axis=0, tiled=False)
-    index = lax.axis_index(axis)
+        return lax.all_gather(block, axis, axis=0, tiled=False), positions
+    if count == 4:
+        partner = [(i, i ^ 1) for i in range(count)]
+        across = lax.ppermute(block, axis, [(i, i ^ 2) for i in range(count)])
+        received = [block, lax.ppermute(block, axis, partner), across, lax.ppermute(across, axis, partner)]
+        return jnp.stack(received), lax.bitwise_xor(index, positions)
     received = [block] + [
         lax.ppermute(block, axis, [(i, (i + d) % count) for i in range(count)])
         for d in range(1, count)
     ]
-    stacked = jnp.stack(received)
-    return jnp.take(stacked, (index - jnp.arange(count)) % count, axis=0)
+    return jnp.stack(received), (index - positions) % count
+
+
+def in_order(block, axis):
+    stacked, slots = gather_blocks(block, axis)
+    return jnp.take(stacked, slots, axis=0)
 
 
 def scatter_blocks(blocks, axis):
@@ -190,7 +207,23 @@
             jnp.float32
         )
     index = lax.axis_index(axis)
-    total = lax.dynamic_index_in_dim(blocks, index, 0, keepdims=False).astype(jnp.float32)
+
+    def pick(i):
+        return lax.dynamic_index_in_dim(blocks, i, 0, keepdims=False)
+
+    if count == 4:
+        partner = [(i, i ^ 1) for i in range(count)]
+        got = lax.ppermute(jnp.stack([pick(index ^ 1), pick(index ^ 3)]), axis, partner)
+        theirs = (pick(index ^ 2).astype(jnp.float32) + got[1].astype(jnp.float32)).astype(
+            blocks.dtype
+        )
+        back = lax.ppermute(theirs, axis, [(i, i ^ 2) for i in range(count)])
+        return (
+            pick(index).astype(jnp.float32)
+            + got[0].astype(jnp.float32)
+            + back.astype(jnp.float32)
+        )
+    total = pick(index).astype(jnp.float32)
     for d in range(1, count):
         part = lax.dynamic_index_in_dim(blocks, (index + d) % count, 0, keepdims=False)
         total = total + lax.ppermute(
@@ -219,8 +252,8 @@
     keyval_heads = key_width // head_dim
     weights = keyval_weight[0]
 
-    layer_params = lax.all_gather(
-        jnp.concatenate([query_gain, gate_logit], axis=1), "section", axis=0, tiled=True
+    layer_params, layer_slots = gather_blocks(
+        jnp.concatenate([query_gain, gate_logit], axis=1)[0], "section"
     )
     gains_all = layer_params[:, : query_gain.shape[1]]
     gates_all = layer_params[:, query_gain.shape[1] :]
@@ -238,12 +271,13 @@
     keyval_rows = jnp.concatenate(
         [key_rows.astype(jnp.bfloat16), raw_rows[:, key_width:].astype(jnp.bfloat16)], axis=1
     )
-    keyval_own = gather_blocks(keyval_rows, "shard").reshape(total_rows, 2 * key_width)
-    keyval_all = gather_blocks(keyval_own, "section")
+    keyval_own = in_order(keyval_rows, "shard").reshape(total_rows, 2 * key_width)
+    keyval_all, _ = gather_blocks(keyval_own, "section")
 
     same_document = text_document[:, :, None] == image_document[:, None, :]
     leaving, grad_local = attention_layers(
         section_index,
+        layer_slots,
         jnp.tanh(gates_all),
         text_queries,
         keyval_all.reshape(section_count, micro_count, image_count, 2 * key_width),
@@ -263,7 +297,7 @@
     raw_grad_rows = jnp.concatenate([key_portion, grad_rows[:, key_width:]], axis=1).astype(
         jnp.bfloat16
     )
-    raw_grad = gather_blocks(raw_grad_rows, "shard").reshape(total_rows, 2 * key_width)
+    raw_grad = in_order(raw_grad_rows, "shard").reshape(total_rows, 2 * key_width)
     owned = image_count // section_count
     raw_grad = (
         raw_grad.reshape(micro_count, section_count, owned, 2 * key_width)

time: 121 us -> 120 us (level)
  waiting for transfers between devices: 46.1 us -> 59.9 us
  starting transfers between devices: 32 us -> 24.3 us
  blocking collectives: 15.5 us -> 10.3 us
  local copies, waits for them, and re-layouts: 4.57 us -> 3.35 us
    ppermute x18, waiting for transfers between devices: 46.1 us -> 59.9 us  [the longest x3 20.3 us: scatter_blocks(): back = lax.ppermute(theirs, axis, [(i, i ^ 2) for i in range(count)])]
    ppermute x18, starting transfers between devices: 32 us -> 24.3 us  [the longest x3 10.4 us: scatter_blocks(): back = lax.ppermute(theirs, axis, [(i, i ^ 2) for i in range(count)])]
    all_gather x1 -> x0, blocking collectives: 5.25 us -> none  [per_device(): lax.all_gather(jnp.concatenate([query_gain, gate_logit], axis=1), 'sectio...]
    select_n x5 -> x3, other arithmetic: 2.27 us -> 0.22 us  [in_order(): return jnp.take(stacked, slots, axis=0)]
    another operation x5 -> x9, other arithmetic: 0.33 us -> 1.66 us  [the longest x5 1.53 us: gather_blocks(): return (jnp.stack(received), lax.bitwise_xor(index, positions))]
  transfers between devices with their start and end apart: 18 -> 18, of which waited for: 15 -> 14; matrix products, arithmetic and copies ran while one was open for 2% -> 3% of each run, Pallas kernels for 0% -> 0%
where the time goes in v4:
time: 120 us
  waiting for transfers between devices  59.9 us (50%)
  starting transfers between devices  24.3 us (20%)
  blocking collectives  10.3 us (9%)
  Pallas kernels  8.22 us (7%)
  matrix products  6.91 us (6%)
  other arithmetic  5.54 us (5%)
  local copies, waits for them, and re-layouts  3.35 us (3%)
    ppermute x3, waiting for transfers between devices, scatter_blocks(): back = lax.ppermute(theirs, axis, [(i, i ^ 2) for i in range(count)])  20.3 us
    ppermute x3, waiting for transfers between devices, scatter_blocks(): lax.ppermute(jnp.stack([pick(index ^ 1), pick(index ^ 3)]), axis, partner)  16.2 us
    ppermute x4, waiting for transfers between devices, gather_blocks(): across = lax.ppermute(block, axis, [(i, i ^ 2) for i in range(count)])  13.7 us
    ppermute x3, starting transfers between devices, scatter_blocks(): back = lax.ppermute(theirs, axis, [(i, i ^ 2) for i in range(count)])  10.4 us
    all_gather x1, blocking collectives, per_device(): gathered = lax.all_gather(image_tokens, 'section', axis=1, tiled=True)  10.3 us
    ppermute x4, waiting for transfers between devices, gather_blocks(): lax.ppermute(across, axis, partner)  9.41 us
    ppermute x4, starting transfers between devices, gather_blocks(): lax.ppermute(block, axis, partner)  8.44 us
    pallas_call x1, Pallas kernels, attention_layers(): pl.pallas_call(functools.partial(attention_kernel, head_count=head_count,...  8.22 us
  transfers between devices with their start and end apart: 18, of which 14 were waited for; matrix products, arithmetic and copies ran while one was open for 3% of the time, Pallas kernels for 0%

profile of v4, /device:TPU:0, one launch (start us, length us, event | category | flops | bytes accessed | tf_op | source)
XLA Modules:
  0.0 119.6 jit_solution(9286931713216179275)
XLA Ops:
  0.6 10.3 %all_gather.3 = bf16[2,96,2048]{2,1,0:T(8,128)(2,1)S(1)} all-gather(bf16[2,24,2048]{2,1,0:T(8,128)(2,1)} %param.11), channel_id=1, replica_groups=mesh['group'=2,'section'=4,'shard'=4] {'section'}, dimensions={1}, use_global_device_ids=true | all-gather | bytes 983040 | tf_op jit(solution)/shard_map/all_gather | solution.py:261
  10.9 3.2 %fusion = f32[4,48,1024]{2,1,0:T(8,128)S(1)} fusion(bf16[4,48,2048]{2,1,0:T(8,128)(2,1)S(1)} %bitcast.68, bf16[1,2048,1024]{2,1,0:T(8,128)(2,1)} %param.12), kind=kOutput, calls=%fused_computation.2 | convolution fusion | flops 805306368 | bytes 5767168 | tf_op jit(solution)/shard_map/dot_general | solution.py:266
  14.2 1.6 %collective-permute-start.3 = (f32[2,48,1024]{2,1,0:T(8,128)S(1)}, f32[2,48,1024]{2,1,0:T(8,128)S(1)}, u32[]{:S(2)}, u32[]{:S(2)}) collective-permute-start(f32[2,48,1024]{2,1,0:T(8,128)S(1)} %pad_maximum_fusion.1), channel_id=1, source_target_pairs={{0,1},{1,0},{2,3},{3,2},{4,5},{5,4},{6,7},{7,6},{8,9},{9,8},{10,11... | collective-permute-start | bytes 1179656 | tf_op jit(solution)/shard_map/ppermute | solution.py:216
  15.8 9.8 %collective-permute-done.3 = f32[2,48,1024]{2,1,0:T(8,128)S(1)} collective-permute-done((f32[2,48,1024]{2,1,0:T(8,128)S(1)}, f32[2,48,1024]{2,1,0:T(8,128)S(1)}, u32[]{:S(2)}, u32[]{:S(2)}) %collective-permute-start.3) | collective-permute-done | bytes 393248 | tf_op jit(solution)/shard_map/ppermute | solution.py:216
  25.6 2.7 %collective-permute-start.4 = (f32[48,1024]{1,0:T(8,128)S(1)}, f32[48,1024]{1,0:T(8,128)S(1)}, u32[]{:S(2)}, u32[]{:S(2)}) collective-permute-start(f32[48,1024]{1,0:T(8,128)S(1)} %fusion.8), channel_id=1, source_target_pairs={{0,2},{1,3},{2,0},{3,1},{4,6},{5,7},{6,4},{7,5},{8,10},{9,11},{10,... | collective-permute-start | bytes 589832 | tf_op jit(solution)/shard_map/ppermute | solution.py:220
  28.3 8.9 %collective-permute-done.4 = f32[48,1024]{1,0:T(8,128)S(1)} collective-permute-done((f32[48,1024]{1,0:T(8,128)S(1)}, f32[48,1024]{1,0:T(8,128)S(1)}, u32[]{:S(2)}, u32[]{:S(2)}) %collective-permute-start.4) | collective-permute-done | bytes 196640 | tf_op jit(solution)/shard_map/ppermute | solution.py:220
  37.7 4.0 %collective-permute-start.5 = (bf16[48,1024]{1,0:T(8,128)(2,1)S(1)}, bf16[48,1024]{1,0:T(8,128)(2,1)S(1)}, u32[]{:S(2)}, u32[]{:S(2)}) collective-permute-start(bf16[48,1024]{1,0:T(8,128)(2,1)S(1)} %get-tuple-element.14), channel_id=1, source_target_pairs={{0,1},{1,0},{2,3},{3,2},{4,5},{5,4},{6,7},{7,6},{8,9},{9,8},{10,11... | collective-permute-start | bytes 294920 | tf_op jit(solution)/shard_map/ppermute | solution.py:189
  41.8 3.6 %collective-permute-done.6 = bf16[48,1024]{1,0:T(8,128)(2,1)S(1)} collective-permute-done((bf16[48,1024]{1,0:T(8,128)(2,1)S(1)}, bf16[48,1024]{1,0:T(8,128)(2,1)S(1)}, u32[]{:S(2)}, u32[]{:S(2)}) %collective-permute-start.6) | collective-permute-done | bytes 98336 | tf_op jit(solution)/shard_map/ppermute | solution.py:188
  45.6 4.3 %collective-permute-done.7 = bf16[48,1024]{1,0:T(8,128)(2,1)S(1)} collective-permute-done((bf16[48,1024]{1,0:T(8,128)(2,1)S(1)}, bf16[48,1024]{1,0:T(8,128)(2,1)S(1)}, u32[]{:S(2)}, u32[]{:S(2)}) %collective-permute-start.7) | collective-permute-done | bytes 98336 | tf_op jit(solution)/shard_map/ppermute | solution.py:189
  50.0 0.6 gather_fusion
  50.7 1.2 collective-permute-start.9
  51.9 1.0 collective-permute-start.1
  53.0 5.7 %collective-permute-done.1 = f32[4128]{0:T(1024)S(1)} collective-permute-done((f32[4128]{0:T(1024)S(1)}, f32[4128]{0:T(1024)S(1)}, u32[]{:S(2)}, u32[]{:S(2)}) %collective-permute-start.1) | collective-permute-done | bytes 16544 | tf_op jit(solution)/shard_map/ppermute | solution.py:188
  59.3 0.9 copy.12
  60.4 0.6 collective-permute-start.8
  61.1 0.7 reshape.129.gains_ref
  62.8 1.4 %pad_maximum_fusion.keyval_ref = bf16[4,2,96,1024]{3,2,1,0:T(8,128)(2,1)} fusion(bf16[1,2,96,1024]{3,2,1,0:T(8,128)(2,1)S(1)} %bitcast.88, bf16[1,2,96,1024]{3,2,1,0:T(8,128)(2,1)S(1)} %bitcast.85, bf16[1,2,96,1024]{3,2,1,0:T(8,128)(2,1)S(1)} %bitcast.87, bf16[1,2,96,1024]{3,2,1,0:T(8,128)(2,1)S(1)} %bitcast.76), kind=kLoop, calls=%fused_computation.7 | loop fusion | flops 2359296 | bytes 3145728 | tf_op jit(solution)/shard_map/stack | solution.py:190
  64.2 8.2 %shard_map.104 = (f32[2,64,4096]{2,1,0:T(8,128)}, f32[2,96,1024]{2,1,0:T(8,128)}) custom-call(s32[1]{0:T(128)} %bitcast.section_ref, s32[4]{0:T(128)} %iota_xor_fusion.slots_ref, f32[4,32]{1,0:T(4,128)} %maximum_tanh_fusion.gates_ref, bf16[2,64,4096]{2,1,0:T(8,128)(2,1)} %queries_ref.1, bf16[4,2,96,1024]{3,2,1,0:T(8,128)(2,1)} %pad_maximum_fusion.keyval_ref, ...), custom_call_target="tpu_custom_call" | custom-call | flops 1409286144 | bytes 6815744 | tf_op jit(solution)/shard_map/pallas_call | solution.py:139
  72.4 1.2 convert_element_type.77
  73.7 1.3 %collective-permute-start.11 = (bf16[2,48,1024]{2,1,0:T(8,128)(2,1)S(1)}, bf16[2,48,1024]{2,1,0:T(8,128)(2,1)S(1)}, u32[]{:S(2)}, u32[]{:S(2)}) collective-permute-start(bf16[2,48,1024]{2,1,0:T(8,128)(2,1)S(1)} %pad_maximum_fusion.5), channel_id=1, source_target_pairs={{0,1},{1,0},{2,3},{3,2},{4,5},{5,4},{6,7},{7,6},{8,9},{9,8},{10,11... | collective-permute-start | bytes 589832 | tf_op jit(solution)/shard_map/ppermute | solution.py:216
  75.0 4.7 %collective-permute-done.11 = bf16[2,48,1024]{2,1,0:T(8,128)(2,1)S(1)} collective-permute-done((bf16[2,48,1024]{2,1,0:T(8,128)(2,1)S(1)}, bf16[2,48,1024]{2,1,0:T(8,128)(2,1)S(1)}, u32[]{:S(2)}, u32[]{:S(2)}) %collective-permute-start.11) | collective-permute-done | bytes 196640 | tf_op jit(solution)/shard_map/ppermute | solution.py:216
  79.7 1.9 %collective-permute-start.12 = (bf16[48,1024]{1,0:T(8,128)(2,1)S(1)}, bf16[48,1024]{1,0:T(8,128)(2,1)S(1)}, u32[]{:S(2)}, u32[]{:S(2)}) collective-permute-start(bf16[48,1024]{1,0:T(8,128)(2,1)S(1)} %fusion.14), channel_id=1, source_target_pairs={{0,2},{1,3},{2,0},{3,1},{4,6},{5,7},{6,4},{7,5},{8,10},{9,11},{10,... | collective-permute-start | bytes 294920 | tf_op jit(solution)/shard_map/ppermute | solution.py:220
  81.6 6.2 %collective-permute-done.12 = bf16[48,1024]{1,0:T(8,128)(2,1)S(1)} collective-permute-done((bf16[48,1024]{1,0:T(8,128)(2,1)S(1)}, bf16[48,1024]{1,0:T(8,128)(2,1)S(1)}, u32[]{:S(2)}, u32[]{:S(2)}) %collective-permute-start.12) | collective-permute-done | bytes 98336 | tf_op jit(solution)/shard_map/ppermute | solution.py:220
  88.3 3.8 %collective-permute-start.13 = (bf16[48,1024]{1,0:T(8,128)(2,1)S(1)}, bf16[48,1024]{1,0:T(8,128)(2,1)S(1)}, u32[]{:S(2)}, u32[]{:S(2)}) collective-permute-start(bf16[48,1024]{1,0:T(8,128)(2,1)S(1)} %pad_maximum_fusion.7), channel_id=1, source_target_pairs={{0,1},{1,0},{2,3},{3,2},{4,5},{5,4},{6,7},{7,6},{8,9},{9,8},{10,11... | collective-permute-start | bytes 294920 | tf_op jit(solution)/shard_map/ppermute | solution.py:189
  92.2 4.4 %collective-permute-done.14 = bf16[48,1024]{1,0:T(8,128)(2,1)S(1)} collective-permute-done((bf16[48,1024]{1,0:T(8,128)(2,1)S(1)}, bf16[48,1024]{1,0:T(8,128)(2,1)S(1)}, u32[]{:S(2)}, u32[]{:S(2)}) %collective-permute-start.14) | collective-permute-done | bytes 98336 | tf_op jit(solution)/shard_map/ppermute | solution.py:188
  96.7 4.5 %collective-permute-done.15 = bf16[48,1024]{1,0:T(8,128)(2,1)S(1)} collective-permute-done((bf16[48,1024]{1,0:T(8,128)(2,1)S(1)}, bf16[48,1024]{1,0:T(8,128)(2,1)S(1)}, u32[]{:S(2)}, u32[]{:S(2)}) %collective-permute-start.15) | collective-permute-done | bytes 98336 | tf_op jit(solution)/shard_map/ppermute | solution.py:189
  101.2 0.6 gather_fusion.1
  102.0 3.7 %fusion.4 = bf16[192,2048]{1,0:T(8,128)(2,1)S(1)} fusion(bf16[192,1024]{1,0:T(8,128)(2,1)S(1)} %bitcast.81, bf16[1,2048,1024]{2,1,0:T(8,128)(2,1)} %param.12), kind=kOutput, calls=%fused_computation.6 | convolution fusion | flops 805699584 | bytes 5373952 | tf_op jit(solution)/shard_map/dot_general | solution.py:307
  105.9 1.7 %collective-permute-done.16 = bf16[2,2,24,2048]{3,2,1,0:T(8,128)(2,1)S(1)} collective-permute-done((bf16[2,2,24,2048]{3,2,1,0:T(8,128)(2,1)S(1)}, bf16[2,2,24,2048]{3,2,1,0:T(8,128)(2,1)S(1)}, u32[]{:S(2)}, u32[]{:S(2)}) %collective-permute-start.16) | collective-permute-done | bytes 393248 | tf_op jit(solution)/shard_map/ppermute | solution.py:216
  107.6 5.9 %collective-permute-start.17 = (bf16[2,24,2048]{2,1,0:T(8,128)(2,1)S(1)}, bf16[2,24,2048]{2,1,0:T(8,128)(2,1)S(1)}, u32[]{:S(2)}, u32[]{:S(2)}) collective-permute-start(bf16[2,24,2048]{2,1,0:T(8,128)(2,1)S(1)} %fusion.7), channel_id=1, source_target_pairs={{0,8},{4,12},{8,0},{12,4},{1,9},{5,13},{9,1},{13,5},{2,10},{6,14},... | collective-permute-start | bytes 589832 | tf_op jit(solution)/shard_map/ppermute | solution.py:220
  113.5 5.2 %collective-permute-done.17 = bf16[2,24,2048]{2,1,0:T(8,128)(2,1)S(1)} collective-permute-done((bf16[2,24,2048]{2,1,0:T(8,128)(2,1)S(1)}, bf16[2,24,2048]{2,1,0:T(8,128)(2,1)S(1)}, u32[]{:S(2)}, u32[]{:S(2)}) %collective-permute-start.17) | collective-permute-done | bytes 196640 | tf_op jit(solution)/shard_map/ppermute | solution.py:220
  118.8 0.8 bitcast_add_fusion
  (74 shorter events, 3.9 us)
Async XLA Ops:
  14.1 14.2 %copy-start.2 = (f32[1,4096]{1,0:T(1,128)S(1)}, f32[1,4096]{1,0:T(1,128)}, u32[]{:S(2)}) copy-start(f32[1,4096]{1,0:T(1,128)} %param.13) | copy-start | bytes 49156
  14.1 23.5 %copy-start.1 = (f32[1,512]{1,0:T(1,128)S(1)}, f32[1,512]{1,0:T(1,128)}, u32[]{:S(2)}) copy-start(f32[1,512]{1,0:T(1,128)} %param.14) | copy-start | bytes 6148
  14.2 11.4 %collective-permute-start.3 = (f32[2,48,1024]{2,1,0:T(8,128)S(1)}, f32[2,48,1024]{2,1,0:T(8,128)S(1)}, u32[]{:S(2)}, u32[]{:S(2)}) collective-permute-start(f32[2,48,1024]{2,1,0:T(8,128)S(1)} %pad_maximum_fusion.1), channel_id=1, source_target_pairs={{0,1},{1,0},{2,3},{3,2},{4,5},{5,4},{6,7},{7,6},{8,9},{9,8},{10,11... | collective-permute-start | bytes 1179656 | tf_op jit(solution)/shard_map/ppermute | solution.py:216
  25.6 11.5 %collective-permute-start.4 = (f32[48,1024]{1,0:T(8,128)S(1)}, f32[48,1024]{1,0:T(8,128)S(1)}, u32[]{:S(2)}, u32[]{:S(2)}) collective-permute-start(f32[48,1024]{1,0:T(8,128)S(1)} %fusion.8), channel_id=1, source_target_pairs={{0,2},{1,3},{2,0},{3,1},{4,6},{5,7},{6,4},{7,5},{8,10},{9,11},{10,... | collective-permute-start | bytes 589832 | tf_op jit(solution)/shard_map/ppermute | solution.py:220
  37.4 14.4 %copy-start.5 = (f32[1,32]{1,0:T(1,128)S(1)}, f32[1,32]{1,0:T(1,128)}, u32[]{:S(2)}) copy-start(f32[1,32]{1,0:T(1,128)} %param.15) | copy-start | bytes 388
  37.4 15.5 %copy-start.3 = (s32[2,96]{1,0:T(2,128)S(1)}, s32[2,96]{1,0:T(2,128)}, u32[]{:S(2)}) copy-start(s32[2,96]{1,0:T(2,128)} %param.18) | copy-start | bytes 2308
  37.4 15.5 %copy-start.4 = (s32[2,64]{1,0:T(2,128)S(1)}, s32[2,64]{1,0:T(2,128)}, u32[]{:S(2)}) copy-start(s32[2,64]{1,0:T(2,128)} %param.17) | copy-start | bytes 1540
  37.6 7.7 %collective-permute-start.6 = (bf16[48,1024]{1,0:T(8,128)(2,1)S(1)}, bf16[48,1024]{1,0:T(8,128)(2,1)S(1)}, u32[]{:S(2)}, u32[]{:S(2)}) collective-permute-start(bf16[48,1024]{1,0:T(8,128)(2,1)S(1)} %get-tuple-element.14), channel_id=1, source_target_pairs={{0,2},{1,3},{2,0},{3,1},{4,6},{5,7},{6,4},{7,5},{8,10},{9,11},{10,... | collective-permute-start | bytes 294920 | tf_op jit(solution)/shard_map/ppermute | solution.py:188
  37.7 7.9 %collective-permute-start.5 = (bf16[48,1024]{1,0:T(8,128)(2,1)S(1)}, bf16[48,1024]{1,0:T(8,128)(2,1)S(1)}, u32[]{:S(2)}, u32[]{:S(2)}) collective-permute-start(bf16[48,1024]{1,0:T(8,128)(2,1)S(1)} %get-tuple-element.14), channel_id=1, source_target_pairs={{0,1},{1,0},{2,3},{3,2},{4,5},{5,4},{6,7},{7,6},{8,9},{9,8},{10,11... | collective-permute-start | bytes 294920 | tf_op jit(solution)/shard_map/ppermute | solution.py:189
  45.3 4.6 %collective-permute-start.7 = (bf16[48,1024]{1,0:T(8,128)(2,1)S(1)}, bf16[48,1024]{1,0:T(8,128)(2,1)S(1)}, u32[]{:S(2)}, u32[]{:S(2)}) collective-permute-start(bf16[48,1024]{1,0:T(8,128)(2,1)S(1)} %collective-permute-done.6), channel_id=1, source_target_pairs={{0,1},{1,0},{2,3},{3,2},{4,5},{5,4},{6,7},{7,6},{8,9},{9,8},{10,11... | collective-permute-start | bytes 294920 | tf_op jit(solution)/shard_map/ppermute | solution.py:189
  50.7 10.2 %collective-permute-start.9 = (bf16[192,1024]{1,0:T(8,128)(2,1)S(1)}, bf16[192,1024]{1,0:T(8,128)(2,1)S(1)}, u32[]{:S(2)}, u32[]{:S(2)}) collective-permute-start(bf16[192,1024]{1,0:T(8,128)(2,1)S(1)} %bitcast.74), channel_id=1, source_target_pairs={{0,8},{4,12},{8,0},{12,4},{1,9},{5,13},{9,1},{13,5},{2,10},{6,14},... | collective-permute-start | bytes 1179656 | tf_op jit(solution)/shard_map/ppermute | solution.py:188
  51.9 6.8 %collective-permute-start.1 = (f32[4128]{0:T(1024)S(1)}, f32[4128]{0:T(1024)S(1)}, u32[]{:S(2)}, u32[]{:S(2)}) collective-permute-start(f32[4128]{0:T(1024)S(1)} %reduce), channel_id=1, source_target_pairs={{0,8},{4,12},{8,0},{12,4},{1,9},{5,13},{9,1},{13,5},{2,10},{6,14},... | collective-permute-start | bytes 49544 | tf_op jit(solution)/shard_map/ppermute | solution.py:188
  52.9 7.4 %collective-permute-start = (f32[4128]{0:T(1024)S(1)}, f32[4128]{0:T(1024)S(1)}, u32[]{:S(2)}, u32[]{:S(2)}) collective-permute-start(f32[4128]{0:T(1024)S(1)} %reduce), channel_id=1, source_target_pairs={{0,4},{4,0},{8,12},{12,8},{1,5},{5,1},{9,13},{13,9},{2,6},{6,2},{1... | collective-permute-start | bytes 49544 | tf_op jit(solution)/shard_map/ppermute | solution.py:189
  58.8 1.6 %collective-permute-start.2 = (f32[4128]{0:T(1024)S(1)}, f32[4128]{0:T(1024)S(1)}, u32[]{:S(2)}, u32[]{:S(2)}) collective-permute-start(f32[4128]{0:T(1024)S(1)} %collective-permute-done.1), channel_id=1, source_target_pairs={{0,4},{4,0},{8,12},{12,8},{1,5},{5,1},{9,13},{13,9},{2,6},{6,2},{1... | collective-permute-start | bytes 49544 | tf_op jit(solution)/shard_map/ppermute | solution.py:189
  59.3 4.9 %copy-start = (f32[2,8,64,96]{3,2,1,0:T(8,128)}, f32[2,8,64,96]{3,2,1,0:T(8,128)S(1)}, u32[]{:S(2)}) copy-start(f32[2,8,64,96]{3,2,1,0:T(8,128)S(1)} %tile.4) | copy-start | bytes 1179652
  60.4 2.0 %collective-permute-start.8 = (bf16[192,1024]{1,0:T(8,128)(2,1)S(1)}, bf16[192,1024]{1,0:T(8,128)(2,1)S(1)}, u32[]{:S(2)}, u32[]{:S(2)}) collective-permute-start(bf16[192,1024]{1,0:T(8,128)(2,1)S(1)} %bitcast.75), channel_id=1, source_target_pairs={{0,4},{4,0},{8,12},{12,8},{1,5},{5,1},{9,13},{13,9},{2,6},{6,2},{1... | collective-permute-start | bytes 1179656 | tf_op jit(solution)/shard_map/ppermute | solution.py:189
  60.9 1.9 %collective-permute-start.10 = (bf16[192,1024]{1,0:T(8,128)(2,1)S(1)}, bf16[192,1024]{1,0:T(8,128)(2,1)S(1)}, u32[]{:S(2)}, u32[]{:S(2)}) collective-permute-start(bf16[192,1024]{1,0:T(8,128)(2,1)S(1)} %collective-permute-done.9), channel_id=1, source_target_pairs={{0,4},{4,0},{8,12},{12,8},{1,5},{5,1},{9,13},{13,9},{2,6},{6,2},{1... | collective-permute-start | bytes 1179656 | tf_op jit(solution)/shard_map/ppermute | solution.py:189
  73.7 6.0 %collective-permute-start.11 = (bf16[2,48,1024]{2,1,0:T(8,128)(2,1)S(1)}, bf16[2,48,1024]{2,1,0:T(8,128)(2,1)S(1)}, u32[]{:S(2)}, u32[]{:S(2)}) collective-permute-start(bf16[2,48,1024]{2,1,0:T(8,128)(2,1)S(1)} %pad_maximum_fusion.5), channel_id=1, source_target_pairs={{0,1},{1,0},{2,3},{3,2},{4,5},{5,4},{6,7},{7,6},{8,9},{9,8},{10,11... | collective-permute-start | bytes 589832 | tf_op jit(solution)/shard_map/ppermute | solution.py:216
  79.7 8.1 %collective-permute-start.12 = (bf16[48,1024]{1,0:T(8,128)(2,1)S(1)}, bf16[48,1024]{1,0:T(8,128)(2,1)S(1)}, u32[]{:S(2)}, u32[]{:S(2)}) collective-permute-start(bf16[48,1024]{1,0:T(8,128)(2,1)S(1)} %fusion.14), channel_id=1, source_target_pairs={{0,2},{1,3},{2,0},{3,1},{4,6},{5,7},{6,4},{7,5},{8,10},{9,11},{10,... | collective-permute-start | bytes 294920 | tf_op jit(solution)/shard_map/ppermute | solution.py:220
  88.2 8.3 %collective-permute-start.14 = (bf16[48,1024]{1,0:T(8,128)(2,1)S(1)}, bf16[48,1024]{1,0:T(8,128)(2,1)S(1)}, u32[]{:S(2)}, u32[]{:S(2)}) collective-permute-start(bf16[48,1024]{1,0:T(8,128)(2,1)S(1)} %pad_maximum_fusion.7), channel_id=1, source_target_pairs={{0,2},{1,3},{2,0},{3,1},{4,6},{5,7},{6,4},{7,5},{8,10},{9,11},{10,... | collective-permute-start | bytes 294920 | tf_op jit(solution)/shard_map/ppermute | solution.py:188
  88.3 8.3 %collective-permute-start.13 = (bf16[48,1024]{1,0:T(8,128)(2,1)S(1)}, bf16[48,1024]{1,0:T(8,128)(2,1)S(1)}, u32[]{:S(2)}, u32[]{:S(2)}) collective-permute-start(bf16[48,1024]{1,0:T(8,128)(2,1)S(1)} %pad_maximum_fusion.7), channel_id=1, source_target_pairs={{0,1},{1,0},{2,3},{3,2},{4,5},{5,4},{6,7},{7,6},{8,9},{9,8},{10,11... | collective-permute-start | bytes 294920 | tf_op jit(solution)/shard_map/ppermute | solution.py:189
  96.6 4.6 %collective-permute-start.15 = (bf16[48,1024]{1,0:T(8,128)(2,1)S(1)}, bf16[48,1024]{1,0:T(8,128)(2,1)S(1)}, u32[]{:S(2)}, u32[]{:S(2)}) collective-permute-start(bf16[48,1024]{1,0:T(8,128)(2,1)S(1)} %collective-permute-done.14), channel_id=1, source_target_pairs={{0,1},{1,0},{2,3},{3,2},{4,5},{5,4},{6,7},{7,6},{8,9},{9,8},{10,11... | collective-permute-start | bytes 294920 | tf_op jit(solution)/shard_map/ppermute | solution.py:189
  105.8 1.8 %collective-permute-start.16 = (bf16[2,2,24,2048]{3,2,1,0:T(8,128)(2,1)S(1)}, bf16[2,2,24,2048]{3,2,1,0:T(8,128)(2,1)S(1)}, u32[]{:S(2)}, u32[]{:S(2)}) collective-permute-start(bf16[2,2,24,2048]{3,2,1,0:T(8,128)(2,1)S(1)} %pad_maximum_fusion.4), channel_id=1, source_target_pairs={{0,4},{4,0},{8,12},{12,8},{1,5},{5,1},{9,13},{13,9},{2,6},{6,2},{1... | collective-permute-start | bytes 1179656 | tf_op jit(solution)/shard_map/ppermute | solution.py:216
  107.6 11.1 %collective-permute-start.17 = (bf16[2,24,2048]{2,1,0:T(8,128)(2,1)S(1)}, bf16[2,24,2048]{2,1,0:T(8,128)(2,1)S(1)}, u32[]{:S(2)}, u32[]{:S(2)}) collective-permute-start(bf16[2,24,2048]{2,1,0:T(8,128)(2,1)S(1)} %fusion.7), channel_id=1, source_target_pairs={{0,8},{4,12},{8,0},{12,4},{1,9},{5,13},{9,1},{13,5},{2,10},{6,14},... | collective-permute-start | bytes 589832 | tf_op jit(solution)/shard_map/ppermute | solution.py:220

commit v5 on v4

--- a/solution.py
+++ b/solution.py
@@ -117,8 +117,8 @@
         inner = jnp.sum(probs_t * prob_grad_t, axis=0, keepdims=True)
         score_grad_t = (probs_t * (prob_grad_t - inner)).astype(jnp.bfloat16)
         key_grad = jnp.dot(score_grad_t, query, preferred_element_type=jnp.float32) * scale
-        grad_ref[:, head_cols(k)] = key_grad
-        grad_ref[:, pl.ds(key_width + k * head_dim, head_dim)] = value_grad
+        grad_ref[:, head_cols(k)] = key_grad.astype(grad_ref.dtype)
+        grad_ref[:, pl.ds(key_width + k * head_dim, head_dim)] = value_grad.astype(grad_ref.dtype)
 
     forward(section)
 
@@ -156,7 +156,7 @@
         ],
         out_shape=[
             jax.ShapeDtypeStruct((micro_count, token_count, query_width), jnp.float32),
-            jax.ShapeDtypeStruct((micro_count, image_count, pair_width), jnp.float32),
+            jax.ShapeDtypeStruct((micro_count, image_count, pair_width), jnp.bfloat16),
         ],
         compiler_params=pltpu.CompilerParams(dimension_semantics=("arbitrary",)),
         cost_estimate=pl.CostEstimate(
@@ -200,7 +200,7 @@
     return jnp.take(stacked, slots, axis=0)
 
 
-def scatter_blocks(blocks, axis):
+def scatter_blocks(blocks, axis, pairs):
     count = lax.axis_size(axis)
     if count > 8:
         return lax.psum_scatter(blocks, axis, scatter_dimension=0, tiled=True)[0].astype(
@@ -211,7 +211,7 @@
     def pick(i):
         return lax.dynamic_index_in_dim(blocks, i, 0, keepdims=False)
 
-    if count == 4:
+    if pairs and count == 4:
         partner = [(i, i ^ 1) for i in range(count)]
         got = lax.ppermute(jnp.stack([pick(index ^ 1), pick(index ^ 3)]), axis, partner)
         theirs = (pick(index ^ 2).astype(jnp.float32) + got[1].astype(jnp.float32)).astype(
@@ -265,7 +265,7 @@
     flat_rows = gathered.reshape(total_rows, gathered.shape[2])
     partial = jnp.dot(flat_rows, weights, preferred_element_type=jnp.float32)
     raw_rows = scatter_blocks(
-        partial.reshape(shard_count, total_rows // shard_count, 2 * key_width), "shard"
+        partial.reshape(shard_count, total_rows // shard_count, 2 * key_width), "shard", False
     )
     key_rows = head_normalize(raw_rows[:, :key_width], key_norm_gain[0], keyval_heads)
     keyval_rows = jnp.concatenate(
@@ -286,10 +286,9 @@
         cotangent[0],
     )
     grad_rows = scatter_blocks(
-        grad_local.astype(jnp.bfloat16).reshape(
-            shard_count, total_rows // shard_count, 2 * key_width
-        ),
+        grad_local.reshape(shard_count, total_rows // shard_count, 2 * key_width),
         "shard",
+        False,
     )
     key_portion = norm_gradient(
         raw_rows[:, :key_width], key_norm_gain[0], grad_rows[:, :key_width], keyval_heads
@@ -310,7 +309,7 @@
     image_part = image_part.astype(jnp.bfloat16).reshape(
         section_count, micro_count, owned, weights.shape[0]
     )
-    image_grad = scatter_blocks(image_part, "section")
+    image_grad = scatter_blocks(image_part, "section", True)
     return (leaving[None], image_grad)
 
 

time: 120 us -> 115 us (0.958)
  waiting for transfers between devices: 59.9 us -> 38.6 us
  starting transfers between devices: 24.3 us -> 39.7 us
    ppermute x0 -> x6, waiting for transfers between devices: none -> 16.6 us  [scatter_blocks(): lax.ppermute(part, axis, [(i, (i + d) % count) for i in range(count)])]
    ppermute x3 -> x1, waiting for transfers between devices: 20.3 us -> 5.2 us  [scatter_blocks(): back = lax.ppermute(theirs, axis, [(i, i ^ 2) for i in range(count)])]
    ppermute x3 -> x1, waiting for transfers between devices: 16.2 us -> 1.7 us  [scatter_blocks(): lax.ppermute(jnp.stack([pick(index ^ 1), pick(index ^ 3)]), axis, partner)]
    ppermute x0 -> x6, starting transfers between devices: none -> 12.5 us  [scatter_blocks(): lax.ppermute(part, axis, [(i, (i + d) % count) for i in range(count)])]
    ppermute x4, starting transfers between devices: 0.12 us -> 8.46 us  [gather_blocks(): lax.ppermute(across, axis, partner)]
    ppermute x4, starting transfers between devices: 2.3 us -> 7.79 us  [gather_blocks(): across = lax.ppermute(block, axis, [(i, i ^ 2) for i in range(count)])]
    ppermute x4, waiting for transfers between devices: 13.7 us -> 8.99 us  [gather_blocks(): across = lax.ppermute(block, axis, [(i, i ^ 2) for i in range(count)])]
    ppermute x3 -> x1, starting transfers between devices: 10.4 us -> 5.92 us  [scatter_blocks(): back = lax.ppermute(theirs, axis, [(i, i ^ 2) for i in range(count)])]
  transfers between devices with their start and end apart: 18 -> 20, of which waited for: 14 -> 13; matrix products, arithmetic and copies ran while one was open for 3% -> 3% of each run, Pallas kernels for 0% -> 0%
where the time goes in v5:
time: 115 us; the launch traced here: 114 us
  starting transfers between devices  39.7 us (35%)
  waiting for transfers between devices  38.6 us (34%)
  blocking collectives  10.3 us (9%)
  Pallas kernels  8.22 us (7%)
  matrix products  6.91 us (6%)
  other arithmetic  5.23 us (5%)
  local copies, waits for them, and re-layouts  4.32 us (4%)
    ppermute x6, waiting for transfers between devices, scatter_blocks(): lax.ppermute(part, axis, [(i, (i + d) % count) for i in range(count)])  16.6 us
    ppermute x6, starting transfers between devices, scatter_blocks(): lax.ppermute(part, axis, [(i, (i + d) % count) for i in range(count)])  12.5 us
    all_gather x1, blocking collectives, per_device(): gathered = lax.all_gather(image_tokens, 'section', axis=1, tiled=True)  10.3 us
    ppermute x4, waiting for transfers between devices, gather_blocks(): across = lax.ppermute(block, axis, [(i, i ^ 2) for i in range(count)])  8.99 us
    ppermute x4, starting transfers between devices, gather_blocks(): lax.ppermute(across, axis, partner)  8.46 us
    pallas_call x1, Pallas kernels, attention_layers(): pl.pallas_call(functools.partial(attention_kernel, head_count=head_count,...  8.22 us
    ppermute x4, starting transfers between devices, gather_blocks(): across = lax.ppermute(block, axis, [(i, i ^ 2) for i in range(count)])  7.79 us
    ppermute x4, waiting for transfers between devices, gather_blocks(): lax.ppermute(across, axis, partner)  6.1 us
  transfers between devices with their start and end apart: 20, of which 13 were waited for; matrix products, arithmetic and copies ran while one was open for 3% of the time, Pallas kernels for 0%

profile of v5, /device:TPU:0, one launch (start us, length us, event | category | flops | bytes accessed | tf_op | source)
XLA Modules:
  0.0 114.3 jit_solution(15464380285690716822)
XLA Ops:
  0.7 10.3 %all_gather.3 = bf16[2,96,2048]{2,1,0:T(8,128)(2,1)S(1)} all-gather(bf16[2,24,2048]{2,1,0:T(8,128)(2,1)} %param.11), channel_id=1, replica_groups=mesh['group'=2,'section'=4,'shard'=4] {'section'}, dimensions={1}, use_global_device_ids=true | all-gather | bytes 983040 | tf_op jit(solution)/shard_map/all_gather | solution.py:261
  10.9 3.2 %fusion = f32[4,48,1024]{2,1,0:T(8,128)S(1)} fusion(bf16[4,48,2048]{2,1,0:T(8,128)(2,1)S(1)} %bitcast.79, bf16[1,2048,1024]{2,1,0:T(8,128)(2,1)} %param.12), kind=kOutput, calls=%fused_computation.2 | convolution fusion | flops 805306368 | bytes 5767168 | tf_op jit(solution)/shard_map/dot_general | solution.py:266
  14.2 1.6 %collective-permute-start.3 = (f32[48,1024]{1,0:T(8,128)S(1)}, f32[48,1024]{1,0:T(8,128)S(1)}, u32[]{:S(2)}, u32[]{:S(2)}) collective-permute-start(f32[48,1024]{1,0:T(8,128)S(1)} %get-tuple-element.9), channel_id=1, source_target_pairs={{0,1},{1,2},{2,3},{3,0},{4,5},{5,6},{6,7},{7,4},{8,9},{9,10},{10,1... | collective-permute-start | bytes 589832 | tf_op jit(solution)/shard_map/ppermute | solution.py:229
  15.8 2.6 %collective-permute-start.4 = (f32[48,1024]{1,0:T(8,128)S(1)}, f32[48,1024]{1,0:T(8,128)S(1)}, u32[]{:S(2)}, u32[]{:S(2)}) collective-permute-start(f32[48,1024]{1,0:T(8,128)S(1)} %get-tuple-element.11), channel_id=1, source_target_pairs={{0,2},{1,3},{2,0},{3,1},{4,6},{5,7},{6,4},{7,5},{8,10},{9,11},{10,... | collective-permute-start | bytes 589832 | tf_op jit(solution)/shard_map/ppermute | solution.py:229
  18.4 1.3 %collective-permute-start.5 = (f32[48,1024]{1,0:T(8,128)S(1)}, f32[48,1024]{1,0:T(8,128)S(1)}, u32[]{:S(2)}, u32[]{:S(2)}) collective-permute-start(f32[48,1024]{1,0:T(8,128)S(1)} %get-tuple-element.10), channel_id=1, source_target_pairs={{0,3},{1,0},{2,1},{3,2},{4,7},{5,4},{6,5},{7,6},{8,11},{9,8},{10,9... | collective-permute-start | bytes 589832 | tf_op jit(solution)/shard_map/ppermute | solution.py:229
  19.8 4.1 %collective-permute-done.3 = f32[48,1024]{1,0:T(8,128)S(1)} collective-permute-done((f32[48,1024]{1,0:T(8,128)S(1)}, f32[48,1024]{1,0:T(8,128)S(1)}, u32[]{:S(2)}, u32[]{:S(2)}) %collective-permute-start.3) | collective-permute-done | bytes 196640 | tf_op jit(solution)/shard_map/ppermute | solution.py:229
  23.9 7.9 %collective-permute-done.4 = f32[48,1024]{1,0:T(8,128)S(1)} collective-permute-done((f32[48,1024]{1,0:T(8,128)S(1)}, f32[48,1024]{1,0:T(8,128)S(1)}, u32[]{:S(2)}, u32[]{:S(2)}) %collective-permute-start.4) | collective-permute-done | bytes 196640 | tf_op jit(solution)/shard_map/ppermute | solution.py:229
  32.3 3.7 %collective-permute-start.7 = (bf16[48,1024]{1,0:T(8,128)(2,1)S(1)}, bf16[48,1024]{1,0:T(8,128)(2,1)S(1)}, u32[]{:S(2)}, u32[]{:S(2)}) collective-permute-start(bf16[48,1024]{1,0:T(8,128)(2,1)S(1)} %get-tuple-element.16), channel_id=1, source_target_pairs={{0,2},{1,3},{2,0},{3,1},{4,6},{5,7},{6,4},{7,5},{8,10},{9,11},{10,... | collective-permute-start | bytes 294920 | tf_op jit(solution)/shard_map/ppermute | solution.py:188
  36.0 2.6 %collective-permute-start.6 = (bf16[48,1024]{1,0:T(8,128)(2,1)S(1)}, bf16[48,1024]{1,0:T(8,128)(2,1)S(1)}, u32[]{:S(2)}, u32[]{:S(2)}) collective-permute-start(bf16[48,1024]{1,0:T(8,128)(2,1)S(1)} %get-tuple-element.16), channel_id=1, source_target_pairs={{0,1},{1,0},{2,3},{3,2},{4,5},{5,4},{6,7},{7,6},{8,9},{9,8},{10,11... | collective-permute-start | bytes 294920 | tf_op jit(solution)/shard_map/ppermute | solution.py:189
  39.0 4.6 %collective-permute-start.8 = (bf16[48,1024]{1,0:T(8,128)(2,1)S(1)}, bf16[48,1024]{1,0:T(8,128)(2,1)S(1)}, u32[]{:S(2)}, u32[]{:S(2)}) collective-permute-start(bf16[48,1024]{1,0:T(8,128)(2,1)S(1)} %collective-permute-done.7), channel_id=1, source_target_pairs={{0,1},{1,0},{2,3},{3,2},{4,5},{5,4},{6,7},{7,6},{8,9},{9,8},{10,11... | collective-permute-start | bytes 294920 | tf_op jit(solution)/shard_map/ppermute | solution.py:189
  43.6 2.6 %collective-permute-done.8 = bf16[48,1024]{1,0:T(8,128)(2,1)S(1)} collective-permute-done((bf16[48,1024]{1,0:T(8,128)(2,1)S(1)}, bf16[48,1024]{1,0:T(8,128)(2,1)S(1)}, u32[]{:S(2)}, u32[]{:S(2)}) %collective-permute-start.8) | collective-permute-done | bytes 98336 | tf_op jit(solution)/shard_map/ppermute | solution.py:189
  46.9 1.2 %collective-permute-start.10 = (bf16[192,1024]{1,0:T(8,128)(2,1)S(1)}, bf16[192,1024]{1,0:T(8,128)(2,1)S(1)}, u32[]{:S(2)}, u32[]{:S(2)}) collective-permute-start(bf16[192,1024]{1,0:T(8,128)(2,1)S(1)} %bitcast.85), channel_id=1, source_target_pairs={{0,8},{4,12},{8,0},{12,4},{1,9},{5,13},{9,1},{13,5},{2,10},{6,14},... | collective-permute-start | bytes 1179656 | tf_op jit(solution)/shard_map/ppermute | solution.py:188
  48.2 1.0 collective-permute-start.1
  49.3 6.6 %collective-permute-done.1 = f32[4128]{0:T(1024)S(1)} collective-permute-done((f32[4128]{0:T(1024)S(1)}, f32[4128]{0:T(1024)S(1)}, u32[]{:S(2)}, u32[]{:S(2)}) %collective-permute-start.1) | collective-permute-done | bytes 16544 | tf_op jit(solution)/shard_map/ppermute | solution.py:188
  60.0 1.4 %pad_maximum_fusion.keyval_ref = bf16[4,2,96,1024]{3,2,1,0:T(8,128)(2,1)} fusion(bf16[1,2,96,1024]{3,2,1,0:T(8,128)(2,1)S(1)} %bitcast.96, bf16[1,2,96,1024]{3,2,1,0:T(8,128)(2,1)S(1)} %bitcast.93, bf16[1,2,96,1024]{3,2,1,0:T(8,128)(2,1)S(1)} %bitcast.95, bf16[1,2,96,1024]{3,2,1,0:T(8,128)(2,1)S(1)} %bitcast.87), kind=kLoop, calls=%fused_computation.7 | loop fusion | flops 2359296 | bytes 3145728 | tf_op jit(solution)/shard_map/stack | solution.py:190
  61.4 8.2 %shard_map.104 = (f32[2,64,4096]{2,1,0:T(8,128)}, bf16[2,96,1024]{2,1,0:T(8,128)(2,1)}) custom-call(s32[1]{0:T(128)} %bitcast.section_ref, s32[4]{0:T(128)} %iota_xor_fusion.slots_ref, f32[4,32]{1,0:T(4,128)} %maximum_tanh_fusion.gates_ref, bf16[2,64,4096]{2,1,0:T(8,128)(2,1)} %queries_ref.1, bf16[4,2,96,1024]{3,2,1,0:T(8,128)(2,1)} %pad_maximum_fusion.keyval_ref, ...), custom_call_target="tpu_custom_call" | custom-call | flops 1409286144 | bytes 6815744 | tf_op jit(solution)/shard_map/pallas_call | solution.py:139
  69.6 1.0 dynamic-slice_bitcast_fusion.5
  70.6 1.8 %collective-permute-start.12 = (bf16[48,1024]{1,0:T(8,128)(2,1)S(1)}, bf16[48,1024]{1,0:T(8,128)(2,1)S(1)}, u32[]{:S(2)}, u32[]{:S(2)}) collective-permute-start(bf16[48,1024]{1,0:T(8,128)(2,1)S(1)} %get-tuple-element.12), channel_id=1, source_target_pairs={{0,1},{1,2},{2,3},{3,0},{4,5},{5,6},{6,7},{7,4},{8,9},{9,10},{10,1... | collective-permute-start | bytes 294920 | tf_op jit(solution)/shard_map/ppermute | solution.py:229
  72.4 3.7 %collective-permute-start.13 = (bf16[48,1024]{1,0:T(8,128)(2,1)S(1)}, bf16[48,1024]{1,0:T(8,128)(2,1)S(1)}, u32[]{:S(2)}, u32[]{:S(2)}) collective-permute-start(bf16[48,1024]{1,0:T(8,128)(2,1)S(1)} %get-tuple-element.14), channel_id=1, source_target_pairs={{0,2},{1,3},{2,0},{3,1},{4,6},{5,7},{6,4},{7,5},{8,10},{9,11},{10,... | collective-permute-start | bytes 294920 | tf_op jit(solution)/shard_map/ppermute | solution.py:229
  76.1 1.5 %collective-permute-start.14 = (bf16[48,1024]{1,0:T(8,128)(2,1)S(1)}, bf16[48,1024]{1,0:T(8,128)(2,1)S(1)}, u32[]{:S(2)}, u32[]{:S(2)}) collective-permute-start(bf16[48,1024]{1,0:T(8,128)(2,1)S(1)} %get-tuple-element.13), channel_id=1, source_target_pairs={{0,3},{1,0},{2,1},{3,2},{4,7},{5,4},{6,5},{7,6},{8,11},{9,8},{10,9... | collective-permute-start | bytes 294920 | tf_op jit(solution)/shard_map/ppermute | solution.py:229
  78.1 1.0 collective-permute-done.13
  79.2 2.9 %collective-permute-done.14 = bf16[48,1024]{1,0:T(8,128)(2,1)S(1)} collective-permute-done((bf16[48,1024]{1,0:T(8,128)(2,1)S(1)}, bf16[48,1024]{1,0:T(8,128)(2,1)S(1)}, u32[]{:S(2)}, u32[]{:S(2)}) %collective-permute-start.14) | collective-permute-done | bytes 98336 | tf_op jit(solution)/shard_map/ppermute | solution.py:229
  82.1 0.9 fusion.9
  83.4 1.9 %collective-permute-start.16 = (bf16[48,1024]{1,0:T(8,128)(2,1)S(1)}, bf16[48,1024]{1,0:T(8,128)(2,1)S(1)}, u32[]{:S(2)}, u32[]{:S(2)}) collective-permute-start(bf16[48,1024]{1,0:T(8,128)(2,1)S(1)} %pad_maximum_fusion.5), channel_id=1, source_target_pairs={{0,2},{1,3},{2,0},{3,1},{4,6},{5,7},{6,4},{7,5},{8,10},{9,11},{10,... | collective-permute-start | bytes 294920 | tf_op jit(solution)/shard_map/ppermute | solution.py:188
  85.3 1.7 %collective-permute-start.15 = (bf16[48,1024]{1,0:T(8,128)(2,1)S(1)}, bf16[48,1024]{1,0:T(8,128)(2,1)S(1)}, u32[]{:S(2)}, u32[]{:S(2)}) collective-permute-start(bf16[48,1024]{1,0:T(8,128)(2,1)S(1)} %pad_maximum_fusion.5), channel_id=1, source_target_pairs={{0,1},{1,0},{2,3},{3,2},{4,5},{5,4},{6,7},{7,6},{8,9},{9,8},{10,11... | collective-permute-start | bytes 294920 | tf_op jit(solution)/shard_map/ppermute | solution.py:189
  87.1 2.0 %collective-permute-done.16 = bf16[48,1024]{1,0:T(8,128)(2,1)S(1)} collective-permute-done((bf16[48,1024]{1,0:T(8,128)(2,1)S(1)}, bf16[48,1024]{1,0:T(8,128)(2,1)S(1)}, u32[]{:S(2)}, u32[]{:S(2)}) %collective-permute-start.16) | collective-permute-done | bytes 98336 | tf_op jit(solution)/shard_map/ppermute | solution.py:188
  89.0 3.8 %collective-permute-start.17 = (bf16[48,1024]{1,0:T(8,128)(2,1)S(1)}, bf16[48,1024]{1,0:T(8,128)(2,1)S(1)}, u32[]{:S(2)}, u32[]{:S(2)}) collective-permute-start(bf16[48,1024]{1,0:T(8,128)(2,1)S(1)} %collective-permute-done.16), channel_id=1, source_target_pairs={{0,1},{1,0},{2,3},{3,2},{4,5},{5,4},{6,7},{7,6},{8,9},{9,8},{10,11... | collective-permute-start | bytes 294920 | tf_op jit(solution)/shard_map/ppermute | solution.py:189
  92.9 3.0 %collective-permute-done.17 = bf16[48,1024]{1,0:T(8,128)(2,1)S(1)} collective-permute-done((bf16[48,1024]{1,0:T(8,128)(2,1)S(1)}, bf16[48,1024]{1,0:T(8,128)(2,1)S(1)}, u32[]{:S(2)}, u32[]{:S(2)}) %collective-permute-start.17) | collective-permute-done | bytes 98336 | tf_op jit(solution)/shard_map/ppermute | solution.py:189
  96.6 3.7 %fusion.4 = bf16[192,2048]{1,0:T(8,128)(2,1)S(1)} fusion(bf16[192,1024]{1,0:T(8,128)(2,1)S(1)} %bitcast.89, bf16[1,2048,1024]{2,1,0:T(8,128)(2,1)} %param.12), kind=kOutput, calls=%fused_computation.6 | convolution fusion | flops 805699584 | bytes 5373952 | tf_op jit(solution)/shard_map/dot_general | solution.py:306
  100.6 1.7 %collective-permute-done.18 = bf16[2,2,24,2048]{3,2,1,0:T(8,128)(2,1)S(1)} collective-permute-done((bf16[2,2,24,2048]{3,2,1,0:T(8,128)(2,1)S(1)}, bf16[2,2,24,2048]{3,2,1,0:T(8,128)(2,1)S(1)}, u32[]{:S(2)}, u32[]{:S(2)}) %collective-permute-start.18) | collective-permute-done | bytes 393248 | tf_op jit(solution)/shard_map/ppermute | solution.py:216
  102.3 5.9 %collective-permute-start.19 = (bf16[2,24,2048]{2,1,0:T(8,128)(2,1)S(1)}, bf16[2,24,2048]{2,1,0:T(8,128)(2,1)S(1)}, u32[]{:S(2)}, u32[]{:S(2)}) collective-permute-start(bf16[2,24,2048]{2,1,0:T(8,128)(2,1)S(1)} %fusion.7), channel_id=1, source_target_pairs={{0,8},{4,12},{8,0},{12,4},{1,9},{5,13},{9,1},{13,5},{2,10},{6,14},... | collective-permute-start | bytes 589832 | tf_op jit(solution)/shard_map/ppermute | solution.py:220
  108.2 5.2 %collective-permute-done.19 = bf16[2,24,2048]{2,1,0:T(8,128)(2,1)S(1)} collective-permute-done((bf16[2,24,2048]{2,1,0:T(8,128)(2,1)S(1)}, bf16[2,24,2048]{2,1,0:T(8,128)(2,1)S(1)}, u32[]{:S(2)}, u32[]{:S(2)}) %collective-permute-start.19) | collective-permute-done | bytes 196640 | tf_op jit(solution)/shard_map/ppermute | solution.py:220
  (73 shorter events, 8.5 us)
Async XLA Ops:
  10.9 8.8 %copy-start.2 = (f32[1,4096]{1,0:T(1,128)S(1)}, f32[1,4096]{1,0:T(1,128)}, u32[]{:S(2)}) copy-start(f32[1,4096]{1,0:T(1,128)} %param.13) | copy-start | bytes 49156
  14.1 18.1 %copy-start.1 = (f32[1,512]{1,0:T(1,128)S(1)}, f32[1,512]{1,0:T(1,128)}, u32[]{:S(2)}) copy-start(f32[1,512]{1,0:T(1,128)} %param.14) | copy-start | bytes 6148
  14.2 9.7 %collective-permute-start.3 = (f32[48,1024]{1,0:T(8,128)S(1)}, f32[48,1024]{1,0:T(8,128)S(1)}, u32[]{:S(2)}, u32[]{:S(2)}) collective-permute-start(f32[48,1024]{1,0:T(8,128)S(1)} %get-tuple-element.9), channel_id=1, source_target_pairs={{0,1},{1,2},{2,3},{3,0},{4,5},{5,6},{6,7},{7,4},{8,9},{9,10},{10,1... | collective-permute-start | bytes 589832 | tf_op jit(solution)/shard_map/ppermute | solution.py:229
  15.8 16.0 %collective-permute-start.4 = (f32[48,1024]{1,0:T(8,128)S(1)}, f32[48,1024]{1,0:T(8,128)S(1)}, u32[]{:S(2)}, u32[]{:S(2)}) collective-permute-start(f32[48,1024]{1,0:T(8,128)S(1)} %get-tuple-element.11), channel_id=1, source_target_pairs={{0,2},{1,3},{2,0},{3,1},{4,6},{5,7},{6,4},{7,5},{8,10},{9,11},{10,... | collective-permute-start | bytes 589832 | tf_op jit(solution)/shard_map/ppermute | solution.py:229
  18.4 13.4 %collective-permute-start.5 = (f32[48,1024]{1,0:T(8,128)S(1)}, f32[48,1024]{1,0:T(8,128)S(1)}, u32[]{:S(2)}, u32[]{:S(2)}) collective-permute-start(f32[48,1024]{1,0:T(8,128)S(1)} %get-tuple-element.10), channel_id=1, source_target_pairs={{0,3},{1,0},{2,1},{3,2},{4,7},{5,4},{6,5},{7,6},{8,11},{9,8},{10,9... | collective-permute-start | bytes 589832 | tf_op jit(solution)/shard_map/ppermute | solution.py:229
  32.1 16.0 %copy-start.5 = (f32[1,32]{1,0:T(1,128)S(1)}, f32[1,32]{1,0:T(1,128)}, u32[]{:S(2)}) copy-start(f32[1,32]{1,0:T(1,128)} %param.15) | copy-start | bytes 388
  32.1 17.1 %copy-start.3 = (s32[2,96]{1,0:T(2,128)S(1)}, s32[2,96]{1,0:T(2,128)}, u32[]{:S(2)}) copy-start(s32[2,96]{1,0:T(2,128)} %param.18) | copy-start | bytes 2308
  32.1 17.1 %copy-start.4 = (s32[2,64]{1,0:T(2,128)S(1)}, s32[2,64]{1,0:T(2,128)}, u32[]{:S(2)}) copy-start(s32[2,64]{1,0:T(2,128)} %param.17) | copy-start | bytes 1540
  32.3 6.8 %collective-permute-start.7 = (bf16[48,1024]{1,0:T(8,128)(2,1)S(1)}, bf16[48,1024]{1,0:T(8,128)(2,1)S(1)}, u32[]{:S(2)}, u32[]{:S(2)}) collective-permute-start(bf16[48,1024]{1,0:T(8,128)(2,1)S(1)} %get-tuple-element.16), channel_id=1, source_target_pairs={{0,2},{1,3},{2,0},{3,1},{4,6},{5,7},{6,4},{7,5},{8,10},{9,11},{10,... | collective-permute-start | bytes 294920 | tf_op jit(solution)/shard_map/ppermute | solution.py:188
  36.0 7.6 %collective-permute-start.6 = (bf16[48,1024]{1,0:T(8,128)(2,1)S(1)}, bf16[48,1024]{1,0:T(8,128)(2,1)S(1)}, u32[]{:S(2)}, u32[]{:S(2)}) collective-permute-start(bf16[48,1024]{1,0:T(8,128)(2,1)S(1)} %get-tuple-element.16), channel_id=1, source_target_pairs={{0,1},{1,0},{2,3},{3,2},{4,5},{5,4},{6,7},{7,6},{8,9},{9,8},{10,11... | collective-permute-start | bytes 294920 | tf_op jit(solution)/shard_map/ppermute | solution.py:189
  39.0 7.2 %collective-permute-start.8 = (bf16[48,1024]{1,0:T(8,128)(2,1)S(1)}, bf16[48,1024]{1,0:T(8,128)(2,1)S(1)}, u32[]{:S(2)}, u32[]{:S(2)}) collective-permute-start(bf16[48,1024]{1,0:T(8,128)(2,1)S(1)} %collective-permute-done.7), channel_id=1, source_target_pairs={{0,1},{1,0},{2,3},{3,2},{4,5},{5,4},{6,7},{7,6},{8,9},{9,8},{10,11... | collective-permute-start | bytes 294920 | tf_op jit(solution)/shard_map/ppermute | solution.py:189
  46.9 11.1 %collective-permute-start.10 = (bf16[192,1024]{1,0:T(8,128)(2,1)S(1)}, bf16[192,1024]{1,0:T(8,128)(2,1)S(1)}, u32[]{:S(2)}, u32[]{:S(2)}) collective-permute-start(bf16[192,1024]{1,0:T(8,128)(2,1)S(1)} %bitcast.85), channel_id=1, source_target_pairs={{0,8},{4,12},{8,0},{12,4},{1,9},{5,13},{9,1},{13,5},{2,10},{6,14},... | collective-permute-start | bytes 1179656 | tf_op jit(solution)/shard_map/ppermute | solution.py:188
  48.2 7.7 %collective-permute-start.1 = (f32[4128]{0:T(1024)S(1)}, f32[4128]{0:T(1024)S(1)}, u32[]{:S(2)}, u32[]{:S(2)}) collective-permute-start(f32[4128]{0:T(1024)S(1)} %reduce), channel_id=1, source_target_pairs={{0,8},{4,12},{8,0},{12,4},{1,9},{5,13},{9,1},{13,5},{2,10},{6,14},... | collective-permute-start | bytes 49544 | tf_op jit(solution)/shard_map/ppermute | solution.py:188
  49.2 8.3 %collective-permute-start = (f32[4128]{0:T(1024)S(1)}, f32[4128]{0:T(1024)S(1)}, u32[]{:S(2)}, u32[]{:S(2)}) collective-permute-start(f32[4128]{0:T(1024)S(1)} %reduce), channel_id=1, source_target_pairs={{0,4},{4,0},{8,12},{12,8},{1,5},{5,1},{9,13},{13,9},{2,6},{6,2},{1... | collective-permute-start | bytes 49544 | tf_op jit(solution)/shard_map/ppermute | solution.py:189
  55.9 1.6 %collective-permute-start.2 = (f32[4128]{0:T(1024)S(1)}, f32[4128]{0:T(1024)S(1)}, u32[]{:S(2)}, u32[]{:S(2)}) collective-permute-start(f32[4128]{0:T(1024)S(1)} %collective-permute-done.1), channel_id=1, source_target_pairs={{0,4},{4,0},{8,12},{12,8},{1,5},{5,1},{9,13},{13,9},{2,6},{6,2},{1... | collective-permute-start | bytes 49544 | tf_op jit(solution)/shard_map/ppermute | solution.py:189
  56.5 4.9 %copy-start = (f32[2,8,64,96]{3,2,1,0:T(8,128)}, f32[2,8,64,96]{3,2,1,0:T(8,128)S(1)}, u32[]{:S(2)}) copy-start(f32[2,8,64,96]{3,2,1,0:T(8,128)S(1)} %tile.4) | copy-start | bytes 1179652
  57.5 2.0 %collective-permute-start.9 = (bf16[192,1024]{1,0:T(8,128)(2,1)S(1)}, bf16[192,1024]{1,0:T(8,128)(2,1)S(1)}, u32[]{:S(2)}, u32[]{:S(2)}) collective-permute-start(bf16[192,1024]{1,0:T(8,128)(2,1)S(1)} %bitcast.86), channel_id=1, source_target_pairs={{0,4},{4,0},{8,12},{12,8},{1,5},{5,1},{9,13},{13,9},{2,6},{6,2},{1... | collective-permute-start | bytes 1179656 | tf_op jit(solution)/shard_map/ppermute | solution.py:189
  58.1 1.9 %collective-permute-start.11 = (bf16[192,1024]{1,0:T(8,128)(2,1)S(1)}, bf16[192,1024]{1,0:T(8,128)(2,1)S(1)}, u32[]{:S(2)}, u32[]{:S(2)}) collective-permute-start(bf16[192,1024]{1,0:T(8,128)(2,1)S(1)} %collective-permute-done.10), channel_id=1, source_target_pairs={{0,4},{4,0},{8,12},{12,8},{1,5},{5,1},{9,13},{13,9},{2,6},{6,2},{1... | collective-permute-start | bytes 1179656 | tf_op jit(solution)/shard_map/ppermute | solution.py:189
  70.6 7.6 %collective-permute-start.12 = (bf16[48,1024]{1,0:T(8,128)(2,1)S(1)}, bf16[48,1024]{1,0:T(8,128)(2,1)S(1)}, u32[]{:S(2)}, u32[]{:S(2)}) collective-permute-start(bf16[48,1024]{1,0:T(8,128)(2,1)S(1)} %get-tuple-element.12), channel_id=1, source_target_pairs={{0,1},{1,2},{2,3},{3,0},{4,5},{5,6},{6,7},{7,4},{8,9},{9,10},{10,1... | collective-permute-start | bytes 294920 | tf_op jit(solution)/shard_map/ppermute | solution.py:229
  72.4 6.8 %collective-permute-start.13 = (bf16[48,1024]{1,0:T(8,128)(2,1)S(1)}, bf16[48,1024]{1,0:T(8,128)(2,1)S(1)}, u32[]{:S(2)}, u32[]{:S(2)}) collective-permute-start(bf16[48,1024]{1,0:T(8,128)(2,1)S(1)} %get-tuple-element.14), channel_id=1, source_target_pairs={{0,2},{1,3},{2,0},{3,1},{4,6},{5,7},{6,4},{7,5},{8,10},{9,11},{10,... | collective-permute-start | bytes 294920 | tf_op jit(solution)/shard_map/ppermute | solution.py:229
  76.1 6.0 %collective-permute-start.14 = (bf16[48,1024]{1,0:T(8,128)(2,1)S(1)}, bf16[48,1024]{1,0:T(8,128)(2,1)S(1)}, u32[]{:S(2)}, u32[]{:S(2)}) collective-permute-start(bf16[48,1024]{1,0:T(8,128)(2,1)S(1)} %get-tuple-element.13), channel_id=1, source_target_pairs={{0,3},{1,0},{2,1},{3,2},{4,7},{5,4},{6,5},{7,6},{8,11},{9,8},{10,9... | collective-permute-start | bytes 294920 | tf_op jit(solution)/shard_map/ppermute | solution.py:229
  83.4 5.6 %collective-permute-start.16 = (bf16[48,1024]{1,0:T(8,128)(2,1)S(1)}, bf16[48,1024]{1,0:T(8,128)(2,1)S(1)}, u32[]{:S(2)}, u32[]{:S(2)}) collective-permute-start(bf16[48,1024]{1,0:T(8,128)(2,1)S(1)} %pad_maximum_fusion.5), channel_id=1, source_target_pairs={{0,2},{1,3},{2,0},{3,1},{4,6},{5,7},{6,4},{7,5},{8,10},{9,11},{10,... | collective-permute-start | bytes 294920 | tf_op jit(solution)/shard_map/ppermute | solution.py:188
  85.3 7.5 %collective-permute-start.15 = (bf16[48,1024]{1,0:T(8,128)(2,1)S(1)}, bf16[48,1024]{1,0:T(8,128)(2,1)S(1)}, u32[]{:S(2)}, u32[]{:S(2)}) collective-permute-start(bf16[48,1024]{1,0:T(8,128)(2,1)S(1)} %pad_maximum_fusion.5), channel_id=1, source_target_pairs={{0,1},{1,0},{2,3},{3,2},{4,5},{5,4},{6,7},{7,6},{8,9},{9,8},{10,11... | collective-permute-start | bytes 294920 | tf_op jit(solution)/shard_map/ppermute | solution.py:189
  89.0 6.9 %collective-permute-start.17 = (bf16[48,1024]{1,0:T(8,128)(2,1)S(1)}, bf16[48,1024]{1,0:T(8,128)(2,1)S(1)}, u32[]{:S(2)}, u32[]{:S(2)}) collective-permute-start(bf16[48,1024]{1,0:T(8,128)(2,1)S(1)} %collective-permute-done.16), channel_id=1, source_target_pairs={{0,1},{1,0},{2,3},{3,2},{4,5},{5,4},{6,7},{7,6},{8,9},{9,8},{10,11... | collective-permute-start | bytes 294920 | tf_op jit(solution)/shard_map/ppermute | solution.py:189
  100.5 1.8 %collective-permute-start.18 = (bf16[2,2,24,2048]{3,2,1,0:T(8,128)(2,1)S(1)}, bf16[2,2,24,2048]{3,2,1,0:T(8,128)(2,1)S(1)}, u32[]{:S(2)}, u32[]{:S(2)}) collective-permute-start(bf16[2,2,24,2048]{3,2,1,0:T(8,128)(2,1)S(1)} %pad_maximum_fusion.3), channel_id=1, source_target_pairs={{0,4},{4,0},{8,12},{12,8},{1,5},{5,1},{9,13},{13,9},{2,6},{6,2},{1... | collective-permute-start | bytes 1179656 | tf_op jit(solution)/shard_map/ppermute | solution.py:216
  102.3 11.1 %collective-permute-start.19 = (bf16[2,24,2048]{2,1,0:T(8,128)(2,1)S(1)}, bf16[2,24,2048]{2,1,0:T(8,128)(2,1)S(1)}, u32[]{:S(2)}, u32[]{:S(2)}) collective-permute-start(bf16[2,24,2048]{2,1,0:T(8,128)(2,1)S(1)} %fusion.7), channel_id=1, source_target_pairs={{0,8},{4,12},{8,0},{12,4},{1,9},{5,13},{9,1},{13,5},{2,10},{6,14},... | collective-permute-start | bytes 589832 | tf_op jit(solution)/shard_map/ppermute | solution.py:220

commit v6 on v5

--- a/solution.py
+++ b/solution.py
@@ -258,14 +258,19 @@
     gains_all = layer_params[:, : query_gain.shape[1]]
     gates_all = layer_params[:, query_gain.shape[1] :]
 
-    gathered = lax.all_gather(image_tokens, "section", axis=1, tiled=True)
+    gathered = in_order(image_tokens, "section")
+    gathered = gathered.transpose(1, 0, 2, 3).reshape(
+        micro_count, -1, image_tokens.shape[2]
+    )
     shard_count = lax.axis_size("shard")
     image_count = gathered.shape[1]
     total_rows = micro_count * image_count
     flat_rows = gathered.reshape(total_rows, gathered.shape[2])
     partial = jnp.dot(flat_rows, weights, preferred_element_type=jnp.float32)
     raw_rows = scatter_blocks(
-        partial.reshape(shard_count, total_rows // shard_count, 2 * key_width), "shard", False
+        partial.astype(jnp.bfloat16).reshape(shard_count, total_rows // shard_count, 2 * key_width),
+        "shard",
+        False,
     )
     key_rows = head_normalize(raw_rows[:, :key_width], key_norm_gain[0], keyval_heads)
     keyval_rows = jnp.concatenate(

time: 115 us -> 107 us (0.930)
  blocking collectives: 10.3 us -> 0 us
  other arithmetic: 5.23 us -> 6.44 us
    all_gather x1 -> x0, blocking collectives: 10.3 us -> none  [per_device(): gathered = lax.all_gather(image_tokens, 'section', axis=1, tiled=True)]
    ppermute x6, waiting for transfers between devices: 16.6 us -> 9.71 us  [scatter_blocks(): lax.ppermute(part, axis, [(i, (i + d) % count) for i in range(count)])]
    ppermute x4 -> x5, waiting for transfers between devices: 8.99 us -> 14.8 us  [gather_blocks(): across = lax.ppermute(block, axis, [(i, i ^ 2) for i in range(count)])]
    ppermute x4 -> x5, waiting for transfers between devices: 6.1 us -> 7.47 us  [gather_blocks(): lax.ppermute(across, axis, partner)]
    ppermute x4 -> x5, starting transfers between devices: 7.79 us -> 8.98 us  [gather_blocks(): across = lax.ppermute(block, axis, [(i, i ^ 2) for i in range(count)])]
    another operation x5 -> x6, other arithmetic: 1.52 us -> 2.57 us  [gather_blocks(): return (jnp.stack(received), lax.bitwise_xor(index, positions))]
    ppermute x4 -> x5, starting transfers between devices: 8.46 us -> 7.61 us  [gather_blocks(): lax.ppermute(across, axis, partner)]
    ppermute x4 -> x5, starting transfers between devices: 4.91 us -> 4.95 us  [gather_blocks(): lax.ppermute(block, axis, partner)]
  transfers between devices with their start and end apart: 20 -> 23, of which waited for: 13 -> 15; matrix products, arithmetic and copies ran while one was open for 3% -> 3% of each run, Pallas kernels for 0% -> 0%
where the time goes in v6:
time: 107 us
  starting transfers between devices  40.5 us (38%)
  waiting for transfers between devices  38.8 us (36%)
  Pallas kernels  8.22 us (8%)
  matrix products  6.94 us (6%)
  other arithmetic  6.44 us (6%)
  local copies, waits for them, and re-layouts  4.97 us (5%)
    ppermute x5, waiting for transfers between devices, gather_blocks(): across = lax.ppermute(block, axis, [(i, i ^ 2) for i in range(count)])  14.8 us
    ppermute x6, starting transfers between devices, scatter_blocks(): lax.ppermute(part, axis, [(i, (i + d) % count) for i in range(count)])  12.5 us
    ppermute x6, waiting for transfers between devices, scatter_blocks(): lax.ppermute(part, axis, [(i, (i + d) % count) for i in range(count)])  9.71 us
    ppermute x5, starting transfers between devices, gather_blocks(): across = lax.ppermute(block, axis, [(i, i ^ 2) for i in range(count)])  8.98 us
    pallas_call x1, Pallas kernels, attention_layers(): pl.pallas_call(functools.partial(attention_kernel, head_count=head_count,...  8.22 us
    ppermute x5, starting transfers between devices, gather_blocks(): lax.ppermute(across, axis, partner)  7.61 us
    ppermute x5, waiting for transfers between devices, gather_blocks(): lax.ppermute(across, axis, partner)  7.47 us
    ppermute x1, starting transfers between devices, scatter_blocks(): back = lax.ppermute(theirs, axis, [(i, i ^ 2) for i in range(count)])  6.35 us
  transfers between devices with their start and end apart: 23, of which 15 were waited for; matrix products, arithmetic and copies ran while one was open for 3% of the time, Pallas kernels for 0%

profile of v6, /device:TPU:0, one launch (start us, length us, event | category | flops | bytes accessed | tf_op | source)
XLA Modules:
  0.0 107.0 jit_solution(16731919891411955488)
XLA Ops:
  0.6 3.0 %collective-permute-start.4 = (bf16[2,24,2048]{2,1,0:T(8,128)(2,1)}, bf16[2,24,2048]{2,1,0:T(8,128)(2,1)S(1)}, u32[]{:S(2)}, u32[]{:S(2)}) collective-permute-start(bf16[2,24,2048]{2,1,0:T(8,128)(2,1)} %param.11), channel_id=1, source_target_pairs={{0,8},{4,12},{8,0},{12,4},{1,9},{5,13},{9,1},{13,5},{2,10},{6,14},... | collective-permute-start | bytes 589832 | tf_op jit(solution)/shard_map/ppermute | solution.py:188
  3.6 5.1 %collective-permute-done.4 = bf16[2,24,2048]{2,1,0:T(8,128)(2,1)S(1)} collective-permute-done((bf16[2,24,2048]{2,1,0:T(8,128)(2,1)}, bf16[2,24,2048]{2,1,0:T(8,128)(2,1)S(1)}, u32[]{:S(2)}, u32[]{:S(2)}) %collective-permute-start.4) | collective-permute-done | bytes 196640 | tf_op jit(solution)/shard_map/ppermute | solution.py:188
  8.8 1.4 %collective-permute-done.5 = bf16[2,24,2048]{2,1,0:T(8,128)(2,1)S(1)} collective-permute-done((bf16[2,24,2048]{2,1,0:T(8,128)(2,1)S(1)}, bf16[2,24,2048]{2,1,0:T(8,128)(2,1)S(1)}, u32[]{:S(2)}, u32[]{:S(2)}) %collective-permute-start.5) | collective-permute-done | bytes 196640 | tf_op jit(solution)/shard_map/ppermute | solution.py:189
  10.2 1.0 pad_maximum_fusion.1
  12.1 3.2 %fusion.7 = bf16[192,1024]{1,0:T(8,128)(2,1)S(1)} fusion(bf16[192,2048]{1,0:T(8,128)(2,1)S(1)} %bitcast.98, bf16[1,2048,1024]{2,1,0:T(8,128)(2,1)} %param.12), kind=kOutput, calls=%fused_computation.9 | convolution fusion | flops 805502976 | bytes 5373952 | tf_op jit(solution)/shard_map/dot_general | solution.py:269
  15.3 1.9 %collective-permute-start.6 = (bf16[48,1024]{1,0:T(8,128)(2,1)S(1)}, bf16[48,1024]{1,0:T(8,128)(2,1)S(1)}, u32[]{:S(2)}, u32[]{:S(2)}) collective-permute-start(bf16[48,1024]{1,0:T(8,128)(2,1)S(1)} %get-tuple-element.12), channel_id=1, source_target_pairs={{0,1},{1,2},{2,3},{3,0},{4,5},{5,6},{6,7},{7,4},{8,9},{9,10},{10,1... | collective-permute-start | bytes 294920 | tf_op jit(solution)/shard_map/ppermute | solution.py:229
  17.2 2.6 %collective-permute-start.7 = (bf16[48,1024]{1,0:T(8,128)(2,1)S(1)}, bf16[48,1024]{1,0:T(8,128)(2,1)S(1)}, u32[]{:S(2)}, u32[]{:S(2)}) collective-permute-start(bf16[48,1024]{1,0:T(8,128)(2,1)S(1)} %get-tuple-element.14), channel_id=1, source_target_pairs={{0,2},{1,3},{2,0},{3,1},{4,6},{5,7},{6,4},{7,5},{8,10},{9,11},{10,... | collective-permute-start | bytes 294920 | tf_op jit(solution)/shard_map/ppermute | solution.py:229
  19.8 1.3 %collective-permute-start.8 = (bf16[48,1024]{1,0:T(8,128)(2,1)S(1)}, bf16[48,1024]{1,0:T(8,128)(2,1)S(1)}, u32[]{:S(2)}, u32[]{:S(2)}) collective-permute-start(bf16[48,1024]{1,0:T(8,128)(2,1)S(1)} %get-tuple-element.13), channel_id=1, source_target_pairs={{0,3},{1,0},{2,1},{3,2},{4,7},{5,4},{6,5},{7,6},{8,11},{9,8},{10,9... | collective-permute-start | bytes 294920 | tf_op jit(solution)/shard_map/ppermute | solution.py:229
  21.1 1.8 %collective-permute-done.6 = bf16[48,1024]{1,0:T(8,128)(2,1)S(1)} collective-permute-done((bf16[48,1024]{1,0:T(8,128)(2,1)S(1)}, bf16[48,1024]{1,0:T(8,128)(2,1)S(1)}, u32[]{:S(2)}, u32[]{:S(2)}) %collective-permute-start.6) | collective-permute-done | bytes 98336 | tf_op jit(solution)/shard_map/ppermute | solution.py:229
  22.9 3.7 %collective-permute-done.7 = bf16[48,1024]{1,0:T(8,128)(2,1)S(1)} collective-permute-done((bf16[48,1024]{1,0:T(8,128)(2,1)S(1)}, bf16[48,1024]{1,0:T(8,128)(2,1)S(1)}, u32[]{:S(2)}, u32[]{:S(2)}) %collective-permute-start.7) | collective-permute-done | bytes 98336 | tf_op jit(solution)/shard_map/ppermute | solution.py:229
  27.1 1.6 %collective-permute-start.10 = (bf16[48,1024]{1,0:T(8,128)(2,1)S(1)}, bf16[48,1024]{1,0:T(8,128)(2,1)S(1)}, u32[]{:S(2)}, u32[]{:S(2)}) collective-permute-start(bf16[48,1024]{1,0:T(8,128)(2,1)S(1)} %get-tuple-element.16), channel_id=1, source_target_pairs={{0,2},{1,3},{2,0},{3,1},{4,6},{5,7},{6,4},{7,5},{8,10},{9,11},{10,... | collective-permute-start | bytes 294920 | tf_op jit(solution)/shard_map/ppermute | solution.py:188
  28.8 2.6 %collective-permute-start.9 = (bf16[48,1024]{1,0:T(8,128)(2,1)S(1)}, bf16[48,1024]{1,0:T(8,128)(2,1)S(1)}, u32[]{:S(2)}, u32[]{:S(2)}) collective-permute-start(bf16[48,1024]{1,0:T(8,128)(2,1)S(1)} %get-tuple-element.16), channel_id=1, source_target_pairs={{0,1},{1,0},{2,3},{3,2},{4,5},{5,4},{6,7},{7,6},{8,9},{9,8},{10,11... | collective-permute-start | bytes 294920 | tf_op jit(solution)/shard_map/ppermute | solution.py:189
  31.4 1.4 %collective-permute-done.10 = bf16[48,1024]{1,0:T(8,128)(2,1)S(1)} collective-permute-done((bf16[48,1024]{1,0:T(8,128)(2,1)S(1)}, bf16[48,1024]{1,0:T(8,128)(2,1)S(1)}, u32[]{:S(2)}, u32[]{:S(2)}) %collective-permute-start.10) | collective-permute-done | bytes 98336 | tf_op jit(solution)/shard_map/ppermute | solution.py:188
  32.8 3.5 %collective-permute-start.11 = (bf16[48,1024]{1,0:T(8,128)(2,1)S(1)}, bf16[48,1024]{1,0:T(8,128)(2,1)S(1)}, u32[]{:S(2)}, u32[]{:S(2)}) collective-permute-start(bf16[48,1024]{1,0:T(8,128)(2,1)S(1)} %collective-permute-done.10), channel_id=1, source_target_pairs={{0,1},{1,0},{2,3},{3,2},{4,5},{5,4},{6,7},{7,6},{8,9},{9,8},{10,11... | collective-permute-start | bytes 294920 | tf_op jit(solution)/shard_map/ppermute | solution.py:189
  36.3 2.6 %collective-permute-done.11 = bf16[48,1024]{1,0:T(8,128)(2,1)S(1)} collective-permute-done((bf16[48,1024]{1,0:T(8,128)(2,1)S(1)}, bf16[48,1024]{1,0:T(8,128)(2,1)S(1)}, u32[]{:S(2)}, u32[]{:S(2)}) %collective-permute-start.11) | collective-permute-done | bytes 98336 | tf_op jit(solution)/shard_map/ppermute | solution.py:189
  39.7 1.6 %collective-permute-start.13 = (bf16[192,1024]{1,0:T(8,128)(2,1)S(1)}, bf16[192,1024]{1,0:T(8,128)(2,1)S(1)}, u32[]{:S(2)}, u32[]{:S(2)}) collective-permute-start(bf16[192,1024]{1,0:T(8,128)(2,1)S(1)} %bitcast.91), channel_id=1, source_target_pairs={{0,8},{4,12},{8,0},{12,4},{1,9},{5,13},{9,1},{13,5},{2,10},{6,14},... | collective-permute-start | bytes 1179656 | tf_op jit(solution)/shard_map/ppermute | solution.py:188
  42.0 6.6 %collective-permute-done.1 = f32[4128]{0:T(1024)S(1)} collective-permute-done((f32[4128]{0:T(1024)S(1)}, f32[4128]{0:T(1024)S(1)}, u32[]{:S(2)}, u32[]{:S(2)}) %collective-permute-start.1) | collective-permute-done | bytes 16544 | tf_op jit(solution)/shard_map/ppermute | solution.py:188
  52.6 1.4 %pad_maximum_fusion.keyval_ref = bf16[4,2,96,1024]{3,2,1,0:T(8,128)(2,1)} fusion(bf16[1,2,96,1024]{3,2,1,0:T(8,128)(2,1)S(1)} %bitcast.103, bf16[1,2,96,1024]{3,2,1,0:T(8,128)(2,1)S(1)} %bitcast.100, bf16[1,2,96,1024]{3,2,1,0:T(8,128)(2,1)S(1)} %bitcast.102, bf16[1,2,96,1024]{3,2,1,0:T(8,128)(2,1)S(1)} %bitcast.93), kind=kLoop, calls=%fused_computation.8 | loop fusion | flops 2359296 | bytes 3145728 | tf_op jit(solution)/shard_map/stack | solution.py:190
  54.0 8.2 %shard_map.104 = (f32[2,64,4096]{2,1,0:T(8,128)}, bf16[2,96,1024]{2,1,0:T(8,128)(2,1)}) custom-call(s32[1]{0:T(128)} %bitcast.section_ref, s32[4]{0:T(128)} %iota_xor_fusion.slots_ref, f32[4,32]{1,0:T(4,128)} %maximum_tanh_fusion.gates_ref, bf16[2,64,4096]{2,1,0:T(8,128)(2,1)} %queries_ref.1, bf16[4,2,96,1024]{3,2,1,0:T(8,128)(2,1)} %pad_maximum_fusion.keyval_ref, ...), custom_call_target="tpu_custom_call" | custom-call | flops 1409286144 | bytes 6815744 | tf_op jit(solution)/shard_map/pallas_call | solution.py:139
  63.3 1.8 %collective-permute-start.15 = (bf16[48,1024]{1,0:T(8,128)(2,1)S(1)}, bf16[48,1024]{1,0:T(8,128)(2,1)S(1)}, u32[]{:S(2)}, u32[]{:S(2)}) collective-permute-start(bf16[48,1024]{1,0:T(8,128)(2,1)S(1)} %get-tuple-element.9), channel_id=1, source_target_pairs={{0,1},{1,2},{2,3},{3,0},{4,5},{5,6},{6,7},{7,4},{8,9},{9,10},{10,1... | collective-permute-start | bytes 294920 | tf_op jit(solution)/shard_map/ppermute | solution.py:229
  65.0 3.3 %collective-permute-start.16 = (bf16[48,1024]{1,0:T(8,128)(2,1)S(1)}, bf16[48,1024]{1,0:T(8,128)(2,1)S(1)}, u32[]{:S(2)}, u32[]{:S(2)}) collective-permute-start(bf16[48,1024]{1,0:T(8,128)(2,1)S(1)} %get-tuple-element.11), channel_id=1, source_target_pairs={{0,2},{1,3},{2,0},{3,1},{4,6},{5,7},{6,4},{7,5},{8,10},{9,11},{10,... | collective-permute-start | bytes 294920 | tf_op jit(solution)/shard_map/ppermute | solution.py:229
  68.3 1.7 %collective-permute-start.17 = (bf16[48,1024]{1,0:T(8,128)(2,1)S(1)}, bf16[48,1024]{1,0:T(8,128)(2,1)S(1)}, u32[]{:S(2)}, u32[]{:S(2)}) collective-permute-start(bf16[48,1024]{1,0:T(8,128)(2,1)S(1)} %get-tuple-element.10), channel_id=1, source_target_pairs={{0,3},{1,0},{2,1},{3,2},{4,7},{5,4},{6,5},{7,6},{8,11},{9,8},{10,9... | collective-permute-start | bytes 294920 | tf_op jit(solution)/shard_map/ppermute | solution.py:229
  71.4 2.8 %collective-permute-done.17 = bf16[48,1024]{1,0:T(8,128)(2,1)S(1)} collective-permute-done((bf16[48,1024]{1,0:T(8,128)(2,1)S(1)}, bf16[48,1024]{1,0:T(8,128)(2,1)S(1)}, u32[]{:S(2)}, u32[]{:S(2)}) %collective-permute-start.17) | collective-permute-done | bytes 98336 | tf_op jit(solution)/shard_map/ppermute | solution.py:229
  75.5 2.2 %collective-permute-start.19 = (bf16[48,1024]{1,0:T(8,128)(2,1)S(1)}, bf16[48,1024]{1,0:T(8,128)(2,1)S(1)}, u32[]{:S(2)}, u32[]{:S(2)}) collective-permute-start(bf16[48,1024]{1,0:T(8,128)(2,1)S(1)} %pad_maximum_fusion.6), channel_id=1, source_target_pairs={{0,2},{1,3},{2,0},{3,1},{4,6},{5,7},{6,4},{7,5},{8,10},{9,11},{10,... | collective-permute-start | bytes 294920 | tf_op jit(solution)/shard_map/ppermute | solution.py:188
  77.8 1.7 %collective-permute-start.18 = (bf16[48,1024]{1,0:T(8,128)(2,1)S(1)}, bf16[48,1024]{1,0:T(8,128)(2,1)S(1)}, u32[]{:S(2)}, u32[]{:S(2)}) collective-permute-start(bf16[48,1024]{1,0:T(8,128)(2,1)S(1)} %pad_maximum_fusion.6), channel_id=1, source_target_pairs={{0,1},{1,0},{2,3},{3,2},{4,5},{5,4},{6,7},{7,6},{8,9},{9,8},{10,11... | collective-permute-start | bytes 294920 | tf_op jit(solution)/shard_map/ppermute | solution.py:189
  79.5 1.7 %collective-permute-done.19 = bf16[48,1024]{1,0:T(8,128)(2,1)S(1)} collective-permute-done((bf16[48,1024]{1,0:T(8,128)(2,1)S(1)}, bf16[48,1024]{1,0:T(8,128)(2,1)S(1)}, u32[]{:S(2)}, u32[]{:S(2)}) %collective-permute-start.19) | collective-permute-done | bytes 98336 | tf_op jit(solution)/shard_map/ppermute | solution.py:188
  81.1 4.0 %collective-permute-start.20 = (bf16[48,1024]{1,0:T(8,128)(2,1)S(1)}, bf16[48,1024]{1,0:T(8,128)(2,1)S(1)}, u32[]{:S(2)}, u32[]{:S(2)}) collective-permute-start(bf16[48,1024]{1,0:T(8,128)(2,1)S(1)} %collective-permute-done.19), channel_id=1, source_target_pairs={{0,1},{1,0},{2,3},{3,2},{4,5},{5,4},{6,7},{7,6},{8,9},{9,8},{10,11... | collective-permute-start | bytes 294920 | tf_op jit(solution)/shard_map/ppermute | solution.py:189
  85.2 3.0 %collective-permute-done.20 = bf16[48,1024]{1,0:T(8,128)(2,1)S(1)} collective-permute-done((bf16[48,1024]{1,0:T(8,128)(2,1)S(1)}, bf16[48,1024]{1,0:T(8,128)(2,1)S(1)}, u32[]{:S(2)}, u32[]{:S(2)}) %collective-permute-start.20) | collective-permute-done | bytes 98336 | tf_op jit(solution)/shard_map/ppermute | solution.py:189
  88.9 3.7 %fusion.4 = bf16[192,2048]{1,0:T(8,128)(2,1)S(1)} fusion(bf16[192,1024]{1,0:T(8,128)(2,1)S(1)} %bitcast.95, bf16[1,2048,1024]{2,1,0:T(8,128)(2,1)} %param.12), kind=kOutput, calls=%fused_computation.7 | convolution fusion | flops 805699584 | bytes 5373952 | tf_op jit(solution)/shard_map/dot_general | solution.py:311
  92.9 1.7 %collective-permute-done.21 = bf16[2,2,24,2048]{3,2,1,0:T(8,128)(2,1)S(1)} collective-permute-done((bf16[2,2,24,2048]{3,2,1,0:T(8,128)(2,1)S(1)}, bf16[2,2,24,2048]{3,2,1,0:T(8,128)(2,1)S(1)}, u32[]{:S(2)}, u32[]{:S(2)}) %collective-permute-start.21) | collective-permute-done | bytes 393248 | tf_op jit(solution)/shard_map/ppermute | solution.py:216
  94.6 6.3 %collective-permute-start.22 = (bf16[2,24,2048]{2,1,0:T(8,128)(2,1)S(1)}, bf16[2,24,2048]{2,1,0:T(8,128)(2,1)S(1)}, u32[]{:S(2)}, u32[]{:S(2)}) collective-permute-start(bf16[2,24,2048]{2,1,0:T(8,128)(2,1)S(1)} %fusion.10), channel_id=1, source_target_pairs={{0,8},{4,12},{8,0},{12,4},{1,9},{5,13},{9,1},{13,5},{2,10},{6,14},... | collective-permute-start | bytes 589832 | tf_op jit(solution)/shard_map/ppermute | solution.py:220
  101.0 5.2 %collective-permute-done.22 = bf16[2,24,2048]{2,1,0:T(8,128)(2,1)S(1)} collective-permute-done((bf16[2,24,2048]{2,1,0:T(8,128)(2,1)S(1)}, bf16[2,24,2048]{2,1,0:T(8,128)(2,1)S(1)}, u32[]{:S(2)}, u32[]{:S(2)}) %collective-permute-start.22) | collective-permute-done | bytes 196640 | tf_op jit(solution)/shard_map/ppermute | solution.py:220
  (84 shorter events, 12.3 us)
Async XLA Ops:
  0.6 8.1 %collective-permute-start.4 = (bf16[2,24,2048]{2,1,0:T(8,128)(2,1)}, bf16[2,24,2048]{2,1,0:T(8,128)(2,1)S(1)}, u32[]{:S(2)}, u32[]{:S(2)}) collective-permute-start(bf16[2,24,2048]{2,1,0:T(8,128)(2,1)} %param.11), channel_id=1, source_target_pairs={{0,8},{4,12},{8,0},{12,4},{1,9},{5,13},{9,1},{13,5},{2,10},{6,14},... | collective-permute-start | bytes 589832 | tf_op jit(solution)/shard_map/ppermute | solution.py:188
  3.6 5.1 %collective-permute-start.3 = (bf16[2,24,2048]{2,1,0:T(8,128)(2,1)}, bf16[2,24,2048]{2,1,0:T(8,128)(2,1)S(1)}, u32[]{:S(2)}, u32[]{:S(2)}) collective-permute-start(bf16[2,24,2048]{2,1,0:T(8,128)(2,1)} %param.11), channel_id=1, source_target_pairs={{0,4},{4,0},{8,12},{12,8},{1,5},{5,1},{9,13},{13,9},{2,6},{6,2},{1... | collective-permute-start | bytes 589832 | tf_op jit(solution)/shard_map/ppermute | solution.py:189
  8.7 1.4 %collective-permute-start.5 = (bf16[2,24,2048]{2,1,0:T(8,128)(2,1)S(1)}, bf16[2,24,2048]{2,1,0:T(8,128)(2,1)S(1)}, u32[]{:S(2)}, u32[]{:S(2)}) collective-permute-start(bf16[2,24,2048]{2,1,0:T(8,128)(2,1)S(1)} %collective-permute-done.4), channel_id=1, source_target_pairs={{0,4},{4,0},{8,12},{12,8},{1,5},{5,1},{9,13},{13,9},{2,6},{6,2},{1... | collective-permute-start | bytes 589832 | tf_op jit(solution)/shard_map/ppermute | solution.py:189
  12.0 9.1 %copy-start.2 = (f32[1,4096]{1,0:T(1,128)S(1)}, f32[1,4096]{1,0:T(1,128)}, u32[]{:S(2)}) copy-start(f32[1,4096]{1,0:T(1,128)} %param.13) | copy-start | bytes 49156
  15.3 11.8 %copy-start.1 = (f32[1,512]{1,0:T(1,128)S(1)}, f32[1,512]{1,0:T(1,128)}, u32[]{:S(2)}) copy-start(f32[1,512]{1,0:T(1,128)} %param.14) | copy-start | bytes 6148
  15.3 7.6 %collective-permute-start.6 = (bf16[48,1024]{1,0:T(8,128)(2,1)S(1)}, bf16[48,1024]{1,0:T(8,128)(2,1)S(1)}, u32[]{:S(2)}, u32[]{:S(2)}) collective-permute-start(bf16[48,1024]{1,0:T(8,128)(2,1)S(1)} %get-tuple-element.12), channel_id=1, source_target_pairs={{0,1},{1,2},{2,3},{3,0},{4,5},{5,6},{6,7},{7,4},{8,9},{9,10},{10,1... | collective-permute-start | bytes 294920 | tf_op jit(solution)/shard_map/ppermute | solution.py:229
  17.2 9.4 %collective-permute-start.7 = (bf16[48,1024]{1,0:T(8,128)(2,1)S(1)}, bf16[48,1024]{1,0:T(8,128)(2,1)S(1)}, u32[]{:S(2)}, u32[]{:S(2)}) collective-permute-start(bf16[48,1024]{1,0:T(8,128)(2,1)S(1)} %get-tuple-element.14), channel_id=1, source_target_pairs={{0,2},{1,3},{2,0},{3,1},{4,6},{5,7},{6,4},{7,5},{8,10},{9,11},{10,... | collective-permute-start | bytes 294920 | tf_op jit(solution)/shard_map/ppermute | solution.py:229
  19.8 6.8 %collective-permute-start.8 = (bf16[48,1024]{1,0:T(8,128)(2,1)S(1)}, bf16[48,1024]{1,0:T(8,128)(2,1)S(1)}, u32[]{:S(2)}, u32[]{:S(2)}) collective-permute-start(bf16[48,1024]{1,0:T(8,128)(2,1)S(1)} %get-tuple-element.13), channel_id=1, source_target_pairs={{0,3},{1,0},{2,1},{3,2},{4,7},{5,4},{6,5},{7,6},{8,11},{9,8},{10,9... | collective-permute-start | bytes 294920 | tf_op jit(solution)/shard_map/ppermute | solution.py:229
  26.9 14.4 %copy-start.5 = (f32[1,32]{1,0:T(1,128)S(1)}, f32[1,32]{1,0:T(1,128)}, u32[]{:S(2)}) copy-start(f32[1,32]{1,0:T(1,128)} %param.15) | copy-start | bytes 388
  26.9 15.0 %copy-start.3 = (s32[2,96]{1,0:T(2,128)S(1)}, s32[2,96]{1,0:T(2,128)}, u32[]{:S(2)}) copy-start(s32[2,96]{1,0:T(2,128)} %param.18) | copy-start | bytes 2308
  26.9 15.0 %copy-start.4 = (s32[2,64]{1,0:T(2,128)S(1)}, s32[2,64]{1,0:T(2,128)}, u32[]{:S(2)}) copy-start(s32[2,64]{1,0:T(2,128)} %param.17) | copy-start | bytes 1540
  27.1 5.7 %collective-permute-start.10 = (bf16[48,1024]{1,0:T(8,128)(2,1)S(1)}, bf16[48,1024]{1,0:T(8,128)(2,1)S(1)}, u32[]{:S(2)}, u32[]{:S(2)}) collective-permute-start(bf16[48,1024]{1,0:T(8,128)(2,1)S(1)} %get-tuple-element.16), channel_id=1, source_target_pairs={{0,2},{1,3},{2,0},{3,1},{4,6},{5,7},{6,4},{7,5},{8,10},{9,11},{10,... | collective-permute-start | bytes 294920 | tf_op jit(solution)/shard_map/ppermute | solution.py:188
  28.8 7.6 %collective-permute-start.9 = (bf16[48,1024]{1,0:T(8,128)(2,1)S(1)}, bf16[48,1024]{1,0:T(8,128)(2,1)S(1)}, u32[]{:S(2)}, u32[]{:S(2)}) collective-permute-start(bf16[48,1024]{1,0:T(8,128)(2,1)S(1)} %get-tuple-element.16), channel_id=1, source_target_pairs={{0,1},{1,0},{2,3},{3,2},{4,5},{5,4},{6,7},{7,6},{8,9},{9,8},{10,11... | collective-permute-start | bytes 294920 | tf_op jit(solution)/shard_map/ppermute | solution.py:189
  32.8 6.1 %collective-permute-start.11 = (bf16[48,1024]{1,0:T(8,128)(2,1)S(1)}, bf16[48,1024]{1,0:T(8,128)(2,1)S(1)}, u32[]{:S(2)}, u32[]{:S(2)}) collective-permute-start(bf16[48,1024]{1,0:T(8,128)(2,1)S(1)} %collective-permute-done.10), channel_id=1, source_target_pairs={{0,1},{1,0},{2,3},{3,2},{4,5},{5,4},{6,7},{7,6},{8,9},{9,8},{10,11... | collective-permute-start | bytes 294920 | tf_op jit(solution)/shard_map/ppermute | solution.py:189
  39.7 11.1 %collective-permute-start.13 = (bf16[192,1024]{1,0:T(8,128)(2,1)S(1)}, bf16[192,1024]{1,0:T(8,128)(2,1)S(1)}, u32[]{:S(2)}, u32[]{:S(2)}) collective-permute-start(bf16[192,1024]{1,0:T(8,128)(2,1)S(1)} %bitcast.91), channel_id=1, source_target_pairs={{0,8},{4,12},{8,0},{12,4},{1,9},{5,13},{9,1},{13,5},{2,10},{6,14},... | collective-permute-start | bytes 1179656 | tf_op jit(solution)/shard_map/ppermute | solution.py:188
  41.3 7.2 %collective-permute-start.1 = (f32[4128]{0:T(1024)S(1)}, f32[4128]{0:T(1024)S(1)}, u32[]{:S(2)}, u32[]{:S(2)}) collective-permute-start(f32[4128]{0:T(1024)S(1)} %reduce), channel_id=1, source_target_pairs={{0,8},{4,12},{8,0},{12,4},{1,9},{5,13},{9,1},{13,5},{2,10},{6,14},... | collective-permute-start | bytes 49544 | tf_op jit(solution)/shard_map/ppermute | solution.py:188
  41.9 8.2 %collective-permute-start = (f32[4128]{0:T(1024)S(1)}, f32[4128]{0:T(1024)S(1)}, u32[]{:S(2)}, u32[]{:S(2)}) collective-permute-start(f32[4128]{0:T(1024)S(1)} %reduce), channel_id=1, source_target_pairs={{0,4},{4,0},{8,12},{12,8},{1,5},{5,1},{9,13},{13,9},{2,6},{6,2},{1... | collective-permute-start | bytes 49544 | tf_op jit(solution)/shard_map/ppermute | solution.py:189
  48.5 1.6 %collective-permute-start.2 = (f32[4128]{0:T(1024)S(1)}, f32[4128]{0:T(1024)S(1)}, u32[]{:S(2)}, u32[]{:S(2)}) collective-permute-start(f32[4128]{0:T(1024)S(1)} %collective-permute-done.1), channel_id=1, source_target_pairs={{0,4},{4,0},{8,12},{12,8},{1,5},{5,1},{9,13},{13,9},{2,6},{6,2},{1... | collective-permute-start | bytes 49544 | tf_op jit(solution)/shard_map/ppermute | solution.py:189
  49.1 4.9 %copy-start = (f32[2,8,64,96]{3,2,1,0:T(8,128)}, f32[2,8,64,96]{3,2,1,0:T(8,128)S(1)}, u32[]{:S(2)}) copy-start(f32[2,8,64,96]{3,2,1,0:T(8,128)S(1)} %tile.4) | copy-start | bytes 1179652
  50.2 2.0 %collective-permute-start.12 = (bf16[192,1024]{1,0:T(8,128)(2,1)S(1)}, bf16[192,1024]{1,0:T(8,128)(2,1)S(1)}, u32[]{:S(2)}, u32[]{:S(2)}) collective-permute-start(bf16[192,1024]{1,0:T(8,128)(2,1)S(1)} %bitcast.92), channel_id=1, source_target_pairs={{0,4},{4,0},{8,12},{12,8},{1,5},{5,1},{9,13},{13,9},{2,6},{6,2},{1... | collective-permute-start | bytes 1179656 | tf_op jit(solution)/shard_map/ppermute | solution.py:189
  50.7 1.9 %collective-permute-start.14 = (bf16[192,1024]{1,0:T(8,128)(2,1)S(1)}, bf16[192,1024]{1,0:T(8,128)(2,1)S(1)}, u32[]{:S(2)}, u32[]{:S(2)}) collective-permute-start(bf16[192,1024]{1,0:T(8,128)(2,1)S(1)} %collective-permute-done.13), channel_id=1, source_target_pairs={{0,4},{4,0},{8,12},{12,8},{1,5},{5,1},{9,13},{13,9},{2,6},{6,2},{1... | collective-permute-start | bytes 1179656 | tf_op jit(solution)/shard_map/ppermute | solution.py:189
  63.3 7.2 %collective-permute-start.15 = (bf16[48,1024]{1,0:T(8,128)(2,1)S(1)}, bf16[48,1024]{1,0:T(8,128)(2,1)S(1)}, u32[]{:S(2)}, u32[]{:S(2)}) collective-permute-start(bf16[48,1024]{1,0:T(8,128)(2,1)S(1)} %get-tuple-element.9), channel_id=1, source_target_pairs={{0,1},{1,2},{2,3},{3,0},{4,5},{5,6},{6,7},{7,4},{8,9},{9,10},{10,1... | collective-permute-start | bytes 294920 | tf_op jit(solution)/shard_map/ppermute | solution.py:229
  65.0 6.4 %collective-permute-start.16 = (bf16[48,1024]{1,0:T(8,128)(2,1)S(1)}, bf16[48,1024]{1,0:T(8,128)(2,1)S(1)}, u32[]{:S(2)}, u32[]{:S(2)}) collective-permute-start(bf16[48,1024]{1,0:T(8,128)(2,1)S(1)} %get-tuple-element.11), channel_id=1, source_target_pairs={{0,2},{1,3},{2,0},{3,1},{4,6},{5,7},{6,4},{7,5},{8,10},{9,11},{10,... | collective-permute-start | bytes 294920 | tf_op jit(solution)/shard_map/ppermute | solution.py:229
  68.3 5.9 %collective-permute-start.17 = (bf16[48,1024]{1,0:T(8,128)(2,1)S(1)}, bf16[48,1024]{1,0:T(8,128)(2,1)S(1)}, u32[]{:S(2)}, u32[]{:S(2)}) collective-permute-start(bf16[48,1024]{1,0:T(8,128)(2,1)S(1)} %get-tuple-element.10), channel_id=1, source_target_pairs={{0,3},{1,0},{2,1},{3,2},{4,7},{5,4},{6,5},{7,6},{8,11},{9,8},{10,9... | collective-permute-start | bytes 294920 | tf_op jit(solution)/shard_map/ppermute | solution.py:229
  75.5 5.6 %collective-permute-start.19 = (bf16[48,1024]{1,0:T(8,128)(2,1)S(1)}, bf16[48,1024]{1,0:T(8,128)(2,1)S(1)}, u32[]{:S(2)}, u32[]{:S(2)}) collective-permute-start(bf16[48,1024]{1,0:T(8,128)(2,1)S(1)} %pad_maximum_fusion.6), channel_id=1, source_target_pairs={{0,2},{1,3},{2,0},{3,1},{4,6},{5,7},{6,4},{7,5},{8,10},{9,11},{10,... | collective-permute-start | bytes 294920 | tf_op jit(solution)/shard_map/ppermute | solution.py:188
  77.8 7.4 %collective-permute-start.18 = (bf16[48,1024]{1,0:T(8,128)(2,1)S(1)}, bf16[48,1024]{1,0:T(8,128)(2,1)S(1)}, u32[]{:S(2)}, u32[]{:S(2)}) collective-permute-start(bf16[48,1024]{1,0:T(8,128)(2,1)S(1)} %pad_maximum_fusion.6), channel_id=1, source_target_pairs={{0,1},{1,0},{2,3},{3,2},{4,5},{5,4},{6,7},{7,6},{8,9},{9,8},{10,11... | collective-permute-start | bytes 294920 | tf_op jit(solution)/shard_map/ppermute | solution.py:189
  81.1 7.0 %collective-permute-start.20 = (bf16[48,1024]{1,0:T(8,128)(2,1)S(1)}, bf16[48,1024]{1,0:T(8,128)(2,1)S(1)}, u32[]{:S(2)}, u32[]{:S(2)}) collective-permute-start(bf16[48,1024]{1,0:T(8,128)(2,1)S(1)} %collective-permute-done.19), channel_id=1, source_target_pairs={{0,1},{1,0},{2,3},{3,2},{4,5},{5,4},{6,7},{7,6},{8,9},{9,8},{10,11... | collective-permute-start | bytes 294920 | tf_op jit(solution)/shard_map/ppermute | solution.py:189
  92.8 1.8 %collective-permute-start.21 = (bf16[2,2,24,2048]{3,2,1,0:T(8,128)(2,1)S(1)}, bf16[2,2,24,2048]{3,2,1,0:T(8,128)(2,1)S(1)}, u32[]{:S(2)}, u32[]{:S(2)}) collective-permute-start(bf16[2,2,24,2048]{3,2,1,0:T(8,128)(2,1)S(1)} %pad_maximum_fusion.4), channel_id=1, source_target_pairs={{0,4},{4,0},{8,12},{12,8},{1,5},{5,1},{9,13},{13,9},{2,6},{6,2},{1... | collective-permute-start | bytes 1179656 | tf_op jit(solution)/shard_map/ppermute | solution.py:216
  94.6 11.5 %collective-permute-start.22 = (bf16[2,24,2048]{2,1,0:T(8,128)(2,1)S(1)}, bf16[2,24,2048]{2,1,0:T(8,128)(2,1)S(1)}, u32[]{:S(2)}, u32[]{:S(2)}) collective-permute-start(bf16[2,24,2048]{2,1,0:T(8,128)(2,1)S(1)} %fusion.10), channel_id=1, source_target_pairs={{0,8},{4,12},{8,0},{12,4},{1,9},{5,13},{9,1},{13,5},{2,10},{6,14},... | collective-permute-start | bytes 589832 | tf_op jit(solution)/shard_map/ppermute | solution.py:220

commit v7 on v6

--- a/solution.py
+++ b/solution.py
@@ -78,7 +78,7 @@
             ) * scale
             scores = jnp.where(same, scores, -jnp.inf)
             powered = jnp.exp(scores - jnp.max(scores, axis=-1, keepdims=True))
-            probs = powered / jnp.sum(powered, axis=-1, keepdims=True)
+            probs = powered * (1.0 / jnp.sum(powered, axis=-1, keepdims=True))
             attended = jnp.dot(
                 probs.astype(jnp.bfloat16), value, preferred_element_type=jnp.float32
             )
@@ -104,7 +104,7 @@
         ) * scale
         scores_t = jnp.where(same_t, scores_t, -jnp.inf)
         powered = jnp.exp(scores_t - jnp.max(scores_t, axis=0, keepdims=True))
-        probs_t = powered / jnp.sum(powered, axis=0, keepdims=True)
+        probs_t = powered * (1.0 / jnp.sum(powered, axis=0, keepdims=True))
         upstream = jnp.concatenate(
             [cot_ref[:, head_cols(k * groups + g)] for g in range(groups)], axis=0
         )
@@ -268,9 +268,7 @@
     flat_rows = gathered.reshape(total_rows, gathered.shape[2])
     partial = jnp.dot(flat_rows, weights, preferred_element_type=jnp.float32)
     raw_rows = scatter_blocks(
-        partial.astype(jnp.bfloat16).reshape(shard_count, total_rows // shard_count, 2 * key_width),
-        "shard",
-        False,
+        partial.reshape(shard_count, total_rows // shard_count, 2 * key_width), "shard", False
     )
     key_rows = head_normalize(raw_rows[:, :key_width], key_norm_gain[0], keyval_heads)
     keyval_rows = jnp.concatenate(

time: 107 us -> 116 us (1.084)
  waiting for transfers between devices: 38.8 us -> 44.2 us
  starting transfers between devices: 40.5 us -> 43.5 us
    ppermute x6, waiting for transfers between devices: 9.71 us -> 16.1 us  [scatter_blocks(): lax.ppermute(part, axis, [(i, (i + d) % count) for i in range(count)])]
    ppermute x5, starting transfers between devices: 8.98 us -> 11.1 us  [gather_blocks(): across = lax.ppermute(block, axis, [(i, i ^ 2) for i in range(count)])]
where the time goes in v7:
time: 116 us; the launch traced here: 115 us
  waiting for transfers between devices  44.2 us (38%)
  starting transfers between devices  43.5 us (38%)
  Pallas kernels  8.22 us (7%)
  matrix products  6.94 us (6%)
  other arithmetic  6.44 us (6%)
  local copies, waits for them, and re-layouts  4.99 us (4%)
    ppermute x6, waiting for transfers between devices, scatter_blocks(): lax.ppermute(part, axis, [(i, (i + d) % count) for i in range(count)])  16.1 us
    ppermute x5, waiting for transfers between devices, gather_blocks(): across = lax.ppermute(block, axis, [(i, i ^ 2) for i in range(count)])  13.8 us
    ppermute x6, starting transfers between devices, scatter_blocks(): lax.ppermute(part, axis, [(i, (i + d) % count) for i in range(count)])  12.5 us
    ppermute x5, starting transfers between devices, gather_blocks(): across = lax.ppermute(block, axis, [(i, i ^ 2) for i in range(count)])  11.1 us
    ppermute x5, starting transfers between devices, gather_blocks(): lax.ppermute(across, axis, partner)  8.65 us
    pallas_call x1, Pallas kernels, attention_layers(): pl.pallas_call(functools.partial(attention_kernel, head_count=head_count,...  8.22 us
    ppermute x5, waiting for transfers between devices, gather_blocks(): lax.ppermute(across, axis, partner)  7.47 us
    ppermute x1, starting transfers between devices, scatter_blocks(): back = lax.ppermute(theirs, axis, [(i, i ^ 2) for i in range(count)])  6.3 us
  transfers between devices with their start and end apart: 23, of which 15 were waited for; matrix products, arithmetic and copies ran while one was open for 3% of the time, Pallas kernels for 0%

profile of v7, /device:TPU:0, one launch (start us, length us, event | category | flops | bytes accessed | tf_op | source)
XLA Modules:
  0.0 115.4 jit_solution(1344590078242827035)
XLA Ops:
  0.6 3.0 %collective-permute-start.4 = (bf16[2,24,2048]{2,1,0:T(8,128)(2,1)}, bf16[2,24,2048]{2,1,0:T(8,128)(2,1)S(1)}, u32[]{:S(2)}, u32[]{:S(2)}) collective-permute-start(bf16[2,24,2048]{2,1,0:T(8,128)(2,1)} %param.11), channel_id=1, source_target_pairs={{0,8},{4,12},{8,0},{12,4},{1,9},{5,13},{9,1},{13,5},{2,10},{6,14},... | collective-permute-start | bytes 589832 | tf_op jit(solution)/shard_map/ppermute | solution.py:188
  3.6 5.1 %collective-permute-done.4 = bf16[2,24,2048]{2,1,0:T(8,128)(2,1)S(1)} collective-permute-done((bf16[2,24,2048]{2,1,0:T(8,128)(2,1)}, bf16[2,24,2048]{2,1,0:T(8,128)(2,1)S(1)}, u32[]{:S(2)}, u32[]{:S(2)}) %collective-permute-start.4) | collective-permute-done | bytes 196640 | tf_op jit(solution)/shard_map/ppermute | solution.py:188
  8.8 1.4 %collective-permute-done.5 = bf16[2,24,2048]{2,1,0:T(8,128)(2,1)S(1)} collective-permute-done((bf16[2,24,2048]{2,1,0:T(8,128)(2,1)S(1)}, bf16[2,24,2048]{2,1,0:T(8,128)(2,1)S(1)}, u32[]{:S(2)}, u32[]{:S(2)}) %collective-permute-start.5) | collective-permute-done | bytes 196640 | tf_op jit(solution)/shard_map/ppermute | solution.py:189
  10.2 1.0 pad_maximum_fusion.1
  12.1 3.2 %fusion = f32[4,48,1024]{2,1,0:T(8,128)S(1)} fusion(bf16[4,48,2048]{2,1,0:T(8,128)(2,1)S(1)} %bitcast.87, bf16[1,2048,1024]{2,1,0:T(8,128)(2,1)} %param.12), kind=kOutput, calls=%fused_computation.3 | convolution fusion | flops 805306368 | bytes 5767168 | tf_op jit(solution)/shard_map/dot_general | solution.py:269
  15.3 1.9 %collective-permute-start.6 = (f32[48,1024]{1,0:T(8,128)S(1)}, f32[48,1024]{1,0:T(8,128)S(1)}, u32[]{:S(2)}, u32[]{:S(2)}) collective-permute-start(f32[48,1024]{1,0:T(8,128)S(1)} %get-tuple-element.9), channel_id=1, source_target_pairs={{0,1},{1,2},{2,3},{3,0},{4,5},{5,6},{6,7},{7,4},{8,9},{9,10},{10,1... | collective-permute-start | bytes 589832 | tf_op jit(solution)/shard_map/ppermute | solution.py:229
  17.2 2.6 %collective-permute-start.7 = (f32[48,1024]{1,0:T(8,128)S(1)}, f32[48,1024]{1,0:T(8,128)S(1)}, u32[]{:S(2)}, u32[]{:S(2)}) collective-permute-start(f32[48,1024]{1,0:T(8,128)S(1)} %get-tuple-element.11), channel_id=1, source_target_pairs={{0,2},{1,3},{2,0},{3,1},{4,6},{5,7},{6,4},{7,5},{8,10},{9,11},{10,... | collective-permute-start | bytes 589832 | tf_op jit(solution)/shard_map/ppermute | solution.py:229
  19.8 1.3 %collective-permute-start.8 = (f32[48,1024]{1,0:T(8,128)S(1)}, f32[48,1024]{1,0:T(8,128)S(1)}, u32[]{:S(2)}, u32[]{:S(2)}) collective-permute-start(f32[48,1024]{1,0:T(8,128)S(1)} %get-tuple-element.10), channel_id=1, source_target_pairs={{0,3},{1,0},{2,1},{3,2},{4,7},{5,4},{6,5},{7,6},{8,11},{9,8},{10,9... | collective-permute-start | bytes 589832 | tf_op jit(solution)/shard_map/ppermute | solution.py:229
  21.2 3.9 %collective-permute-done.6 = f32[48,1024]{1,0:T(8,128)S(1)} collective-permute-done((f32[48,1024]{1,0:T(8,128)S(1)}, f32[48,1024]{1,0:T(8,128)S(1)}, u32[]{:S(2)}, u32[]{:S(2)}) %collective-permute-start.6) | collective-permute-done | bytes 196640 | tf_op jit(solution)/shard_map/ppermute | solution.py:229
  25.1 7.9 %collective-permute-done.7 = f32[48,1024]{1,0:T(8,128)S(1)} collective-permute-done((f32[48,1024]{1,0:T(8,128)S(1)}, f32[48,1024]{1,0:T(8,128)S(1)}, u32[]{:S(2)}, u32[]{:S(2)}) %collective-permute-start.7) | collective-permute-done | bytes 196640 | tf_op jit(solution)/shard_map/ppermute | solution.py:229
  33.5 3.7 %collective-permute-start.10 = (bf16[48,1024]{1,0:T(8,128)(2,1)S(1)}, bf16[48,1024]{1,0:T(8,128)(2,1)S(1)}, u32[]{:S(2)}, u32[]{:S(2)}) collective-permute-start(bf16[48,1024]{1,0:T(8,128)(2,1)S(1)} %get-tuple-element.16), channel_id=1, source_target_pairs={{0,2},{1,3},{2,0},{3,1},{4,6},{5,7},{6,4},{7,5},{8,10},{9,11},{10,... | collective-permute-start | bytes 294920 | tf_op jit(solution)/shard_map/ppermute | solution.py:188
  37.2 2.6 %collective-permute-start.9 = (bf16[48,1024]{1,0:T(8,128)(2,1)S(1)}, bf16[48,1024]{1,0:T(8,128)(2,1)S(1)}, u32[]{:S(2)}, u32[]{:S(2)}) collective-permute-start(bf16[48,1024]{1,0:T(8,128)(2,1)S(1)} %get-tuple-element.16), channel_id=1, source_target_pairs={{0,1},{1,0},{2,3},{3,2},{4,5},{5,4},{6,7},{7,6},{8,9},{9,8},{10,11... | collective-permute-start | bytes 294920 | tf_op jit(solution)/shard_map/ppermute | solution.py:189
  40.3 4.5 %collective-permute-start.11 = (bf16[48,1024]{1,0:T(8,128)(2,1)S(1)}, bf16[48,1024]{1,0:T(8,128)(2,1)S(1)}, u32[]{:S(2)}, u32[]{:S(2)}) collective-permute-start(bf16[48,1024]{1,0:T(8,128)(2,1)S(1)} %collective-permute-done.10), channel_id=1, source_target_pairs={{0,1},{1,0},{2,3},{3,2},{4,5},{5,4},{6,7},{7,6},{8,9},{9,8},{10,11... | collective-permute-start | bytes 294920 | tf_op jit(solution)/shard_map/ppermute | solution.py:189
  44.8 2.6 %collective-permute-done.11 = bf16[48,1024]{1,0:T(8,128)(2,1)S(1)} collective-permute-done((bf16[48,1024]{1,0:T(8,128)(2,1)S(1)}, bf16[48,1024]{1,0:T(8,128)(2,1)S(1)}, u32[]{:S(2)}, u32[]{:S(2)}) %collective-permute-start.11) | collective-permute-done | bytes 98336 | tf_op jit(solution)/shard_map/ppermute | solution.py:189
  48.1 1.5 %collective-permute-start.13 = (bf16[192,1024]{1,0:T(8,128)(2,1)S(1)}, bf16[192,1024]{1,0:T(8,128)(2,1)S(1)}, u32[]{:S(2)}, u32[]{:S(2)}) collective-permute-start(bf16[192,1024]{1,0:T(8,128)(2,1)S(1)} %bitcast.93), channel_id=1, source_target_pairs={{0,8},{4,12},{8,0},{12,4},{1,9},{5,13},{9,1},{13,5},{2,10},{6,14},... | collective-permute-start | bytes 1179656 | tf_op jit(solution)/shard_map/ppermute | solution.py:188
  50.5 6.6 %collective-permute-done.1 = f32[4128]{0:T(1024)S(1)} collective-permute-done((f32[4128]{0:T(1024)S(1)}, f32[4128]{0:T(1024)S(1)}, u32[]{:S(2)}, u32[]{:S(2)}) %collective-permute-start.1) | collective-permute-done | bytes 16544 | tf_op jit(solution)/shard_map/ppermute | solution.py:188
  61.1 1.4 %pad_maximum_fusion.keyval_ref = bf16[4,2,96,1024]{3,2,1,0:T(8,128)(2,1)} fusion(bf16[1,2,96,1024]{3,2,1,0:T(8,128)(2,1)S(1)} %bitcast.104, bf16[1,2,96,1024]{3,2,1,0:T(8,128)(2,1)S(1)} %bitcast.101, bf16[1,2,96,1024]{3,2,1,0:T(8,128)(2,1)S(1)} %bitcast.103, bf16[1,2,96,1024]{3,2,1,0:T(8,128)(2,1)S(1)} %bitcast.95), kind=kLoop, calls=%fused_computation.8 | loop fusion | flops 2359296 | bytes 3145728 | tf_op jit(solution)/shard_map/stack | solution.py:190
  62.5 8.2 %shard_map.104 = (f32[2,64,4096]{2,1,0:T(8,128)}, bf16[2,96,1024]{2,1,0:T(8,128)(2,1)}) custom-call(s32[1]{0:T(128)} %bitcast.section_ref, s32[4]{0:T(128)} %iota_xor_fusion.slots_ref, f32[4,32]{1,0:T(4,128)} %maximum_tanh_fusion.gates_ref, bf16[2,64,4096]{2,1,0:T(8,128)(2,1)} %queries_ref.1, bf16[4,2,96,1024]{3,2,1,0:T(8,128)(2,1)} %pad_maximum_fusion.keyval_ref, ...), custom_call_target="tpu_custom_call" | custom-call | flops 1409286144 | bytes 6815744 | tf_op jit(solution)/shard_map/pallas_call | solution.py:139
  71.7 1.8 %collective-permute-start.15 = (bf16[48,1024]{1,0:T(8,128)(2,1)S(1)}, bf16[48,1024]{1,0:T(8,128)(2,1)S(1)}, u32[]{:S(2)}, u32[]{:S(2)}) collective-permute-start(bf16[48,1024]{1,0:T(8,128)(2,1)S(1)} %get-tuple-element.12), channel_id=1, source_target_pairs={{0,1},{1,2},{2,3},{3,0},{4,5},{5,6},{6,7},{7,4},{8,9},{9,10},{10,1... | collective-permute-start | bytes 294920 | tf_op jit(solution)/shard_map/ppermute | solution.py:229
  73.5 3.3 %collective-permute-start.16 = (bf16[48,1024]{1,0:T(8,128)(2,1)S(1)}, bf16[48,1024]{1,0:T(8,128)(2,1)S(1)}, u32[]{:S(2)}, u32[]{:S(2)}) collective-permute-start(bf16[48,1024]{1,0:T(8,128)(2,1)S(1)} %get-tuple-element.14), channel_id=1, source_target_pairs={{0,2},{1,3},{2,0},{3,1},{4,6},{5,7},{6,4},{7,5},{8,10},{9,11},{10,... | collective-permute-start | bytes 294920 | tf_op jit(solution)/shard_map/ppermute | solution.py:229
  76.8 1.6 %collective-permute-start.17 = (bf16[48,1024]{1,0:T(8,128)(2,1)S(1)}, bf16[48,1024]{1,0:T(8,128)(2,1)S(1)}, u32[]{:S(2)}, u32[]{:S(2)}) collective-permute-start(bf16[48,1024]{1,0:T(8,128)(2,1)S(1)} %get-tuple-element.13), channel_id=1, source_target_pairs={{0,3},{1,0},{2,1},{3,2},{4,7},{5,4},{6,5},{7,6},{8,11},{9,8},{10,9... | collective-permute-start | bytes 294920 | tf_op jit(solution)/shard_map/ppermute | solution.py:229
  78.9 1.0 collective-permute-done.16
  79.9 2.8 %collective-permute-done.17 = bf16[48,1024]{1,0:T(8,128)(2,1)S(1)} collective-permute-done((bf16[48,1024]{1,0:T(8,128)(2,1)S(1)}, bf16[48,1024]{1,0:T(8,128)(2,1)S(1)}, u32[]{:S(2)}, u32[]{:S(2)}) %collective-permute-start.17) | collective-permute-done | bytes 98336 | tf_op jit(solution)/shard_map/ppermute | solution.py:229
  84.0 2.2 %collective-permute-start.19 = (bf16[48,1024]{1,0:T(8,128)(2,1)S(1)}, bf16[48,1024]{1,0:T(8,128)(2,1)S(1)}, u32[]{:S(2)}, u32[]{:S(2)}) collective-permute-start(bf16[48,1024]{1,0:T(8,128)(2,1)S(1)} %pad_maximum_fusion.6), channel_id=1, source_target_pairs={{0,2},{1,3},{2,0},{3,1},{4,6},{5,7},{6,4},{7,5},{8,10},{9,11},{10,... | collective-permute-start | bytes 294920 | tf_op jit(solution)/shard_map/ppermute | solution.py:188
  86.2 1.7 %collective-permute-start.18 = (bf16[48,1024]{1,0:T(8,128)(2,1)S(1)}, bf16[48,1024]{1,0:T(8,128)(2,1)S(1)}, u32[]{:S(2)}, u32[]{:S(2)}) collective-permute-start(bf16[48,1024]{1,0:T(8,128)(2,1)S(1)} %pad_maximum_fusion.6), channel_id=1, source_target_pairs={{0,1},{1,0},{2,3},{3,2},{4,5},{5,4},{6,7},{7,6},{8,9},{9,8},{10,11... | collective-permute-start | bytes 294920 | tf_op jit(solution)/shard_map/ppermute | solution.py:189
  88.0 1.7 %collective-permute-done.19 = bf16[48,1024]{1,0:T(8,128)(2,1)S(1)} collective-permute-done((bf16[48,1024]{1,0:T(8,128)(2,1)S(1)}, bf16[48,1024]{1,0:T(8,128)(2,1)S(1)}, u32[]{:S(2)}, u32[]{:S(2)}) %collective-permute-start.19) | collective-permute-done | bytes 98336 | tf_op jit(solution)/shard_map/ppermute | solution.py:188
  89.6 4.0 %collective-permute-start.20 = (bf16[48,1024]{1,0:T(8,128)(2,1)S(1)}, bf16[48,1024]{1,0:T(8,128)(2,1)S(1)}, u32[]{:S(2)}, u32[]{:S(2)}) collective-permute-start(bf16[48,1024]{1,0:T(8,128)(2,1)S(1)} %collective-permute-done.19), channel_id=1, source_target_pairs={{0,1},{1,0},{2,3},{3,2},{4,5},{5,4},{6,7},{7,6},{8,9},{9,8},{10,11... | collective-permute-start | bytes 294920 | tf_op jit(solution)/shard_map/ppermute | solution.py:189
  93.7 3.0 %collective-permute-done.20 = bf16[48,1024]{1,0:T(8,128)(2,1)S(1)} collective-permute-done((bf16[48,1024]{1,0:T(8,128)(2,1)S(1)}, bf16[48,1024]{1,0:T(8,128)(2,1)S(1)}, u32[]{:S(2)}, u32[]{:S(2)}) %collective-permute-start.20) | collective-permute-done | bytes 98336 | tf_op jit(solution)/shard_map/ppermute | solution.py:189
  97.4 3.7 %fusion.4 = bf16[192,2048]{1,0:T(8,128)(2,1)S(1)} fusion(bf16[192,1024]{1,0:T(8,128)(2,1)S(1)} %bitcast.97, bf16[1,2048,1024]{2,1,0:T(8,128)(2,1)} %param.12), kind=kOutput, calls=%fused_computation.7 | convolution fusion | flops 805699584 | bytes 5373952 | tf_op jit(solution)/shard_map/dot_general | solution.py:309
  101.3 1.7 %collective-permute-done.21 = bf16[2,2,24,2048]{3,2,1,0:T(8,128)(2,1)S(1)} collective-permute-done((bf16[2,2,24,2048]{3,2,1,0:T(8,128)(2,1)S(1)}, bf16[2,2,24,2048]{3,2,1,0:T(8,128)(2,1)S(1)}, u32[]{:S(2)}, u32[]{:S(2)}) %collective-permute-start.21) | collective-permute-done | bytes 393248 | tf_op jit(solution)/shard_map/ppermute | solution.py:216
  103.1 6.3 %collective-permute-start.22 = (bf16[2,24,2048]{2,1,0:T(8,128)(2,1)S(1)}, bf16[2,24,2048]{2,1,0:T(8,128)(2,1)S(1)}, u32[]{:S(2)}, u32[]{:S(2)}) collective-permute-start(bf16[2,24,2048]{2,1,0:T(8,128)(2,1)S(1)} %fusion.7), channel_id=1, source_target_pairs={{0,8},{4,12},{8,0},{12,4},{1,9},{5,13},{9,1},{13,5},{2,10},{6,14},... | collective-permute-start | bytes 589832 | tf_op jit(solution)/shard_map/ppermute | solution.py:220
  109.4 5.2 %collective-permute-done.22 = bf16[2,24,2048]{2,1,0:T(8,128)(2,1)S(1)} collective-permute-done((bf16[2,24,2048]{2,1,0:T(8,128)(2,1)S(1)}, bf16[2,24,2048]{2,1,0:T(8,128)(2,1)S(1)}, u32[]{:S(2)}, u32[]{:S(2)}) %collective-permute-start.22) | collective-permute-done | bytes 196640 | tf_op jit(solution)/shard_map/ppermute | solution.py:220
  (84 shorter events, 11.7 us)
Async XLA Ops:
  0.6 8.1 %collective-permute-start.4 = (bf16[2,24,2048]{2,1,0:T(8,128)(2,1)}, bf16[2,24,2048]{2,1,0:T(8,128)(2,1)S(1)}, u32[]{:S(2)}, u32[]{:S(2)}) collective-permute-start(bf16[2,24,2048]{2,1,0:T(8,128)(2,1)} %param.11), channel_id=1, source_target_pairs={{0,8},{4,12},{8,0},{12,4},{1,9},{5,13},{9,1},{13,5},{2,10},{6,14},... | collective-permute-start | bytes 589832 | tf_op jit(solution)/shard_map/ppermute | solution.py:188
  3.6 5.1 %collective-permute-start.3 = (bf16[2,24,2048]{2,1,0:T(8,128)(2,1)}, bf16[2,24,2048]{2,1,0:T(8,128)(2,1)S(1)}, u32[]{:S(2)}, u32[]{:S(2)}) collective-permute-start(bf16[2,24,2048]{2,1,0:T(8,128)(2,1)} %param.11), channel_id=1, source_target_pairs={{0,4},{4,0},{8,12},{12,8},{1,5},{5,1},{9,13},{13,9},{2,6},{6,2},{1... | collective-permute-start | bytes 589832 | tf_op jit(solution)/shard_map/ppermute | solution.py:189
  8.7 1.4 %collective-permute-start.5 = (bf16[2,24,2048]{2,1,0:T(8,128)(2,1)S(1)}, bf16[2,24,2048]{2,1,0:T(8,128)(2,1)S(1)}, u32[]{:S(2)}, u32[]{:S(2)}) collective-permute-start(bf16[2,24,2048]{2,1,0:T(8,128)(2,1)S(1)} %collective-permute-done.4), channel_id=1, source_target_pairs={{0,4},{4,0},{8,12},{12,8},{1,5},{5,1},{9,13},{13,9},{2,6},{6,2},{1... | collective-permute-start | bytes 589832 | tf_op jit(solution)/shard_map/ppermute | solution.py:189
  12.0 9.1 %copy-start.2 = (f32[1,4096]{1,0:T(1,128)S(1)}, f32[1,4096]{1,0:T(1,128)}, u32[]{:S(2)}) copy-start(f32[1,4096]{1,0:T(1,128)} %param.13) | copy-start | bytes 49156
  15.3 18.2 %copy-start.1 = (f32[1,512]{1,0:T(1,128)S(1)}, f32[1,512]{1,0:T(1,128)}, u32[]{:S(2)}) copy-start(f32[1,512]{1,0:T(1,128)} %param.14) | copy-start | bytes 6148
  15.3 9.7 %collective-permute-start.6 = (f32[48,1024]{1,0:T(8,128)S(1)}, f32[48,1024]{1,0:T(8,128)S(1)}, u32[]{:S(2)}, u32[]{:S(2)}) collective-permute-start(f32[48,1024]{1,0:T(8,128)S(1)} %get-tuple-element.9), channel_id=1, source_target_pairs={{0,1},{1,2},{2,3},{3,0},{4,5},{5,6},{6,7},{7,4},{8,9},{9,10},{10,1... | collective-permute-start | bytes 589832 | tf_op jit(solution)/shard_map/ppermute | solution.py:229
  17.2 15.8 %collective-permute-start.7 = (f32[48,1024]{1,0:T(8,128)S(1)}, f32[48,1024]{1,0:T(8,128)S(1)}, u32[]{:S(2)}, u32[]{:S(2)}) collective-permute-start(f32[48,1024]{1,0:T(8,128)S(1)} %get-tuple-element.11), channel_id=1, source_target_pairs={{0,2},{1,3},{2,0},{3,1},{4,6},{5,7},{6,4},{7,5},{8,10},{9,11},{10,... | collective-permute-start | bytes 589832 | tf_op jit(solution)/shard_map/ppermute | solution.py:229
  19.8 13.2 %collective-permute-start.8 = (f32[48,1024]{1,0:T(8,128)S(1)}, f32[48,1024]{1,0:T(8,128)S(1)}, u32[]{:S(2)}, u32[]{:S(2)}) collective-permute-start(f32[48,1024]{1,0:T(8,128)S(1)} %get-tuple-element.10), channel_id=1, source_target_pairs={{0,3},{1,0},{2,1},{3,2},{4,7},{5,4},{6,5},{7,6},{8,11},{9,8},{10,9... | collective-permute-start | bytes 589832 | tf_op jit(solution)/shard_map/ppermute | solution.py:229
  33.3 16.4 %copy-start.5 = (f32[1,32]{1,0:T(1,128)S(1)}, f32[1,32]{1,0:T(1,128)}, u32[]{:S(2)}) copy-start(f32[1,32]{1,0:T(1,128)} %param.15) | copy-start | bytes 388
  33.3 17.1 %copy-start.3 = (s32[2,96]{1,0:T(2,128)S(1)}, s32[2,96]{1,0:T(2,128)}, u32[]{:S(2)}) copy-start(s32[2,96]{1,0:T(2,128)} %param.18) | copy-start | bytes 2308
  33.3 17.1 %copy-start.4 = (s32[2,64]{1,0:T(2,128)S(1)}, s32[2,64]{1,0:T(2,128)}, u32[]{:S(2)}) copy-start(s32[2,64]{1,0:T(2,128)} %param.17) | copy-start | bytes 1540
  33.5 6.8 %collective-permute-start.10 = (bf16[48,1024]{1,0:T(8,128)(2,1)S(1)}, bf16[48,1024]{1,0:T(8,128)(2,1)S(1)}, u32[]{:S(2)}, u32[]{:S(2)}) collective-permute-start(bf16[48,1024]{1,0:T(8,128)(2,1)S(1)} %get-tuple-element.16), channel_id=1, source_target_pairs={{0,2},{1,3},{2,0},{3,1},{4,6},{5,7},{6,4},{7,5},{8,10},{9,11},{10,... | collective-permute-start | bytes 294920 | tf_op jit(solution)/shard_map/ppermute | solution.py:188
  37.2 7.6 %collective-permute-start.9 = (bf16[48,1024]{1,0:T(8,128)(2,1)S(1)}, bf16[48,1024]{1,0:T(8,128)(2,1)S(1)}, u32[]{:S(2)}, u32[]{:S(2)}) collective-permute-start(bf16[48,1024]{1,0:T(8,128)(2,1)S(1)} %get-tuple-element.16), channel_id=1, source_target_pairs={{0,1},{1,0},{2,3},{3,2},{4,5},{5,4},{6,7},{7,6},{8,9},{9,8},{10,11... | collective-permute-start | bytes 294920 | tf_op jit(solution)/shard_map/ppermute | solution.py:189
  40.3 7.1 %collective-permute-start.11 = (bf16[48,1024]{1,0:T(8,128)(2,1)S(1)}, bf16[48,1024]{1,0:T(8,128)(2,1)S(1)}, u32[]{:S(2)}, u32[]{:S(2)}) collective-permute-start(bf16[48,1024]{1,0:T(8,128)(2,1)S(1)} %collective-permute-done.10), channel_id=1, source_target_pairs={{0,1},{1,0},{2,3},{3,2},{4,5},{5,4},{6,7},{7,6},{8,9},{9,8},{10,11... | collective-permute-start | bytes 294920 | tf_op jit(solution)/shard_map/ppermute | solution.py:189
  48.1 11.1 %collective-permute-start.13 = (bf16[192,1024]{1,0:T(8,128)(2,1)S(1)}, bf16[192,1024]{1,0:T(8,128)(2,1)S(1)}, u32[]{:S(2)}, u32[]{:S(2)}) collective-permute-start(bf16[192,1024]{1,0:T(8,128)(2,1)S(1)} %bitcast.93), channel_id=1, source_target_pairs={{0,8},{4,12},{8,0},{12,4},{1,9},{5,13},{9,1},{13,5},{2,10},{6,14},... | collective-permute-start | bytes 1179656 | tf_op jit(solution)/shard_map/ppermute | solution.py:188
  49.8 7.3 %collective-permute-start.1 = (f32[4128]{0:T(1024)S(1)}, f32[4128]{0:T(1024)S(1)}, u32[]{:S(2)}, u32[]{:S(2)}) collective-permute-start(f32[4128]{0:T(1024)S(1)} %reduce), channel_id=1, source_target_pairs={{0,8},{4,12},{8,0},{12,4},{1,9},{5,13},{9,1},{13,5},{2,10},{6,14},... | collective-permute-start | bytes 49544 | tf_op jit(solution)/shard_map/ppermute | solution.py:188
  50.4 8.2 %collective-permute-start = (f32[4128]{0:T(1024)S(1)}, f32[4128]{0:T(1024)S(1)}, u32[]{:S(2)}, u32[]{:S(2)}) collective-permute-start(f32[4128]{0:T(1024)S(1)} %reduce), channel_id=1, source_target_pairs={{0,4},{4,0},{8,12},{12,8},{1,5},{5,1},{9,13},{13,9},{2,6},{6,2},{1... | collective-permute-start | bytes 49544 | tf_op jit(solution)/shard_map/ppermute | solution.py:189
  57.0 1.6 %collective-permute-start.2 = (f32[4128]{0:T(1024)S(1)}, f32[4128]{0:T(1024)S(1)}, u32[]{:S(2)}, u32[]{:S(2)}) collective-permute-start(f32[4128]{0:T(1024)S(1)} %collective-permute-done.1), channel_id=1, source_target_pairs={{0,4},{4,0},{8,12},{12,8},{1,5},{5,1},{9,13},{13,9},{2,6},{6,2},{1... | collective-permute-start | bytes 49544 | tf_op jit(solution)/shard_map/ppermute | solution.py:189
  57.6 4.9 %copy-start = (f32[2,8,64,96]{3,2,1,0:T(8,128)}, f32[2,8,64,96]{3,2,1,0:T(8,128)S(1)}, u32[]{:S(2)}) copy-start(f32[2,8,64,96]{3,2,1,0:T(8,128)S(1)} %tile.4) | copy-start | bytes 1179652
  58.6 2.0 %collective-permute-start.12 = (bf16[192,1024]{1,0:T(8,128)(2,1)S(1)}, bf16[192,1024]{1,0:T(8,128)(2,1)S(1)}, u32[]{:S(2)}, u32[]{:S(2)}) collective-permute-start(bf16[192,1024]{1,0:T(8,128)(2,1)S(1)} %bitcast.94), channel_id=1, source_target_pairs={{0,4},{4,0},{8,12},{12,8},{1,5},{5,1},{9,13},{13,9},{2,6},{6,2},{1... | collective-permute-start | bytes 1179656 | tf_op jit(solution)/shard_map/ppermute | solution.py:189
  59.2 1.9 %collective-permute-start.14 = (bf16[192,1024]{1,0:T(8,128)(2,1)S(1)}, bf16[192,1024]{1,0:T(8,128)(2,1)S(1)}, u32[]{:S(2)}, u32[]{:S(2)}) collective-permute-start(bf16[192,1024]{1,0:T(8,128)(2,1)S(1)} %collective-permute-done.13), channel_id=1, source_target_pairs={{0,4},{4,0},{8,12},{12,8},{1,5},{5,1},{9,13},{13,9},{2,6},{6,2},{1... | collective-permute-start | bytes 1179656 | tf_op jit(solution)/shard_map/ppermute | solution.py:189
  71.7 7.2 %collective-permute-start.15 = (bf16[48,1024]{1,0:T(8,128)(2,1)S(1)}, bf16[48,1024]{1,0:T(8,128)(2,1)S(1)}, u32[]{:S(2)}, u32[]{:S(2)}) collective-permute-start(bf16[48,1024]{1,0:T(8,128)(2,1)S(1)} %get-tuple-element.12), channel_id=1, source_target_pairs={{0,1},{1,2},{2,3},{3,0},{4,5},{5,6},{6,7},{7,4},{8,9},{9,10},{10,1... | collective-permute-start | bytes 294920 | tf_op jit(solution)/shard_map/ppermute | solution.py:229
  73.5 6.4 %collective-permute-start.16 = (bf16[48,1024]{1,0:T(8,128)(2,1)S(1)}, bf16[48,1024]{1,0:T(8,128)(2,1)S(1)}, u32[]{:S(2)}, u32[]{:S(2)}) collective-permute-start(bf16[48,1024]{1,0:T(8,128)(2,1)S(1)} %get-tuple-element.14), channel_id=1, source_target_pairs={{0,2},{1,3},{2,0},{3,1},{4,6},{5,7},{6,4},{7,5},{8,10},{9,11},{10,... | collective-permute-start | bytes 294920 | tf_op jit(solution)/shard_map/ppermute | solution.py:229
  76.8 5.9 %collective-permute-start.17 = (bf16[48,1024]{1,0:T(8,128)(2,1)S(1)}, bf16[48,1024]{1,0:T(8,128)(2,1)S(1)}, u32[]{:S(2)}, u32[]{:S(2)}) collective-permute-start(bf16[48,1024]{1,0:T(8,128)(2,1)S(1)} %get-tuple-element.13), channel_id=1, source_target_pairs={{0,3},{1,0},{2,1},{3,2},{4,7},{5,4},{6,5},{7,6},{8,11},{9,8},{10,9... | collective-permute-start | bytes 294920 | tf_op jit(solution)/shard_map/ppermute | solution.py:229
  84.0 5.6 %collective-permute-start.19 = (bf16[48,1024]{1,0:T(8,128)(2,1)S(1)}, bf16[48,1024]{1,0:T(8,128)(2,1)S(1)}, u32[]{:S(2)}, u32[]{:S(2)}) collective-permute-start(bf16[48,1024]{1,0:T(8,128)(2,1)S(1)} %pad_maximum_fusion.6), channel_id=1, source_target_pairs={{0,2},{1,3},{2,0},{3,1},{4,6},{5,7},{6,4},{7,5},{8,10},{9,11},{10,... | collective-permute-start | bytes 294920 | tf_op jit(solution)/shard_map/ppermute | solution.py:188
  86.2 7.4 %collective-permute-start.18 = (bf16[48,1024]{1,0:T(8,128)(2,1)S(1)}, bf16[48,1024]{1,0:T(8,128)(2,1)S(1)}, u32[]{:S(2)}, u32[]{:S(2)}) collective-permute-start(bf16[48,1024]{1,0:T(8,128)(2,1)S(1)} %pad_maximum_fusion.6), channel_id=1, source_target_pairs={{0,1},{1,0},{2,3},{3,2},{4,5},{5,4},{6,7},{7,6},{8,9},{9,8},{10,11... | collective-permute-start | bytes 294920 | tf_op jit(solution)/shard_map/ppermute | solution.py:189
  89.6 7.0 %collective-permute-start.20 = (bf16[48,1024]{1,0:T(8,128)(2,1)S(1)}, bf16[48,1024]{1,0:T(8,128)(2,1)S(1)}, u32[]{:S(2)}, u32[]{:S(2)}) collective-permute-start(bf16[48,1024]{1,0:T(8,128)(2,1)S(1)} %collective-permute-done.19), channel_id=1, source_target_pairs={{0,1},{1,0},{2,3},{3,2},{4,5},{5,4},{6,7},{7,6},{8,9},{9,8},{10,11... | collective-permute-start | bytes 294920 | tf_op jit(solution)/shard_map/ppermute | solution.py:189
  101.3 1.8 %collective-permute-start.21 = (bf16[2,2,24,2048]{3,2,1,0:T(8,128)(2,1)S(1)}, bf16[2,2,24,2048]{3,2,1,0:T(8,128)(2,1)S(1)}, u32[]{:S(2)}, u32[]{:S(2)}) collective-permute-start(bf16[2,2,24,2048]{3,2,1,0:T(8,128)(2,1)S(1)} %pad_maximum_fusion.4), channel_id=1, source_target_pairs={{0,4},{4,0},{8,12},{12,8},{1,5},{5,1},{9,13},{13,9},{2,6},{6,2},{1... | collective-permute-start | bytes 1179656 | tf_op jit(solution)/shard_map/ppermute | solution.py:216
  103.1 11.5 %collective-permute-start.22 = (bf16[2,24,2048]{2,1,0:T(8,128)(2,1)S(1)}, bf16[2,24,2048]{2,1,0:T(8,128)(2,1)S(1)}, u32[]{:S(2)}, u32[]{:S(2)}) collective-permute-start(bf16[2,24,2048]{2,1,0:T(8,128)(2,1)S(1)} %fusion.7), channel_id=1, source_target_pairs={{0,8},{4,12},{8,0},{12,4},{1,9},{5,13},{9,1},{13,5},{2,10},{6,14},... | collective-permute-start | bytes 589832 | tf_op jit(solution)/shard_map/ppermute | solution.py:220

commit v8 on v7

--- a/solution.py
+++ b/solution.py
@@ -258,61 +258,57 @@
     gains_all = layer_params[:, : query_gain.shape[1]]
     gates_all = layer_params[:, query_gain.shape[1] :]
 
-    gathered = in_order(image_tokens, "section")
-    gathered = gathered.transpose(1, 0, 2, 3).reshape(
-        micro_count, -1, image_tokens.shape[2]
-    )
     shard_count = lax.axis_size("shard")
-    image_count = gathered.shape[1]
-    total_rows = micro_count * image_count
-    flat_rows = gathered.reshape(total_rows, gathered.shape[2])
-    partial = jnp.dot(flat_rows, weights, preferred_element_type=jnp.float32)
-    raw_rows = scatter_blocks(
-        partial.reshape(shard_count, total_rows // shard_count, 2 * key_width), "shard", False
-    )
-    key_rows = head_normalize(raw_rows[:, :key_width], key_norm_gain[0], keyval_heads)
-    keyval_rows = jnp.concatenate(
-        [key_rows.astype(jnp.bfloat16), raw_rows[:, key_width:].astype(jnp.bfloat16)], axis=1
-    )
-    keyval_own = in_order(keyval_rows, "shard").reshape(total_rows, 2 * key_width)
-    keyval_all, _ = gather_blocks(keyval_own, "section")
-
     same_document = text_document[:, :, None] == image_document[:, None, :]
-    leaving, grad_local = attention_layers(
-        section_index,
-        layer_slots,
-        jnp.tanh(gates_all),
-        text_queries,
-        keyval_all.reshape(section_count, micro_count, image_count, 2 * key_width),
-        gains_all,
-        same_document,
-        cotangent[0],
-    )
-    grad_rows = scatter_blocks(
-        grad_local.reshape(shard_count, total_rows // shard_count, 2 * key_width),
-        "shard",
-        False,
-    )
-    key_portion = norm_gradient(
-        raw_rows[:, :key_width], key_norm_gain[0], grad_rows[:, :key_width], keyval_heads
-    )
-    raw_grad_rows = jnp.concatenate([key_portion, grad_rows[:, key_width:]], axis=1).astype(
-        jnp.bfloat16
-    )
-    raw_grad = in_order(raw_grad_rows, "shard").reshape(total_rows, 2 * key_width)
-    owned = image_count // section_count
-    raw_grad = (
-        raw_grad.reshape(micro_count, section_count, owned, 2 * key_width)
-        .transpose(1, 0, 2, 3)
-        .reshape(total_rows, 2 * key_width)
-    )
-    image_part = lax.dot_general(
-        raw_grad, weights, (((1,), (1,)), ((), ())), preferred_element_type=jnp.float32
-    )
-    image_part = image_part.astype(jnp.bfloat16).reshape(
-        section_count, micro_count, owned, weights.shape[0]
-    )
-    image_grad = scatter_blocks(image_part, "section", True)
+    gate_factors = jnp.tanh(gates_all)
+
+    def micro_chain(m):
+        gathered = in_order(image_tokens[m], "section")
+        image_count = gathered.shape[0] * gathered.shape[1]
+        block_rows = image_count // shard_count
+        flat_rows = gathered.reshape(image_count, gathered.shape[2])
+        partial = jnp.dot(flat_rows, weights, preferred_element_type=jnp.float32)
+        raw_rows = scatter_blocks(
+            partial.reshape(shard_count, block_rows, 2 * key_width), "shard", False
+        )
+        key_rows = head_normalize(raw_rows[:, :key_width], key_norm_gain[0], keyval_heads)
+        keyval_rows = jnp.concatenate(
+            [key_rows.astype(jnp.bfloat16), raw_rows[:, key_width:].astype(jnp.bfloat16)],
+            axis=1,
+        )
+        keyval_own = in_order(keyval_rows, "shard").reshape(image_count, 2 * key_width)
+        keyval_all, _ = gather_blocks(keyval_own, "section")
+        leaving, grad_local = attention_layers(
+            section_index,
+            layer_slots,
+            gate_factors,
+            text_queries[m : m + 1],
+            keyval_all[:, None],
+            gains_all,
+            same_document[m : m + 1],
+            cotangent[0, m : m + 1],
+        )
+        grad_rows = scatter_blocks(
+            grad_local.reshape(shard_count, block_rows, 2 * key_width), "shard", False
+        )
+        key_portion = norm_gradient(
+            raw_rows[:, :key_width], key_norm_gain[0], grad_rows[:, :key_width], keyval_heads
+        )
+        raw_grad_rows = jnp.concatenate(
+            [key_portion, grad_rows[:, key_width:]], axis=1
+        ).astype(jnp.bfloat16)
+        raw_grad = in_order(raw_grad_rows, "shard").reshape(image_count, 2 * key_width)
+        image_part = lax.dot_general(
+            raw_grad, weights, (((1,), (1,)), ((), ())), preferred_element_type=jnp.float32
+        )
+        image_part = image_part.astype(jnp.bfloat16).reshape(
+            section_count, image_count // section_count, weights.shape[0]
+        )
+        return leaving[0], scatter_blocks(image_part, "section", True)
+
+    chains = [micro_chain(m) for m in range(micro_count)]
+    leaving = jnp.stack([c[0] for c in chains])
+    image_grad = jnp.stack([c[1] for c in chains])
     return (leaving[None], image_grad)
 
 

time: 116 us -> 127 us (1.095)
  waiting for transfers between devices: 44.2 us -> 24.2 us
  starting transfers between devices: 43.5 us -> 53.6 us
  local copies, waits for them, and re-layouts: 4.99 us -> 15 us
  matrix products: 6.94 us -> 11.2 us
  other arithmetic: 6.44 us -> 9.54 us
  Pallas kernels: 8.22 us -> 11 us
    ppermute x6 -> x12, waiting for transfers between devices: 16.1 us -> 6.04 us  [scatter_blocks(): lax.ppermute(part, axis, [(i, (i + d) % count) for i in range(count)])]
    ppermute x6 -> x12, starting transfers between devices: 12.5 us -> 20 us  [scatter_blocks(): lax.ppermute(part, axis, [(i, (i + d) % count) for i in range(count)])]
    ppermute x5 -> x9, waiting for transfers between devices: 13.8 us -> 7.09 us  [gather_blocks(): across = lax.ppermute(block, axis, [(i, i ^ 2) for i in range(count)])]
    broadcast_in_dim x0 -> x3, other arithmetic: none -> 4.68 us  [the longest x1 2.69 us: per_device(): return (leaving[None], image_grad)]
    dot_general x2 -> x4, matrix products: 6.94 us -> 11.2 us  [the longest x2 6.08 us: micro_chain(): partial = jnp.dot(flat_rows, weights, preferred_element_type=jnp.float32)]
    ppermute x5 -> x9, starting transfers between devices: 4.91 us -> 8.51 us  [gather_blocks(): lax.ppermute(block, axis, partner)]
    slice x4 -> x10, local copies, waits for them, and re-layouts: 0.04 us -> 3.29 us  [the longest x1 2.26 us: micro_chain(): text_queries[m:m + 1]]
    ppermute x5 -> x9, starting transfers between devices: 8.65 us -> 5.68 us  [gather_blocks(): lax.ppermute(across, axis, partner)]
  transfers between devices with their start and end apart: 23 -> 43, of which waited for: 15 -> 15; matrix products, arithmetic and copies ran while one was open for 3% -> 22% of each run, Pallas kernels for 0% -> 9%
where the time goes in v8:
time: 127 us; the launch traced here: 126 us
  starting transfers between devices  53.6 us (42%)
  waiting for transfers between devices  24.2 us (19%)
  local copies, waits for them, and re-layouts  15 us (12%)
  matrix products  11.2 us (9%)
  Pallas kernels  11 us (9%)
  other arithmetic  9.54 us (8%)
  between operations  1.28 us (1%)
    ppermute x12, starting transfers between devices, scatter_blocks(): lax.ppermute(part, axis, [(i, (i + d) % count) for i in range(count)])  20 us
    ppermute x9, starting transfers between devices, gather_blocks(): across = lax.ppermute(block, axis, [(i, i ^ 2) for i in range(count)])  11.4 us
    pallas_call x2, Pallas kernels, attention_layers(): pl.pallas_call(functools.partial(attention_kernel, head_count=head_count,...  11 us
    ppermute x9, starting transfers between devices, gather_blocks(): lax.ppermute(block, axis, partner)  8.51 us
    ppermute x2, starting transfers between devices, scatter_blocks(): back = lax.ppermute(theirs, axis, [(i, i ^ 2) for i in range(count)])  7.37 us
    ppermute x9, waiting for transfers between devices, gather_blocks(): across = lax.ppermute(block, axis, [(i, i ^ 2) for i in range(count)])  7.09 us
    dot_general x2, matrix products, micro_chain(): partial = jnp.dot(flat_rows, weights, preferred_element_type=jnp.float32)  6.08 us
    ppermute x12, waiting for transfers between devices, scatter_blocks(): lax.ppermute(part, axis, [(i, (i + d) % count) for i in range(count)])  6.04 us
  transfers between devices with their start and end apart: 43, of which 15 were waited for; matrix products, arithmetic and copies ran while one was open for 22% of the time, Pallas kernels for 9%

profile of v8, /device:TPU:0, one launch (start us, length us, event | category | flops | bytes accessed | tf_op | source)
XLA Modules:
  0.0 125.9 jit_solution(1876932168631217161)
XLA Ops:
  1.6 3.0 %collective-permute-start.16 = (bf16[24,2048]{1,0:T(8,128)(2,1)S(1)}, bf16[24,2048]{1,0:T(8,128)(2,1)S(1)}, u32[]{:S(2)}, u32[]{:S(2)}) collective-permute-start(bf16[24,2048]{1,0:T(8,128)(2,1)S(1)} %get-tuple-element.36), channel_id=1, source_target_pairs={{0,8},{4,12},{8,0},{12,4},{1,9},{5,13},{9,1},{13,5},{2,10},{6,14},... | collective-permute-start | bytes 294920 | tf_op jit(solution)/shard_map/ppermute | solution.py:188
  6.6 1.8 %collective-permute-start.1 = (f32[4128]{0:T(1024)S(1)}, f32[4128]{0:T(1024)S(1)}, u32[]{:S(2)}, u32[]{:S(2)}) collective-permute-start(f32[4128]{0:T(1024)S(1)} %reduce), channel_id=1, source_target_pairs={{0,8},{4,12},{8,0},{12,4},{1,9},{5,13},{9,1},{13,5},{2,10},{6,14},... | collective-permute-start | bytes 49544 | tf_op jit(solution)/shard_map/ppermute | solution.py:188
  8.4 2.3 %slice_bitcast_fusion.1 = (bf16[1,64,4096]{2,1,0:T(8,128)(2,1)}, bf16[1,64,4096]{2,1,0:T(8,128)(2,1)}) fusion(bf16[1,2,64,4096]{3,2,1,0:T(8,128)(2,1)} %param.21), kind=kLoop, calls=%fused_computation.20 | loop fusion | bytes 2097152 | tf_op jit(solution)/shard_map/squeeze | solution.py:289
  10.7 2.3 %fusion.42 = (bf16[1,64,4096]{2,1,0:T(8,128)(2,1)}, bf16[1,64,4096]{2,1,0:T(8,128)(2,1)}) fusion(bf16[2,64,4096]{2,1,0:T(8,128)(2,1)} %param.18), kind=kLoop, calls=%fused_computation.128 | loop fusion | bytes 2097152 | tf_op jit(solution)/shard_map/slice | solution.py:285
  15.1 3.0 %fusion = f32[4,24,1024]{2,1,0:T(8,128)S(1)} fusion(bf16[1,2048,1024]{2,1,0:T(8,128)(2,1)} %param.14, bf16[4,24,2048]{2,1,0:T(8,128)(2,1)S(1)} %gather_fusion.2, pred[4]{0:T(512)(128)(4,1)S(1)} %get-tuple-element.53), kind=kOutput, calls=%fused_computation.6 | convolution fusion | flops 402849792 | bytes 4980740 | tf_op jit(solution)/shard_map/dot_general | solution.py:270
  18.1 1.6 %collective-permute-start.18 = (f32[24,1024]{1,0:T(8,128)S(1)}, f32[24,1024]{1,0:T(8,128)S(1)}, u32[]{:S(2)}, u32[]{:S(2)}) collective-permute-start(f32[24,1024]{1,0:T(8,128)S(1)} %get-tuple-element.25), channel_id=1, source_target_pairs={{0,1},{1,2},{2,3},{3,0},{4,5},{5,6},{6,7},{7,4},{8,9},{9,10},{10,1... | collective-permute-start | bytes 294920 | tf_op jit(solution)/shard_map/ppermute | solution.py:229
  19.8 2.6 %collective-permute-start.19 = (f32[24,1024]{1,0:T(8,128)S(1)}, f32[24,1024]{1,0:T(8,128)S(1)}, u32[]{:S(2)}, u32[]{:S(2)}) collective-permute-start(f32[24,1024]{1,0:T(8,128)S(1)} %get-tuple-element.27), channel_id=1, source_target_pairs={{0,2},{1,3},{2,0},{3,1},{4,6},{5,7},{6,4},{7,5},{8,10},{9,11},{10,... | collective-permute-start | bytes 294920 | tf_op jit(solution)/shard_map/ppermute | solution.py:229
  24.4 3.0 %fusion.2 = f32[4,24,1024]{2,1,0:T(8,128)S(1)} fusion(bf16[1,2048,1024]{2,1,0:T(8,128)(2,1)} %param.14, bf16[4,24,2048]{2,1,0:T(8,128)(2,1)S(1)} %gather_fusion, pred[4]{0:T(512)(128)(4,1)S(1)} %get-tuple-element.53), kind=kOutput, calls=%fused_computation.8 | convolution fusion | flops 402849792 | bytes 4980740 | tf_op jit(solution)/shard_map/dot_general | solution.py:270
  29.3 1.4 %collective-permute-start.7 = (f32[24,1024]{1,0:T(8,128)S(1)}, f32[24,1024]{1,0:T(8,128)S(1)}, u32[]{:S(2)}, u32[]{:S(2)}) collective-permute-start(f32[24,1024]{1,0:T(8,128)S(1)} %get-tuple-element.24), channel_id=1, source_target_pairs={{0,2},{1,3},{2,0},{3,1},{4,6},{5,7},{6,4},{7,5},{8,10},{9,11},{10,... | collective-permute-start | bytes 294920 | tf_op jit(solution)/shard_map/ppermute | solution.py:229
  30.7 3.0 %collective-permute-start.8 = (f32[24,1024]{1,0:T(8,128)S(1)}, f32[24,1024]{1,0:T(8,128)S(1)}, u32[]{:S(2)}, u32[]{:S(2)}) collective-permute-start(f32[24,1024]{1,0:T(8,128)S(1)} %get-tuple-element.23), channel_id=1, source_target_pairs={{0,3},{1,0},{2,1},{3,2},{4,7},{5,4},{6,5},{7,6},{8,11},{9,8},{10,9... | collective-permute-start | bytes 294920 | tf_op jit(solution)/shard_map/ppermute | solution.py:229
  34.9 3.4 %collective-permute-done.7 = f32[24,1024]{1,0:T(8,128)S(1)} collective-permute-done((f32[24,1024]{1,0:T(8,128)S(1)}, f32[24,1024]{1,0:T(8,128)S(1)}, u32[]{:S(2)}, u32[]{:S(2)}) %collective-permute-start.7) | collective-permute-done | bytes 98336 | tf_op jit(solution)/shard_map/ppermute | solution.py:229
  40.1 2.8 %collective-permute-start.21 = (bf16[24,1024]{1,0:T(8,128)(2,1)S(1)}, bf16[24,1024]{1,0:T(8,128)(2,1)S(1)}, u32[]{:S(2)}, u32[]{:S(2)}) collective-permute-start(bf16[24,1024]{1,0:T(8,128)(2,1)S(1)} %get-tuple-element.41), channel_id=1, source_target_pairs={{0,1},{1,0},{2,3},{3,2},{4,5},{5,4},{6,7},{7,6},{8,9},{9,8},{10,11... | collective-permute-start | bytes 147464 | tf_op jit(solution)/shard_map/ppermute | solution.py:189
  44.1 2.5 %collective-permute-start.23 = (bf16[24,1024]{1,0:T(8,128)(2,1)S(1)}, bf16[24,1024]{1,0:T(8,128)(2,1)S(1)}, u32[]{:S(2)}, u32[]{:S(2)}) collective-permute-start(bf16[24,1024]{1,0:T(8,128)(2,1)S(1)} %collective-permute-done.22), channel_id=1, source_target_pairs={{0,1},{1,0},{2,3},{3,2},{4,5},{5,4},{6,7},{7,6},{8,9},{9,8},{10,11... | collective-permute-start | bytes 147464 | tf_op jit(solution)/shard_map/ppermute | solution.py:189
  49.4 1.5 %collective-permute-done.9 = bf16[24,1024]{1,0:T(8,128)(2,1)S(1)} collective-permute-done((bf16[24,1024]{1,0:T(8,128)(2,1)S(1)}, bf16[24,1024]{1,0:T(8,128)(2,1)S(1)}, u32[]{:S(2)}, u32[]{:S(2)}) %collective-permute-start.9) | collective-permute-done | bytes 49184 | tf_op jit(solution)/shard_map/ppermute | solution.py:189
  50.8 1.5 %collective-permute-done.11 = bf16[24,1024]{1,0:T(8,128)(2,1)S(1)} collective-permute-done((bf16[24,1024]{1,0:T(8,128)(2,1)S(1)}, bf16[24,1024]{1,0:T(8,128)(2,1)S(1)}, u32[]{:S(2)}, u32[]{:S(2)}) %collective-permute-start.11) | collective-permute-done | bytes 49184 | tf_op jit(solution)/shard_map/ppermute | solution.py:189
  56.5 1.5 %collective-permute-start.13 = (bf16[96,1024]{1,0:T(8,128)(2,1)S(1)}, bf16[96,1024]{1,0:T(8,128)(2,1)S(1)}, u32[]{:S(2)}, u32[]{:S(2)}) collective-permute-start(bf16[96,1024]{1,0:T(8,128)(2,1)S(1)} %bitcast.183), channel_id=1, source_target_pairs={{0,8},{4,12},{8,0},{12,4},{1,9},{5,13},{9,1},{13,5},{2,10},{6,14},... | collective-permute-start | bytes 589832 | tf_op jit(solution)/shard_map/ppermute | solution.py:188
  60.6 2.8 %collective-permute-done.13 = bf16[96,1024]{1,0:T(8,128)(2,1)S(1)} collective-permute-done((bf16[96,1024]{1,0:T(8,128)(2,1)S(1)}, bf16[96,1024]{1,0:T(8,128)(2,1)S(1)}, u32[]{:S(2)}, u32[]{:S(2)}) %collective-permute-start.13) | collective-permute-done | bytes 196640 | tf_op jit(solution)/shard_map/ppermute | solution.py:188
  64.4 5.4 %shard_map.105 = (f32[1,64,4096]{2,1,0:T(8,128)}, bf16[1,96,1024]{2,1,0:T(8,128)(2,1)}) custom-call(s32[1]{0:T(128)} %bitcast.section_ref, s32[4]{0:T(128)} %iota_xor_fusion.slots_ref, f32[4,32]{1,0:T(4,128)} %maximum_tanh_fusion.gates_ref, bf16[1,64,4096]{2,1,0:T(8,128)(2,1)} %get-tuple-element.17.queries_ref, ...), custom_call_target="tpu_custom_call" | custom-call | flops 704643072 | bytes 3407872 | tf_op jit(solution)/shard_map/pallas_call | solution.py:139
  71.4 1.6 %collective-permute-start.36 = (bf16[24,1024]{1,0:T(8,128)(2,1)S(1)}, bf16[24,1024]{1,0:T(8,128)(2,1)S(1)}, u32[]{:S(2)}, u32[]{:S(2)}) collective-permute-start(bf16[24,1024]{1,0:T(8,128)(2,1)S(1)} %get-tuple-element.33), channel_id=1, source_target_pairs={{0,2},{1,3},{2,0},{3,1},{4,6},{5,7},{6,4},{7,5},{8,10},{9,11},{10,... | collective-permute-start | bytes 147464 | tf_op jit(solution)/shard_map/ppermute | solution.py:229
  73.0 2.1 %collective-permute-start.37 = (bf16[24,1024]{1,0:T(8,128)(2,1)S(1)}, bf16[24,1024]{1,0:T(8,128)(2,1)S(1)}, u32[]{:S(2)}, u32[]{:S(2)}) collective-permute-start(bf16[24,1024]{1,0:T(8,128)(2,1)S(1)} %get-tuple-element.32), channel_id=1, source_target_pairs={{0,3},{1,0},{2,1},{3,2},{4,7},{5,4},{6,5},{7,6},{8,11},{9,8},{10,9... | collective-permute-start | bytes 147464 | tf_op jit(solution)/shard_map/ppermute | solution.py:229
  76.1 5.6 %shard_map.104 = (f32[1,64,4096]{2,1,0:T(8,128)}, bf16[1,96,1024]{2,1,0:T(8,128)(2,1)}) custom-call(s32[1]{0:T(128)} %bitcast.section_ref, s32[4]{0:T(128)} %iota_xor_fusion.slots_ref, f32[4,32]{1,0:T(4,128)} %maximum_tanh_fusion.gates_ref, bf16[1,64,4096]{2,1,0:T(8,128)(2,1)} %get-tuple-element.16.queries_ref, ...), custom_call_target="tpu_custom_call" | custom-call | flops 704643072 | bytes 3407872 | tf_op jit(solution)/shard_map/pallas_call | solution.py:139
  82.7 1.5 %collective-permute-start.28 = (bf16[24,1024]{1,0:T(8,128)(2,1)S(1)}, bf16[24,1024]{1,0:T(8,128)(2,1)S(1)}, u32[]{:S(2)}, u32[]{:S(2)}) collective-permute-start(bf16[24,1024]{1,0:T(8,128)(2,1)S(1)} %get-tuple-element.30), channel_id=1, source_target_pairs={{0,2},{1,3},{2,0},{3,1},{4,6},{5,7},{6,4},{7,5},{8,10},{9,11},{10,... | collective-permute-start | bytes 147464 | tf_op jit(solution)/shard_map/ppermute | solution.py:229
  84.3 2.7 %maximum_bitcast_fusion = f32[1,2,64,4096]{3,2,1,0:T(8,128)} fusion(f32[1,64,4096]{2,1,0:T(8,128)S(1)} %copy-done.3, f32[1,64,4096]{2,1,0:T(8,128)} %get-tuple-element.8), kind=kLoop, calls=%fused_computation.16 | loop fusion | flops 524288 | bytes 4194304 | tf_op jit(solution)/shard_map/broadcast_in_dim | solution.py:312
  87.0 2.8 %collective-permute-start.29 = (bf16[24,1024]{1,0:T(8,128)(2,1)S(1)}, bf16[24,1024]{1,0:T(8,128)(2,1)S(1)}, u32[]{:S(2)}, u32[]{:S(2)}) collective-permute-start(bf16[24,1024]{1,0:T(8,128)(2,1)S(1)} %get-tuple-element.29), channel_id=1, source_target_pairs={{0,3},{1,0},{2,1},{3,2},{4,7},{5,4},{6,5},{7,6},{8,11},{9,8},{10,9... | collective-permute-start | bytes 147464 | tf_op jit(solution)/shard_map/ppermute | solution.py:229
  94.2 3.5 %collective-permute-start.38 = (bf16[24,1024]{1,0:T(8,128)(2,1)S(1)}, bf16[24,1024]{1,0:T(8,128)(2,1)S(1)}, u32[]{:S(2)}, u32[]{:S(2)}) collective-permute-start(bf16[24,1024]{1,0:T(8,128)(2,1)S(1)} %pad_maximum_fusion.15), channel_id=1, source_target_pairs={{0,1},{1,0},{2,3},{3,2},{4,5},{5,4},{6,7},{7,6},{8,9},{9,8},{10,11... | collective-permute-start | bytes 147464 | tf_op jit(solution)/shard_map/ppermute | solution.py:189
  98.2 2.3 %collective-permute-start.40 = (bf16[24,1024]{1,0:T(8,128)(2,1)S(1)}, bf16[24,1024]{1,0:T(8,128)(2,1)S(1)}, u32[]{:S(2)}, u32[]{:S(2)}) collective-permute-start(bf16[24,1024]{1,0:T(8,128)(2,1)S(1)} %collective-permute-done.39), channel_id=1, source_target_pairs={{0,1},{1,0},{2,3},{3,2},{4,5},{5,4},{6,7},{7,6},{8,9},{9,8},{10,11... | collective-permute-start | bytes 147464 | tf_op jit(solution)/shard_map/ppermute | solution.py:189
  100.5 2.4 %collective-permute-done.31 = bf16[24,1024]{1,0:T(8,128)(2,1)S(1)} collective-permute-done((bf16[24,1024]{1,0:T(8,128)(2,1)S(1)}, bf16[24,1024]{1,0:T(8,128)(2,1)S(1)}, u32[]{:S(2)}, u32[]{:S(2)}) %collective-permute-start.31) | collective-permute-done | bytes 49184 | tf_op jit(solution)/shard_map/ppermute | solution.py:188
  104.0 3.0 %collective-permute-done.32 = bf16[24,1024]{1,0:T(8,128)(2,1)S(1)} collective-permute-done((bf16[24,1024]{1,0:T(8,128)(2,1)S(1)}, bf16[24,1024]{1,0:T(8,128)(2,1)S(1)}, u32[]{:S(2)}, u32[]{:S(2)}) %collective-permute-start.32) | collective-permute-done | bytes 49184 | tf_op jit(solution)/shard_map/ppermute | solution.py:189
  107.7 3.8 %fusion.8 = bf16[96,2048]{1,0:T(8,128)(2,1)S(1)} fusion(bf16[96,1024]{1,0:T(8,128)(2,1)S(1)} %bitcast.182, bf16[1,2048,1024]{2,1,0:T(8,128)(2,1)} %param.14), kind=kOutput, calls=%fused_computation.14 | convolution fusion | flops 402849792 | bytes 4784128 | tf_op jit(solution)/shard_map/dot_general | solution.py:301
  113.7 6.3 %collective-permute-start.34 = (bf16[24,2048]{1,0:T(8,128)(2,1)S(1)}, bf16[24,2048]{1,0:T(8,128)(2,1)S(1)}, u32[]{:S(2)}, u32[]{:S(2)}) collective-permute-start(bf16[24,2048]{1,0:T(8,128)(2,1)S(1)} %fusion.22), channel_id=1, source_target_pairs={{0,8},{4,12},{8,0},{12,4},{1,9},{5,13},{9,1},{13,5},{2,10},{6,14},... | collective-permute-start | bytes 294920 | tf_op jit(solution)/shard_map/ppermute | solution.py:220
  121.1 2.5 %collective-permute-done.34 = bf16[24,2048]{1,0:T(8,128)(2,1)S(1)} collective-permute-done((bf16[24,2048]{1,0:T(8,128)(2,1)S(1)}, bf16[24,2048]{1,0:T(8,128)(2,1)S(1)}, u32[]{:S(2)}, u32[]{:S(2)}) %collective-permute-start.34) | collective-permute-done | bytes 98336 | tf_op jit(solution)/shard_map/ppermute | solution.py:220
  123.6 1.5 %collective-permute-done.42 = bf16[24,2048]{1,0:T(8,128)(2,1)S(1)} collective-permute-done((bf16[24,2048]{1,0:T(8,128)(2,1)S(1)}, bf16[24,2048]{1,0:T(8,128)(2,1)S(1)}, u32[]{:S(2)}, u32[]{:S(2)}) %collective-permute-start.42) | collective-permute-done | bytes 98336 | tf_op jit(solution)/shard_map/ppermute | solution.py:220
  (163 shorter events, 37.6 us)
Async XLA Ops:
  1.6 11.4 %collective-permute-start.16 = (bf16[24,2048]{1,0:T(8,128)(2,1)S(1)}, bf16[24,2048]{1,0:T(8,128)(2,1)S(1)}, u32[]{:S(2)}, u32[]{:S(2)}) collective-permute-start(bf16[24,2048]{1,0:T(8,128)(2,1)S(1)} %get-tuple-element.36), channel_id=1, source_target_pairs={{0,8},{4,12},{8,0},{12,4},{1,9},{5,13},{9,1},{13,5},{2,10},{6,14},... | collective-permute-start | bytes 294920 | tf_op jit(solution)/shard_map/ppermute | solution.py:188
  4.6 8.5 %collective-permute-start.15 = (bf16[24,2048]{1,0:T(8,128)(2,1)S(1)}, bf16[24,2048]{1,0:T(8,128)(2,1)S(1)}, u32[]{:S(2)}, u32[]{:S(2)}) collective-permute-start(bf16[24,2048]{1,0:T(8,128)(2,1)S(1)} %get-tuple-element.36), channel_id=1, source_target_pairs={{0,4},{4,0},{8,12},{12,8},{1,5},{5,1},{9,13},{13,9},{2,6},{6,2},{1... | collective-permute-start | bytes 294920 | tf_op jit(solution)/shard_map/ppermute | solution.py:189
  4.6 9.0 %collective-permute-start.4 = (bf16[24,2048]{1,0:T(8,128)(2,1)S(1)}, bf16[24,2048]{1,0:T(8,128)(2,1)S(1)}, u32[]{:S(2)}, u32[]{:S(2)}) collective-permute-start(bf16[24,2048]{1,0:T(8,128)(2,1)S(1)} %get-tuple-element.35), channel_id=1, source_target_pairs={{0,8},{4,12},{8,0},{12,4},{1,9},{5,13},{9,1},{13,5},{2,10},{6,14},... | collective-permute-start | bytes 294920 | tf_op jit(solution)/shard_map/ppermute | solution.py:188
  4.8 15.0 %collective-permute-start.3 = (bf16[24,2048]{1,0:T(8,128)(2,1)S(1)}, bf16[24,2048]{1,0:T(8,128)(2,1)S(1)}, u32[]{:S(2)}, u32[]{:S(2)}) collective-permute-start(bf16[24,2048]{1,0:T(8,128)(2,1)S(1)} %get-tuple-element.35), channel_id=1, source_target_pairs={{0,4},{4,0},{8,12},{12,8},{1,5},{5,1},{9,13},{13,9},{2,6},{6,2},{1... | collective-permute-start | bytes 294920 | tf_op jit(solution)/shard_map/ppermute | solution.py:189
  6.6 47.0 %collective-permute-start.1 = (f32[4128]{0:T(1024)S(1)}, f32[4128]{0:T(1024)S(1)}, u32[]{:S(2)}, u32[]{:S(2)}) collective-permute-start(f32[4128]{0:T(1024)S(1)} %reduce), channel_id=1, source_target_pairs={{0,8},{4,12},{8,0},{12,4},{1,9},{5,13},{9,1},{13,5},{2,10},{6,14},... | collective-permute-start | bytes 49544 | tf_op jit(solution)/shard_map/ppermute | solution.py:188
  13.2 42.7 %collective-permute-start = (f32[4128]{0:T(1024)S(1)}, f32[4128]{0:T(1024)S(1)}, u32[]{:S(2)}, u32[]{:S(2)}) collective-permute-start(f32[4128]{0:T(1024)S(1)} %reduce), channel_id=1, source_target_pairs={{0,4},{4,0},{8,12},{12,8},{1,5},{5,1},{9,13},{13,9},{2,6},{6,2},{1... | collective-permute-start | bytes 49544 | tf_op jit(solution)/shard_map/ppermute | solution.py:189
  13.7 8.7 %collective-permute-start.5 = (bf16[24,2048]{1,0:T(8,128)(2,1)S(1)}, bf16[24,2048]{1,0:T(8,128)(2,1)S(1)}, u32[]{:S(2)}, u32[]{:S(2)}) collective-permute-start(bf16[24,2048]{1,0:T(8,128)(2,1)S(1)} %collective-permute-done.4), channel_id=1, source_target_pairs={{0,4},{4,0},{8,12},{12,8},{1,5},{5,1},{9,13},{13,9},{2,6},{6,2},{1... | collective-permute-start | bytes 294920 | tf_op jit(solution)/shard_map/ppermute | solution.py:189
  18.1 9.3 %collective-permute-start.18 = (f32[24,1024]{1,0:T(8,128)S(1)}, f32[24,1024]{1,0:T(8,128)S(1)}, u32[]{:S(2)}, u32[]{:S(2)}) collective-permute-start(f32[24,1024]{1,0:T(8,128)S(1)} %get-tuple-element.25), channel_id=1, source_target_pairs={{0,1},{1,2},{2,3},{3,0},{4,5},{5,6},{6,7},{7,4},{8,9},{9,10},{10,1... | collective-permute-start | bytes 294920 | tf_op jit(solution)/shard_map/ppermute | solution.py:229
  19.8 9.5 %collective-permute-start.19 = (f32[24,1024]{1,0:T(8,128)S(1)}, f32[24,1024]{1,0:T(8,128)S(1)}, u32[]{:S(2)}, u32[]{:S(2)}) collective-permute-start(f32[24,1024]{1,0:T(8,128)S(1)} %get-tuple-element.27), channel_id=1, source_target_pairs={{0,2},{1,3},{2,0},{3,1},{4,6},{5,7},{6,4},{7,5},{8,10},{9,11},{10,... | collective-permute-start | bytes 294920 | tf_op jit(solution)/shard_map/ppermute | solution.py:229
  22.4 8.3 %collective-permute-start.20 = (f32[24,1024]{1,0:T(8,128)S(1)}, f32[24,1024]{1,0:T(8,128)S(1)}, u32[]{:S(2)}, u32[]{:S(2)}) collective-permute-start(f32[24,1024]{1,0:T(8,128)S(1)} %get-tuple-element.26), channel_id=1, source_target_pairs={{0,3},{1,0},{2,1},{3,2},{4,7},{5,4},{6,5},{7,6},{8,11},{9,8},{10,9... | collective-permute-start | bytes 294920 | tf_op jit(solution)/shard_map/ppermute | solution.py:229
  27.5 7.4 %collective-permute-start.6 = (f32[24,1024]{1,0:T(8,128)S(1)}, f32[24,1024]{1,0:T(8,128)S(1)}, u32[]{:S(2)}, u32[]{:S(2)}) collective-permute-start(f32[24,1024]{1,0:T(8,128)S(1)} %get-tuple-element.22), channel_id=1, source_target_pairs={{0,1},{1,2},{2,3},{3,0},{4,5},{5,6},{6,7},{7,4},{8,9},{9,10},{10,1... | collective-permute-start | bytes 294920 | tf_op jit(solution)/shard_map/ppermute | solution.py:229
  29.3 9.0 %collective-permute-start.7 = (f32[24,1024]{1,0:T(8,128)S(1)}, f32[24,1024]{1,0:T(8,128)S(1)}, u32[]{:S(2)}, u32[]{:S(2)}) collective-permute-start(f32[24,1024]{1,0:T(8,128)S(1)} %get-tuple-element.24), channel_id=1, source_target_pairs={{0,2},{1,3},{2,0},{3,1},{4,6},{5,7},{6,4},{7,5},{8,10},{9,11},{10,... | collective-permute-start | bytes 294920 | tf_op jit(solution)/shard_map/ppermute | solution.py:229
  30.7 7.5 %collective-permute-start.8 = (f32[24,1024]{1,0:T(8,128)S(1)}, f32[24,1024]{1,0:T(8,128)S(1)}, u32[]{:S(2)}, u32[]{:S(2)}) collective-permute-start(f32[24,1024]{1,0:T(8,128)S(1)} %get-tuple-element.23), channel_id=1, source_target_pairs={{0,3},{1,0},{2,1},{3,2},{4,7},{5,4},{6,5},{7,6},{8,11},{9,8},{10,9... | collective-permute-start | bytes 294920 | tf_op jit(solution)/shard_map/ppermute | solution.py:229
  38.7 5.5 %collective-permute-start.22 = (bf16[24,1024]{1,0:T(8,128)(2,1)S(1)}, bf16[24,1024]{1,0:T(8,128)(2,1)S(1)}, u32[]{:S(2)}, u32[]{:S(2)}) collective-permute-start(bf16[24,1024]{1,0:T(8,128)(2,1)S(1)} %get-tuple-element.41), channel_id=1, source_target_pairs={{0,2},{1,3},{2,0},{3,1},{4,6},{5,7},{6,4},{7,5},{8,10},{9,11},{10,... | collective-permute-start | bytes 147464 | tf_op jit(solution)/shard_map/ppermute | solution.py:188
  40.1 6.6 %collective-permute-start.21 = (bf16[24,1024]{1,0:T(8,128)(2,1)S(1)}, bf16[24,1024]{1,0:T(8,128)(2,1)S(1)}, u32[]{:S(2)}, u32[]{:S(2)}) collective-permute-start(bf16[24,1024]{1,0:T(8,128)(2,1)S(1)} %get-tuple-element.41), channel_id=1, source_target_pairs={{0,1},{1,0},{2,3},{3,2},{4,5},{5,4},{6,7},{7,6},{8,9},{9,8},{10,11... | collective-permute-start | bytes 147464 | tf_op jit(solution)/shard_map/ppermute | solution.py:189
  42.9 5.3 %collective-permute-start.10 = (bf16[24,1024]{1,0:T(8,128)(2,1)S(1)}, bf16[24,1024]{1,0:T(8,128)(2,1)S(1)}, u32[]{:S(2)}, u32[]{:S(2)}) collective-permute-start(bf16[24,1024]{1,0:T(8,128)(2,1)S(1)} %get-tuple-element.39), channel_id=1, source_target_pairs={{0,2},{1,3},{2,0},{3,1},{4,6},{5,7},{6,4},{7,5},{8,10},{9,11},{10,... | collective-permute-start | bytes 147464 | tf_op jit(solution)/shard_map/ppermute | solution.py:188
  53.0 5.7 %collective-permute-start.25 = (bf16[96,1024]{1,0:T(8,128)(2,1)S(1)}, bf16[96,1024]{1,0:T(8,128)(2,1)S(1)}, u32[]{:S(2)}, u32[]{:S(2)}) collective-permute-start(bf16[96,1024]{1,0:T(8,128)(2,1)S(1)} %bitcast.186), channel_id=1, source_target_pairs={{0,8},{4,12},{8,0},{12,4},{1,9},{5,13},{9,1},{13,5},{2,10},{6,14},... | collective-permute-start | bytes 589832 | tf_op jit(solution)/shard_map/ppermute | solution.py:188
  56.0 7.5 %collective-permute-start.24 = (bf16[96,1024]{1,0:T(8,128)(2,1)S(1)}, bf16[96,1024]{1,0:T(8,128)(2,1)S(1)}, u32[]{:S(2)}, u32[]{:S(2)}) collective-permute-start(bf16[96,1024]{1,0:T(8,128)(2,1)S(1)} %bitcast.187), channel_id=1, source_target_pairs={{0,4},{4,0},{8,12},{12,8},{1,5},{5,1},{9,13},{13,9},{2,6},{6,2},{1... | collective-permute-start | bytes 589832 | tf_op jit(solution)/shard_map/ppermute | solution.py:189
  56.5 6.9 %collective-permute-start.13 = (bf16[96,1024]{1,0:T(8,128)(2,1)S(1)}, bf16[96,1024]{1,0:T(8,128)(2,1)S(1)}, u32[]{:S(2)}, u32[]{:S(2)}) collective-permute-start(bf16[96,1024]{1,0:T(8,128)(2,1)S(1)} %bitcast.183), channel_id=1, source_target_pairs={{0,8},{4,12},{8,0},{12,4},{1,9},{5,13},{9,1},{13,5},{2,10},{6,14},... | collective-permute-start | bytes 589832 | tf_op jit(solution)/shard_map/ppermute | solution.py:188
  60.1 15.0 %collective-permute-start.12 = (bf16[96,1024]{1,0:T(8,128)(2,1)S(1)}, bf16[96,1024]{1,0:T(8,128)(2,1)S(1)}, u32[]{:S(2)}, u32[]{:S(2)}) collective-permute-start(bf16[96,1024]{1,0:T(8,128)(2,1)S(1)} %bitcast.184), channel_id=1, source_target_pairs={{0,4},{4,0},{8,12},{12,8},{1,5},{5,1},{9,13},{13,9},{2,6},{6,2},{1... | collective-permute-start | bytes 589832 | tf_op jit(solution)/shard_map/ppermute | solution.py:189
  63.4 11.7 %collective-permute-start.14 = (bf16[96,1024]{1,0:T(8,128)(2,1)S(1)}, bf16[96,1024]{1,0:T(8,128)(2,1)S(1)}, u32[]{:S(2)}, u32[]{:S(2)}) collective-permute-start(bf16[96,1024]{1,0:T(8,128)(2,1)S(1)} %collective-permute-done.13), channel_id=1, source_target_pairs={{0,4},{4,0},{8,12},{12,8},{1,5},{5,1},{9,13},{13,9},{2,6},{6,2},{1... | collective-permute-start | bytes 589832 | tf_op jit(solution)/shard_map/ppermute | solution.py:189
  70.8 16.2 %collective-permute-start.35 = (bf16[24,1024]{1,0:T(8,128)(2,1)S(1)}, bf16[24,1024]{1,0:T(8,128)(2,1)S(1)}, u32[]{:S(2)}, u32[]{:S(2)}) collective-permute-start(bf16[24,1024]{1,0:T(8,128)(2,1)S(1)} %get-tuple-element.31), channel_id=1, source_target_pairs={{0,1},{1,2},{2,3},{3,0},{4,5},{5,6},{6,7},{7,4},{8,9},{9,10},{10,1... | collective-permute-start | bytes 147464 | tf_op jit(solution)/shard_map/ppermute | solution.py:229
  71.4 18.4 %collective-permute-start.36 = (bf16[24,1024]{1,0:T(8,128)(2,1)S(1)}, bf16[24,1024]{1,0:T(8,128)(2,1)S(1)}, u32[]{:S(2)}, u32[]{:S(2)}) collective-permute-start(bf16[24,1024]{1,0:T(8,128)(2,1)S(1)} %get-tuple-element.33), channel_id=1, source_target_pairs={{0,2},{1,3},{2,0},{3,1},{4,6},{5,7},{6,4},{7,5},{8,10},{9,11},{10,... | collective-permute-start | bytes 147464 | tf_op jit(solution)/shard_map/ppermute | solution.py:229
  73.0 16.8 %collective-permute-start.37 = (bf16[24,1024]{1,0:T(8,128)(2,1)S(1)}, bf16[24,1024]{1,0:T(8,128)(2,1)S(1)}, u32[]{:S(2)}, u32[]{:S(2)}) collective-permute-start(bf16[24,1024]{1,0:T(8,128)(2,1)S(1)} %get-tuple-element.32), channel_id=1, source_target_pairs={{0,3},{1,0},{2,1},{3,2},{4,7},{5,4},{6,5},{7,6},{8,11},{9,8},{10,9... | collective-permute-start | bytes 147464 | tf_op jit(solution)/shard_map/ppermute | solution.py:229
  82.5 8.2 %collective-permute-start.27 = (bf16[24,1024]{1,0:T(8,128)(2,1)S(1)}, bf16[24,1024]{1,0:T(8,128)(2,1)S(1)}, u32[]{:S(2)}, u32[]{:S(2)}) collective-permute-start(bf16[24,1024]{1,0:T(8,128)(2,1)S(1)} %get-tuple-element.28), channel_id=1, source_target_pairs={{0,1},{1,2},{2,3},{3,0},{4,5},{5,6},{6,7},{7,4},{8,9},{9,10},{10,1... | collective-permute-start | bytes 147464 | tf_op jit(solution)/shard_map/ppermute | solution.py:229
  82.7 8.0 %collective-permute-start.28 = (bf16[24,1024]{1,0:T(8,128)(2,1)S(1)}, bf16[24,1024]{1,0:T(8,128)(2,1)S(1)}, u32[]{:S(2)}, u32[]{:S(2)}) collective-permute-start(bf16[24,1024]{1,0:T(8,128)(2,1)S(1)} %get-tuple-element.30), channel_id=1, source_target_pairs={{0,2},{1,3},{2,0},{3,1},{4,6},{5,7},{6,4},{7,5},{8,10},{9,11},{10,... | collective-permute-start | bytes 147464 | tf_op jit(solution)/shard_map/ppermute | solution.py:229
  93.0 5.2 %collective-permute-start.39 = (bf16[24,1024]{1,0:T(8,128)(2,1)S(1)}, bf16[24,1024]{1,0:T(8,128)(2,1)S(1)}, u32[]{:S(2)}, u32[]{:S(2)}) collective-permute-start(bf16[24,1024]{1,0:T(8,128)(2,1)S(1)} %pad_maximum_fusion.15), channel_id=1, source_target_pairs={{0,2},{1,3},{2,0},{3,1},{4,6},{5,7},{6,4},{7,5},{8,10},{9,11},{10,... | collective-permute-start | bytes 147464 | tf_op jit(solution)/shard_map/ppermute | solution.py:188
  94.2 8.7 %collective-permute-start.38 = (bf16[24,1024]{1,0:T(8,128)(2,1)S(1)}, bf16[24,1024]{1,0:T(8,128)(2,1)S(1)}, u32[]{:S(2)}, u32[]{:S(2)}) collective-permute-start(bf16[24,1024]{1,0:T(8,128)(2,1)S(1)} %pad_maximum_fusion.15), channel_id=1, source_target_pairs={{0,1},{1,0},{2,3},{3,2},{4,5},{5,4},{6,7},{7,6},{8,9},{9,8},{10,11... | collective-permute-start | bytes 147464 | tf_op jit(solution)/shard_map/ppermute | solution.py:189
  97.7 5.2 %collective-permute-start.31 = (bf16[24,1024]{1,0:T(8,128)(2,1)S(1)}, bf16[24,1024]{1,0:T(8,128)(2,1)S(1)}, u32[]{:S(2)}, u32[]{:S(2)}) collective-permute-start(bf16[24,1024]{1,0:T(8,128)(2,1)S(1)} %pad_maximum_fusion.14), channel_id=1, source_target_pairs={{0,2},{1,3},{2,0},{3,1},{4,6},{5,7},{6,4},{7,5},{8,10},{9,11},{10,... | collective-permute-start | bytes 147464 | tf_op jit(solution)/shard_map/ppermute | solution.py:188
  98.2 5.8 %collective-permute-start.30 = (bf16[24,1024]{1,0:T(8,128)(2,1)S(1)}, bf16[24,1024]{1,0:T(8,128)(2,1)S(1)}, u32[]{:S(2)}, u32[]{:S(2)}) collective-permute-start(bf16[24,1024]{1,0:T(8,128)(2,1)S(1)} %pad_maximum_fusion.14), channel_id=1, source_target_pairs={{0,1},{1,0},{2,3},{3,2},{4,5},{5,4},{6,7},{7,6},{8,9},{9,8},{10,11... | collective-permute-start | bytes 147464 | tf_op jit(solution)/shard_map/ppermute | solution.py:189
  113.1 6.9 %collective-permute-start.41 = (bf16[2,24,2048]{2,1,0:T(8,128)(2,1)S(1)}, bf16[2,24,2048]{2,1,0:T(8,128)(2,1)S(1)}, u32[]{:S(2)}, u32[]{:S(2)}) collective-permute-start(bf16[2,24,2048]{2,1,0:T(8,128)(2,1)S(1)} %pad_maximum_fusion.8), channel_id=1, source_target_pairs={{0,4},{4,0},{8,12},{12,8},{1,5},{5,1},{9,13},{13,9},{2,6},{6,2},{1... | collective-permute-start | bytes 589832 | tf_op jit(solution)/shard_map/ppermute | solution.py:216
  113.7 9.9 %collective-permute-start.34 = (bf16[24,2048]{1,0:T(8,128)(2,1)S(1)}, bf16[24,2048]{1,0:T(8,128)(2,1)S(1)}, u32[]{:S(2)}, u32[]{:S(2)}) collective-permute-start(bf16[24,2048]{1,0:T(8,128)(2,1)S(1)} %fusion.22), channel_id=1, source_target_pairs={{0,8},{4,12},{8,0},{12,4},{1,9},{5,13},{9,1},{13,5},{2,10},{6,14},... | collective-permute-start | bytes 294920 | tf_op jit(solution)/shard_map/ppermute | solution.py:220
  (18 other events, 131.1 us)

commit v9 on v7

--- a/solution.py
+++ b/solution.py
@@ -252,12 +252,6 @@
     keyval_heads = key_width // head_dim
     weights = keyval_weight[0]
 
-    layer_params, layer_slots = gather_blocks(
-        jnp.concatenate([query_gain, gate_logit], axis=1)[0], "section"
-    )
-    gains_all = layer_params[:, : query_gain.shape[1]]
-    gates_all = layer_params[:, query_gain.shape[1] :]
-
     gathered = in_order(image_tokens, "section")
     gathered = gathered.transpose(1, 0, 2, 3).reshape(
         micro_count, -1, image_tokens.shape[2]
@@ -275,7 +269,22 @@
         [key_rows.astype(jnp.bfloat16), raw_rows[:, key_width:].astype(jnp.bfloat16)], axis=1
     )
     keyval_own = in_order(keyval_rows, "shard").reshape(total_rows, 2 * key_width)
-    keyval_all, _ = gather_blocks(keyval_own, "section")
+    params = jnp.concatenate([query_gain, gate_logit], axis=1)[0]
+    high = params.astype(jnp.bfloat16)
+    rest = params - high.astype(jnp.float32)
+    middle = rest.astype(jnp.bfloat16)
+    low = (rest - middle.astype(jnp.float32)).astype(jnp.bfloat16)
+    coded = jnp.concatenate([high, middle, low])
+    param_rows = -(-coded.shape[0] // (2 * key_width))
+    coded = jnp.pad(coded, (0, param_rows * 2 * key_width - coded.shape[0]))
+    payload = jnp.concatenate([keyval_own, coded.reshape(param_rows, 2 * key_width)], axis=0)
+    payload_all, layer_slots = gather_blocks(payload, "section")
+    keyval_all = payload_all[:, :total_rows]
+    coded_all = payload_all[:, total_rows:].reshape(section_count, -1)[:, : 3 * params.shape[0]]
+    coded_all = coded_all.astype(jnp.float32).reshape(section_count, 3, params.shape[0])
+    layer_params = (coded_all[:, 0] + coded_all[:, 1]) + coded_all[:, 2]
+    gains_all = layer_params[:, : query_gain.shape[1]]
+    gates_all = layer_params[:, query_gain.shape[1] :]
 
     same_document = text_document[:, :, None] == image_document[:, None, :]
     leaving, grad_local = attention_layers(

time: 116 us -> 115 us (level)
  starting transfers between devices: 43.5 us -> 42.3 us
    ppermute x5 -> x4, starting transfers between devices: 11.1 us -> 10.5 us  [gather_blocks(): across = lax.ppermute(block, axis, [(i, i ^ 2) for i in range(count)])]
    ppermute x5 -> x4, starting transfers between devices: 4.91 us -> 4.34 us  [gather_blocks(): lax.ppermute(block, axis, partner)]
    ppermute x5 -> x4, waiting for transfers between devices: 7.47 us -> 7.12 us  [gather_blocks(): lax.ppermute(across, axis, partner)]
    ppermute x5 -> x4, waiting for transfers between devices: 13.8 us -> 14 us  [gather_blocks(): across = lax.ppermute(block, axis, [(i, i ^ 2) for i in range(count)])]
    ppermute x5 -> x4, starting transfers between devices: 8.65 us -> 8.58 us  [gather_blocks(): lax.ppermute(across, axis, partner)]
  transfers between devices with their start and end apart: 23 -> 20, of which waited for: 15 -> 15; matrix products, arithmetic and copies ran while one was open for 3% -> 2% of each run, Pallas kernels for 0% -> 0%
where the time goes in v9:
time: 115 us
  waiting for transfers between devices  43.9 us (38%)
  starting transfers between devices  42.3 us (37%)
  Pallas kernels  8.2 us (7%)
  matrix products  6.94 us (6%)
  other arithmetic  6.57 us (6%)
  local copies, waits for them, and re-layouts  6.09 us (5%)
    ppermute x6, waiting for transfers between devices, scatter_blocks(): lax.ppermute(part, axis, [(i, (i + d) % count) for i in range(count)])  15.9 us
    ppermute x4, waiting for transfers between devices, gather_blocks(): across = lax.ppermute(block, axis, [(i, i ^ 2) for i in range(count)])  14 us
    ppermute x6, starting transfers between devices, scatter_blocks(): lax.ppermute(part, axis, [(i, (i + d) % count) for i in range(count)])  12.5 us
    ppermute x4, starting transfers between devices, gather_blocks(): across = lax.ppermute(block, axis, [(i, i ^ 2) for i in range(count)])  10.5 us
    ppermute x4, starting transfers between devices, gather_blocks(): lax.ppermute(across, axis, partner)  8.58 us
    pallas_call x1, Pallas kernels, attention_layers(): pl.pallas_call(functools.partial(attention_kernel, head_count=head_count,...  8.2 us
    ppermute x4, waiting for transfers between devices, gather_blocks(): lax.ppermute(across, axis, partner)  7.12 us
    ppermute x1, starting transfers between devices, scatter_blocks(): back = lax.ppermute(theirs, axis, [(i, i ^ 2) for i in range(count)])  6.3 us
  transfers between devices with their start and end apart: 20, of which 15 were waited for; matrix products, arithmetic and copies ran while one was open for 2% of the time, Pallas kernels for 0%

profile of v9, /device:TPU:0, one launch (start us, length us, event | category | flops | bytes accessed | tf_op | source)
XLA Modules:
  0.0 115.1 jit_solution(1685782381227856943)
XLA Ops:
  0.6 3.0 %collective-permute-start.1 = (bf16[2,24,2048]{2,1,0:T(8,128)(2,1)}, bf16[2,24,2048]{2,1,0:T(8,128)(2,1)S(1)}, u32[]{:S(2)}, u32[]{:S(2)}) collective-permute-start(bf16[2,24,2048]{2,1,0:T(8,128)(2,1)} %param.11), channel_id=1, source_target_pairs={{0,8},{4,12},{8,0},{12,4},{1,9},{5,13},{9,1},{13,5},{2,10},{6,14},... | collective-permute-start | bytes 589832 | tf_op jit(solution)/shard_map/ppermute | solution.py:188
  4.4 4.3 %collective-permute-done.1 = bf16[2,24,2048]{2,1,0:T(8,128)(2,1)S(1)} collective-permute-done((bf16[2,24,2048]{2,1,0:T(8,128)(2,1)}, bf16[2,24,2048]{2,1,0:T(8,128)(2,1)S(1)}, u32[]{:S(2)}, u32[]{:S(2)}) %collective-permute-start.1) | collective-permute-done | bytes 196640 | tf_op jit(solution)/shard_map/ppermute | solution.py:188
  8.8 1.4 %collective-permute-done.2 = bf16[2,24,2048]{2,1,0:T(8,128)(2,1)S(1)} collective-permute-done((bf16[2,24,2048]{2,1,0:T(8,128)(2,1)S(1)}, bf16[2,24,2048]{2,1,0:T(8,128)(2,1)S(1)}, u32[]{:S(2)}, u32[]{:S(2)}) %collective-permute-start.2) | collective-permute-done | bytes 196640 | tf_op jit(solution)/shard_map/ppermute | solution.py:189
  10.2 1.0 pad_maximum_fusion.3
  12.0 3.2 %fusion = f32[4,48,1024]{2,1,0:T(8,128)S(1)} fusion(bf16[4,48,2048]{2,1,0:T(8,128)(2,1)S(1)} %bitcast.94, bf16[1,2048,1024]{2,1,0:T(8,128)(2,1)} %param.12), kind=kOutput, calls=%fused_computation.3 | convolution fusion | flops 805306368 | bytes 5767168 | tf_op jit(solution)/shard_map/dot_general | solution.py:263
  15.4 1.9 %collective-permute-start.3 = (f32[48,1024]{1,0:T(8,128)S(1)}, f32[48,1024]{1,0:T(8,128)S(1)}, u32[]{:S(2)}, u32[]{:S(2)}) collective-permute-start(f32[48,1024]{1,0:T(8,128)S(1)} %get-tuple-element.9), channel_id=1, source_target_pairs={{0,1},{1,2},{2,3},{3,0},{4,5},{5,6},{6,7},{7,4},{8,9},{9,10},{10,1... | collective-permute-start | bytes 589832 | tf_op jit(solution)/shard_map/ppermute | solution.py:229
  17.2 2.6 %collective-permute-start.4 = (f32[48,1024]{1,0:T(8,128)S(1)}, f32[48,1024]{1,0:T(8,128)S(1)}, u32[]{:S(2)}, u32[]{:S(2)}) collective-permute-start(f32[48,1024]{1,0:T(8,128)S(1)} %get-tuple-element.11), channel_id=1, source_target_pairs={{0,2},{1,3},{2,0},{3,1},{4,6},{5,7},{6,4},{7,5},{8,10},{9,11},{10,... | collective-permute-start | bytes 589832 | tf_op jit(solution)/shard_map/ppermute | solution.py:229
  19.8 1.4 %collective-permute-start.5 = (f32[48,1024]{1,0:T(8,128)S(1)}, f32[48,1024]{1,0:T(8,128)S(1)}, u32[]{:S(2)}, u32[]{:S(2)}) collective-permute-start(f32[48,1024]{1,0:T(8,128)S(1)} %get-tuple-element.10), channel_id=1, source_target_pairs={{0,3},{1,0},{2,1},{3,2},{4,7},{5,4},{6,5},{7,6},{8,11},{9,8},{10,9... | collective-permute-start | bytes 589832 | tf_op jit(solution)/shard_map/ppermute | solution.py:229
  21.3 3.7 %collective-permute-done.3 = f32[48,1024]{1,0:T(8,128)S(1)} collective-permute-done((f32[48,1024]{1,0:T(8,128)S(1)}, f32[48,1024]{1,0:T(8,128)S(1)}, u32[]{:S(2)}, u32[]{:S(2)}) %collective-permute-start.3) | collective-permute-done | bytes 196640 | tf_op jit(solution)/shard_map/ppermute | solution.py:229
  25.1 7.9 %collective-permute-done.4 = f32[48,1024]{1,0:T(8,128)S(1)} collective-permute-done((f32[48,1024]{1,0:T(8,128)S(1)}, f32[48,1024]{1,0:T(8,128)S(1)}, u32[]{:S(2)}, u32[]{:S(2)}) %collective-permute-start.4) | collective-permute-done | bytes 196640 | tf_op jit(solution)/shard_map/ppermute | solution.py:229
  33.5 3.7 %collective-permute-start.7 = (bf16[48,1024]{1,0:T(8,128)(2,1)S(1)}, bf16[48,1024]{1,0:T(8,128)(2,1)S(1)}, u32[]{:S(2)}, u32[]{:S(2)}) collective-permute-start(bf16[48,1024]{1,0:T(8,128)(2,1)S(1)} %get-tuple-element.21), channel_id=1, source_target_pairs={{0,2},{1,3},{2,0},{3,1},{4,6},{5,7},{6,4},{7,5},{8,10},{9,11},{10,... | collective-permute-start | bytes 294920 | tf_op jit(solution)/shard_map/ppermute | solution.py:188
  37.2 2.6 %collective-permute-start.6 = (bf16[48,1024]{1,0:T(8,128)(2,1)S(1)}, bf16[48,1024]{1,0:T(8,128)(2,1)S(1)}, u32[]{:S(2)}, u32[]{:S(2)}) collective-permute-start(bf16[48,1024]{1,0:T(8,128)(2,1)S(1)} %get-tuple-element.21), channel_id=1, source_target_pairs={{0,1},{1,0},{2,3},{3,2},{4,5},{5,4},{6,7},{7,6},{8,9},{9,8},{10,11... | collective-permute-start | bytes 294920 | tf_op jit(solution)/shard_map/ppermute | solution.py:189
  40.2 4.5 %collective-permute-start.8 = (bf16[48,1024]{1,0:T(8,128)(2,1)S(1)}, bf16[48,1024]{1,0:T(8,128)(2,1)S(1)}, u32[]{:S(2)}, u32[]{:S(2)}) collective-permute-start(bf16[48,1024]{1,0:T(8,128)(2,1)S(1)} %collective-permute-done.7), channel_id=1, source_target_pairs={{0,1},{1,0},{2,3},{3,2},{4,5},{5,4},{6,7},{7,6},{8,9},{9,8},{10,11... | collective-permute-start | bytes 294920 | tf_op jit(solution)/shard_map/ppermute | solution.py:189
  44.8 2.6 %collective-permute-done.8 = bf16[48,1024]{1,0:T(8,128)(2,1)S(1)} collective-permute-done((bf16[48,1024]{1,0:T(8,128)(2,1)S(1)}, bf16[48,1024]{1,0:T(8,128)(2,1)S(1)}, u32[]{:S(2)}, u32[]{:S(2)}) %collective-permute-start.8) | collective-permute-done | bytes 98336 | tf_op jit(solution)/shard_map/ppermute | solution.py:189
  48.2 1.6 %collective-permute-start.10 = (bf16[205,1024]{1,0:T(8,128)(2,1)S(1)}, bf16[205,1024]{1,0:T(8,128)(2,1)S(1)}, u32[]{:S(2)}, u32[]{:S(2)}) collective-permute-start(bf16[205,1024]{1,0:T(8,128)(2,1)S(1)} %get-tuple-element.13), channel_id=1, source_target_pairs={{0,8},{4,12},{8,0},{12,4},{1,9},{5,13},{9,1},{13,5},{2,10},{6,14},... | collective-permute-start | bytes 1259528 | tf_op jit(solution)/shard_map/ppermute | solution.py:188
  49.8 7.6 %collective-permute-done.10 = bf16[205,1024]{1,0:T(8,128)(2,1)S(1)} collective-permute-done((bf16[205,1024]{1,0:T(8,128)(2,1)S(1)}, bf16[205,1024]{1,0:T(8,128)(2,1)S(1)}, u32[]{:S(2)}, u32[]{:S(2)}) %collective-permute-start.10) | collective-permute-done | bytes 419872 | tf_op jit(solution)/shard_map/ppermute | solution.py:188
  59.1 1.3 %pad_maximum_fusion = bf16[4,192,1024]{2,1,0:T(8,128)(2,1)} fusion(bf16[1,205,1024]{2,1,0:T(8,128)(2,1)S(1)} %bitcast.104, bf16[1,205,1024]{2,1,0:T(8,128)(2,1)S(1)} %bitcast.100, bf16[1,205,1024]{2,1,0:T(8,128)(2,1)S(1)} %bitcast.102, bf16[1,205,1024]{2,1,0:T(8,128)(2,1)S(1)} %get-tuple-element.12), kind=kLoop, calls=%fused_computation.8 | loop fusion | flops 6291456 | bytes 3252224 | tf_op jit(solution)/shard_map/stack | solution.py:190
  62.2 8.2 %shard_map.104 = (f32[2,64,4096]{2,1,0:T(8,128)}, bf16[2,96,1024]{2,1,0:T(8,128)(2,1)}) custom-call(s32[1]{0:T(128)} %bitcast.section_ref, s32[4]{0:T(128)} %iota_xor_fusion.slots_ref, f32[4,32]{1,0:T(4,128)} %slice_tanh_fusion.gates_ref, bf16[2,64,4096]{2,1,0:T(8,128)(2,1)} %queries_ref.1, bf16[4,2,96,1024]{3,2,1,0:T(8,128)(2,1)} %bitcast.106, ...), custom_call_target="tpu_custom_call" | custom-call | flops 1409286144 | bytes 6815744 | tf_op jit(solution)/shard_map/pallas_call | solution.py:139
  71.4 1.8 %collective-permute-start.12 = (bf16[48,1024]{1,0:T(8,128)(2,1)S(1)}, bf16[48,1024]{1,0:T(8,128)(2,1)S(1)}, u32[]{:S(2)}, u32[]{:S(2)}) collective-permute-start(bf16[48,1024]{1,0:T(8,128)(2,1)S(1)} %get-tuple-element.14), channel_id=1, source_target_pairs={{0,1},{1,2},{2,3},{3,0},{4,5},{5,6},{6,7},{7,4},{8,9},{9,10},{10,1... | collective-permute-start | bytes 294920 | tf_op jit(solution)/shard_map/ppermute | solution.py:229
  73.2 3.3 %collective-permute-start.13 = (bf16[48,1024]{1,0:T(8,128)(2,1)S(1)}, bf16[48,1024]{1,0:T(8,128)(2,1)S(1)}, u32[]{:S(2)}, u32[]{:S(2)}) collective-permute-start(bf16[48,1024]{1,0:T(8,128)(2,1)S(1)} %get-tuple-element.16), channel_id=1, source_target_pairs={{0,2},{1,3},{2,0},{3,1},{4,6},{5,7},{6,4},{7,5},{8,10},{9,11},{10,... | collective-permute-start | bytes 294920 | tf_op jit(solution)/shard_map/ppermute | solution.py:229
  76.5 1.6 %collective-permute-start.14 = (bf16[48,1024]{1,0:T(8,128)(2,1)S(1)}, bf16[48,1024]{1,0:T(8,128)(2,1)S(1)}, u32[]{:S(2)}, u32[]{:S(2)}) collective-permute-start(bf16[48,1024]{1,0:T(8,128)(2,1)S(1)} %get-tuple-element.15), channel_id=1, source_target_pairs={{0,3},{1,0},{2,1},{3,2},{4,7},{5,4},{6,5},{7,6},{8,11},{9,8},{10,9... | collective-permute-start | bytes 294920 | tf_op jit(solution)/shard_map/ppermute | solution.py:229
  78.6 1.0 collective-permute-done.13
  79.6 2.8 %collective-permute-done.14 = bf16[48,1024]{1,0:T(8,128)(2,1)S(1)} collective-permute-done((bf16[48,1024]{1,0:T(8,128)(2,1)S(1)}, bf16[48,1024]{1,0:T(8,128)(2,1)S(1)}, u32[]{:S(2)}, u32[]{:S(2)}) %collective-permute-start.14) | collective-permute-done | bytes 98336 | tf_op jit(solution)/shard_map/ppermute | solution.py:229
  83.7 2.2 %collective-permute-start.16 = (bf16[48,1024]{1,0:T(8,128)(2,1)S(1)}, bf16[48,1024]{1,0:T(8,128)(2,1)S(1)}, u32[]{:S(2)}, u32[]{:S(2)}) collective-permute-start(bf16[48,1024]{1,0:T(8,128)(2,1)S(1)} %pad_maximum_fusion.9), channel_id=1, source_target_pairs={{0,2},{1,3},{2,0},{3,1},{4,6},{5,7},{6,4},{7,5},{8,10},{9,11},{10,... | collective-permute-start | bytes 294920 | tf_op jit(solution)/shard_map/ppermute | solution.py:188
  85.9 1.7 %collective-permute-start.15 = (bf16[48,1024]{1,0:T(8,128)(2,1)S(1)}, bf16[48,1024]{1,0:T(8,128)(2,1)S(1)}, u32[]{:S(2)}, u32[]{:S(2)}) collective-permute-start(bf16[48,1024]{1,0:T(8,128)(2,1)S(1)} %pad_maximum_fusion.9), channel_id=1, source_target_pairs={{0,1},{1,0},{2,3},{3,2},{4,5},{5,4},{6,7},{7,6},{8,9},{9,8},{10,11... | collective-permute-start | bytes 294920 | tf_op jit(solution)/shard_map/ppermute | solution.py:189
  87.6 1.7 %collective-permute-done.16 = bf16[48,1024]{1,0:T(8,128)(2,1)S(1)} collective-permute-done((bf16[48,1024]{1,0:T(8,128)(2,1)S(1)}, bf16[48,1024]{1,0:T(8,128)(2,1)S(1)}, u32[]{:S(2)}, u32[]{:S(2)}) %collective-permute-start.16) | collective-permute-done | bytes 98336 | tf_op jit(solution)/shard_map/ppermute | solution.py:188
  89.3 4.0 %collective-permute-start.17 = (bf16[48,1024]{1,0:T(8,128)(2,1)S(1)}, bf16[48,1024]{1,0:T(8,128)(2,1)S(1)}, u32[]{:S(2)}, u32[]{:S(2)}) collective-permute-start(bf16[48,1024]{1,0:T(8,128)(2,1)S(1)} %collective-permute-done.16), channel_id=1, source_target_pairs={{0,1},{1,0},{2,3},{3,2},{4,5},{5,4},{6,7},{7,6},{8,9},{9,8},{10,11... | collective-permute-start | bytes 294920 | tf_op jit(solution)/shard_map/ppermute | solution.py:189
  93.4 3.0 %collective-permute-done.17 = bf16[48,1024]{1,0:T(8,128)(2,1)S(1)} collective-permute-done((bf16[48,1024]{1,0:T(8,128)(2,1)S(1)}, bf16[48,1024]{1,0:T(8,128)(2,1)S(1)}, u32[]{:S(2)}, u32[]{:S(2)}) %collective-permute-start.17) | collective-permute-done | bytes 98336 | tf_op jit(solution)/shard_map/ppermute | solution.py:189
  97.1 3.7 %fusion.4 = bf16[192,2048]{1,0:T(8,128)(2,1)S(1)} fusion(bf16[192,1024]{1,0:T(8,128)(2,1)S(1)} %bitcast.109, bf16[1,2048,1024]{2,1,0:T(8,128)(2,1)} %param.12), kind=kOutput, calls=%fused_computation.7 | convolution fusion | flops 805699584 | bytes 5373952 | tf_op jit(solution)/shard_map/dot_general | solution.py:318
  101.0 1.7 %collective-permute-done.18 = bf16[2,2,24,2048]{3,2,1,0:T(8,128)(2,1)S(1)} collective-permute-done((bf16[2,2,24,2048]{3,2,1,0:T(8,128)(2,1)S(1)}, bf16[2,2,24,2048]{3,2,1,0:T(8,128)(2,1)S(1)}, u32[]{:S(2)}, u32[]{:S(2)}) %collective-permute-start.18) | collective-permute-done | bytes 393248 | tf_op jit(solution)/shard_map/ppermute | solution.py:216
  102.8 6.3 %collective-permute-start.19 = (bf16[2,24,2048]{2,1,0:T(8,128)(2,1)S(1)}, bf16[2,24,2048]{2,1,0:T(8,128)(2,1)S(1)}, u32[]{:S(2)}, u32[]{:S(2)}) collective-permute-start(bf16[2,24,2048]{2,1,0:T(8,128)(2,1)S(1)} %fusion.7), channel_id=1, source_target_pairs={{0,8},{4,12},{8,0},{12,4},{1,9},{5,13},{9,1},{13,5},{2,10},{6,14},... | collective-permute-start | bytes 589832 | tf_op jit(solution)/shard_map/ppermute | solution.py:220
  109.1 5.2 %collective-permute-done.19 = bf16[2,24,2048]{2,1,0:T(8,128)(2,1)S(1)} collective-permute-done((bf16[2,24,2048]{2,1,0:T(8,128)(2,1)S(1)}, bf16[2,24,2048]{2,1,0:T(8,128)(2,1)S(1)}, u32[]{:S(2)}, u32[]{:S(2)}) %collective-permute-start.19) | collective-permute-done | bytes 196640 | tf_op jit(solution)/shard_map/ppermute | solution.py:220
  (80 shorter events, 11.4 us)
Async XLA Ops:
  0.6 8.1 %collective-permute-start.1 = (bf16[2,24,2048]{2,1,0:T(8,128)(2,1)}, bf16[2,24,2048]{2,1,0:T(8,128)(2,1)S(1)}, u32[]{:S(2)}, u32[]{:S(2)}) collective-permute-start(bf16[2,24,2048]{2,1,0:T(8,128)(2,1)} %param.11), channel_id=1, source_target_pairs={{0,8},{4,12},{8,0},{12,4},{1,9},{5,13},{9,1},{13,5},{2,10},{6,14},... | collective-permute-start | bytes 589832 | tf_op jit(solution)/shard_map/ppermute | solution.py:188
  3.6 5.1 %collective-permute-start = (bf16[2,24,2048]{2,1,0:T(8,128)(2,1)}, bf16[2,24,2048]{2,1,0:T(8,128)(2,1)S(1)}, u32[]{:S(2)}, u32[]{:S(2)}) collective-permute-start(bf16[2,24,2048]{2,1,0:T(8,128)(2,1)} %param.11), channel_id=1, source_target_pairs={{0,4},{4,0},{8,12},{12,8},{1,5},{5,1},{9,13},{13,9},{2,6},{6,2},{1... | collective-permute-start | bytes 589832 | tf_op jit(solution)/shard_map/ppermute | solution.py:189
  8.7 1.4 %collective-permute-start.2 = (bf16[2,24,2048]{2,1,0:T(8,128)(2,1)S(1)}, bf16[2,24,2048]{2,1,0:T(8,128)(2,1)S(1)}, u32[]{:S(2)}, u32[]{:S(2)}) collective-permute-start(bf16[2,24,2048]{2,1,0:T(8,128)(2,1)S(1)} %collective-permute-done.1), channel_id=1, source_target_pairs={{0,4},{4,0},{8,12},{12,8},{1,5},{5,1},{9,13},{13,9},{2,6},{6,2},{1... | collective-permute-start | bytes 589832 | tf_op jit(solution)/shard_map/ppermute | solution.py:189
  15.3 18.2 %copy-start.1 = (f32[1,512]{1,0:T(1,128)S(1)}, f32[1,512]{1,0:T(1,128)}, u32[]{:S(2)}) copy-start(f32[1,512]{1,0:T(1,128)} %param.14) | copy-start | bytes 6148
  15.3 42.0 %copy-start.2 = (s32[2,96]{1,0:T(2,128)S(1)}, s32[2,96]{1,0:T(2,128)}, u32[]{:S(2)}) copy-start(s32[2,96]{1,0:T(2,128)} %param.18) | copy-start | bytes 2308
  15.3 42.0 %copy-start.3 = (s32[2,64]{1,0:T(2,128)S(1)}, s32[2,64]{1,0:T(2,128)}, u32[]{:S(2)}) copy-start(s32[2,64]{1,0:T(2,128)} %param.17) | copy-start | bytes 1540
  15.4 9.7 %collective-permute-start.3 = (f32[48,1024]{1,0:T(8,128)S(1)}, f32[48,1024]{1,0:T(8,128)S(1)}, u32[]{:S(2)}, u32[]{:S(2)}) collective-permute-start(f32[48,1024]{1,0:T(8,128)S(1)} %get-tuple-element.9), channel_id=1, source_target_pairs={{0,1},{1,2},{2,3},{3,0},{4,5},{5,6},{6,7},{7,4},{8,9},{9,10},{10,1... | collective-permute-start | bytes 589832 | tf_op jit(solution)/shard_map/ppermute | solution.py:229
  17.2 15.8 %collective-permute-start.4 = (f32[48,1024]{1,0:T(8,128)S(1)}, f32[48,1024]{1,0:T(8,128)S(1)}, u32[]{:S(2)}, u32[]{:S(2)}) collective-permute-start(f32[48,1024]{1,0:T(8,128)S(1)} %get-tuple-element.11), channel_id=1, source_target_pairs={{0,2},{1,3},{2,0},{3,1},{4,6},{5,7},{6,4},{7,5},{8,10},{9,11},{10,... | collective-permute-start | bytes 589832 | tf_op jit(solution)/shard_map/ppermute | solution.py:229
  19.8 13.2 %collective-permute-start.5 = (f32[48,1024]{1,0:T(8,128)S(1)}, f32[48,1024]{1,0:T(8,128)S(1)}, u32[]{:S(2)}, u32[]{:S(2)}) collective-permute-start(f32[48,1024]{1,0:T(8,128)S(1)} %get-tuple-element.10), channel_id=1, source_target_pairs={{0,3},{1,0},{2,1},{3,2},{4,7},{5,4},{6,5},{7,6},{8,11},{9,8},{10,9... | collective-permute-start | bytes 589832 | tf_op jit(solution)/shard_map/ppermute | solution.py:229
  33.5 6.8 %collective-permute-start.7 = (bf16[48,1024]{1,0:T(8,128)(2,1)S(1)}, bf16[48,1024]{1,0:T(8,128)(2,1)S(1)}, u32[]{:S(2)}, u32[]{:S(2)}) collective-permute-start(bf16[48,1024]{1,0:T(8,128)(2,1)S(1)} %get-tuple-element.21), channel_id=1, source_target_pairs={{0,2},{1,3},{2,0},{3,1},{4,6},{5,7},{6,4},{7,5},{8,10},{9,11},{10,... | collective-permute-start | bytes 294920 | tf_op jit(solution)/shard_map/ppermute | solution.py:188
  37.2 7.6 %collective-permute-start.6 = (bf16[48,1024]{1,0:T(8,128)(2,1)S(1)}, bf16[48,1024]{1,0:T(8,128)(2,1)S(1)}, u32[]{:S(2)}, u32[]{:S(2)}) collective-permute-start(bf16[48,1024]{1,0:T(8,128)(2,1)S(1)} %get-tuple-element.21), channel_id=1, source_target_pairs={{0,1},{1,0},{2,3},{3,2},{4,5},{5,4},{6,7},{7,6},{8,9},{9,8},{10,11... | collective-permute-start | bytes 294920 | tf_op jit(solution)/shard_map/ppermute | solution.py:189
  40.2 7.1 %collective-permute-start.8 = (bf16[48,1024]{1,0:T(8,128)(2,1)S(1)}, bf16[48,1024]{1,0:T(8,128)(2,1)S(1)}, u32[]{:S(2)}, u32[]{:S(2)}) collective-permute-start(bf16[48,1024]{1,0:T(8,128)(2,1)S(1)} %collective-permute-done.7), channel_id=1, source_target_pairs={{0,1},{1,0},{2,3},{3,2},{4,5},{5,4},{6,7},{7,6},{8,9},{9,8},{10,11... | collective-permute-start | bytes 294920 | tf_op jit(solution)/shard_map/ppermute | solution.py:189
  48.2 9.2 %collective-permute-start.10 = (bf16[205,1024]{1,0:T(8,128)(2,1)S(1)}, bf16[205,1024]{1,0:T(8,128)(2,1)S(1)}, u32[]{:S(2)}, u32[]{:S(2)}) collective-permute-start(bf16[205,1024]{1,0:T(8,128)(2,1)S(1)} %get-tuple-element.13), channel_id=1, source_target_pairs={{0,8},{4,12},{8,0},{12,4},{1,9},{5,13},{9,1},{13,5},{2,10},{6,14},... | collective-permute-start | bytes 1259528 | tf_op jit(solution)/shard_map/ppermute | solution.py:188
  49.8 9.2 %collective-permute-start.9 = (bf16[205,1024]{1,0:T(8,128)(2,1)S(1)}, bf16[205,1024]{1,0:T(8,128)(2,1)S(1)}, u32[]{:S(2)}, u32[]{:S(2)}) collective-permute-start(bf16[205,1024]{1,0:T(8,128)(2,1)S(1)} %get-tuple-element.13), channel_id=1, source_target_pairs={{0,4},{4,0},{8,12},{12,8},{1,5},{5,1},{9,13},{13,9},{2,6},{6,2},{1... | collective-permute-start | bytes 1259528 | tf_op jit(solution)/shard_map/ppermute | solution.py:189
  57.4 1.8 %collective-permute-start.11 = (bf16[205,1024]{1,0:T(8,128)(2,1)S(1)}, bf16[205,1024]{1,0:T(8,128)(2,1)S(1)}, u32[]{:S(2)}, u32[]{:S(2)}) collective-permute-start(bf16[205,1024]{1,0:T(8,128)(2,1)S(1)} %collective-permute-done.10), channel_id=1, source_target_pairs={{0,4},{4,0},{8,12},{12,8},{1,5},{5,1},{9,13},{13,9},{2,6},{6,2},{1... | collective-permute-start | bytes 1259528 | tf_op jit(solution)/shard_map/ppermute | solution.py:189
  57.5 3.0 %copy-start = (f32[2,8,64,96]{3,2,1,0:T(8,128)}, f32[2,8,64,96]{3,2,1,0:T(8,128)S(1)}, u32[]{:S(2)}) copy-start(f32[2,8,64,96]{3,2,1,0:T(8,128)S(1)} %tile.4) | copy-start | bytes 1179652
  71.4 7.2 %collective-permute-start.12 = (bf16[48,1024]{1,0:T(8,128)(2,1)S(1)}, bf16[48,1024]{1,0:T(8,128)(2,1)S(1)}, u32[]{:S(2)}, u32[]{:S(2)}) collective-permute-start(bf16[48,1024]{1,0:T(8,128)(2,1)S(1)} %get-tuple-element.14), channel_id=1, source_target_pairs={{0,1},{1,2},{2,3},{3,0},{4,5},{5,6},{6,7},{7,4},{8,9},{9,10},{10,1... | collective-permute-start | bytes 294920 | tf_op jit(solution)/shard_map/ppermute | solution.py:229
  73.2 6.4 %collective-permute-start.13 = (bf16[48,1024]{1,0:T(8,128)(2,1)S(1)}, bf16[48,1024]{1,0:T(8,128)(2,1)S(1)}, u32[]{:S(2)}, u32[]{:S(2)}) collective-permute-start(bf16[48,1024]{1,0:T(8,128)(2,1)S(1)} %get-tuple-element.16), channel_id=1, source_target_pairs={{0,2},{1,3},{2,0},{3,1},{4,6},{5,7},{6,4},{7,5},{8,10},{9,11},{10,... | collective-permute-start | bytes 294920 | tf_op jit(solution)/shard_map/ppermute | solution.py:229
  76.5 5.9 %collective-permute-start.14 = (bf16[48,1024]{1,0:T(8,128)(2,1)S(1)}, bf16[48,1024]{1,0:T(8,128)(2,1)S(1)}, u32[]{:S(2)}, u32[]{:S(2)}) collective-permute-start(bf16[48,1024]{1,0:T(8,128)(2,1)S(1)} %get-tuple-element.15), channel_id=1, source_target_pairs={{0,3},{1,0},{2,1},{3,2},{4,7},{5,4},{6,5},{7,6},{8,11},{9,8},{10,9... | collective-permute-start | bytes 294920 | tf_op jit(solution)/shard_map/ppermute | solution.py:229
  83.7 5.6 %collective-permute-start.16 = (bf16[48,1024]{1,0:T(8,128)(2,1)S(1)}, bf16[48,1024]{1,0:T(8,128)(2,1)S(1)}, u32[]{:S(2)}, u32[]{:S(2)}) collective-permute-start(bf16[48,1024]{1,0:T(8,128)(2,1)S(1)} %pad_maximum_fusion.9), channel_id=1, source_target_pairs={{0,2},{1,3},{2,0},{3,1},{4,6},{5,7},{6,4},{7,5},{8,10},{9,11},{10,... | collective-permute-start | bytes 294920 | tf_op jit(solution)/shard_map/ppermute | solution.py:188
  85.9 7.4 %collective-permute-start.15 = (bf16[48,1024]{1,0:T(8,128)(2,1)S(1)}, bf16[48,1024]{1,0:T(8,128)(2,1)S(1)}, u32[]{:S(2)}, u32[]{:S(2)}) collective-permute-start(bf16[48,1024]{1,0:T(8,128)(2,1)S(1)} %pad_maximum_fusion.9), channel_id=1, source_target_pairs={{0,1},{1,0},{2,3},{3,2},{4,5},{5,4},{6,7},{7,6},{8,9},{9,8},{10,11... | collective-permute-start | bytes 294920 | tf_op jit(solution)/shard_map/ppermute | solution.py:189
  89.3 7.0 %collective-permute-start.17 = (bf16[48,1024]{1,0:T(8,128)(2,1)S(1)}, bf16[48,1024]{1,0:T(8,128)(2,1)S(1)}, u32[]{:S(2)}, u32[]{:S(2)}) collective-permute-start(bf16[48,1024]{1,0:T(8,128)(2,1)S(1)} %collective-permute-done.16), channel_id=1, source_target_pairs={{0,1},{1,0},{2,3},{3,2},{4,5},{5,4},{6,7},{7,6},{8,9},{9,8},{10,11... | collective-permute-start | bytes 294920 | tf_op jit(solution)/shard_map/ppermute | solution.py:189
  100.9 1.8 %collective-permute-start.18 = (bf16[2,2,24,2048]{3,2,1,0:T(8,128)(2,1)S(1)}, bf16[2,2,24,2048]{3,2,1,0:T(8,128)(2,1)S(1)}, u32[]{:S(2)}, u32[]{:S(2)}) collective-permute-start(bf16[2,2,24,2048]{3,2,1,0:T(8,128)(2,1)S(1)} %pad_maximum_fusion.7), channel_id=1, source_target_pairs={{0,4},{4,0},{8,12},{12,8},{1,5},{5,1},{9,13},{13,9},{2,6},{6,2},{1... | collective-permute-start | bytes 1179656 | tf_op jit(solution)/shard_map/ppermute | solution.py:216
  102.8 11.5 %collective-permute-start.19 = (bf16[2,24,2048]{2,1,0:T(8,128)(2,1)S(1)}, bf16[2,24,2048]{2,1,0:T(8,128)(2,1)S(1)}, u32[]{:S(2)}, u32[]{:S(2)}) collective-permute-start(bf16[2,24,2048]{2,1,0:T(8,128)(2,1)S(1)} %fusion.7), channel_id=1, source_target_pairs={{0,8},{4,12},{8,0},{12,4},{1,9},{5,13},{9,1},{13,5},{2,10},{6,14},... | collective-permute-start | bytes 589832 | tf_op jit(solution)/shard_map/ppermute | solution.py:220

commit v10 on v7

--- a/solution.py
+++ b/solution.py
@@ -258,23 +258,66 @@
     gains_all = layer_params[:, : query_gain.shape[1]]
     gates_all = layer_params[:, query_gain.shape[1] :]
 
-    gathered = in_order(image_tokens, "section")
-    gathered = gathered.transpose(1, 0, 2, 3).reshape(
-        micro_count, -1, image_tokens.shape[2]
-    )
     shard_count = lax.axis_size("shard")
-    image_count = gathered.shape[1]
+    owned = image_tokens.shape[1]
+    image_count = owned * section_count
     total_rows = micro_count * image_count
-    flat_rows = gathered.reshape(total_rows, gathered.shape[2])
-    partial = jnp.dot(flat_rows, weights, preferred_element_type=jnp.float32)
-    raw_rows = scatter_blocks(
-        partial.reshape(shard_count, total_rows // shard_count, 2 * key_width), "shard", False
-    )
+    pair_width = 2 * key_width
+    phased = section_count == 4 and shard_count == 2 * micro_count
+    if phased:
+        images, _ = gather_blocks(image_tokens, "section")
+        raw_parts = []
+        for phase in range(2):
+            block = images[2 * phase : 2 * phase + 2].transpose(1, 0, 2, 3)
+            block = block.reshape(-1, image_tokens.shape[2])
+            partial = jnp.dot(block, weights, preferred_element_type=jnp.float32)
+            raw_parts.append(
+                scatter_blocks(partial.reshape(shard_count, owned, pair_width), "shard", False)
+            )
+        raw_rows = jnp.stack(raw_parts)
+        sections = jnp.arange(section_count, dtype=jnp.int32)
+        distance = lax.bitwise_xor(section_index, sections)
+        micro_ids = jnp.arange(micro_count, dtype=jnp.int32)
+        natural = (2 * micro_ids[:, None] + distance[None, :] % 2) * 2 + distance[None, :] // 2
+        owners = jnp.arange(shard_count, dtype=jnp.int32)[:, None]
+        phases = jnp.arange(2, dtype=jnp.int32)[None, :]
+        held = (owners // 2) * section_count + lax.bitwise_xor(
+            section_index, 2 * phases + owners % 2
+        )
+
+        def to_natural(rows):
+            blocks = in_order(rows.reshape(2, owned, pair_width), "shard")
+            return jnp.take(
+                blocks.reshape(2 * shard_count, owned, pair_width), natural.reshape(-1), axis=0
+            ).reshape(total_rows, pair_width)
+
+        def to_owned(rows):
+            return jnp.take(
+                rows.reshape(micro_count * section_count, owned, pair_width),
+                held.reshape(-1),
+                axis=0,
+            ).reshape(shard_count, 2 * owned, pair_width)
+
+    else:
+        gathered = in_order(image_tokens, "section")
+        gathered = gathered.transpose(1, 0, 2, 3).reshape(total_rows, image_tokens.shape[2])
+        partial = jnp.dot(gathered, weights, preferred_element_type=jnp.float32)
+        raw_rows = scatter_blocks(
+            partial.reshape(shard_count, total_rows // shard_count, pair_width), "shard", False
+        )
+
+        def to_natural(rows):
+            return in_order(rows, "shard").reshape(total_rows, pair_width)
+
+        def to_owned(rows):
+            return rows.reshape(shard_count, total_rows // shard_count, pair_width)
+
+    raw_rows = raw_rows.reshape(-1, pair_width)
     key_rows = head_normalize(raw_rows[:, :key_width], key_norm_gain[0], keyval_heads)
     keyval_rows = jnp.concatenate(
         [key_rows.astype(jnp.bfloat16), raw_rows[:, key_width:].astype(jnp.bfloat16)], axis=1
     )
-    keyval_own = in_order(keyval_rows, "shard").reshape(total_rows, 2 * key_width)
+    keyval_own = to_natural(keyval_rows)
     keyval_all, _ = gather_blocks(keyval_own, "section")
 
     same_document = text_document[:, :, None] == image_document[:, None, :]
@@ -288,18 +331,14 @@
         same_document,
         cotangent[0],
     )
-    grad_rows = scatter_blocks(
-        grad_local.reshape(shard_count, total_rows // shard_count, 2 * key_width),
-        "shard",
-        False,
-    )
+    grad_rows = scatter_blocks(to_owned(grad_local), "shard", False).reshape(-1, pair_width)
     key_portion = norm_gradient(
         raw_rows[:, :key_width], key_norm_gain[0], grad_rows[:, :key_width], keyval_heads
     )
     raw_grad_rows = jnp.concatenate([key_portion, grad_rows[:, key_width:]], axis=1).astype(
         jnp.bfloat16
     )
-    raw_grad = in_order(raw_grad_rows, "shard").reshape(total_rows, 2 * key_width)
+    raw_grad = to_natural(raw_grad_rows)
     owned = image_count // section_count
     raw_grad = (
         raw_grad.reshape(micro_count, section_count, owned, 2 * key_width)

time: 116 us -> 113 us (0.974)
  starting transfers between devices: 43.5 us -> 38.6 us
  local copies, waits for them, and re-layouts: 4.99 us -> 7.63 us
  waiting for transfers between devices: 44.2 us -> 43 us
    ppermute x6 -> x9, starting transfers between devices: 12.5 us -> 19.1 us  [scatter_blocks(): lax.ppermute(part, axis, [(i, (i + d) % count) for i in range(count)])]
    ppermute x5, starting transfers between devices: 8.65 us -> 3.47 us  [gather_blocks(): lax.ppermute(across, axis, partner)]
    ppermute x5, starting transfers between devices: 11.1 us -> 6.29 us  [gather_blocks(): across = lax.ppermute(block, axis, [(i, i ^ 2) for i in range(count)])]
    gather x0 -> x3, local copies, waits for them, and re-layouts: none -> 2.71 us  [the longest x1 1.57 us: to_owned(): jnp.take(rows.reshape(micro_count * section_count, owned, pair_width), he...]
    ppermute x5, starting transfers between devices: 4.91 us -> 3.43 us  [gather_blocks(): lax.ppermute(block, axis, partner)]
    ppermute x6 -> x9, waiting for transfers between devices: 16.1 us -> 14.8 us  [scatter_blocks(): lax.ppermute(part, axis, [(i, (i + d) % count) for i in range(count)])]
    another operation x6 -> x4, other arithmetic: 2.57 us -> 1.52 us  [gather_blocks(): return (jnp.stack(received), lax.bitwise_xor(index, positions))]
    dot_general x1 -> x2, matrix products: 3.2 us -> 3.81 us  [per_device(): partial = jnp.dot(block, weights, preferred_element_type=jnp.float32)]
  transfers between devices with their start and end apart: 23 -> 26, of which waited for: 15 -> 16; matrix products, arithmetic and copies ran while one was open for 3% -> 11% of each run, Pallas kernels for 0% -> 0%
where the time goes in v10:
time: 113 us
  waiting for transfers between devices  43 us (38%)
  starting transfers between devices  38.6 us (34%)
  Pallas kernels  8.22 us (7%)
  local copies, waits for them, and re-layouts  7.63 us (7%)
  matrix products  7.55 us (7%)
  other arithmetic  6.55 us (6%)
    ppermute x9, starting transfers between devices, scatter_blocks(): lax.ppermute(part, axis, [(i, (i + d) % count) for i in range(count)])  19.1 us
    ppermute x9, waiting for transfers between devices, scatter_blocks(): lax.ppermute(part, axis, [(i, (i + d) % count) for i in range(count)])  14.8 us
    ppermute x5, waiting for transfers between devices, gather_blocks(): across = lax.ppermute(block, axis, [(i, i ^ 2) for i in range(count)])  13.6 us
    pallas_call x1, Pallas kernels, attention_layers(): pl.pallas_call(functools.partial(attention_kernel, head_count=head_count,...  8.22 us
    ppermute x5, waiting for transfers between devices, gather_blocks(): lax.ppermute(across, axis, partner)  6.58 us
    ppermute x1, starting transfers between devices, scatter_blocks(): back = lax.ppermute(theirs, axis, [(i, i ^ 2) for i in range(count)])  6.31 us
    ppermute x5, starting transfers between devices, gather_blocks(): across = lax.ppermute(block, axis, [(i, i ^ 2) for i in range(count)])  6.29 us
    ppermute x1, waiting for transfers between devices, scatter_blocks(): back = lax.ppermute(theirs, axis, [(i, i ^ 2) for i in range(count)])  5.2 us
  transfers between devices with their start and end apart: 26, of which 16 were waited for; matrix products, arithmetic and copies ran while one was open for 11% of the time, Pallas kernels for 0%

profile of v10, /device:TPU:0, one launch (start us, length us, event | category | flops | bytes accessed | tf_op | source)
XLA Modules:
  0.0 112.7 jit_solution(9188654201691703419)
XLA Ops:
  1.1 2.6 %collective-permute-start.7 = (bf16[2,24,2048]{2,1,0:T(8,128)(2,1)}, bf16[2,24,2048]{2,1,0:T(8,128)(2,1)S(1)}, u32[]{:S(2)}, u32[]{:S(2)}) collective-permute-start(bf16[2,24,2048]{2,1,0:T(8,128)(2,1)} %param.13), channel_id=1, source_target_pairs={{0,8},{4,12},{8,0},{12,4},{1,9},{5,13},{9,1},{13,5},{2,10},{6,14},... | collective-permute-start | bytes 589832 | tf_op jit(solution)/shard_map/ppermute | solution.py:188
  7.7 2.0 %collective-permute-done.7 = bf16[2,24,2048]{2,1,0:T(8,128)(2,1)S(1)} collective-permute-done((bf16[2,24,2048]{2,1,0:T(8,128)(2,1)}, bf16[2,24,2048]{2,1,0:T(8,128)(2,1)S(1)}, u32[]{:S(2)}, u32[]{:S(2)}) %collective-permute-start.7) | collective-permute-done | bytes 196640 | tf_op jit(solution)/shard_map/ppermute | solution.py:188
  9.6 3.0 %fusion.2 = f32[4,24,1024]{2,1,0:T(8,128)S(1)} fusion(bf16[4,24,2048]{2,1,0:T(8,128)(2,1)S(1)} %bitcast.121, bf16[1,2048,1024]{2,1,0:T(8,128)(2,1)} %param.14), kind=kOutput, calls=%fused_computation.7 | convolution fusion | flops 402653184 | bytes 4980736 | tf_op jit(solution)/shard_map/dot_general | solution.py:273
  12.7 1.9 %collective-permute-start.4 = (f32[24,1024]{1,0:T(8,128)S(1)}, f32[24,1024]{1,0:T(8,128)S(1)}, u32[]{:S(2)}, u32[]{:S(2)}) collective-permute-start(f32[24,1024]{1,0:T(8,128)S(1)} %get-tuple-element.13), channel_id=1, source_target_pairs={{0,1},{1,2},{2,3},{3,0},{4,5},{5,6},{6,7},{7,4},{8,9},{9,10},{10,1... | collective-permute-start | bytes 294920 | tf_op jit(solution)/shard_map/ppermute | solution.py:229
  14.6 2.6 %collective-permute-start.5 = (f32[24,1024]{1,0:T(8,128)S(1)}, f32[24,1024]{1,0:T(8,128)S(1)}, u32[]{:S(2)}, u32[]{:S(2)}) collective-permute-start(f32[24,1024]{1,0:T(8,128)S(1)} %get-tuple-element.15), channel_id=1, source_target_pairs={{0,2},{1,3},{2,0},{3,1},{4,6},{5,7},{6,4},{7,5},{8,10},{9,11},{10,... | collective-permute-start | bytes 294920 | tf_op jit(solution)/shard_map/ppermute | solution.py:229
  17.2 1.4 %collective-permute-start.6 = (f32[24,1024]{1,0:T(8,128)S(1)}, f32[24,1024]{1,0:T(8,128)S(1)}, u32[]{:S(2)}, u32[]{:S(2)}) collective-permute-start(f32[24,1024]{1,0:T(8,128)S(1)} %get-tuple-element.14), channel_id=1, source_target_pairs={{0,3},{1,0},{2,1},{3,2},{4,7},{5,4},{6,5},{7,6},{8,11},{9,8},{10,9... | collective-permute-start | bytes 294920 | tf_op jit(solution)/shard_map/ppermute | solution.py:229
  20.3 6.1 %collective-permute-start.10 = (f32[24,1024]{1,0:T(8,128)S(1)}, f32[24,1024]{1,0:T(8,128)S(1)}, u32[]{:S(2)}, u32[]{:S(2)}) collective-permute-start(f32[24,1024]{1,0:T(8,128)S(1)} %get-tuple-element.18), channel_id=1, source_target_pairs={{0,2},{1,3},{2,0},{3,1},{4,6},{5,7},{6,4},{7,5},{8,10},{9,11},{10,... | collective-permute-start | bytes 294920 | tf_op jit(solution)/shard_map/ppermute | solution.py:229
  26.4 3.0 %collective-permute-start.11 = (f32[24,1024]{1,0:T(8,128)S(1)}, f32[24,1024]{1,0:T(8,128)S(1)}, u32[]{:S(2)}, u32[]{:S(2)}) collective-permute-start(f32[24,1024]{1,0:T(8,128)S(1)} %get-tuple-element.17), channel_id=1, source_target_pairs={{0,3},{1,0},{2,1},{3,2},{4,7},{5,4},{6,5},{7,6},{8,11},{9,8},{10,9... | collective-permute-start | bytes 294920 | tf_op jit(solution)/shard_map/ppermute | solution.py:229
  29.5 1.2 %collective-permute-done.10 = f32[24,1024]{1,0:T(8,128)S(1)} collective-permute-done((f32[24,1024]{1,0:T(8,128)S(1)}, f32[24,1024]{1,0:T(8,128)S(1)}, u32[]{:S(2)}, u32[]{:S(2)}) %collective-permute-start.10) | collective-permute-done | bytes 98336 | tf_op jit(solution)/shard_map/ppermute | solution.py:229
  30.7 1.4 %collective-permute-done.11 = f32[24,1024]{1,0:T(8,128)S(1)} collective-permute-done((f32[24,1024]{1,0:T(8,128)S(1)}, f32[24,1024]{1,0:T(8,128)S(1)}, u32[]{:S(2)}, u32[]{:S(2)}) %collective-permute-start.11) | collective-permute-done | bytes 98336 | tf_op jit(solution)/shard_map/ppermute | solution.py:229
  32.1 3.8 %collective-permute-done.9 = f32[24,1024]{1,0:T(8,128)S(1)} collective-permute-done((f32[24,1024]{1,0:T(8,128)S(1)}, f32[24,1024]{1,0:T(8,128)S(1)}, u32[]{:S(2)}, u32[]{:S(2)}) %collective-permute-start.9) | collective-permute-done | bytes 98336 | tf_op jit(solution)/shard_map/ppermute | solution.py:229
  37.5 4.7 %collective-permute-done.13 = bf16[2,24,1024]{2,1,0:T(8,128)(2,1)S(1)} collective-permute-done((bf16[2,24,1024]{2,1,0:T(8,128)(2,1)S(1)}, bf16[2,24,1024]{2,1,0:T(8,128)(2,1)S(1)}, u32[]{:S(2)}, u32[]{:S(2)}) %collective-permute-start.13) | collective-permute-done | bytes 98336 | tf_op jit(solution)/shard_map/ppermute | solution.py:188
  42.2 1.0 collective-permute-done.12
  43.2 3.6 %collective-permute-done.14 = bf16[2,24,1024]{2,1,0:T(8,128)(2,1)S(1)} collective-permute-done((bf16[2,24,1024]{2,1,0:T(8,128)(2,1)S(1)}, bf16[2,24,1024]{2,1,0:T(8,128)(2,1)S(1)}, u32[]{:S(2)}, u32[]{:S(2)}) %collective-permute-start.14) | collective-permute-done | bytes 98336 | tf_op jit(solution)/shard_map/ppermute | solution.py:189
  48.3 1.6 %collective-permute-start.16 = (bf16[192,1024]{1,0:T(8,128)(2,1)S(1)}, bf16[192,1024]{1,0:T(8,128)(2,1)S(1)}, u32[]{:S(2)}, u32[]{:S(2)}) collective-permute-start(bf16[192,1024]{1,0:T(8,128)(2,1)S(1)} %bitcast.123), channel_id=1, source_target_pairs={{0,8},{4,12},{8,0},{12,4},{1,9},{5,13},{9,1},{13,5},{2,10},{6,14},... | collective-permute-start | bytes 1179656 | tf_op jit(solution)/shard_map/ppermute | solution.py:188
  52.1 4.1 %collective-permute-done.16 = bf16[192,1024]{1,0:T(8,128)(2,1)S(1)} collective-permute-done((bf16[192,1024]{1,0:T(8,128)(2,1)S(1)}, bf16[192,1024]{1,0:T(8,128)(2,1)S(1)}, u32[]{:S(2)}, u32[]{:S(2)}) %collective-permute-start.16) | collective-permute-done | bytes 393248 | tf_op jit(solution)/shard_map/ppermute | solution.py:188
  57.9 1.4 %pad_maximum_fusion.keyval_ref = bf16[4,2,96,1024]{3,2,1,0:T(8,128)(2,1)} fusion(bf16[1,2,96,1024]{3,2,1,0:T(8,128)(2,1)S(1)} %bitcast.145, bf16[1,2,96,1024]{3,2,1,0:T(8,128)(2,1)S(1)} %bitcast.142, bf16[1,2,96,1024]{3,2,1,0:T(8,128)(2,1)S(1)} %bitcast.144, bf16[1,2,96,1024]{3,2,1,0:T(8,128)(2,1)S(1)} %bitcast.125), kind=kLoop, calls=%fused_computation.12 | loop fusion | flops 2359296 | bytes 3145728 | tf_op jit(solution)/shard_map/stack | solution.py:190
  59.3 8.2 %shard_map.104 = (f32[2,64,4096]{2,1,0:T(8,128)}, bf16[2,96,1024]{2,1,0:T(8,128)(2,1)}) custom-call(s32[1]{0:T(128)} %bitcast.section_ref, s32[4]{0:T(128)} %iota_xor_fusion.slots_ref, f32[4,32]{1,0:T(4,128)} %maximum_tanh_fusion.gates_ref, bf16[2,64,4096]{2,1,0:T(8,128)(2,1)} %queries_ref.1, bf16[4,2,96,1024]{3,2,1,0:T(8,128)(2,1)} %pad_maximum_fusion.keyval_ref, ...), custom_call_target="tpu_custom_call" | custom-call | flops 1409286144 | bytes 6815744 | tf_op jit(solution)/shard_map/pallas_call | solution.py:139
  67.5 1.6 %gather_fusion.2 = bf16[8,24,1024]{2,1,0:T(8,128)(2,1)S(1)} fusion(bf16[8,24,1024]{2,1,0:T(8,128)(2,1)} %bitcast.150, s32[1024]{0:T(1024)S(1)} %pad_clamp_fusion), kind=kCustom, calls=%fused_computation.3.clone | custom fusion | bytes 786464 | tf_op jit(solution)/shard_map/jit(_take)/gather | solution.py:295
  70.2 1.7 %collective-permute-start.19 = (bf16[48,1024]{1,0:T(8,128)(2,1)S(1)}, bf16[48,1024]{1,0:T(8,128)(2,1)S(1)}, u32[]{:S(2)}, u32[]{:S(2)}) collective-permute-start(bf16[48,1024]{1,0:T(8,128)(2,1)S(1)} %get-tuple-element.12), channel_id=1, source_target_pairs={{0,2},{1,3},{2,0},{3,1},{4,6},{5,7},{6,4},{7,5},{8,10},{9,11},{10,... | collective-permute-start | bytes 294920 | tf_op jit(solution)/shard_map/ppermute | solution.py:229
  71.8 1.5 %collective-permute-start.20 = (bf16[48,1024]{1,0:T(8,128)(2,1)S(1)}, bf16[48,1024]{1,0:T(8,128)(2,1)S(1)}, u32[]{:S(2)}, u32[]{:S(2)}) collective-permute-start(bf16[48,1024]{1,0:T(8,128)(2,1)S(1)} %get-tuple-element.11), channel_id=1, source_target_pairs={{0,3},{1,0},{2,1},{3,2},{4,7},{5,4},{6,5},{7,6},{8,11},{9,8},{10,9... | collective-permute-start | bytes 294920 | tf_op jit(solution)/shard_map/ppermute | solution.py:229
  73.3 2.5 %collective-permute-done.18 = bf16[48,1024]{1,0:T(8,128)(2,1)S(1)} collective-permute-done((bf16[48,1024]{1,0:T(8,128)(2,1)S(1)}, bf16[48,1024]{1,0:T(8,128)(2,1)S(1)}, u32[]{:S(2)}, u32[]{:S(2)}) %collective-permute-start.18) | collective-permute-done | bytes 98336 | tf_op jit(solution)/shard_map/ppermute | solution.py:229
  75.8 5.1 %collective-permute-done.19 = bf16[48,1024]{1,0:T(8,128)(2,1)S(1)} collective-permute-done((bf16[48,1024]{1,0:T(8,128)(2,1)S(1)}, bf16[48,1024]{1,0:T(8,128)(2,1)S(1)}, u32[]{:S(2)}, u32[]{:S(2)}) %collective-permute-start.19) | collective-permute-done | bytes 98336 | tf_op jit(solution)/shard_map/ppermute | solution.py:229
  81.3 1.7 %collective-permute-start.22 = (bf16[2,24,1024]{2,1,0:T(8,128)(2,1)S(1)}, bf16[2,24,1024]{2,1,0:T(8,128)(2,1)S(1)}, u32[]{:S(2)}, u32[]{:S(2)}) collective-permute-start(bf16[2,24,1024]{2,1,0:T(8,128)(2,1)S(1)} %pad_maximum_fusion.6), channel_id=1, source_target_pairs={{0,2},{1,3},{2,0},{3,1},{4,6},{5,7},{6,4},{7,5},{8,10},{9,11},{10,... | collective-permute-start | bytes 294920 | tf_op jit(solution)/shard_map/ppermute | solution.py:188
  83.1 1.3 %collective-permute-start.21 = (bf16[2,24,1024]{2,1,0:T(8,128)(2,1)S(1)}, bf16[2,24,1024]{2,1,0:T(8,128)(2,1)S(1)}, u32[]{:S(2)}, u32[]{:S(2)}) collective-permute-start(bf16[2,24,1024]{2,1,0:T(8,128)(2,1)S(1)} %pad_maximum_fusion.6), channel_id=1, source_target_pairs={{0,1},{1,0},{2,3},{3,2},{4,5},{5,4},{6,7},{7,6},{8,9},{9,8},{10,11... | collective-permute-start | bytes 294920 | tf_op jit(solution)/shard_map/ppermute | solution.py:189
  84.3 2.9 %collective-permute-done.22 = bf16[2,24,1024]{2,1,0:T(8,128)(2,1)S(1)} collective-permute-done((bf16[2,24,1024]{2,1,0:T(8,128)(2,1)S(1)}, bf16[2,24,1024]{2,1,0:T(8,128)(2,1)S(1)}, u32[]{:S(2)}, u32[]{:S(2)}) %collective-permute-start.22) | collective-permute-done | bytes 98336 | tf_op jit(solution)/shard_map/ppermute | solution.py:188
  87.2 3.4 %collective-permute-start.23 = (bf16[2,24,1024]{2,1,0:T(8,128)(2,1)S(1)}, bf16[2,24,1024]{2,1,0:T(8,128)(2,1)S(1)}, u32[]{:S(2)}, u32[]{:S(2)}) collective-permute-start(bf16[2,24,1024]{2,1,0:T(8,128)(2,1)S(1)} %collective-permute-done.22), channel_id=1, source_target_pairs={{0,1},{1,0},{2,3},{3,2},{4,5},{5,4},{6,7},{7,6},{8,9},{9,8},{10,11... | collective-permute-start | bytes 294920 | tf_op jit(solution)/shard_map/ppermute | solution.py:189
  90.6 2.6 %collective-permute-done.23 = bf16[2,24,1024]{2,1,0:T(8,128)(2,1)S(1)} collective-permute-done((bf16[2,24,1024]{2,1,0:T(8,128)(2,1)S(1)}, bf16[2,24,1024]{2,1,0:T(8,128)(2,1)S(1)}, u32[]{:S(2)}, u32[]{:S(2)}) %collective-permute-start.23) | collective-permute-done | bytes 98336 | tf_op jit(solution)/shard_map/ppermute | solution.py:189
  94.7 3.7 %fusion.6 = bf16[192,2048]{1,0:T(8,128)(2,1)S(1)} fusion(bf16[192,1024]{1,0:T(8,128)(2,1)S(1)} %bitcast.131, bf16[1,2048,1024]{2,1,0:T(8,128)(2,1)} %param.14), kind=kOutput, calls=%fused_computation.11 | convolution fusion | flops 805699584 | bytes 5373952 | tf_op jit(solution)/shard_map/dot_general | solution.py:348
  98.6 1.7 %collective-permute-done.24 = bf16[2,2,24,2048]{3,2,1,0:T(8,128)(2,1)S(1)} collective-permute-done((bf16[2,2,24,2048]{3,2,1,0:T(8,128)(2,1)S(1)}, bf16[2,2,24,2048]{3,2,1,0:T(8,128)(2,1)S(1)}, u32[]{:S(2)}, u32[]{:S(2)}) %collective-permute-start.24) | collective-permute-done | bytes 393248 | tf_op jit(solution)/shard_map/ppermute | solution.py:216
  100.3 6.3 %collective-permute-start.25 = (bf16[2,24,2048]{2,1,0:T(8,128)(2,1)S(1)}, bf16[2,24,2048]{2,1,0:T(8,128)(2,1)S(1)}, u32[]{:S(2)}, u32[]{:S(2)}) collective-permute-start(bf16[2,24,2048]{2,1,0:T(8,128)(2,1)S(1)} %fusion.9), channel_id=1, source_target_pairs={{0,8},{4,12},{8,0},{12,4},{1,9},{5,13},{9,1},{13,5},{2,10},{6,14},... | collective-permute-start | bytes 589832 | tf_op jit(solution)/shard_map/ppermute | solution.py:220
  106.7 5.2 %collective-permute-done.25 = bf16[2,24,2048]{2,1,0:T(8,128)(2,1)S(1)} collective-permute-done((bf16[2,24,2048]{2,1,0:T(8,128)(2,1)S(1)}, bf16[2,24,2048]{2,1,0:T(8,128)(2,1)S(1)}, u32[]{:S(2)}, u32[]{:S(2)}) %collective-permute-start.25) | collective-permute-done | bytes 196640 | tf_op jit(solution)/shard_map/ppermute | solution.py:220
  (104 shorter events, 17.1 us)
Async XLA Ops:
  0.6 6.0 %collective-permute-start.3 = (bf16[2,24,2048]{2,1,0:T(8,128)(2,1)}, bf16[2,24,2048]{2,1,0:T(8,128)(2,1)S(1)}, u32[]{:S(2)}, u32[]{:S(2)}) collective-permute-start(bf16[2,24,2048]{2,1,0:T(8,128)(2,1)} %param.13), channel_id=1, source_target_pairs={{0,4},{4,0},{8,12},{12,8},{1,5},{5,1},{9,13},{13,9},{2,6},{6,2},{1... | collective-permute-start | bytes 589832 | tf_op jit(solution)/shard_map/ppermute | solution.py:189
  1.1 8.5 %collective-permute-start.7 = (bf16[2,24,2048]{2,1,0:T(8,128)(2,1)}, bf16[2,24,2048]{2,1,0:T(8,128)(2,1)S(1)}, u32[]{:S(2)}, u32[]{:S(2)}) collective-permute-start(bf16[2,24,2048]{2,1,0:T(8,128)(2,1)} %param.13), channel_id=1, source_target_pairs={{0,8},{4,12},{8,0},{12,4},{1,9},{5,13},{9,1},{13,5},{2,10},{6,14},... | collective-permute-start | bytes 589832 | tf_op jit(solution)/shard_map/ppermute | solution.py:188
  5.1 44.7 %collective-permute-start.1 = (f32[4128]{0:T(1024)S(1)}, f32[4128]{0:T(1024)S(1)}, u32[]{:S(2)}, u32[]{:S(2)}) collective-permute-start(f32[4128]{0:T(1024)S(1)} %reduce), channel_id=1, source_target_pairs={{0,8},{4,12},{8,0},{12,4},{1,9},{5,13},{9,1},{13,5},{2,10},{6,14},... | collective-permute-start | bytes 49544 | tf_op jit(solution)/shard_map/ppermute | solution.py:188
  5.2 46.2 %collective-permute-start = (f32[4128]{0:T(1024)S(1)}, f32[4128]{0:T(1024)S(1)}, u32[]{:S(2)}, u32[]{:S(2)}) collective-permute-start(f32[4128]{0:T(1024)S(1)} %reduce), channel_id=1, source_target_pairs={{0,4},{4,0},{8,12},{12,8},{1,5},{5,1},{9,13},{13,9},{2,6},{6,2},{1... | collective-permute-start | bytes 49544 | tf_op jit(solution)/shard_map/ppermute | solution.py:189
  7.6 11.0 %copy-start = (bf16[1,2048,1024]{2,1,0:T(8,128)(2,1)S(1)}, bf16[1,2048,1024]{2,1,0:T(8,128)(2,1)}, u32[]{:S(2)}) copy-start(bf16[1,2048,1024]{2,1,0:T(8,128)(2,1)} %param.14) | copy-start | bytes 12582916
  9.6 7.5 %collective-permute-start.8 = (bf16[2,24,2048]{2,1,0:T(8,128)(2,1)S(1)}, bf16[2,24,2048]{2,1,0:T(8,128)(2,1)S(1)}, u32[]{:S(2)}, u32[]{:S(2)}) collective-permute-start(bf16[2,24,2048]{2,1,0:T(8,128)(2,1)S(1)} %collective-permute-done.7), channel_id=1, source_target_pairs={{0,4},{4,0},{8,12},{12,8},{1,5},{5,1},{9,13},{13,9},{2,6},{6,2},{1... | collective-permute-start | bytes 589832 | tf_op jit(solution)/shard_map/ppermute | solution.py:189
  12.7 7.7 %collective-permute-start.4 = (f32[24,1024]{1,0:T(8,128)S(1)}, f32[24,1024]{1,0:T(8,128)S(1)}, u32[]{:S(2)}, u32[]{:S(2)}) collective-permute-start(f32[24,1024]{1,0:T(8,128)S(1)} %get-tuple-element.13), channel_id=1, source_target_pairs={{0,1},{1,2},{2,3},{3,0},{4,5},{5,6},{6,7},{7,4},{8,9},{9,10},{10,1... | collective-permute-start | bytes 294920 | tf_op jit(solution)/shard_map/ppermute | solution.py:229
  14.6 11.9 %collective-permute-start.5 = (f32[24,1024]{1,0:T(8,128)S(1)}, f32[24,1024]{1,0:T(8,128)S(1)}, u32[]{:S(2)}, u32[]{:S(2)}) collective-permute-start(f32[24,1024]{1,0:T(8,128)S(1)} %get-tuple-element.15), channel_id=1, source_target_pairs={{0,2},{1,3},{2,0},{3,1},{4,6},{5,7},{6,4},{7,5},{8,10},{9,11},{10,... | collective-permute-start | bytes 294920 | tf_op jit(solution)/shard_map/ppermute | solution.py:229
  17.2 12.3 %collective-permute-start.6 = (f32[24,1024]{1,0:T(8,128)S(1)}, f32[24,1024]{1,0:T(8,128)S(1)}, u32[]{:S(2)}, u32[]{:S(2)}) collective-permute-start(f32[24,1024]{1,0:T(8,128)S(1)} %get-tuple-element.14), channel_id=1, source_target_pairs={{0,3},{1,0},{2,1},{3,2},{4,7},{5,4},{6,5},{7,6},{8,11},{9,8},{10,9... | collective-permute-start | bytes 294920 | tf_op jit(solution)/shard_map/ppermute | solution.py:229
  18.6 17.7 %copy-start.2 = (f32[1,512]{1,0:T(1,128)S(1)}, f32[1,512]{1,0:T(1,128)}, u32[]{:S(2)}) copy-start(f32[1,512]{1,0:T(1,128)} %param.16) | copy-start | bytes 6148
  20.3 10.3 %collective-permute-start.10 = (f32[24,1024]{1,0:T(8,128)S(1)}, f32[24,1024]{1,0:T(8,128)S(1)}, u32[]{:S(2)}, u32[]{:S(2)}) collective-permute-start(f32[24,1024]{1,0:T(8,128)S(1)} %get-tuple-element.18), channel_id=1, source_target_pairs={{0,2},{1,3},{2,0},{3,1},{4,6},{5,7},{6,4},{7,5},{8,10},{9,11},{10,... | collective-permute-start | bytes 294920 | tf_op jit(solution)/shard_map/ppermute | solution.py:229
  26.4 5.6 %collective-permute-start.11 = (f32[24,1024]{1,0:T(8,128)S(1)}, f32[24,1024]{1,0:T(8,128)S(1)}, u32[]{:S(2)}, u32[]{:S(2)}) collective-permute-start(f32[24,1024]{1,0:T(8,128)S(1)} %get-tuple-element.17), channel_id=1, source_target_pairs={{0,3},{1,0},{2,1},{3,2},{4,7},{5,4},{6,5},{7,6},{8,11},{9,8},{10,9... | collective-permute-start | bytes 294920 | tf_op jit(solution)/shard_map/ppermute | solution.py:229
  29.5 6.4 %collective-permute-start.9 = (f32[24,1024]{1,0:T(8,128)S(1)}, f32[24,1024]{1,0:T(8,128)S(1)}, u32[]{:S(2)}, u32[]{:S(2)}) collective-permute-start(f32[24,1024]{1,0:T(8,128)S(1)} %get-tuple-element.16), channel_id=1, source_target_pairs={{0,1},{1,2},{2,3},{3,0},{4,5},{5,6},{6,7},{7,4},{8,9},{9,10},{10,1... | collective-permute-start | bytes 294920 | tf_op jit(solution)/shard_map/ppermute | solution.py:229
  36.3 5.9 %collective-permute-start.13 = (bf16[2,24,1024]{2,1,0:T(8,128)(2,1)S(1)}, bf16[2,24,1024]{2,1,0:T(8,128)(2,1)S(1)}, u32[]{:S(2)}, u32[]{:S(2)}) collective-permute-start(bf16[2,24,1024]{2,1,0:T(8,128)(2,1)S(1)} %bitcast.146), channel_id=1, source_target_pairs={{0,2},{1,3},{2,0},{3,1},{4,6},{5,7},{6,4},{7,5},{8,10},{9,11},{10,... | collective-permute-start | bytes 294920 | tf_op jit(solution)/shard_map/ppermute | solution.py:188
  36.7 6.6 %collective-permute-start.12 = (bf16[2,24,1024]{2,1,0:T(8,128)(2,1)S(1)}, bf16[2,24,1024]{2,1,0:T(8,128)(2,1)S(1)}, u32[]{:S(2)}, u32[]{:S(2)}) collective-permute-start(bf16[2,24,1024]{2,1,0:T(8,128)(2,1)S(1)} %bitcast.147), channel_id=1, source_target_pairs={{0,1},{1,0},{2,3},{3,2},{4,5},{5,4},{6,7},{7,6},{8,9},{9,8},{10,11... | collective-permute-start | bytes 294920 | tf_op jit(solution)/shard_map/ppermute | solution.py:189
  42.2 4.6 %collective-permute-start.14 = (bf16[2,24,1024]{2,1,0:T(8,128)(2,1)S(1)}, bf16[2,24,1024]{2,1,0:T(8,128)(2,1)S(1)}, u32[]{:S(2)}, u32[]{:S(2)}) collective-permute-start(bf16[2,24,1024]{2,1,0:T(8,128)(2,1)S(1)} %collective-permute-done.13), channel_id=1, source_target_pairs={{0,1},{1,0},{2,3},{3,2},{4,5},{5,4},{6,7},{7,6},{8,9},{9,8},{10,11... | collective-permute-start | bytes 294920 | tf_op jit(solution)/shard_map/ppermute | solution.py:189
  48.3 7.9 %collective-permute-start.16 = (bf16[192,1024]{1,0:T(8,128)(2,1)S(1)}, bf16[192,1024]{1,0:T(8,128)(2,1)S(1)}, u32[]{:S(2)}, u32[]{:S(2)}) collective-permute-start(bf16[192,1024]{1,0:T(8,128)(2,1)S(1)} %bitcast.123), channel_id=1, source_target_pairs={{0,8},{4,12},{8,0},{12,4},{1,9},{5,13},{9,1},{13,5},{2,10},{6,14},... | collective-permute-start | bytes 1179656 | tf_op jit(solution)/shard_map/ppermute | solution.py:188
  49.9 1.6 %collective-permute-start.2 = (f32[4128]{0:T(1024)S(1)}, f32[4128]{0:T(1024)S(1)}, u32[]{:S(2)}, u32[]{:S(2)}) collective-permute-start(f32[4128]{0:T(1024)S(1)} %collective-permute-done.1), channel_id=1, source_target_pairs={{0,4},{4,0},{8,12},{12,8},{1,5},{5,1},{9,13},{13,9},{2,6},{6,2},{1... | collective-permute-start | bytes 49544 | tf_op jit(solution)/shard_map/ppermute | solution.py:189
  50.5 8.8 %copy-start.1 = (f32[2,8,64,96]{3,2,1,0:T(8,128)}, f32[2,8,64,96]{3,2,1,0:T(8,128)S(1)}, u32[]{:S(2)}) copy-start(f32[2,8,64,96]{3,2,1,0:T(8,128)S(1)} %tile.4) | copy-start | bytes 1179652
  51.5 6.0 %collective-permute-start.15 = (bf16[192,1024]{1,0:T(8,128)(2,1)S(1)}, bf16[192,1024]{1,0:T(8,128)(2,1)S(1)}, u32[]{:S(2)}, u32[]{:S(2)}) collective-permute-start(bf16[192,1024]{1,0:T(8,128)(2,1)S(1)} %bitcast.124), channel_id=1, source_target_pairs={{0,4},{4,0},{8,12},{12,8},{1,5},{5,1},{9,13},{13,9},{2,6},{6,2},{1... | collective-permute-start | bytes 1179656 | tf_op jit(solution)/shard_map/ppermute | solution.py:189
  56.2 1.7 %collective-permute-start.17 = (bf16[192,1024]{1,0:T(8,128)(2,1)S(1)}, bf16[192,1024]{1,0:T(8,128)(2,1)S(1)}, u32[]{:S(2)}, u32[]{:S(2)}) collective-permute-start(bf16[192,1024]{1,0:T(8,128)(2,1)S(1)} %collective-permute-done.16), channel_id=1, source_target_pairs={{0,4},{4,0},{8,12},{12,8},{1,5},{5,1},{9,13},{13,9},{2,6},{6,2},{1... | collective-permute-start | bytes 1179656 | tf_op jit(solution)/shard_map/ppermute | solution.py:189
  69.2 6.6 %collective-permute-start.18 = (bf16[48,1024]{1,0:T(8,128)(2,1)S(1)}, bf16[48,1024]{1,0:T(8,128)(2,1)S(1)}, u32[]{:S(2)}, u32[]{:S(2)}) collective-permute-start(bf16[48,1024]{1,0:T(8,128)(2,1)S(1)} %get-tuple-element.10), channel_id=1, source_target_pairs={{0,1},{1,2},{2,3},{3,0},{4,5},{5,6},{6,7},{7,4},{8,9},{9,10},{10,1... | collective-permute-start | bytes 294920 | tf_op jit(solution)/shard_map/ppermute | solution.py:229
  70.2 10.7 %collective-permute-start.19 = (bf16[48,1024]{1,0:T(8,128)(2,1)S(1)}, bf16[48,1024]{1,0:T(8,128)(2,1)S(1)}, u32[]{:S(2)}, u32[]{:S(2)}) collective-permute-start(bf16[48,1024]{1,0:T(8,128)(2,1)S(1)} %get-tuple-element.12), channel_id=1, source_target_pairs={{0,2},{1,3},{2,0},{3,1},{4,6},{5,7},{6,4},{7,5},{8,10},{9,11},{10,... | collective-permute-start | bytes 294920 | tf_op jit(solution)/shard_map/ppermute | solution.py:229
  71.8 9.0 %collective-permute-start.20 = (bf16[48,1024]{1,0:T(8,128)(2,1)S(1)}, bf16[48,1024]{1,0:T(8,128)(2,1)S(1)}, u32[]{:S(2)}, u32[]{:S(2)}) collective-permute-start(bf16[48,1024]{1,0:T(8,128)(2,1)S(1)} %get-tuple-element.11), channel_id=1, source_target_pairs={{0,3},{1,0},{2,1},{3,2},{4,7},{5,4},{6,5},{7,6},{8,11},{9,8},{10,9... | collective-permute-start | bytes 294920 | tf_op jit(solution)/shard_map/ppermute | solution.py:229
  81.3 5.9 %collective-permute-start.22 = (bf16[2,24,1024]{2,1,0:T(8,128)(2,1)S(1)}, bf16[2,24,1024]{2,1,0:T(8,128)(2,1)S(1)}, u32[]{:S(2)}, u32[]{:S(2)}) collective-permute-start(bf16[2,24,1024]{2,1,0:T(8,128)(2,1)S(1)} %pad_maximum_fusion.6), channel_id=1, source_target_pairs={{0,2},{1,3},{2,0},{3,1},{4,6},{5,7},{6,4},{7,5},{8,10},{9,11},{10,... | collective-permute-start | bytes 294920 | tf_op jit(solution)/shard_map/ppermute | solution.py:188
  83.1 7.6 %collective-permute-start.21 = (bf16[2,24,1024]{2,1,0:T(8,128)(2,1)S(1)}, bf16[2,24,1024]{2,1,0:T(8,128)(2,1)S(1)}, u32[]{:S(2)}, u32[]{:S(2)}) collective-permute-start(bf16[2,24,1024]{2,1,0:T(8,128)(2,1)S(1)} %pad_maximum_fusion.6), channel_id=1, source_target_pairs={{0,1},{1,0},{2,3},{3,2},{4,5},{5,4},{6,7},{7,6},{8,9},{9,8},{10,11... | collective-permute-start | bytes 294920 | tf_op jit(solution)/shard_map/ppermute | solution.py:189
  87.2 6.0 %collective-permute-start.23 = (bf16[2,24,1024]{2,1,0:T(8,128)(2,1)S(1)}, bf16[2,24,1024]{2,1,0:T(8,128)(2,1)S(1)}, u32[]{:S(2)}, u32[]{:S(2)}) collective-permute-start(bf16[2,24,1024]{2,1,0:T(8,128)(2,1)S(1)} %collective-permute-done.22), channel_id=1, source_target_pairs={{0,1},{1,0},{2,3},{3,2},{4,5},{5,4},{6,7},{7,6},{8,9},{9,8},{10,11... | collective-permute-start | bytes 294920 | tf_op jit(solution)/shard_map/ppermute | solution.py:189
  98.5 1.8 %collective-permute-start.24 = (bf16[2,2,24,2048]{3,2,1,0:T(8,128)(2,1)S(1)}, bf16[2,2,24,2048]{3,2,1,0:T(8,128)(2,1)S(1)}, u32[]{:S(2)}, u32[]{:S(2)}) collective-permute-start(bf16[2,2,24,2048]{3,2,1,0:T(8,128)(2,1)S(1)} %pad_maximum_fusion.3), channel_id=1, source_target_pairs={{0,4},{4,0},{8,12},{12,8},{1,5},{5,1},{9,13},{13,9},{2,6},{6,2},{1... | collective-permute-start | bytes 1179656 | tf_op jit(solution)/shard_map/ppermute | solution.py:216
  100.3 11.5 %collective-permute-start.25 = (bf16[2,24,2048]{2,1,0:T(8,128)(2,1)S(1)}, bf16[2,24,2048]{2,1,0:T(8,128)(2,1)S(1)}, u32[]{:S(2)}, u32[]{:S(2)}) collective-permute-start(bf16[2,24,2048]{2,1,0:T(8,128)(2,1)S(1)} %fusion.9), channel_id=1, source_target_pairs={{0,8},{4,12},{8,0},{12,4},{1,9},{5,13},{9,1},{13,5},{2,10},{6,14},... | collective-permute-start | bytes 589832 | tf_op jit(solution)/shard_map/ppermute | solution.py:220

commit v11 on v10

--- a/solution.py
+++ b/solution.py
@@ -195,6 +195,13 @@
     return jnp.stack(received), (index - positions) % count
 
 
+def gather_parts(block, axis):
+    count = lax.axis_size(axis)
+    partner = [(i, i ^ 1) for i in range(count)]
+    across = lax.ppermute(block, axis, [(i, i ^ 2) for i in range(count)])
+    return [block, lax.ppermute(block, axis, partner), across, lax.ppermute(across, axis, partner)]
+
+
 def in_order(block, axis):
     stacked, slots = gather_blocks(block, axis)
     return jnp.take(stacked, slots, axis=0)
@@ -266,6 +273,11 @@
     phased = section_count == 4 and shard_count == 2 * micro_count
     if phased:
         images, _ = gather_blocks(image_tokens, "section")
+        images, gains_all, gates_all, layer_slots = lax.optimization_barrier(
+            (images, gains_all.reshape(section_count, 1, -1), jnp.tanh(gates_all), layer_slots)
+        )
+        gains_all = gains_all.reshape(section_count, -1)
+        gate_factors = gates_all
         raw_parts = []
         for phase in range(2):
             block = images[2 * phase : 2 * phase + 2].transpose(1, 0, 2, 3)
@@ -299,6 +311,7 @@
             ).reshape(shard_count, 2 * owned, pair_width)
 
     else:
+        gate_factors = jnp.tanh(gates_all)
         gathered = in_order(image_tokens, "section")
         gathered = gathered.transpose(1, 0, 2, 3).reshape(total_rows, image_tokens.shape[2])
         partial = jnp.dot(gathered, weights, preferred_element_type=jnp.float32)
@@ -324,7 +337,7 @@
     leaving, grad_local = attention_layers(
         section_index,
         layer_slots,
-        jnp.tanh(gates_all),
+        gate_factors,
         text_queries,
         keyval_all.reshape(section_count, micro_count, image_count, 2 * key_width),
         gains_all,
@@ -338,19 +351,37 @@
     raw_grad_rows = jnp.concatenate([key_portion, grad_rows[:, key_width:]], axis=1).astype(
         jnp.bfloat16
     )
-    raw_grad = to_natural(raw_grad_rows)
     owned = image_count // section_count
-    raw_grad = (
-        raw_grad.reshape(micro_count, section_count, owned, 2 * key_width)
-        .transpose(1, 0, 2, 3)
-        .reshape(total_rows, 2 * key_width)
-    )
-    image_part = lax.dot_general(
-        raw_grad, weights, (((1,), (1,)), ((), ())), preferred_element_type=jnp.float32
-    )
-    image_part = image_part.astype(jnp.bfloat16).reshape(
-        section_count, micro_count, owned, weights.shape[0]
-    )
+    if phased:
+        shard_index = lax.axis_index("shard")
+        products = []
+        for part in gather_parts(raw_grad_rows.reshape(2, owned, pair_width), "shard"):
+            product = lax.dot_general(
+                part.reshape(2 * owned, pair_width),
+                weights,
+                (((1,), (1,)), ((), ())),
+                preferred_element_type=jnp.float32,
+            )
+            products.append(product.astype(jnp.bfloat16).reshape(2, owned, weights.shape[0]))
+        step = lax.bitwise_xor(section_index, sections)[:, None]
+        source = 2 * micro_ids[None, :] + step % 2
+        where = lax.bitwise_xor(shard_index, source) * 2 + step // 2
+        image_part = jnp.take(
+            jnp.stack(products).reshape(-1, owned, weights.shape[0]), where.reshape(-1), axis=0
+        ).reshape(section_count, micro_count, owned, weights.shape[0])
+    else:
+        raw_grad = to_natural(raw_grad_rows)
+        raw_grad = (
+            raw_grad.reshape(micro_count, section_count, owned, 2 * key_width)
+            .transpose(1, 0, 2, 3)
+            .reshape(total_rows, 2 * key_width)
+        )
+        image_part = lax.dot_general(
+            raw_grad, weights, (((1,), (1,)), ((), ())), preferred_element_type=jnp.float32
+        )
+        image_part = image_part.astype(jnp.bfloat16).reshape(
+            section_count, micro_count, owned, weights.shape[0]
+        )
     image_grad = scatter_blocks(image_part, "section", True)
     return (leaving[None], image_grad)
 

time: 113 us -> 118 us (1.044)
  waiting for transfers between devices: 43 us -> 50.5 us
  starting transfers between devices: 38.6 us -> 34 us
  matrix products: 7.55 us -> 9.32 us
    ppermute x0 -> x3, waiting for transfers between devices: none -> 8.45 us  [the longest x1 5.12 us: gather_parts(): across = lax.ppermute(block, axis, [(i, i ^ 2) for i in range(count)])]
    ppermute x9, starting transfers between devices: 19.1 us -> 13.7 us  [scatter_blocks(): lax.ppermute(part, axis, [(i, (i + d) % count) for i in range(count)])]
    dot_general x1 -> x4, matrix products: 3.74 us -> 7.69 us  [per_device(): lax.dot_general(part.reshape(2 * owned, pair_width), weights, (((1,), (1,...]
    ppermute x0 -> x3, starting transfers between devices: none -> 3.77 us  [the longest x1 2.73 us: gather_parts(): lax.ppermute(block, axis, partner)]
    ppermute x5 -> x4, starting transfers between devices: 3.43 us -> 0.82 us  [gather_blocks(): lax.ppermute(block, axis, partner)]
    dot_general x2, matrix products: 3.81 us -> 1.64 us  [per_device(): partial = jnp.dot(block, weights, preferred_element_type=jnp.float32)]
    ppermute x9, waiting for transfers between devices: 14.8 us -> 16.8 us  [scatter_blocks(): lax.ppermute(part, axis, [(i, (i + d) % count) for i in range(count)])]
    ppermute x5 -> x4, waiting for transfers between devices: 6.58 us -> 5.01 us  [gather_blocks(): lax.ppermute(across, axis, partner)]
  transfers between devices with their start and end apart: 26 -> 26, of which waited for: 16 -> 15; matrix products, arithmetic and copies ran while one was open for 11% -> 10% of each run, Pallas kernels for 0% -> 0%
where the time goes in v11:
time: 118 us; the launch traced here: 117 us
  waiting for transfers between devices  50.5 us (43%)
  starting transfers between devices  34 us (29%)
  matrix products  9.32 us (8%)
  Pallas kernels  8.22 us (7%)
  local copies, waits for them, and re-layouts  7.37 us (6%)
  other arithmetic  6.78 us (6%)
    ppermute x9, waiting for transfers between devices, scatter_blocks(): lax.ppermute(part, axis, [(i, (i + d) % count) for i in range(count)])  16.8 us
    ppermute x9, starting transfers between devices, scatter_blocks(): lax.ppermute(part, axis, [(i, (i + d) % count) for i in range(count)])  13.7 us
    ppermute x4, waiting for transfers between devices, gather_blocks(): across = lax.ppermute(block, axis, [(i, i ^ 2) for i in range(count)])  13.4 us
    pallas_call x1, Pallas kernels, attention_layers(): pl.pallas_call(functools.partial(attention_kernel, head_count=head_count,...  8.22 us
    dot_general x4, matrix products, per_device(): lax.dot_general(part.reshape(2 * owned, pair_width), weights, (((1,), (1,...  7.69 us
    ppermute x4, starting transfers between devices, gather_blocks(): across = lax.ppermute(block, axis, [(i, i ^ 2) for i in range(count)])  6.55 us
    ppermute x1, starting transfers between devices, scatter_blocks(): back = lax.ppermute(theirs, axis, [(i, i ^ 2) for i in range(count)])  5.36 us
    ppermute x1, waiting for transfers between devices, scatter_blocks(): back = lax.ppermute(theirs, axis, [(i, i ^ 2) for i in range(count)])  5.2 us
  transfers between devices with their start and end apart: 26, of which 15 were waited for; matrix products, arithmetic and copies ran while one was open for 10% of the time, Pallas kernels for 0%

profile of v11, /device:TPU:0, one launch (start us, length us, event | category | flops | bytes accessed | tf_op | source)
XLA Modules:
  0.0 117.3 jit_solution(3825595510481869522)
XLA Ops:
  2.1 3.0 %collective-permute-start.4 = (f32[4128]{0:T(1024)S(1)}, f32[4128]{0:T(1024)S(1)}, u32[]{:S(2)}, u32[]{:S(2)}) collective-permute-start(f32[4128]{0:T(1024)S(1)} %reduce), channel_id=1, source_target_pairs={{0,8},{4,12},{8,0},{12,4},{1,9},{5,13},{9,1},{13,5},{2,10},{6,14},... | collective-permute-start | bytes 49544 | tf_op jit(solution)/shard_map/ppermute | solution.py:188
  8.5 4.1 %collective-permute-done.1 = bf16[2,24,2048]{2,1,0:T(8,128)(2,1)S(1)} collective-permute-done((bf16[2,24,2048]{2,1,0:T(8,128)(2,1)}, bf16[2,24,2048]{2,1,0:T(8,128)(2,1)S(1)}, u32[]{:S(2)}, u32[]{:S(2)}) %collective-permute-start.1) | collective-permute-done | bytes 196640 | tf_op jit(solution)/shard_map/ppermute | solution.py:188
  16.0 1.6 %collective-permute-start.6 = (f32[24,1024]{1,0:T(8,128)S(1)}, f32[24,1024]{1,0:T(8,128)S(1)}, u32[]{:S(2)}, u32[]{:S(2)}) collective-permute-start(f32[24,1024]{1,0:T(8,128)S(1)} %get-tuple-element.22), channel_id=1, source_target_pairs={{0,1},{1,2},{2,3},{3,0},{4,5},{5,6},{6,7},{7,4},{8,9},{9,10},{10,1... | collective-permute-start | bytes 294920 | tf_op jit(solution)/shard_map/ppermute | solution.py:236
  17.7 2.6 %collective-permute-start.7 = (f32[24,1024]{1,0:T(8,128)S(1)}, f32[24,1024]{1,0:T(8,128)S(1)}, u32[]{:S(2)}, u32[]{:S(2)}) collective-permute-start(f32[24,1024]{1,0:T(8,128)S(1)} %get-tuple-element.24), channel_id=1, source_target_pairs={{0,2},{1,3},{2,0},{3,1},{4,6},{5,7},{6,4},{7,5},{8,10},{9,11},{10,... | collective-permute-start | bytes 294920 | tf_op jit(solution)/shard_map/ppermute | solution.py:236
  20.2 1.3 %collective-permute-start.8 = (f32[24,1024]{1,0:T(8,128)S(1)}, f32[24,1024]{1,0:T(8,128)S(1)}, u32[]{:S(2)}, u32[]{:S(2)}) collective-permute-start(f32[24,1024]{1,0:T(8,128)S(1)} %get-tuple-element.23), channel_id=1, source_target_pairs={{0,3},{1,0},{2,1},{3,2},{4,7},{5,4},{6,5},{7,6},{8,11},{9,8},{10,9... | collective-permute-start | bytes 294920 | tf_op jit(solution)/shard_map/ppermute | solution.py:236
  22.9 2.7 %collective-permute-start.11 = (f32[24,1024]{1,0:T(8,128)S(1)}, f32[24,1024]{1,0:T(8,128)S(1)}, u32[]{:S(2)}, u32[]{:S(2)}) collective-permute-start(f32[24,1024]{1,0:T(8,128)S(1)} %get-tuple-element.26), channel_id=1, source_target_pairs={{0,3},{1,0},{2,1},{3,2},{4,7},{5,4},{6,5},{7,6},{8,11},{9,8},{10,9... | collective-permute-start | bytes 294920 | tf_op jit(solution)/shard_map/ppermute | solution.py:236
  25.6 2.2 %collective-permute-done.7 = f32[24,1024]{1,0:T(8,128)S(1)} collective-permute-done((f32[24,1024]{1,0:T(8,128)S(1)}, f32[24,1024]{1,0:T(8,128)S(1)}, u32[]{:S(2)}, u32[]{:S(2)}) %collective-permute-start.7) | collective-permute-done | bytes 98336 | tf_op jit(solution)/shard_map/ppermute | solution.py:236
  27.8 8.0 %collective-permute-done.10 = f32[24,1024]{1,0:T(8,128)S(1)} collective-permute-done((f32[24,1024]{1,0:T(8,128)S(1)}, f32[24,1024]{1,0:T(8,128)S(1)}, u32[]{:S(2)}, u32[]{:S(2)}) %collective-permute-start.10) | collective-permute-done | bytes 98336 | tf_op jit(solution)/shard_map/ppermute | solution.py:236
  36.3 2.8 %collective-permute-start.13 = (bf16[2,24,1024]{2,1,0:T(8,128)(2,1)S(1)}, bf16[2,24,1024]{2,1,0:T(8,128)(2,1)S(1)}, u32[]{:S(2)}, u32[]{:S(2)}) collective-permute-start(bf16[2,24,1024]{2,1,0:T(8,128)(2,1)S(1)} %bitcast.160), channel_id=1, source_target_pairs={{0,2},{1,3},{2,0},{3,1},{4,6},{5,7},{6,4},{7,5},{8,10},{9,11},{10,... | collective-permute-start | bytes 294920 | tf_op jit(solution)/shard_map/ppermute | solution.py:188
  39.5 2.6 %collective-permute-done.13 = bf16[2,24,1024]{2,1,0:T(8,128)(2,1)S(1)} collective-permute-done((bf16[2,24,1024]{2,1,0:T(8,128)(2,1)S(1)}, bf16[2,24,1024]{2,1,0:T(8,128)(2,1)S(1)}, u32[]{:S(2)}, u32[]{:S(2)}) %collective-permute-start.13) | collective-permute-done | bytes 98336 | tf_op jit(solution)/shard_map/ppermute | solution.py:188
  42.0 3.5 %collective-permute-start.14 = (bf16[2,24,1024]{2,1,0:T(8,128)(2,1)S(1)}, bf16[2,24,1024]{2,1,0:T(8,128)(2,1)S(1)}, u32[]{:S(2)}, u32[]{:S(2)}) collective-permute-start(bf16[2,24,1024]{2,1,0:T(8,128)(2,1)S(1)} %collective-permute-done.13), channel_id=1, source_target_pairs={{0,1},{1,0},{2,3},{3,2},{4,5},{5,4},{6,7},{7,6},{8,9},{9,8},{10,11... | collective-permute-start | bytes 294920 | tf_op jit(solution)/shard_map/ppermute | solution.py:189
  45.5 2.6 %collective-permute-done.14 = bf16[2,24,1024]{2,1,0:T(8,128)(2,1)S(1)} collective-permute-done((bf16[2,24,1024]{2,1,0:T(8,128)(2,1)S(1)}, bf16[2,24,1024]{2,1,0:T(8,128)(2,1)S(1)}, u32[]{:S(2)}, u32[]{:S(2)}) %collective-permute-start.14) | collective-permute-done | bytes 98336 | tf_op jit(solution)/shard_map/ppermute | solution.py:189
  51.3 6.7 %collective-permute-done.16 = bf16[192,1024]{1,0:T(8,128)(2,1)S(1)} collective-permute-done((bf16[192,1024]{1,0:T(8,128)(2,1)S(1)}, bf16[192,1024]{1,0:T(8,128)(2,1)S(1)}, u32[]{:S(2)}, u32[]{:S(2)}) %collective-permute-start.16) | collective-permute-done | bytes 393248 | tf_op jit(solution)/shard_map/ppermute | solution.py:188
  58.1 1.6 %collective-permute-done.17 = bf16[192,1024]{1,0:T(8,128)(2,1)S(1)} collective-permute-done((bf16[192,1024]{1,0:T(8,128)(2,1)S(1)}, bf16[192,1024]{1,0:T(8,128)(2,1)S(1)}, u32[]{:S(2)}, u32[]{:S(2)}) %collective-permute-start.17) | collective-permute-done | bytes 393248 | tf_op jit(solution)/shard_map/ppermute | solution.py:189
  59.7 1.4 %pad_maximum_fusion.keyval_ref = bf16[4,2,96,1024]{3,2,1,0:T(8,128)(2,1)} fusion(bf16[1,2,96,1024]{3,2,1,0:T(8,128)(2,1)S(1)} %bitcast.159, bf16[1,2,96,1024]{3,2,1,0:T(8,128)(2,1)S(1)} %bitcast.156, bf16[1,2,96,1024]{3,2,1,0:T(8,128)(2,1)S(1)} %bitcast.158, bf16[1,2,96,1024]{3,2,1,0:T(8,128)(2,1)S(1)} %bitcast.141), kind=kLoop, calls=%fused_computation.20 | loop fusion | flops 2359296 | bytes 3145728 | tf_op jit(solution)/shard_map/stack | solution.py:190
  61.1 8.2 %shard_map.104 = (f32[2,64,4096]{2,1,0:T(8,128)}, bf16[2,96,1024]{2,1,0:T(8,128)(2,1)}) custom-call(s32[1]{0:T(128)} %bitcast.section_ref, s32[4]{0:T(128)} %iota_xor_fusion.slots_ref, f32[4,32]{1,0:T(4,128)} %maximum_tanh_fusion.gates_ref, bf16[2,64,4096]{2,1,0:T(8,128)(2,1)} %queries_ref.1, bf16[4,2,96,1024]{3,2,1,0:T(8,128)(2,1)} %pad_maximum_fusion.keyval_ref, ...), custom_call_target="tpu_custom_call" | custom-call | flops 1409286144 | bytes 6815744 | tf_op jit(solution)/shard_map/pallas_call | solution.py:139
  69.4 1.6 %gather_fusion.3 = bf16[8,24,1024]{2,1,0:T(8,128)(2,1)S(1)} fusion(bf16[8,24,1024]{2,1,0:T(8,128)(2,1)} %bitcast.164, s32[1024]{0:T(1024)S(1)} %pad_clamp_fusion.1), kind=kCustom, calls=%fused_computation.1.clone | custom fusion | bytes 786464 | tf_op jit(solution)/shard_map/jit(_take)/gather | solution.py:307
  71.1 1.8 %collective-permute-start.18 = (bf16[48,1024]{1,0:T(8,128)(2,1)S(1)}, bf16[48,1024]{1,0:T(8,128)(2,1)S(1)}, u32[]{:S(2)}, u32[]{:S(2)}) collective-permute-start(bf16[48,1024]{1,0:T(8,128)(2,1)S(1)} %get-tuple-element.19), channel_id=1, source_target_pairs={{0,1},{1,2},{2,3},{3,0},{4,5},{5,6},{6,7},{7,4},{8,9},{9,10},{10,1... | collective-permute-start | bytes 294920 | tf_op jit(solution)/shard_map/ppermute | solution.py:236
  72.9 1.2 %collective-permute-start.19 = (bf16[48,1024]{1,0:T(8,128)(2,1)S(1)}, bf16[48,1024]{1,0:T(8,128)(2,1)S(1)}, u32[]{:S(2)}, u32[]{:S(2)}) collective-permute-start(bf16[48,1024]{1,0:T(8,128)(2,1)S(1)} %get-tuple-element.21), channel_id=1, source_target_pairs={{0,2},{1,3},{2,0},{3,1},{4,6},{5,7},{6,4},{7,5},{8,10},{9,11},{10,... | collective-permute-start | bytes 294920 | tf_op jit(solution)/shard_map/ppermute | solution.py:236
  74.1 2.0 %collective-permute-start.20 = (bf16[48,1024]{1,0:T(8,128)(2,1)S(1)}, bf16[48,1024]{1,0:T(8,128)(2,1)S(1)}, u32[]{:S(2)}, u32[]{:S(2)}) collective-permute-start(bf16[48,1024]{1,0:T(8,128)(2,1)S(1)} %get-tuple-element.20), channel_id=1, source_target_pairs={{0,3},{1,0},{2,1},{3,2},{4,7},{5,4},{6,5},{7,6},{8,11},{9,8},{10,9... | collective-permute-start | bytes 294920 | tf_op jit(solution)/shard_map/ppermute | solution.py:236
  76.1 1.4 %collective-permute-done.18 = bf16[48,1024]{1,0:T(8,128)(2,1)S(1)} collective-permute-done((bf16[48,1024]{1,0:T(8,128)(2,1)S(1)}, bf16[48,1024]{1,0:T(8,128)(2,1)S(1)}, u32[]{:S(2)}, u32[]{:S(2)}) %collective-permute-start.18) | collective-permute-done | bytes 98336 | tf_op jit(solution)/shard_map/ppermute | solution.py:236
  77.6 5.1 %collective-permute-done.19 = bf16[48,1024]{1,0:T(8,128)(2,1)S(1)} collective-permute-done((bf16[48,1024]{1,0:T(8,128)(2,1)S(1)}, bf16[48,1024]{1,0:T(8,128)(2,1)S(1)}, u32[]{:S(2)}, u32[]{:S(2)}) %collective-permute-start.19) | collective-permute-done | bytes 98336 | tf_op jit(solution)/shard_map/ppermute | solution.py:236
  83.2 2.7 %collective-permute-start.21 = (bf16[2,24,1024]{2,1,0:T(8,128)(2,1)S(1)}, bf16[2,24,1024]{2,1,0:T(8,128)(2,1)S(1)}, u32[]{:S(2)}, u32[]{:S(2)}) collective-permute-start(bf16[2,24,1024]{2,1,0:T(8,128)(2,1)S(1)} %pad_maximum_fusion.7), channel_id=1, source_target_pairs={{0,1},{1,0},{2,3},{3,2},{4,5},{5,4},{6,7},{7,6},{8,9},{9,8},{10,11... | collective-permute-start | bytes 294920 | tf_op jit(solution)/shard_map/ppermute | solution.py:202
  85.9 3.6 %fusion.18 = bf16[48,2048]{1,0:T(8,128)(2,1)S(1)} fusion(bf16[1,2048,1024]{2,1,0:T(8,128)(2,1)} %param.12, bf16[48,512]{1,0:T(8,128)(2,1)S(1)} %slice.66, bf16[48,512]{1,0:T(8,128)(2,1)S(1)} %fusion.29), kind=kOutput, calls=%fused_computation.18 | convolution fusion | flops 201621504 | bytes 4489216 | tf_op jit(solution)/shard_map/dot_general | solution.py:359
  90.5 1.4 %fusion.21 = bf16[48,2048]{1,0:T(8,128)(2,1)S(1)} fusion(bf16[48,1024]{1,0:T(8,128)(2,1)S(1)} %bitcast.173, bf16[1,2048,1024]{2,1,0:T(8,128)(2,1)S(1)} %copy-done.1), kind=kOutput, calls=%fused_computation.19 | convolution fusion | flops 201424896 | bytes 4489216 | tf_op jit(solution)/shard_map/dot_general | solution.py:359
  91.9 5.1 %collective-permute-done.22 = bf16[2,24,1024]{2,1,0:T(8,128)(2,1)S(1)} collective-permute-done((bf16[2,24,1024]{2,1,0:T(8,128)(2,1)S(1)}, bf16[2,24,1024]{2,1,0:T(8,128)(2,1)S(1)}, u32[]{:S(2)}, u32[]{:S(2)}) %collective-permute-start.22) | collective-permute-done | bytes 98336 | tf_op jit(solution)/shard_map/ppermute | solution.py:201
  97.0 1.4 %fusion.12 = bf16[48,2048]{1,0:T(8,128)(2,1)S(1)} fusion(bf16[48,1024]{1,0:T(8,128)(2,1)S(1)} %bitcast.172, bf16[1,2048,1024]{2,1,0:T(8,128)(2,1)S(1)} %copy-done.1), kind=kOutput, calls=%fused_computation.16 | convolution fusion | flops 201424896 | bytes 4489216 | tf_op jit(solution)/shard_map/dot_general | solution.py:359
  98.4 3.3 %collective-permute-done.23 = bf16[2,24,1024]{2,1,0:T(8,128)(2,1)S(1)} collective-permute-done((bf16[2,24,1024]{2,1,0:T(8,128)(2,1)S(1)}, bf16[2,24,1024]{2,1,0:T(8,128)(2,1)S(1)}, u32[]{:S(2)}, u32[]{:S(2)}) %collective-permute-start.23) | collective-permute-done | bytes 98336 | tf_op jit(solution)/shard_map/ppermute | solution.py:202
  101.7 1.4 %fusion.15 = bf16[48,2048]{1,0:T(8,128)(2,1)S(1)} fusion(bf16[48,1024]{1,0:T(8,128)(2,1)S(1)} %bitcast.174, bf16[1,2048,1024]{2,1,0:T(8,128)(2,1)S(1)} %copy-done.1), kind=kOutput, calls=%fused_computation.17 | convolution fusion | flops 201424896 | bytes 4489216 | tf_op jit(solution)/shard_map/dot_general | solution.py:359
  104.2 1.7 %collective-permute-done.24 = bf16[2,2,24,2048]{3,2,1,0:T(8,128)(2,1)S(1)} collective-permute-done((bf16[2,2,24,2048]{3,2,1,0:T(8,128)(2,1)S(1)}, bf16[2,2,24,2048]{3,2,1,0:T(8,128)(2,1)S(1)}, u32[]{:S(2)}, u32[]{:S(2)}) %collective-permute-start.24) | collective-permute-done | bytes 393248 | tf_op jit(solution)/shard_map/ppermute | solution.py:223
  105.9 5.4 %collective-permute-start.25 = (bf16[2,24,2048]{2,1,0:T(8,128)(2,1)S(1)}, bf16[2,24,2048]{2,1,0:T(8,128)(2,1)S(1)}, u32[]{:S(2)}, u32[]{:S(2)}) collective-permute-start(bf16[2,24,2048]{2,1,0:T(8,128)(2,1)S(1)} %fusion.24), channel_id=1, source_target_pairs={{0,8},{4,12},{8,0},{12,4},{1,9},{5,13},{9,1},{13,5},{2,10},{6,14},... | collective-permute-start | bytes 589832 | tf_op jit(solution)/shard_map/ppermute | solution.py:227
  111.3 5.2 %collective-permute-done.25 = bf16[2,24,2048]{2,1,0:T(8,128)(2,1)S(1)} collective-permute-done((bf16[2,24,2048]{2,1,0:T(8,128)(2,1)S(1)}, bf16[2,24,2048]{2,1,0:T(8,128)(2,1)S(1)}, u32[]{:S(2)}, u32[]{:S(2)}) %collective-permute-start.25) | collective-permute-done | bytes 196640 | tf_op jit(solution)/shard_map/ppermute | solution.py:227
  (113 shorter events, 17.0 us)
Async XLA Ops:
  2.1 5.2 %collective-permute-start.4 = (f32[4128]{0:T(1024)S(1)}, f32[4128]{0:T(1024)S(1)}, u32[]{:S(2)}, u32[]{:S(2)}) collective-permute-start(f32[4128]{0:T(1024)S(1)} %reduce), channel_id=1, source_target_pairs={{0,8},{4,12},{8,0},{12,4},{1,9},{5,13},{9,1},{13,5},{2,10},{6,14},... | collective-permute-start | bytes 49544 | tf_op jit(solution)/shard_map/ppermute | solution.py:188
  5.1 2.7 %collective-permute-start.3 = (f32[4128]{0:T(1024)S(1)}, f32[4128]{0:T(1024)S(1)}, u32[]{:S(2)}, u32[]{:S(2)}) collective-permute-start(f32[4128]{0:T(1024)S(1)} %reduce), channel_id=1, source_target_pairs={{0,4},{4,0},{8,12},{12,8},{1,5},{5,1},{9,13},{13,9},{2,6},{6,2},{1... | collective-permute-start | bytes 49544 | tf_op jit(solution)/shard_map/ppermute | solution.py:189
  5.1 7.5 %collective-permute-start.1 = (bf16[2,24,2048]{2,1,0:T(8,128)(2,1)}, bf16[2,24,2048]{2,1,0:T(8,128)(2,1)S(1)}, u32[]{:S(2)}, u32[]{:S(2)}) collective-permute-start(bf16[2,24,2048]{2,1,0:T(8,128)(2,1)} %param.11), channel_id=1, source_target_pairs={{0,8},{4,12},{8,0},{12,4},{1,9},{5,13},{9,1},{13,5},{2,10},{6,14},... | collective-permute-start | bytes 589832 | tf_op jit(solution)/shard_map/ppermute | solution.py:188
  5.2 8.7 %collective-permute-start = (bf16[2,24,2048]{2,1,0:T(8,128)(2,1)}, bf16[2,24,2048]{2,1,0:T(8,128)(2,1)S(1)}, u32[]{:S(2)}, u32[]{:S(2)}) collective-permute-start(bf16[2,24,2048]{2,1,0:T(8,128)(2,1)} %param.11), channel_id=1, source_target_pairs={{0,4},{4,0},{8,12},{12,8},{1,5},{5,1},{9,13},{13,9},{2,6},{6,2},{1... | collective-permute-start | bytes 589832 | tf_op jit(solution)/shard_map/ppermute | solution.py:189
  7.2 1.3 %collective-permute-start.5 = (f32[4128]{0:T(1024)S(1)}, f32[4128]{0:T(1024)S(1)}, u32[]{:S(2)}, u32[]{:S(2)}) collective-permute-start(f32[4128]{0:T(1024)S(1)} %collective-permute-done.4), channel_id=1, source_target_pairs={{0,4},{4,0},{8,12},{12,8},{1,5},{5,1},{9,13},{13,9},{2,6},{6,2},{1... | collective-permute-start | bytes 49544 | tf_op jit(solution)/shard_map/ppermute | solution.py:189
  7.7 7.4 %copy-start = (bf16[1,2048,1024]{2,1,0:T(8,128)(2,1)S(1)}, bf16[1,2048,1024]{2,1,0:T(8,128)(2,1)}, u32[]{:S(2)}) copy-start(bf16[1,2048,1024]{2,1,0:T(8,128)(2,1)} %param.12) | copy-start | bytes 12582916
  12.6 1.4 %collective-permute-start.2 = (bf16[2,24,2048]{2,1,0:T(8,128)(2,1)S(1)}, bf16[2,24,2048]{2,1,0:T(8,128)(2,1)S(1)}, u32[]{:S(2)}, u32[]{:S(2)}) collective-permute-start(bf16[2,24,2048]{2,1,0:T(8,128)(2,1)S(1)} %collective-permute-done.1), channel_id=1, source_target_pairs={{0,4},{4,0},{8,12},{12,8},{1,5},{5,1},{9,13},{13,9},{2,6},{6,2},{1... | collective-permute-start | bytes 589832 | tf_op jit(solution)/shard_map/ppermute | solution.py:189
  16.0 9.6 %collective-permute-start.6 = (f32[24,1024]{1,0:T(8,128)S(1)}, f32[24,1024]{1,0:T(8,128)S(1)}, u32[]{:S(2)}, u32[]{:S(2)}) collective-permute-start(f32[24,1024]{1,0:T(8,128)S(1)} %get-tuple-element.22), channel_id=1, source_target_pairs={{0,1},{1,2},{2,3},{3,0},{4,5},{5,6},{6,7},{7,4},{8,9},{9,10},{10,1... | collective-permute-start | bytes 294920 | tf_op jit(solution)/shard_map/ppermute | solution.py:236
  17.7 10.2 %collective-permute-start.7 = (f32[24,1024]{1,0:T(8,128)S(1)}, f32[24,1024]{1,0:T(8,128)S(1)}, u32[]{:S(2)}, u32[]{:S(2)}) collective-permute-start(f32[24,1024]{1,0:T(8,128)S(1)} %get-tuple-element.24), channel_id=1, source_target_pairs={{0,2},{1,3},{2,0},{3,1},{4,6},{5,7},{6,4},{7,5},{8,10},{9,11},{10,... | collective-permute-start | bytes 294920 | tf_op jit(solution)/shard_map/ppermute | solution.py:236
  20.2 7.6 %collective-permute-start.8 = (f32[24,1024]{1,0:T(8,128)S(1)}, f32[24,1024]{1,0:T(8,128)S(1)}, u32[]{:S(2)}, u32[]{:S(2)}) collective-permute-start(f32[24,1024]{1,0:T(8,128)S(1)} %get-tuple-element.23), channel_id=1, source_target_pairs={{0,3},{1,0},{2,1},{3,2},{4,7},{5,4},{6,5},{7,6},{8,11},{9,8},{10,9... | collective-permute-start | bytes 294920 | tf_op jit(solution)/shard_map/ppermute | solution.py:236
  21.6 14.6 %copy-start.3 = (f32[1,512]{1,0:T(1,128)S(1)}, f32[1,512]{1,0:T(1,128)}, u32[]{:S(2)}) copy-start(f32[1,512]{1,0:T(1,128)} %param.14) | copy-start | bytes 6148
  22.5 13.3 %collective-permute-start.10 = (f32[24,1024]{1,0:T(8,128)S(1)}, f32[24,1024]{1,0:T(8,128)S(1)}, u32[]{:S(2)}, u32[]{:S(2)}) collective-permute-start(f32[24,1024]{1,0:T(8,128)S(1)} %get-tuple-element.27), channel_id=1, source_target_pairs={{0,2},{1,3},{2,0},{3,1},{4,6},{5,7},{6,4},{7,5},{8,10},{9,11},{10,... | collective-permute-start | bytes 294920 | tf_op jit(solution)/shard_map/ppermute | solution.py:236
  22.9 12.9 %collective-permute-start.11 = (f32[24,1024]{1,0:T(8,128)S(1)}, f32[24,1024]{1,0:T(8,128)S(1)}, u32[]{:S(2)}, u32[]{:S(2)}) collective-permute-start(f32[24,1024]{1,0:T(8,128)S(1)} %get-tuple-element.26), channel_id=1, source_target_pairs={{0,3},{1,0},{2,1},{3,2},{4,7},{5,4},{6,5},{7,6},{8,11},{9,8},{10,9... | collective-permute-start | bytes 294920 | tf_op jit(solution)/shard_map/ppermute | solution.py:236
  25.6 10.2 %collective-permute-start.9 = (f32[24,1024]{1,0:T(8,128)S(1)}, f32[24,1024]{1,0:T(8,128)S(1)}, u32[]{:S(2)}, u32[]{:S(2)}) collective-permute-start(f32[24,1024]{1,0:T(8,128)S(1)} %get-tuple-element.25), channel_id=1, source_target_pairs={{0,1},{1,2},{2,3},{3,0},{4,5},{5,6},{6,7},{7,4},{8,9},{9,10},{10,1... | collective-permute-start | bytes 294920 | tf_op jit(solution)/shard_map/ppermute | solution.py:236
  36.3 5.8 %collective-permute-start.13 = (bf16[2,24,1024]{2,1,0:T(8,128)(2,1)S(1)}, bf16[2,24,1024]{2,1,0:T(8,128)(2,1)S(1)}, u32[]{:S(2)}, u32[]{:S(2)}) collective-permute-start(bf16[2,24,1024]{2,1,0:T(8,128)(2,1)S(1)} %bitcast.160), channel_id=1, source_target_pairs={{0,2},{1,3},{2,0},{3,1},{4,6},{5,7},{6,4},{7,5},{8,10},{9,11},{10,... | collective-permute-start | bytes 294920 | tf_op jit(solution)/shard_map/ppermute | solution.py:188
  39.1 6.4 %collective-permute-start.12 = (bf16[2,24,1024]{2,1,0:T(8,128)(2,1)S(1)}, bf16[2,24,1024]{2,1,0:T(8,128)(2,1)S(1)}, u32[]{:S(2)}, u32[]{:S(2)}) collective-permute-start(bf16[2,24,1024]{2,1,0:T(8,128)(2,1)S(1)} %bitcast.161), channel_id=1, source_target_pairs={{0,1},{1,0},{2,3},{3,2},{4,5},{5,4},{6,7},{7,6},{8,9},{9,8},{10,11... | collective-permute-start | bytes 294920 | tf_op jit(solution)/shard_map/ppermute | solution.py:189
  42.0 6.0 %collective-permute-start.14 = (bf16[2,24,1024]{2,1,0:T(8,128)(2,1)S(1)}, bf16[2,24,1024]{2,1,0:T(8,128)(2,1)S(1)}, u32[]{:S(2)}, u32[]{:S(2)}) collective-permute-start(bf16[2,24,1024]{2,1,0:T(8,128)(2,1)S(1)} %collective-permute-done.13), channel_id=1, source_target_pairs={{0,1},{1,0},{2,3},{3,2},{4,5},{5,4},{6,7},{7,6},{8,9},{9,8},{10,11... | collective-permute-start | bytes 294920 | tf_op jit(solution)/shard_map/ppermute | solution.py:189
  49.5 8.5 %collective-permute-start.16 = (bf16[192,1024]{1,0:T(8,128)(2,1)S(1)}, bf16[192,1024]{1,0:T(8,128)(2,1)S(1)}, u32[]{:S(2)}, u32[]{:S(2)}) collective-permute-start(bf16[192,1024]{1,0:T(8,128)(2,1)S(1)} %bitcast.139), channel_id=1, source_target_pairs={{0,8},{4,12},{8,0},{12,4},{1,9},{5,13},{9,1},{13,5},{2,10},{6,14},... | collective-permute-start | bytes 1179656 | tf_op jit(solution)/shard_map/ppermute | solution.py:188
  50.2 11.0 %copy-start.2 = (f32[2,8,64,96]{3,2,1,0:T(8,128)}, f32[2,8,64,96]{3,2,1,0:T(8,128)S(1)}, u32[]{:S(2)}) copy-start(f32[2,8,64,96]{3,2,1,0:T(8,128)S(1)} %tile.4) | copy-start | bytes 1179652
  51.2 6.9 %collective-permute-start.15 = (bf16[192,1024]{1,0:T(8,128)(2,1)S(1)}, bf16[192,1024]{1,0:T(8,128)(2,1)S(1)}, u32[]{:S(2)}, u32[]{:S(2)}) collective-permute-start(bf16[192,1024]{1,0:T(8,128)(2,1)S(1)} %bitcast.140), channel_id=1, source_target_pairs={{0,4},{4,0},{8,12},{12,8},{1,5},{5,1},{9,13},{13,9},{2,6},{6,2},{1... | collective-permute-start | bytes 1179656 | tf_op jit(solution)/shard_map/ppermute | solution.py:189
  58.0 1.7 %collective-permute-start.17 = (bf16[192,1024]{1,0:T(8,128)(2,1)S(1)}, bf16[192,1024]{1,0:T(8,128)(2,1)S(1)}, u32[]{:S(2)}, u32[]{:S(2)}) collective-permute-start(bf16[192,1024]{1,0:T(8,128)(2,1)S(1)} %collective-permute-done.16), channel_id=1, source_target_pairs={{0,4},{4,0},{8,12},{12,8},{1,5},{5,1},{9,13},{13,9},{2,6},{6,2},{1... | collective-permute-start | bytes 1179656 | tf_op jit(solution)/shard_map/ppermute | solution.py:189
  71.1 6.5 %collective-permute-start.18 = (bf16[48,1024]{1,0:T(8,128)(2,1)S(1)}, bf16[48,1024]{1,0:T(8,128)(2,1)S(1)}, u32[]{:S(2)}, u32[]{:S(2)}) collective-permute-start(bf16[48,1024]{1,0:T(8,128)(2,1)S(1)} %get-tuple-element.19), channel_id=1, source_target_pairs={{0,1},{1,2},{2,3},{3,0},{4,5},{5,6},{6,7},{7,4},{8,9},{9,10},{10,1... | collective-permute-start | bytes 294920 | tf_op jit(solution)/shard_map/ppermute | solution.py:236
  72.9 9.8 %collective-permute-start.19 = (bf16[48,1024]{1,0:T(8,128)(2,1)S(1)}, bf16[48,1024]{1,0:T(8,128)(2,1)S(1)}, u32[]{:S(2)}, u32[]{:S(2)}) collective-permute-start(bf16[48,1024]{1,0:T(8,128)(2,1)S(1)} %get-tuple-element.21), channel_id=1, source_target_pairs={{0,2},{1,3},{2,0},{3,1},{4,6},{5,7},{6,4},{7,5},{8,10},{9,11},{10,... | collective-permute-start | bytes 294920 | tf_op jit(solution)/shard_map/ppermute | solution.py:236
  74.1 8.6 %collective-permute-start.20 = (bf16[48,1024]{1,0:T(8,128)(2,1)S(1)}, bf16[48,1024]{1,0:T(8,128)(2,1)S(1)}, u32[]{:S(2)}, u32[]{:S(2)}) collective-permute-start(bf16[48,1024]{1,0:T(8,128)(2,1)S(1)} %get-tuple-element.20), channel_id=1, source_target_pairs={{0,3},{1,0},{2,1},{3,2},{4,7},{5,4},{6,5},{7,6},{8,11},{9,8},{10,9... | collective-permute-start | bytes 294920 | tf_op jit(solution)/shard_map/ppermute | solution.py:236
  82.8 7.7 %copy-start.1 = (bf16[1,2048,1024]{2,1,0:T(8,128)(2,1)S(1)}, bf16[1,2048,1024]{2,1,0:T(8,128)(2,1)}, u32[]{:S(2)}) copy-start(bf16[1,2048,1024]{2,1,0:T(8,128)(2,1)} %param.12) | copy-start | bytes 12582916
  83.2 7.3 %collective-permute-start.21 = (bf16[2,24,1024]{2,1,0:T(8,128)(2,1)S(1)}, bf16[2,24,1024]{2,1,0:T(8,128)(2,1)S(1)}, u32[]{:S(2)}, u32[]{:S(2)}) collective-permute-start(bf16[2,24,1024]{2,1,0:T(8,128)(2,1)S(1)} %pad_maximum_fusion.7), channel_id=1, source_target_pairs={{0,1},{1,0},{2,3},{3,2},{4,5},{5,4},{6,7},{7,6},{8,9},{9,8},{10,11... | collective-permute-start | bytes 294920 | tf_op jit(solution)/shard_map/ppermute | solution.py:202
  89.5 7.5 %collective-permute-start.22 = (bf16[2,24,1024]{2,1,0:T(8,128)(2,1)S(1)}, bf16[2,24,1024]{2,1,0:T(8,128)(2,1)S(1)}, u32[]{:S(2)}, u32[]{:S(2)}) collective-permute-start(bf16[2,24,1024]{2,1,0:T(8,128)(2,1)S(1)} %pad_maximum_fusion.7), channel_id=1, source_target_pairs={{0,2},{1,3},{2,0},{3,1},{4,6},{5,7},{6,4},{7,5},{8,10},{9,11},{10,... | collective-permute-start | bytes 294920 | tf_op jit(solution)/shard_map/ppermute | solution.py:201
  97.0 4.7 %collective-permute-start.23 = (bf16[2,24,1024]{2,1,0:T(8,128)(2,1)S(1)}, bf16[2,24,1024]{2,1,0:T(8,128)(2,1)S(1)}, u32[]{:S(2)}, u32[]{:S(2)}) collective-permute-start(bf16[2,24,1024]{2,1,0:T(8,128)(2,1)S(1)} %collective-permute-done.22), channel_id=1, source_target_pairs={{0,1},{1,0},{2,3},{3,2},{4,5},{5,4},{6,7},{7,6},{8,9},{9,8},{10,11... | collective-permute-start | bytes 294920 | tf_op jit(solution)/shard_map/ppermute | solution.py:202
  104.1 1.8 %collective-permute-start.24 = (bf16[2,2,24,2048]{3,2,1,0:T(8,128)(2,1)S(1)}, bf16[2,2,24,2048]{3,2,1,0:T(8,128)(2,1)S(1)}, u32[]{:S(2)}, u32[]{:S(2)}) collective-permute-start(bf16[2,2,24,2048]{3,2,1,0:T(8,128)(2,1)S(1)} %pad_maximum_fusion.4), channel_id=1, source_target_pairs={{0,4},{4,0},{8,12},{12,8},{1,5},{5,1},{9,13},{13,9},{2,6},{6,2},{1... | collective-permute-start | bytes 1179656 | tf_op jit(solution)/shard_map/ppermute | solution.py:223
  105.9 10.6 %collective-permute-start.25 = (bf16[2,24,2048]{2,1,0:T(8,128)(2,1)S(1)}, bf16[2,24,2048]{2,1,0:T(8,128)(2,1)S(1)}, u32[]{:S(2)}, u32[]{:S(2)}) collective-permute-start(bf16[2,24,2048]{2,1,0:T(8,128)(2,1)S(1)} %fusion.24), channel_id=1, source_target_pairs={{0,8},{4,12},{8,0},{12,4},{1,9},{5,13},{9,1},{13,5},{2,10},{6,14},... | collective-permute-start | bytes 589832 | tf_op jit(solution)/shard_map/ppermute | solution.py:227

commit v12 on v10

--- a/solution.py
+++ b/solution.py
@@ -312,13 +312,32 @@
         def to_owned(rows):
             return rows.reshape(shard_count, total_rows // shard_count, pair_width)
 
+    def keyval_of(raw):
+        keys = head_normalize(raw[:, :key_width], key_norm_gain[0], keyval_heads)
+        return jnp.concatenate(
+            [keys.astype(jnp.bfloat16), raw[:, key_width:].astype(jnp.bfloat16)], axis=1
+        )
+
+    if phased:
+        per_phase = []
+        for phase in range(2):
+            blocks = in_order(keyval_of(raw_parts[phase]), "shard")
+            per_phase.append(gather_blocks(blocks, "section")[0])
+        both = jnp.stack(per_phase, axis=1)
+        slot_ids = sections[:, None, None]
+        crossing = lax.bitwise_xor(
+            lax.bitwise_xor(section_index, slot_ids), sections[None, None, :]
+        )
+        holder = 2 * micro_ids[None, :, None] + crossing % 2
+        flat = (slot_ids * 2 + crossing // 2) * shard_count + holder
+        keyval_all = jnp.take(
+            both.reshape(-1, owned, pair_width), flat.reshape(-1), axis=0
+        ).reshape(section_count, total_rows, pair_width)
+    else:
+        keyval_all, _ = gather_blocks(
+            to_natural(keyval_of(raw_rows.reshape(-1, pair_width))), "section"
+        )
     raw_rows = raw_rows.reshape(-1, pair_width)
-    key_rows = head_normalize(raw_rows[:, :key_width], key_norm_gain[0], keyval_heads)
-    keyval_rows = jnp.concatenate(
-        [key_rows.astype(jnp.bfloat16), raw_rows[:, key_width:].astype(jnp.bfloat16)], axis=1
-    )
-    keyval_own = to_natural(keyval_rows)
-    keyval_all, _ = gather_blocks(keyval_own, "section")
 
     same_document = text_document[:, :, None] == image_document[:, None, :]
     leaving, grad_local = attention_layers(

time: 113 us -> 118 us (1.044)
  starting transfers between devices: 38.6 us -> 46 us
  waiting for transfers between devices: 43 us -> 36.8 us
  matrix products: 7.55 us -> 9.73 us
  local copies, waits for them, and re-layouts: 7.63 us -> 8.9 us
    ppermute x5 -> x7, waiting for transfers between devices: 13.6 us -> 7.44 us  [gather_blocks(): across = lax.ppermute(block, axis, [(i, i ^ 2) for i in range(count)])]
    ppermute x5 -> x7, starting transfers between devices: 3.43 us -> 7.61 us  [gather_blocks(): lax.ppermute(block, axis, partner)]
    ppermute x5 -> x7, starting transfers between devices: 6.29 us -> 9.83 us  [gather_blocks(): across = lax.ppermute(block, axis, [(i, i ^ 2) for i in range(count)])]
    ppermute x5 -> x7, starting transfers between devices: 3.47 us -> 6.94 us  [gather_blocks(): lax.ppermute(across, axis, partner)]
    ppermute x9, starting transfers between devices: 19.1 us -> 15.8 us  [scatter_blocks(): lax.ppermute(part, axis, [(i, (i + d) % count) for i in range(count)])]
    dot_general x2, matrix products: 3.81 us -> 5.99 us  [per_device(): partial = jnp.dot(block, weights, preferred_element_type=jnp.float32)]
    select_n x0 -> x2, other arithmetic: none -> 1.41 us  [per_device(): jnp.take(both.reshape(-1, owned, pair_width), flat.reshape(-1), axis=0)]
    another operation x4 -> x5, other arithmetic: 1.52 us -> 0.17 us  [gather_blocks(): return (jnp.stack(received), lax.bitwise_xor(index, positions))]
  transfers between devices with their start and end apart: 26 -> 32, of which waited for: 16 -> 17; matrix products, arithmetic and copies ran while one was open for 11% -> 12% of each run, Pallas kernels for 0% -> 0%
where the time goes in v12:
time: 118 us
  starting transfers between devices  46 us (39%)
  waiting for transfers between devices  36.8 us (31%)
  matrix products  9.73 us (8%)
  local copies, waits for them, and re-layouts  8.9 us (8%)
  Pallas kernels  8.21 us (7%)
  other arithmetic  6.69 us (6%)
  between operations  1.34 us (1%)
    ppermute x9, waiting for transfers between devices, scatter_blocks(): lax.ppermute(part, axis, [(i, (i + d) % count) for i in range(count)])  16 us
    ppermute x9, starting transfers between devices, scatter_blocks(): lax.ppermute(part, axis, [(i, (i + d) % count) for i in range(count)])  15.8 us
    ppermute x7, starting transfers between devices, gather_blocks(): across = lax.ppermute(block, axis, [(i, i ^ 2) for i in range(count)])  9.83 us
    pallas_call x1, Pallas kernels, attention_layers(): pl.pallas_call(functools.partial(attention_kernel, head_count=head_count,...  8.21 us
    ppermute x7, starting transfers between devices, gather_blocks(): lax.ppermute(block, axis, partner)  7.61 us
    ppermute x7, waiting for transfers between devices, gather_blocks(): across = lax.ppermute(block, axis, [(i, i ^ 2) for i in range(count)])  7.44 us
    ppermute x7, starting transfers between devices, gather_blocks(): lax.ppermute(across, axis, partner)  6.94 us
    dot_general x2, matrix products, per_device(): partial = jnp.dot(block, weights, preferred_element_type=jnp.float32)  5.99 us
  transfers between devices with their start and end apart: 32, of which 17 were waited for; matrix products, arithmetic and copies ran while one was open for 12% of the time, Pallas kernels for 0%

profile of v12, /device:TPU:0, one launch (start us, length us, event | category | flops | bytes accessed | tf_op | source)
XLA Modules:
  0.0 117.7 jit_solution(17077034931864681382)
XLA Ops:
  1.1 2.6 %collective-permute-start.13 = (bf16[2,24,2048]{2,1,0:T(8,128)(2,1)}, bf16[2,24,2048]{2,1,0:T(8,128)(2,1)S(1)}, u32[]{:S(2)}, u32[]{:S(2)}) collective-permute-start(bf16[2,24,2048]{2,1,0:T(8,128)(2,1)} %param.13), channel_id=1, source_target_pairs={{0,8},{4,12},{8,0},{12,4},{1,9},{5,13},{9,1},{13,5},{2,10},{6,14},... | collective-permute-start | bytes 589832 | tf_op jit(solution)/shard_map/ppermute | solution.py:188
  7.8 3.0 %fusion.2 = f32[4,24,1024]{2,1,0:T(8,128)S(1)} fusion(bf16[4,24,2048]{2,1,0:T(8,128)(2,1)S(1)} %bitcast.146, bf16[1,2048,1024]{2,1,0:T(8,128)(2,1)} %param.14), kind=kOutput, calls=%fused_computation.8 | convolution fusion | flops 402653184 | bytes 4980736 | tf_op jit(solution)/shard_map/dot_general | solution.py:273
  10.8 2.1 %collective-permute-start.4 = (f32[24,1024]{1,0:T(8,128)S(1)}, f32[24,1024]{1,0:T(8,128)S(1)}, u32[]{:S(2)}, u32[]{:S(2)}) collective-permute-start(f32[24,1024]{1,0:T(8,128)S(1)} %get-tuple-element.17), channel_id=1, source_target_pairs={{0,1},{1,2},{2,3},{3,0},{4,5},{5,6},{6,7},{7,4},{8,9},{9,10},{10,1... | collective-permute-start | bytes 294920 | tf_op jit(solution)/shard_map/ppermute | solution.py:229
  12.9 2.6 %collective-permute-start.5 = (f32[24,1024]{1,0:T(8,128)S(1)}, f32[24,1024]{1,0:T(8,128)S(1)}, u32[]{:S(2)}, u32[]{:S(2)}) collective-permute-start(f32[24,1024]{1,0:T(8,128)S(1)} %get-tuple-element.19), channel_id=1, source_target_pairs={{0,2},{1,3},{2,0},{3,1},{4,6},{5,7},{6,4},{7,5},{8,10},{9,11},{10,... | collective-permute-start | bytes 294920 | tf_op jit(solution)/shard_map/ppermute | solution.py:229
  16.9 1.7 %collective-permute-done.4 = f32[24,1024]{1,0:T(8,128)S(1)} collective-permute-done((f32[24,1024]{1,0:T(8,128)S(1)}, f32[24,1024]{1,0:T(8,128)S(1)}, u32[]{:S(2)}, u32[]{:S(2)}) %collective-permute-start.4) | collective-permute-done | bytes 98336 | tf_op jit(solution)/shard_map/ppermute | solution.py:229
  18.6 3.5 %collective-permute-done.5 = f32[24,1024]{1,0:T(8,128)S(1)} collective-permute-done((f32[24,1024]{1,0:T(8,128)S(1)}, f32[24,1024]{1,0:T(8,128)S(1)}, u32[]{:S(2)}, u32[]{:S(2)}) %collective-permute-start.5) | collective-permute-done | bytes 98336 | tf_op jit(solution)/shard_map/ppermute | solution.py:229
  22.4 3.0 %fusion = f32[4,24,1024]{2,1,0:T(8,128)S(1)} fusion(bf16[4,24,2048]{2,1,0:T(8,128)(2,1)S(1)} %bitcast.147, bf16[1,2048,1024]{2,1,0:T(8,128)(2,1)} %param.14), kind=kOutput, calls=%fused_computation.6 | convolution fusion | flops 402653184 | bytes 4980736 | tf_op jit(solution)/shard_map/dot_general | solution.py:273
  25.4 2.6 %collective-permute-start.15 = (f32[24,1024]{1,0:T(8,128)S(1)}, f32[24,1024]{1,0:T(8,128)S(1)}, u32[]{:S(2)}, u32[]{:S(2)}) collective-permute-start(f32[24,1024]{1,0:T(8,128)S(1)} %get-tuple-element.20), channel_id=1, source_target_pairs={{0,1},{1,2},{2,3},{3,0},{4,5},{5,6},{6,7},{7,4},{8,9},{9,10},{10,1... | collective-permute-start | bytes 294920 | tf_op jit(solution)/shard_map/ppermute | solution.py:229
  28.1 1.6 %collective-permute-start.16 = (f32[24,1024]{1,0:T(8,128)S(1)}, f32[24,1024]{1,0:T(8,128)S(1)}, u32[]{:S(2)}, u32[]{:S(2)}) collective-permute-start(f32[24,1024]{1,0:T(8,128)S(1)} %get-tuple-element.22), channel_id=1, source_target_pairs={{0,2},{1,3},{2,0},{3,1},{4,6},{5,7},{6,4},{7,5},{8,10},{9,11},{10,... | collective-permute-start | bytes 294920 | tf_op jit(solution)/shard_map/ppermute | solution.py:229
  29.7 1.7 %collective-permute-start.17 = (f32[24,1024]{1,0:T(8,128)S(1)}, f32[24,1024]{1,0:T(8,128)S(1)}, u32[]{:S(2)}, u32[]{:S(2)}) collective-permute-start(f32[24,1024]{1,0:T(8,128)S(1)} %get-tuple-element.21), channel_id=1, source_target_pairs={{0,3},{1,0},{2,1},{3,2},{4,7},{5,4},{6,5},{7,6},{8,11},{9,8},{10,9... | collective-permute-start | bytes 294920 | tf_op jit(solution)/shard_map/ppermute | solution.py:229
  32.2 4.1 %collective-permute-done.16 = f32[24,1024]{1,0:T(8,128)S(1)} collective-permute-done((f32[24,1024]{1,0:T(8,128)S(1)}, f32[24,1024]{1,0:T(8,128)S(1)}, u32[]{:S(2)}, u32[]{:S(2)}) %collective-permute-start.16) | collective-permute-done | bytes 98336 | tf_op jit(solution)/shard_map/ppermute | solution.py:229
  36.7 2.1 %collective-permute-start.19 = (bf16[24,1024]{1,0:T(8,128)(2,1)S(1)}, bf16[24,1024]{1,0:T(8,128)(2,1)S(1)}, u32[]{:S(2)}, u32[]{:S(2)}) collective-permute-start(bf16[24,1024]{1,0:T(8,128)(2,1)S(1)} %get-tuple-element.26), channel_id=1, source_target_pairs={{0,2},{1,3},{2,0},{3,1},{4,6},{5,7},{6,4},{7,5},{8,10},{9,11},{10,... | collective-permute-start | bytes 147464 | tf_op jit(solution)/shard_map/ppermute | solution.py:188
  38.8 2.8 %collective-permute-start.18 = (bf16[24,1024]{1,0:T(8,128)(2,1)S(1)}, bf16[24,1024]{1,0:T(8,128)(2,1)S(1)}, u32[]{:S(2)}, u32[]{:S(2)}) collective-permute-start(bf16[24,1024]{1,0:T(8,128)(2,1)S(1)} %get-tuple-element.26), channel_id=1, source_target_pairs={{0,1},{1,0},{2,3},{3,2},{4,5},{5,4},{6,7},{7,6},{8,9},{9,8},{10,11... | collective-permute-start | bytes 147464 | tf_op jit(solution)/shard_map/ppermute | solution.py:189
  42.3 2.5 %collective-permute-start.20 = (bf16[24,1024]{1,0:T(8,128)(2,1)S(1)}, bf16[24,1024]{1,0:T(8,128)(2,1)S(1)}, u32[]{:S(2)}, u32[]{:S(2)}) collective-permute-start(bf16[24,1024]{1,0:T(8,128)(2,1)S(1)} %collective-permute-done.19), channel_id=1, source_target_pairs={{0,1},{1,0},{2,3},{3,2},{4,5},{5,4},{6,7},{7,6},{8,9},{9,8},{10,11... | collective-permute-start | bytes 147464 | tf_op jit(solution)/shard_map/ppermute | solution.py:189
  48.9 2.1 %collective-permute-done.9 = bf16[24,1024]{1,0:T(8,128)(2,1)S(1)} collective-permute-done((bf16[24,1024]{1,0:T(8,128)(2,1)S(1)}, bf16[24,1024]{1,0:T(8,128)(2,1)S(1)}, u32[]{:S(2)}, u32[]{:S(2)}) %collective-permute-start.9) | collective-permute-done | bytes 49184 | tf_op jit(solution)/shard_map/ppermute | solution.py:189
  51.7 1.6 %collective-permute-start.11 = (bf16[4,24,1024]{2,1,0:T(8,128)(2,1)S(1)}, bf16[4,24,1024]{2,1,0:T(8,128)(2,1)S(1)}, u32[]{:S(2)}, u32[]{:S(2)}) collective-permute-start(bf16[4,24,1024]{2,1,0:T(8,128)(2,1)S(1)} %get-tuple-element.31), channel_id=1, source_target_pairs={{0,8},{4,12},{8,0},{12,4},{1,9},{5,13},{9,1},{13,5},{2,10},{6,14},... | collective-permute-start | bytes 589832 | tf_op jit(solution)/shard_map/ppermute | solution.py:188
  55.9 1.5 %collective-permute-done.11 = bf16[4,24,1024]{2,1,0:T(8,128)(2,1)S(1)} collective-permute-done((bf16[4,24,1024]{2,1,0:T(8,128)(2,1)S(1)}, bf16[4,24,1024]{2,1,0:T(8,128)(2,1)S(1)}, u32[]{:S(2)}, u32[]{:S(2)}) %collective-permute-start.11) | collective-permute-done | bytes 196640 | tf_op jit(solution)/shard_map/ppermute | solution.py:188
  58.7 3.6 %collective-permute-done.22 = bf16[4,24,1024]{2,1,0:T(8,128)(2,1)S(1)} collective-permute-done((bf16[4,24,1024]{2,1,0:T(8,128)(2,1)S(1)}, bf16[4,24,1024]{2,1,0:T(8,128)(2,1)S(1)}, u32[]{:S(2)}, u32[]{:S(2)}) %collective-permute-start.22) | collective-permute-done | bytes 196640 | tf_op jit(solution)/shard_map/ppermute | solution.py:188
  66.0 8.2 %shard_map.104 = (f32[2,64,4096]{2,1,0:T(8,128)}, bf16[2,96,1024]{2,1,0:T(8,128)(2,1)}) custom-call(s32[1]{0:T(128)} %bitcast.section_ref, s32[4]{0:T(128)} %copy-done.2, f32[4,32]{1,0:T(4,128)} %maximum_tanh_fusion.gates_ref, bf16[2,64,4096]{2,1,0:T(8,128)(2,1)} %queries_ref.1, bf16[4,2,96,1024]{3,2,1,0:T(8,128)(2,1)} %broadcast_select_fusion.keyval_ref, ...), custom_call_target="tpu_custom_call" | custom-call | flops 1409286144 | bytes 6815744 | tf_op jit(solution)/shard_map/pallas_call | solution.py:139
  74.2 1.6 %gather_fusion.4 = bf16[8,24,1024]{2,1,0:T(8,128)(2,1)S(1)} fusion(bf16[8,24,1024]{2,1,0:T(8,128)(2,1)} %bitcast.165, s32[1024]{0:T(1024)S(1)} %pad_clamp_fusion.2), kind=kCustom, calls=%fused_computation.1.clone | custom fusion | bytes 786464 | tf_op jit(solution)/shard_map/jit(_take)/gather | solution.py:295
  76.3 1.6 %collective-permute-start.25 = (bf16[48,1024]{1,0:T(8,128)(2,1)S(1)}, bf16[48,1024]{1,0:T(8,128)(2,1)S(1)}, u32[]{:S(2)}, u32[]{:S(2)}) collective-permute-start(bf16[48,1024]{1,0:T(8,128)(2,1)S(1)} %get-tuple-element.16), channel_id=1, source_target_pairs={{0,2},{1,3},{2,0},{3,1},{4,6},{5,7},{6,4},{7,5},{8,10},{9,11},{10,... | collective-permute-start | bytes 294920 | tf_op jit(solution)/shard_map/ppermute | solution.py:229
  77.9 1.9 %collective-permute-start.26 = (bf16[48,1024]{1,0:T(8,128)(2,1)S(1)}, bf16[48,1024]{1,0:T(8,128)(2,1)S(1)}, u32[]{:S(2)}, u32[]{:S(2)}) collective-permute-start(bf16[48,1024]{1,0:T(8,128)(2,1)S(1)} %get-tuple-element.15), channel_id=1, source_target_pairs={{0,3},{1,0},{2,1},{3,2},{4,7},{5,4},{6,5},{7,6},{8,11},{9,8},{10,9... | collective-permute-start | bytes 294920 | tf_op jit(solution)/shard_map/ppermute | solution.py:229
  79.9 2.7 %collective-permute-done.24 = bf16[48,1024]{1,0:T(8,128)(2,1)S(1)} collective-permute-done((bf16[48,1024]{1,0:T(8,128)(2,1)S(1)}, bf16[48,1024]{1,0:T(8,128)(2,1)S(1)}, u32[]{:S(2)}, u32[]{:S(2)}) %collective-permute-start.24) | collective-permute-done | bytes 98336 | tf_op jit(solution)/shard_map/ppermute | solution.py:229
  82.6 3.0 %collective-permute-done.25 = bf16[48,1024]{1,0:T(8,128)(2,1)S(1)} collective-permute-done((bf16[48,1024]{1,0:T(8,128)(2,1)S(1)}, bf16[48,1024]{1,0:T(8,128)(2,1)S(1)}, u32[]{:S(2)}, u32[]{:S(2)}) %collective-permute-start.25) | collective-permute-done | bytes 98336 | tf_op jit(solution)/shard_map/ppermute | solution.py:229
  86.4 2.3 %collective-permute-start.28 = (bf16[2,24,1024]{2,1,0:T(8,128)(2,1)S(1)}, bf16[2,24,1024]{2,1,0:T(8,128)(2,1)S(1)}, u32[]{:S(2)}, u32[]{:S(2)}) collective-permute-start(bf16[2,24,1024]{2,1,0:T(8,128)(2,1)S(1)} %pad_maximum_fusion.6), channel_id=1, source_target_pairs={{0,2},{1,3},{2,0},{3,1},{4,6},{5,7},{6,4},{7,5},{8,10},{9,11},{10,... | collective-permute-start | bytes 294920 | tf_op jit(solution)/shard_map/ppermute | solution.py:188
  88.7 2.4 %collective-permute-start.27 = (bf16[2,24,1024]{2,1,0:T(8,128)(2,1)S(1)}, bf16[2,24,1024]{2,1,0:T(8,128)(2,1)S(1)}, u32[]{:S(2)}, u32[]{:S(2)}) collective-permute-start(bf16[2,24,1024]{2,1,0:T(8,128)(2,1)S(1)} %pad_maximum_fusion.6), channel_id=1, source_target_pairs={{0,1},{1,0},{2,3},{3,2},{4,5},{5,4},{6,7},{7,6},{8,9},{9,8},{10,11... | collective-permute-start | bytes 294920 | tf_op jit(solution)/shard_map/ppermute | solution.py:189
  92.2 4.1 %collective-permute-start.29 = (bf16[2,24,1024]{2,1,0:T(8,128)(2,1)S(1)}, bf16[2,24,1024]{2,1,0:T(8,128)(2,1)S(1)}, u32[]{:S(2)}, u32[]{:S(2)}) collective-permute-start(bf16[2,24,1024]{2,1,0:T(8,128)(2,1)S(1)} %collective-permute-done.28), channel_id=1, source_target_pairs={{0,1},{1,0},{2,3},{3,2},{4,5},{5,4},{6,7},{7,6},{8,9},{9,8},{10,11... | collective-permute-start | bytes 294920 | tf_op jit(solution)/shard_map/ppermute | solution.py:189
  96.2 2.6 %collective-permute-done.29 = bf16[2,24,1024]{2,1,0:T(8,128)(2,1)S(1)} collective-permute-done((bf16[2,24,1024]{2,1,0:T(8,128)(2,1)S(1)}, bf16[2,24,1024]{2,1,0:T(8,128)(2,1)S(1)}, u32[]{:S(2)}, u32[]{:S(2)}) %collective-permute-start.29) | collective-permute-done | bytes 98336 | tf_op jit(solution)/shard_map/ppermute | solution.py:189
  100.3 3.7 %fusion.6 = bf16[192,2048]{1,0:T(8,128)(2,1)S(1)} fusion(bf16[192,1024]{1,0:T(8,128)(2,1)S(1)} %bitcast.151, bf16[1,2048,1024]{2,1,0:T(8,128)(2,1)} %param.14), kind=kOutput, calls=%fused_computation.12 | convolution fusion | flops 805699584 | bytes 5373952 | tf_op jit(solution)/shard_map/dot_general | solution.py:367
  104.2 1.7 %collective-permute-done.30 = bf16[2,2,24,2048]{3,2,1,0:T(8,128)(2,1)S(1)} collective-permute-done((bf16[2,2,24,2048]{3,2,1,0:T(8,128)(2,1)S(1)}, bf16[2,2,24,2048]{3,2,1,0:T(8,128)(2,1)S(1)}, u32[]{:S(2)}, u32[]{:S(2)}) %collective-permute-start.30) | collective-permute-done | bytes 393248 | tf_op jit(solution)/shard_map/ppermute | solution.py:216
  106.0 5.7 %collective-permute-start.31 = (bf16[2,24,2048]{2,1,0:T(8,128)(2,1)S(1)}, bf16[2,24,2048]{2,1,0:T(8,128)(2,1)S(1)}, u32[]{:S(2)}, u32[]{:S(2)}) collective-permute-start(bf16[2,24,2048]{2,1,0:T(8,128)(2,1)S(1)} %fusion.9), channel_id=1, source_target_pairs={{0,8},{4,12},{8,0},{12,4},{1,9},{5,13},{9,1},{13,5},{2,10},{6,14},... | collective-permute-start | bytes 589832 | tf_op jit(solution)/shard_map/ppermute | solution.py:220
  111.7 5.2 %collective-permute-done.31 = bf16[2,24,2048]{2,1,0:T(8,128)(2,1)S(1)} collective-permute-done((bf16[2,24,2048]{2,1,0:T(8,128)(2,1)S(1)}, bf16[2,24,2048]{2,1,0:T(8,128)(2,1)S(1)}, u32[]{:S(2)}, u32[]{:S(2)}) %collective-permute-start.31) | collective-permute-done | bytes 196640 | tf_op jit(solution)/shard_map/ppermute | solution.py:220
  (144 shorter events, 25.3 us)
Async XLA Ops:
  0.6 6.1 %collective-permute-start.3 = (bf16[2,24,2048]{2,1,0:T(8,128)(2,1)}, bf16[2,24,2048]{2,1,0:T(8,128)(2,1)S(1)}, u32[]{:S(2)}, u32[]{:S(2)}) collective-permute-start(bf16[2,24,2048]{2,1,0:T(8,128)(2,1)} %param.13), channel_id=1, source_target_pairs={{0,4},{4,0},{8,12},{12,8},{1,5},{5,1},{9,13},{13,9},{2,6},{6,2},{1... | collective-permute-start | bytes 589832 | tf_op jit(solution)/shard_map/ppermute | solution.py:189
  1.1 15.7 %collective-permute-start.13 = (bf16[2,24,2048]{2,1,0:T(8,128)(2,1)}, bf16[2,24,2048]{2,1,0:T(8,128)(2,1)S(1)}, u32[]{:S(2)}, u32[]{:S(2)}) collective-permute-start(bf16[2,24,2048]{2,1,0:T(8,128)(2,1)} %param.13), channel_id=1, source_target_pairs={{0,8},{4,12},{8,0},{12,4},{1,9},{5,13},{9,1},{13,5},{2,10},{6,14},... | collective-permute-start | bytes 589832 | tf_op jit(solution)/shard_map/ppermute | solution.py:188
  5.1 48.1 %collective-permute-start.1 = (f32[4128]{0:T(1024)S(1)}, f32[4128]{0:T(1024)S(1)}, u32[]{:S(2)}, u32[]{:S(2)}) collective-permute-start(f32[4128]{0:T(1024)S(1)} %reduce), channel_id=1, source_target_pairs={{0,8},{4,12},{8,0},{12,4},{1,9},{5,13},{9,1},{13,5},{2,10},{6,14},... | collective-permute-start | bytes 49544 | tf_op jit(solution)/shard_map/ppermute | solution.py:188
  10.8 7.8 %collective-permute-start.4 = (f32[24,1024]{1,0:T(8,128)S(1)}, f32[24,1024]{1,0:T(8,128)S(1)}, u32[]{:S(2)}, u32[]{:S(2)}) collective-permute-start(f32[24,1024]{1,0:T(8,128)S(1)} %get-tuple-element.17), channel_id=1, source_target_pairs={{0,1},{1,2},{2,3},{3,0},{4,5},{5,6},{6,7},{7,4},{8,9},{9,10},{10,1... | collective-permute-start | bytes 294920 | tf_op jit(solution)/shard_map/ppermute | solution.py:229
  12.9 9.2 %collective-permute-start.5 = (f32[24,1024]{1,0:T(8,128)S(1)}, f32[24,1024]{1,0:T(8,128)S(1)}, u32[]{:S(2)}, u32[]{:S(2)}) collective-permute-start(f32[24,1024]{1,0:T(8,128)S(1)} %get-tuple-element.19), channel_id=1, source_target_pairs={{0,2},{1,3},{2,0},{3,1},{4,6},{5,7},{6,4},{7,5},{8,10},{9,11},{10,... | collective-permute-start | bytes 294920 | tf_op jit(solution)/shard_map/ppermute | solution.py:229
  15.5 6.6 %collective-permute-start.6 = (f32[24,1024]{1,0:T(8,128)S(1)}, f32[24,1024]{1,0:T(8,128)S(1)}, u32[]{:S(2)}, u32[]{:S(2)}) collective-permute-start(f32[24,1024]{1,0:T(8,128)S(1)} %get-tuple-element.18), channel_id=1, source_target_pairs={{0,3},{1,0},{2,1},{3,2},{4,7},{5,4},{6,5},{7,6},{8,11},{9,8},{10,9... | collective-permute-start | bytes 294920 | tf_op jit(solution)/shard_map/ppermute | solution.py:229
  16.9 37.9 %collective-permute-start = (f32[4128]{0:T(1024)S(1)}, f32[4128]{0:T(1024)S(1)}, u32[]{:S(2)}, u32[]{:S(2)}) collective-permute-start(f32[4128]{0:T(1024)S(1)} %reduce), channel_id=1, source_target_pairs={{0,4},{4,0},{8,12},{12,8},{1,5},{5,1},{9,13},{13,9},{2,6},{6,2},{1... | collective-permute-start | bytes 49544 | tf_op jit(solution)/shard_map/ppermute | solution.py:189
  18.6 3.7 %collective-permute-start.14 = (bf16[2,24,2048]{2,1,0:T(8,128)(2,1)S(1)}, bf16[2,24,2048]{2,1,0:T(8,128)(2,1)S(1)}, u32[]{:S(2)}, u32[]{:S(2)}) collective-permute-start(bf16[2,24,2048]{2,1,0:T(8,128)(2,1)S(1)} %collective-permute-done.13), channel_id=1, source_target_pairs={{0,4},{4,0},{8,12},{12,8},{1,5},{5,1},{9,13},{13,9},{2,6},{6,2},{1... | collective-permute-start | bytes 589832 | tf_op jit(solution)/shard_map/ppermute | solution.py:189
  25.4 6.7 %collective-permute-start.15 = (f32[24,1024]{1,0:T(8,128)S(1)}, f32[24,1024]{1,0:T(8,128)S(1)}, u32[]{:S(2)}, u32[]{:S(2)}) collective-permute-start(f32[24,1024]{1,0:T(8,128)S(1)} %get-tuple-element.20), channel_id=1, source_target_pairs={{0,1},{1,2},{2,3},{3,0},{4,5},{5,6},{6,7},{7,4},{8,9},{9,10},{10,1... | collective-permute-start | bytes 294920 | tf_op jit(solution)/shard_map/ppermute | solution.py:229
  28.1 8.2 %collective-permute-start.16 = (f32[24,1024]{1,0:T(8,128)S(1)}, f32[24,1024]{1,0:T(8,128)S(1)}, u32[]{:S(2)}, u32[]{:S(2)}) collective-permute-start(f32[24,1024]{1,0:T(8,128)S(1)} %get-tuple-element.22), channel_id=1, source_target_pairs={{0,2},{1,3},{2,0},{3,1},{4,6},{5,7},{6,4},{7,5},{8,10},{9,11},{10,... | collective-permute-start | bytes 294920 | tf_op jit(solution)/shard_map/ppermute | solution.py:229
  29.7 6.6 %collective-permute-start.17 = (f32[24,1024]{1,0:T(8,128)S(1)}, f32[24,1024]{1,0:T(8,128)S(1)}, u32[]{:S(2)}, u32[]{:S(2)}) collective-permute-start(f32[24,1024]{1,0:T(8,128)S(1)} %get-tuple-element.21), channel_id=1, source_target_pairs={{0,3},{1,0},{2,1},{3,2},{4,7},{5,4},{6,5},{7,6},{8,11},{9,8},{10,9... | collective-permute-start | bytes 294920 | tf_op jit(solution)/shard_map/ppermute | solution.py:229
  36.7 5.5 %collective-permute-start.19 = (bf16[24,1024]{1,0:T(8,128)(2,1)S(1)}, bf16[24,1024]{1,0:T(8,128)(2,1)S(1)}, u32[]{:S(2)}, u32[]{:S(2)}) collective-permute-start(bf16[24,1024]{1,0:T(8,128)(2,1)S(1)} %get-tuple-element.26), channel_id=1, source_target_pairs={{0,2},{1,3},{2,0},{3,1},{4,6},{5,7},{6,4},{7,5},{8,10},{9,11},{10,... | collective-permute-start | bytes 147464 | tf_op jit(solution)/shard_map/ppermute | solution.py:188
  38.8 6.0 %collective-permute-start.18 = (bf16[24,1024]{1,0:T(8,128)(2,1)S(1)}, bf16[24,1024]{1,0:T(8,128)(2,1)S(1)}, u32[]{:S(2)}, u32[]{:S(2)}) collective-permute-start(bf16[24,1024]{1,0:T(8,128)(2,1)S(1)} %get-tuple-element.26), channel_id=1, source_target_pairs={{0,1},{1,0},{2,3},{3,2},{4,5},{5,4},{6,7},{7,6},{8,9},{9,8},{10,11... | collective-permute-start | bytes 147464 | tf_op jit(solution)/shard_map/ppermute | solution.py:189
  41.6 5.4 %collective-permute-start.8 = (bf16[24,1024]{1,0:T(8,128)(2,1)S(1)}, bf16[24,1024]{1,0:T(8,128)(2,1)S(1)}, u32[]{:S(2)}, u32[]{:S(2)}) collective-permute-start(bf16[24,1024]{1,0:T(8,128)(2,1)S(1)} %get-tuple-element.37), channel_id=1, source_target_pairs={{0,2},{1,3},{2,0},{3,1},{4,6},{5,7},{6,4},{7,5},{8,10},{9,11},{10,... | collective-permute-start | bytes 147464 | tf_op jit(solution)/shard_map/ppermute | solution.py:188
  42.3 4.9 %collective-permute-start.20 = (bf16[24,1024]{1,0:T(8,128)(2,1)S(1)}, bf16[24,1024]{1,0:T(8,128)(2,1)S(1)}, u32[]{:S(2)}, u32[]{:S(2)}) collective-permute-start(bf16[24,1024]{1,0:T(8,128)(2,1)S(1)} %collective-permute-done.19), channel_id=1, source_target_pairs={{0,1},{1,0},{2,3},{3,2},{4,5},{5,4},{6,7},{7,6},{8,9},{9,8},{10,11... | collective-permute-start | bytes 147464 | tf_op jit(solution)/shard_map/ppermute | solution.py:189
  44.8 4.2 %collective-permute-start.7 = (bf16[24,1024]{1,0:T(8,128)(2,1)S(1)}, bf16[24,1024]{1,0:T(8,128)(2,1)S(1)}, u32[]{:S(2)}, u32[]{:S(2)}) collective-permute-start(bf16[24,1024]{1,0:T(8,128)(2,1)S(1)} %get-tuple-element.37), channel_id=1, source_target_pairs={{0,1},{1,0},{2,3},{3,2},{4,5},{5,4},{6,7},{7,6},{8,9},{9,8},{10,11... | collective-permute-start | bytes 147464 | tf_op jit(solution)/shard_map/ppermute | solution.py:189
  46.9 4.1 %collective-permute-start.9 = (bf16[24,1024]{1,0:T(8,128)(2,1)S(1)}, bf16[24,1024]{1,0:T(8,128)(2,1)S(1)}, u32[]{:S(2)}, u32[]{:S(2)}) collective-permute-start(bf16[24,1024]{1,0:T(8,128)(2,1)S(1)} %collective-permute-done.8), channel_id=1, source_target_pairs={{0,1},{1,0},{2,3},{3,2},{4,5},{5,4},{6,7},{7,6},{8,9},{9,8},{10,11... | collective-permute-start | bytes 147464 | tf_op jit(solution)/shard_map/ppermute | solution.py:189
  51.7 5.7 %collective-permute-start.11 = (bf16[4,24,1024]{2,1,0:T(8,128)(2,1)S(1)}, bf16[4,24,1024]{2,1,0:T(8,128)(2,1)S(1)}, u32[]{:S(2)}, u32[]{:S(2)}) collective-permute-start(bf16[4,24,1024]{2,1,0:T(8,128)(2,1)S(1)} %get-tuple-element.31), channel_id=1, source_target_pairs={{0,8},{4,12},{8,0},{12,4},{1,9},{5,13},{9,1},{13,5},{2,10},{6,14},... | collective-permute-start | bytes 589832 | tf_op jit(solution)/shard_map/ppermute | solution.py:188
  53.3 1.5 %collective-permute-start.2 = (f32[4128]{0:T(1024)S(1)}, f32[4128]{0:T(1024)S(1)}, u32[]{:S(2)}, u32[]{:S(2)}) collective-permute-start(f32[4128]{0:T(1024)S(1)} %collective-permute-done.1), channel_id=1, source_target_pairs={{0,4},{4,0},{8,12},{12,8},{1,5},{5,1},{9,13},{13,9},{2,6},{6,2},{1... | collective-permute-start | bytes 49544 | tf_op jit(solution)/shard_map/ppermute | solution.py:189
  54.8 8.0 %collective-permute-start.10 = (bf16[4,24,1024]{2,1,0:T(8,128)(2,1)S(1)}, bf16[4,24,1024]{2,1,0:T(8,128)(2,1)S(1)}, u32[]{:S(2)}, u32[]{:S(2)}) collective-permute-start(bf16[4,24,1024]{2,1,0:T(8,128)(2,1)S(1)} %get-tuple-element.31), channel_id=1, source_target_pairs={{0,4},{4,0},{8,12},{12,8},{1,5},{5,1},{9,13},{13,9},{2,6},{6,2},{1... | collective-permute-start | bytes 589832 | tf_op jit(solution)/shard_map/ppermute | solution.py:189
  55.4 6.9 %collective-permute-start.22 = (bf16[4,24,1024]{2,1,0:T(8,128)(2,1)S(1)}, bf16[4,24,1024]{2,1,0:T(8,128)(2,1)S(1)}, u32[]{:S(2)}, u32[]{:S(2)}) collective-permute-start(bf16[4,24,1024]{2,1,0:T(8,128)(2,1)S(1)} %get-tuple-element.32), channel_id=1, source_target_pairs={{0,8},{4,12},{8,0},{12,4},{1,9},{5,13},{9,1},{13,5},{2,10},{6,14},... | collective-permute-start | bytes 589832 | tf_op jit(solution)/shard_map/ppermute | solution.py:188
  57.5 5.4 %collective-permute-start.12 = (bf16[4,24,1024]{2,1,0:T(8,128)(2,1)S(1)}, bf16[4,24,1024]{2,1,0:T(8,128)(2,1)S(1)}, u32[]{:S(2)}, u32[]{:S(2)}) collective-permute-start(bf16[4,24,1024]{2,1,0:T(8,128)(2,1)S(1)} %collective-permute-done.11), channel_id=1, source_target_pairs={{0,4},{4,0},{8,12},{12,8},{1,5},{5,1},{9,13},{13,9},{2,6},{6,2},{1... | collective-permute-start | bytes 589832 | tf_op jit(solution)/shard_map/ppermute | solution.py:189
  58.2 4.8 %collective-permute-start.21 = (bf16[4,24,1024]{2,1,0:T(8,128)(2,1)S(1)}, bf16[4,24,1024]{2,1,0:T(8,128)(2,1)S(1)}, u32[]{:S(2)}, u32[]{:S(2)}) collective-permute-start(bf16[4,24,1024]{2,1,0:T(8,128)(2,1)S(1)} %get-tuple-element.32), channel_id=1, source_target_pairs={{0,4},{4,0},{8,12},{12,8},{1,5},{5,1},{9,13},{13,9},{2,6},{6,2},{1... | collective-permute-start | bytes 589832 | tf_op jit(solution)/shard_map/ppermute | solution.py:189
  62.2 1.4 %collective-permute-start.23 = (bf16[4,24,1024]{2,1,0:T(8,128)(2,1)S(1)}, bf16[4,24,1024]{2,1,0:T(8,128)(2,1)S(1)}, u32[]{:S(2)}, u32[]{:S(2)}) collective-permute-start(bf16[4,24,1024]{2,1,0:T(8,128)(2,1)S(1)} %collective-permute-done.22), channel_id=1, source_target_pairs={{0,4},{4,0},{8,12},{12,8},{1,5},{5,1},{9,13},{13,9},{2,6},{6,2},{1... | collective-permute-start | bytes 589832 | tf_op jit(solution)/shard_map/ppermute | solution.py:189
  75.9 6.6 %collective-permute-start.24 = (bf16[48,1024]{1,0:T(8,128)(2,1)S(1)}, bf16[48,1024]{1,0:T(8,128)(2,1)S(1)}, u32[]{:S(2)}, u32[]{:S(2)}) collective-permute-start(bf16[48,1024]{1,0:T(8,128)(2,1)S(1)} %get-tuple-element.14), channel_id=1, source_target_pairs={{0,1},{1,2},{2,3},{3,0},{4,5},{5,6},{6,7},{7,4},{8,9},{9,10},{10,1... | collective-permute-start | bytes 294920 | tf_op jit(solution)/shard_map/ppermute | solution.py:229
  76.3 9.2 %collective-permute-start.25 = (bf16[48,1024]{1,0:T(8,128)(2,1)S(1)}, bf16[48,1024]{1,0:T(8,128)(2,1)S(1)}, u32[]{:S(2)}, u32[]{:S(2)}) collective-permute-start(bf16[48,1024]{1,0:T(8,128)(2,1)S(1)} %get-tuple-element.16), channel_id=1, source_target_pairs={{0,2},{1,3},{2,0},{3,1},{4,6},{5,7},{6,4},{7,5},{8,10},{9,11},{10,... | collective-permute-start | bytes 294920 | tf_op jit(solution)/shard_map/ppermute | solution.py:229
  77.9 7.9 %collective-permute-start.26 = (bf16[48,1024]{1,0:T(8,128)(2,1)S(1)}, bf16[48,1024]{1,0:T(8,128)(2,1)S(1)}, u32[]{:S(2)}, u32[]{:S(2)}) collective-permute-start(bf16[48,1024]{1,0:T(8,128)(2,1)S(1)} %get-tuple-element.15), channel_id=1, source_target_pairs={{0,3},{1,0},{2,1},{3,2},{4,7},{5,4},{6,5},{7,6},{8,11},{9,8},{10,9... | collective-permute-start | bytes 294920 | tf_op jit(solution)/shard_map/ppermute | solution.py:229
  86.4 5.7 %collective-permute-start.28 = (bf16[2,24,1024]{2,1,0:T(8,128)(2,1)S(1)}, bf16[2,24,1024]{2,1,0:T(8,128)(2,1)S(1)}, u32[]{:S(2)}, u32[]{:S(2)}) collective-permute-start(bf16[2,24,1024]{2,1,0:T(8,128)(2,1)S(1)} %pad_maximum_fusion.6), channel_id=1, source_target_pairs={{0,2},{1,3},{2,0},{3,1},{4,6},{5,7},{6,4},{7,5},{8,10},{9,11},{10,... | collective-permute-start | bytes 294920 | tf_op jit(solution)/shard_map/ppermute | solution.py:188
  88.7 7.5 %collective-permute-start.27 = (bf16[2,24,1024]{2,1,0:T(8,128)(2,1)S(1)}, bf16[2,24,1024]{2,1,0:T(8,128)(2,1)S(1)}, u32[]{:S(2)}, u32[]{:S(2)}) collective-permute-start(bf16[2,24,1024]{2,1,0:T(8,128)(2,1)S(1)} %pad_maximum_fusion.6), channel_id=1, source_target_pairs={{0,1},{1,0},{2,3},{3,2},{4,5},{5,4},{6,7},{7,6},{8,9},{9,8},{10,11... | collective-permute-start | bytes 294920 | tf_op jit(solution)/shard_map/ppermute | solution.py:189
  92.2 6.7 %collective-permute-start.29 = (bf16[2,24,1024]{2,1,0:T(8,128)(2,1)S(1)}, bf16[2,24,1024]{2,1,0:T(8,128)(2,1)S(1)}, u32[]{:S(2)}, u32[]{:S(2)}) collective-permute-start(bf16[2,24,1024]{2,1,0:T(8,128)(2,1)S(1)} %collective-permute-done.28), channel_id=1, source_target_pairs={{0,1},{1,0},{2,3},{3,2},{4,5},{5,4},{6,7},{7,6},{8,9},{9,8},{10,11... | collective-permute-start | bytes 294920 | tf_op jit(solution)/shard_map/ppermute | solution.py:189
  104.1 1.8 %collective-permute-start.30 = (bf16[2,2,24,2048]{3,2,1,0:T(8,128)(2,1)S(1)}, bf16[2,2,24,2048]{3,2,1,0:T(8,128)(2,1)S(1)}, u32[]{:S(2)}, u32[]{:S(2)}) collective-permute-start(bf16[2,2,24,2048]{3,2,1,0:T(8,128)(2,1)S(1)} %pad_maximum_fusion.2), channel_id=1, source_target_pairs={{0,4},{4,0},{8,12},{12,8},{1,5},{5,1},{9,13},{13,9},{2,6},{6,2},{1... | collective-permute-start | bytes 1179656 | tf_op jit(solution)/shard_map/ppermute | solution.py:216
  106.0 10.9 %collective-permute-start.31 = (bf16[2,24,2048]{2,1,0:T(8,128)(2,1)S(1)}, bf16[2,24,2048]{2,1,0:T(8,128)(2,1)S(1)}, u32[]{:S(2)}, u32[]{:S(2)}) collective-permute-start(bf16[2,24,2048]{2,1,0:T(8,128)(2,1)S(1)} %fusion.9), channel_id=1, source_target_pairs={{0,8},{4,12},{8,0},{12,4},{1,9},{5,13},{9,1},{13,5},{2,10},{6,14},... | collective-permute-start | bytes 589832 | tf_op jit(solution)/shard_map/ppermute | solution.py:220
  (3 other events, 26.8 us)

commit v13 on v10

--- a/solution.py
+++ b/solution.py
@@ -331,20 +331,50 @@
         same_document,
         cotangent[0],
     )
-    grad_rows = scatter_blocks(to_owned(grad_local), "shard", False).reshape(-1, pair_width)
+    if phased and shard_count <= 8:
+        shard_index = lax.axis_index("shard")
+        grad_blocks = grad_local.reshape(micro_count * section_count, owned, pair_width)
+        held_flat = held.reshape(-1)
+
+        def owned_rows(j):
+            return jnp.concatenate(
+                [
+                    lax.dynamic_index_in_dim(grad_blocks, held_flat[2 * j + h], 0, keepdims=False)
+                    for h in range(2)
+                ],
+                axis=0,
+            )
+
+        grad_rows = owned_rows(shard_index).astype(jnp.float32)
+        for d in range(1, shard_count):
+            grad_rows = grad_rows + lax.ppermute(
+                owned_rows((shard_index + d) % shard_count),
+                "shard",
+                [(i, (i + d) % shard_count) for i in range(shard_count)],
+            ).astype(jnp.float32)
+    else:
+        grad_rows = scatter_blocks(to_owned(grad_local), "shard", False).reshape(-1, pair_width)
     key_portion = norm_gradient(
         raw_rows[:, :key_width], key_norm_gain[0], grad_rows[:, :key_width], keyval_heads
     )
     raw_grad_rows = jnp.concatenate([key_portion, grad_rows[:, key_width:]], axis=1).astype(
         jnp.bfloat16
     )
-    raw_grad = to_natural(raw_grad_rows)
     owned = image_count // section_count
-    raw_grad = (
-        raw_grad.reshape(micro_count, section_count, owned, 2 * key_width)
-        .transpose(1, 0, 2, 3)
-        .reshape(total_rows, 2 * key_width)
-    )
+    if phased:
+        raw_blocks = in_order(raw_grad_rows.reshape(2, owned, pair_width), "shard")
+        raw_grad = jnp.take(
+            raw_blocks.reshape(2 * shard_count, owned, pair_width),
+            natural.T.reshape(-1),
+            axis=0,
+        ).reshape(total_rows, pair_width)
+    else:
+        raw_grad = to_natural(raw_grad_rows)
+        raw_grad = (
+            raw_grad.reshape(micro_count, section_count, owned, 2 * key_width)
+            .transpose(1, 0, 2, 3)
+            .reshape(total_rows, 2 * key_width)
+        )
     image_part = lax.dot_general(
         raw_grad, weights, (((1,), (1,)), ((), ())), preferred_element_type=jnp.float32
     )

time: 113 us -> 122 us (1.080)
  between operations: 1.12 us -> 16.3 us
  waiting for transfers between devices: 43 us -> 33.6 us
  starting transfers between devices: 38.6 us -> 41.7 us
    ppermute x9 -> x6, waiting for transfers between devices: 14.8 us -> 7.26 us  [scatter_blocks(): lax.ppermute(part, axis, [(i, (i + d) % count) for i in range(count)])]
    ppermute x5, waiting for transfers between devices: 13.6 us -> 6.87 us  [gather_blocks(): across = lax.ppermute(block, axis, [(i, i ^ 2) for i in range(count)])]
    ppermute x0 -> x3, waiting for transfers between devices: none -> 4.71 us  [per_device(): lax.ppermute(owned_rows((shard_index + d) % shard_count), 'shard', [(i, (...]
    ppermute x9 -> x6, starting transfers between devices: 19.1 us -> 14.9 us  [scatter_blocks(): lax.ppermute(part, axis, [(i, (i + d) % count) for i in range(count)])]
    ppermute x0 -> x3, starting transfers between devices: none -> 4.1 us  [per_device(): lax.ppermute(owned_rows((shard_index + d) % shard_count), 'shard', [(i, (...]
    ppermute x5, starting transfers between devices: 3.43 us -> 5.62 us  [gather_blocks(): lax.ppermute(block, axis, partner)]
  transfers between devices with their start and end apart: 26 -> 26, of which waited for: 16 -> 15; matrix products, arithmetic and copies ran while one was open for 11% -> 11% of each run, Pallas kernels for 0% -> 0%
where the time goes in v13:
time: 122 us
  starting transfers between devices  41.7 us (34%)
  waiting for transfers between devices  33.6 us (28%)
  between operations  16.3 us (13%)
  Pallas kernels  8.22 us (7%)
  local copies, waits for them, and re-layouts  7.78 us (6%)
  matrix products  7.55 us (6%)
  other arithmetic  6.49 us (5%)
    ppermute x6, starting transfers between devices, scatter_blocks(): lax.ppermute(part, axis, [(i, (i + d) % count) for i in range(count)])  14.9 us
    pallas_call x1, Pallas kernels, attention_layers(): pl.pallas_call(functools.partial(attention_kernel, head_count=head_count,...  8.22 us
    ppermute x5, starting transfers between devices, gather_blocks(): across = lax.ppermute(block, axis, [(i, i ^ 2) for i in range(count)])  7.41 us
    ppermute x6, waiting for transfers between devices, scatter_blocks(): lax.ppermute(part, axis, [(i, (i + d) % count) for i in range(count)])  7.26 us
    ppermute x5, waiting for transfers between devices, gather_blocks(): across = lax.ppermute(block, axis, [(i, i ^ 2) for i in range(count)])  6.87 us
    ppermute x5, waiting for transfers between devices, gather_blocks(): lax.ppermute(across, axis, partner)  6.8 us
    ppermute x5, starting transfers between devices, gather_blocks(): lax.ppermute(block, axis, partner)  5.62 us
    ppermute x1, starting transfers between devices, scatter_blocks(): back = lax.ppermute(theirs, axis, [(i, i ^ 2) for i in range(count)])  5.36 us
  transfers between devices with their start and end apart: 26, of which 15 were waited for; matrix products, arithmetic and copies ran while one was open for 11% of the time, Pallas kernels for 0%

profile of v13, /device:TPU:0, one launch (start us, length us, event | category | flops | bytes accessed | tf_op | source)
XLA Modules:
  0.0 121.6 jit_solution(1643633436668245213)
XLA Ops:
  1.1 2.6 %collective-permute-start.7 = (bf16[2,24,2048]{2,1,0:T(8,128)(2,1)}, bf16[2,24,2048]{2,1,0:T(8,128)(2,1)S(1)}, u32[]{:S(2)}, u32[]{:S(2)}) collective-permute-start(bf16[2,24,2048]{2,1,0:T(8,128)(2,1)} %param.13), channel_id=1, source_target_pairs={{0,8},{4,12},{8,0},{12,4},{1,9},{5,13},{9,1},{13,5},{2,10},{6,14},... | collective-permute-start | bytes 589832 | tf_op jit(solution)/shard_map/ppermute | solution.py:188
  6.5 1.0 maximum_bitcast_fusion
  7.5 2.2 %collective-permute-done.7 = bf16[2,24,2048]{2,1,0:T(8,128)(2,1)S(1)} collective-permute-done((bf16[2,24,2048]{2,1,0:T(8,128)(2,1)}, bf16[2,24,2048]{2,1,0:T(8,128)(2,1)S(1)}, u32[]{:S(2)}, u32[]{:S(2)}) %collective-permute-start.7) | collective-permute-done | bytes 196640 | tf_op jit(solution)/shard_map/ppermute | solution.py:188
  9.6 3.0 %fusion.2 = f32[4,24,1024]{2,1,0:T(8,128)S(1)} fusion(bf16[4,24,2048]{2,1,0:T(8,128)(2,1)S(1)} %bitcast.132, bf16[1,2048,1024]{2,1,0:T(8,128)(2,1)} %param.14), kind=kOutput, calls=%fused_computation.6 | convolution fusion | flops 402653184 | bytes 4980736 | tf_op jit(solution)/shard_map/dot_general | solution.py:273
  12.7 1.9 %collective-permute-start.4 = (f32[24,1024]{1,0:T(8,128)S(1)}, f32[24,1024]{1,0:T(8,128)S(1)}, u32[]{:S(2)}, u32[]{:S(2)}) collective-permute-start(f32[24,1024]{1,0:T(8,128)S(1)} %get-tuple-element.18), channel_id=1, source_target_pairs={{0,1},{1,2},{2,3},{3,0},{4,5},{5,6},{6,7},{7,4},{8,9},{9,10},{10,1... | collective-permute-start | bytes 294920 | tf_op jit(solution)/shard_map/ppermute | solution.py:229
  14.6 2.6 %collective-permute-start.5 = (f32[24,1024]{1,0:T(8,128)S(1)}, f32[24,1024]{1,0:T(8,128)S(1)}, u32[]{:S(2)}, u32[]{:S(2)}) collective-permute-start(f32[24,1024]{1,0:T(8,128)S(1)} %get-tuple-element.20), channel_id=1, source_target_pairs={{0,2},{1,3},{2,0},{3,1},{4,6},{5,7},{6,4},{7,5},{8,10},{9,11},{10,... | collective-permute-start | bytes 294920 | tf_op jit(solution)/shard_map/ppermute | solution.py:229
  17.2 1.4 %collective-permute-start.6 = (f32[24,1024]{1,0:T(8,128)S(1)}, f32[24,1024]{1,0:T(8,128)S(1)}, u32[]{:S(2)}, u32[]{:S(2)}) collective-permute-start(f32[24,1024]{1,0:T(8,128)S(1)} %get-tuple-element.19), channel_id=1, source_target_pairs={{0,3},{1,0},{2,1},{3,2},{4,7},{5,4},{6,5},{7,6},{8,11},{9,8},{10,9... | collective-permute-start | bytes 294920 | tf_op jit(solution)/shard_map/ppermute | solution.py:229
  20.3 6.1 %collective-permute-start.10 = (f32[24,1024]{1,0:T(8,128)S(1)}, f32[24,1024]{1,0:T(8,128)S(1)}, u32[]{:S(2)}, u32[]{:S(2)}) collective-permute-start(f32[24,1024]{1,0:T(8,128)S(1)} %get-tuple-element.23), channel_id=1, source_target_pairs={{0,2},{1,3},{2,0},{3,1},{4,6},{5,7},{6,4},{7,5},{8,10},{9,11},{10,... | collective-permute-start | bytes 294920 | tf_op jit(solution)/shard_map/ppermute | solution.py:229
  26.4 3.0 %collective-permute-start.11 = (f32[24,1024]{1,0:T(8,128)S(1)}, f32[24,1024]{1,0:T(8,128)S(1)}, u32[]{:S(2)}, u32[]{:S(2)}) collective-permute-start(f32[24,1024]{1,0:T(8,128)S(1)} %get-tuple-element.22), channel_id=1, source_target_pairs={{0,3},{1,0},{2,1},{3,2},{4,7},{5,4},{6,5},{7,6},{8,11},{9,8},{10,9... | collective-permute-start | bytes 294920 | tf_op jit(solution)/shard_map/ppermute | solution.py:229
  29.5 1.2 collective-permute-done.10
  30.7 1.4 %collective-permute-done.11 = f32[24,1024]{1,0:T(8,128)S(1)} collective-permute-done((f32[24,1024]{1,0:T(8,128)S(1)}, f32[24,1024]{1,0:T(8,128)S(1)}, u32[]{:S(2)}, u32[]{:S(2)}) %collective-permute-start.11) | collective-permute-done | bytes 98336 | tf_op jit(solution)/shard_map/ppermute | solution.py:229
  32.1 3.8 %collective-permute-done.9 = f32[24,1024]{1,0:T(8,128)S(1)} collective-permute-done((f32[24,1024]{1,0:T(8,128)S(1)}, f32[24,1024]{1,0:T(8,128)S(1)}, u32[]{:S(2)}, u32[]{:S(2)}) %collective-permute-start.9) | collective-permute-done | bytes 98336 | tf_op jit(solution)/shard_map/ppermute | solution.py:229
  37.5 4.7 %collective-permute-done.13 = bf16[2,24,1024]{2,1,0:T(8,128)(2,1)S(1)} collective-permute-done((bf16[2,24,1024]{2,1,0:T(8,128)(2,1)S(1)}, bf16[2,24,1024]{2,1,0:T(8,128)(2,1)S(1)}, u32[]{:S(2)}, u32[]{:S(2)}) %collective-permute-start.13) | collective-permute-done | bytes 98336 | tf_op jit(solution)/shard_map/ppermute | solution.py:188
  42.2 1.0 collective-permute-done.12
  43.2 3.6 %collective-permute-done.14 = bf16[2,24,1024]{2,1,0:T(8,128)(2,1)S(1)} collective-permute-done((bf16[2,24,1024]{2,1,0:T(8,128)(2,1)S(1)}, bf16[2,24,1024]{2,1,0:T(8,128)(2,1)S(1)}, u32[]{:S(2)}, u32[]{:S(2)}) %collective-permute-start.14) | collective-permute-done | bytes 98336 | tf_op jit(solution)/shard_map/ppermute | solution.py:189
  48.3 1.6 %collective-permute-start.16 = (bf16[192,1024]{1,0:T(8,128)(2,1)S(1)}, bf16[192,1024]{1,0:T(8,128)(2,1)S(1)}, u32[]{:S(2)}, u32[]{:S(2)}) collective-permute-start(bf16[192,1024]{1,0:T(8,128)(2,1)S(1)} %bitcast.134), channel_id=1, source_target_pairs={{0,8},{4,12},{8,0},{12,4},{1,9},{5,13},{9,1},{13,5},{2,10},{6,14},... | collective-permute-start | bytes 1179656 | tf_op jit(solution)/shard_map/ppermute | solution.py:188
  61.5 0.9 copy.16
  70.1 1.4 %pad_maximum_fusion.keyval_ref = bf16[4,2,96,1024]{3,2,1,0:T(8,128)(2,1)} fusion(bf16[1,2,96,1024]{3,2,1,0:T(8,128)(2,1)S(1)} %bitcast.153, bf16[1,2,96,1024]{3,2,1,0:T(8,128)(2,1)S(1)} %bitcast.150, bf16[1,2,96,1024]{3,2,1,0:T(8,128)(2,1)S(1)} %bitcast.152, bf16[1,2,96,1024]{3,2,1,0:T(8,128)(2,1)S(1)} %bitcast.136), kind=kLoop, calls=%fused_computation.11 | loop fusion | flops 2359296 | bytes 3145728 | tf_op jit(solution)/shard_map/stack | solution.py:190
  71.5 8.2 %shard_map.104 = (f32[2,64,4096]{2,1,0:T(8,128)}, bf16[2,96,1024]{2,1,0:T(8,128)(2,1)}) custom-call(s32[1]{0:T(128)} %bitcast.section_ref, s32[4]{0:T(128)} %iota_xor_fusion.slots_ref, f32[4,32]{1,0:T(4,128)} %maximum_tanh_fusion.gates_ref, bf16[2,64,4096]{2,1,0:T(8,128)(2,1)} %queries_ref.1, bf16[4,2,96,1024]{3,2,1,0:T(8,128)(2,1)} %pad_maximum_fusion.keyval_ref, ...), custom_call_target="tpu_custom_call" | custom-call | flops 1409286144 | bytes 6815744 | tf_op jit(solution)/shard_map/pallas_call | solution.py:139
  79.7 1.0 dynamic-slice_bitcast_fusion.13
  80.8 2.7 %collective-permute-start.19 = (bf16[48,1024]{1,0:T(8,128)(2,1)S(1)}, bf16[48,1024]{1,0:T(8,128)(2,1)S(1)}, u32[]{:S(2)}, u32[]{:S(2)}) collective-permute-start(bf16[48,1024]{1,0:T(8,128)(2,1)S(1)} %pad_maximum_fusion.7), channel_id=1, source_target_pairs={{0,2},{1,3},{2,0},{3,1},{4,6},{5,7},{6,4},{7,5},{8,10},{9,11},{10,... | collective-permute-start | bytes 294920 | tf_op jit(solution)/shard_map/ppermute | solution.py:350
  83.5 1.4 %collective-permute-start.20 = (bf16[48,1024]{1,0:T(8,128)(2,1)S(1)}, bf16[48,1024]{1,0:T(8,128)(2,1)S(1)}, u32[]{:S(2)}, u32[]{:S(2)}) collective-permute-start(bf16[48,1024]{1,0:T(8,128)(2,1)S(1)} %pad_maximum_fusion.8), channel_id=1, source_target_pairs={{0,3},{1,0},{2,1},{3,2},{4,7},{5,4},{6,5},{7,6},{8,11},{9,8},{10,9... | collective-permute-start | bytes 294920 | tf_op jit(solution)/shard_map/ppermute | solution.py:350
  84.9 2.5 %collective-permute-done.18 = bf16[48,1024]{1,0:T(8,128)(2,1)S(1)} collective-permute-done((bf16[48,1024]{1,0:T(8,128)(2,1)S(1)}, bf16[48,1024]{1,0:T(8,128)(2,1)S(1)}, u32[]{:S(2)}, u32[]{:S(2)}) %collective-permute-start.18) | collective-permute-done | bytes 98336 | tf_op jit(solution)/shard_map/ppermute | solution.py:350
  87.3 1.9 %collective-permute-done.19 = bf16[48,1024]{1,0:T(8,128)(2,1)S(1)} collective-permute-done((bf16[48,1024]{1,0:T(8,128)(2,1)S(1)}, bf16[48,1024]{1,0:T(8,128)(2,1)S(1)}, u32[]{:S(2)}, u32[]{:S(2)}) %collective-permute-start.19) | collective-permute-done | bytes 98336 | tf_op jit(solution)/shard_map/ppermute | solution.py:350
  90.0 2.8 %collective-permute-start.22 = (bf16[2,24,1024]{2,1,0:T(8,128)(2,1)S(1)}, bf16[2,24,1024]{2,1,0:T(8,128)(2,1)S(1)}, u32[]{:S(2)}, u32[]{:S(2)}) collective-permute-start(bf16[2,24,1024]{2,1,0:T(8,128)(2,1)S(1)} %pad_maximum_fusion.9), channel_id=1, source_target_pairs={{0,2},{1,3},{2,0},{3,1},{4,6},{5,7},{6,4},{7,5},{8,10},{9,11},{10,... | collective-permute-start | bytes 294920 | tf_op jit(solution)/shard_map/ppermute | solution.py:188
  92.9 3.5 %collective-permute-start.21 = (bf16[2,24,1024]{2,1,0:T(8,128)(2,1)S(1)}, bf16[2,24,1024]{2,1,0:T(8,128)(2,1)S(1)}, u32[]{:S(2)}, u32[]{:S(2)}) collective-permute-start(bf16[2,24,1024]{2,1,0:T(8,128)(2,1)S(1)} %pad_maximum_fusion.9), channel_id=1, source_target_pairs={{0,1},{1,0},{2,3},{3,2},{4,5},{5,4},{6,7},{7,6},{8,9},{9,8},{10,11... | collective-permute-start | bytes 294920 | tf_op jit(solution)/shard_map/ppermute | solution.py:189
  96.4 4.1 %collective-permute-start.23 = (bf16[2,24,1024]{2,1,0:T(8,128)(2,1)S(1)}, bf16[2,24,1024]{2,1,0:T(8,128)(2,1)S(1)}, u32[]{:S(2)}, u32[]{:S(2)}) collective-permute-start(bf16[2,24,1024]{2,1,0:T(8,128)(2,1)S(1)} %collective-permute-done.22), channel_id=1, source_target_pairs={{0,1},{1,0},{2,3},{3,2},{4,5},{5,4},{6,7},{7,6},{8,9},{9,8},{10,11... | collective-permute-start | bytes 294920 | tf_op jit(solution)/shard_map/ppermute | solution.py:189
  100.5 2.7 %collective-permute-done.23 = bf16[2,24,1024]{2,1,0:T(8,128)(2,1)S(1)} collective-permute-done((bf16[2,24,1024]{2,1,0:T(8,128)(2,1)S(1)}, bf16[2,24,1024]{2,1,0:T(8,128)(2,1)S(1)}, u32[]{:S(2)}, u32[]{:S(2)}) %collective-permute-start.23) | collective-permute-done | bytes 98336 | tf_op jit(solution)/shard_map/ppermute | solution.py:189
  104.6 3.7 %fusion.6 = bf16[192,2048]{1,0:T(8,128)(2,1)S(1)} fusion(bf16[192,1024]{1,0:T(8,128)(2,1)S(1)} %bitcast.139, bf16[1,2048,1024]{2,1,0:T(8,128)(2,1)} %param.14), kind=kOutput, calls=%fused_computation.10 | convolution fusion | flops 805699584 | bytes 5373952 | tf_op jit(solution)/shard_map/dot_general | solution.py:378
  108.5 1.7 %collective-permute-done.24 = bf16[2,2,24,2048]{3,2,1,0:T(8,128)(2,1)S(1)} collective-permute-done((bf16[2,2,24,2048]{3,2,1,0:T(8,128)(2,1)S(1)}, bf16[2,2,24,2048]{3,2,1,0:T(8,128)(2,1)S(1)}, u32[]{:S(2)}, u32[]{:S(2)}) %collective-permute-start.24) | collective-permute-done | bytes 393248 | tf_op jit(solution)/shard_map/ppermute | solution.py:216
  110.3 5.4 %collective-permute-start.25 = (bf16[2,24,2048]{2,1,0:T(8,128)(2,1)S(1)}, bf16[2,24,2048]{2,1,0:T(8,128)(2,1)S(1)}, u32[]{:S(2)}, u32[]{:S(2)}) collective-permute-start(bf16[2,24,2048]{2,1,0:T(8,128)(2,1)S(1)} %fusion.9), channel_id=1, source_target_pairs={{0,8},{4,12},{8,0},{12,4},{1,9},{5,13},{9,1},{13,5},{2,10},{6,14},... | collective-permute-start | bytes 589832 | tf_op jit(solution)/shard_map/ppermute | solution.py:220
  115.6 5.2 %collective-permute-done.25 = bf16[2,24,2048]{2,1,0:T(8,128)(2,1)S(1)} collective-permute-done((bf16[2,24,2048]{2,1,0:T(8,128)(2,1)S(1)}, bf16[2,24,2048]{2,1,0:T(8,128)(2,1)S(1)}, u32[]{:S(2)}, u32[]{:S(2)}) %collective-permute-start.25) | collective-permute-done | bytes 196640 | tf_op jit(solution)/shard_map/ppermute | solution.py:220
  (106 shorter events, 15.3 us)
Async XLA Ops:
  0.6 5.8 %collective-permute-start.3 = (bf16[2,24,2048]{2,1,0:T(8,128)(2,1)}, bf16[2,24,2048]{2,1,0:T(8,128)(2,1)S(1)}, u32[]{:S(2)}, u32[]{:S(2)}) collective-permute-start(bf16[2,24,2048]{2,1,0:T(8,128)(2,1)} %param.13), channel_id=1, source_target_pairs={{0,4},{4,0},{8,12},{12,8},{1,5},{5,1},{9,13},{13,9},{2,6},{6,2},{1... | collective-permute-start | bytes 589832 | tf_op jit(solution)/shard_map/ppermute | solution.py:189
  1.1 8.5 %collective-permute-start.7 = (bf16[2,24,2048]{2,1,0:T(8,128)(2,1)}, bf16[2,24,2048]{2,1,0:T(8,128)(2,1)S(1)}, u32[]{:S(2)}, u32[]{:S(2)}) collective-permute-start(bf16[2,24,2048]{2,1,0:T(8,128)(2,1)} %param.13), channel_id=1, source_target_pairs={{0,8},{4,12},{8,0},{12,4},{1,9},{5,13},{9,1},{13,5},{2,10},{6,14},... | collective-permute-start | bytes 589832 | tf_op jit(solution)/shard_map/ppermute | solution.py:188
  5.1 44.8 %collective-permute-start.1 = (f32[4128]{0:T(1024)S(1)}, f32[4128]{0:T(1024)S(1)}, u32[]{:S(2)}, u32[]{:S(2)}) collective-permute-start(f32[4128]{0:T(1024)S(1)} %reduce), channel_id=1, source_target_pairs={{0,8},{4,12},{8,0},{12,4},{1,9},{5,13},{9,1},{13,5},{2,10},{6,14},... | collective-permute-start | bytes 49544 | tf_op jit(solution)/shard_map/ppermute | solution.py:188
  5.2 62.4 %collective-permute-start = (f32[4128]{0:T(1024)S(1)}, f32[4128]{0:T(1024)S(1)}, u32[]{:S(2)}, u32[]{:S(2)}) collective-permute-start(f32[4128]{0:T(1024)S(1)} %reduce), channel_id=1, source_target_pairs={{0,4},{4,0},{8,12},{12,8},{1,5},{5,1},{9,13},{13,9},{2,6},{6,2},{1... | collective-permute-start | bytes 49544 | tf_op jit(solution)/shard_map/ppermute | solution.py:189
  7.5 11.1 %copy-start = (bf16[1,2048,1024]{2,1,0:T(8,128)(2,1)S(1)}, bf16[1,2048,1024]{2,1,0:T(8,128)(2,1)}, u32[]{:S(2)}) copy-start(bf16[1,2048,1024]{2,1,0:T(8,128)(2,1)} %param.14) | copy-start | bytes 12582916
  9.6 7.5 %collective-permute-start.8 = (bf16[2,24,2048]{2,1,0:T(8,128)(2,1)S(1)}, bf16[2,24,2048]{2,1,0:T(8,128)(2,1)S(1)}, u32[]{:S(2)}, u32[]{:S(2)}) collective-permute-start(bf16[2,24,2048]{2,1,0:T(8,128)(2,1)S(1)} %collective-permute-done.7), channel_id=1, source_target_pairs={{0,4},{4,0},{8,12},{12,8},{1,5},{5,1},{9,13},{13,9},{2,6},{6,2},{1... | collective-permute-start | bytes 589832 | tf_op jit(solution)/shard_map/ppermute | solution.py:189
  12.7 7.7 %collective-permute-start.4 = (f32[24,1024]{1,0:T(8,128)S(1)}, f32[24,1024]{1,0:T(8,128)S(1)}, u32[]{:S(2)}, u32[]{:S(2)}) collective-permute-start(f32[24,1024]{1,0:T(8,128)S(1)} %get-tuple-element.18), channel_id=1, source_target_pairs={{0,1},{1,2},{2,3},{3,0},{4,5},{5,6},{6,7},{7,4},{8,9},{9,10},{10,1... | collective-permute-start | bytes 294920 | tf_op jit(solution)/shard_map/ppermute | solution.py:229
  14.6 11.9 %collective-permute-start.5 = (f32[24,1024]{1,0:T(8,128)S(1)}, f32[24,1024]{1,0:T(8,128)S(1)}, u32[]{:S(2)}, u32[]{:S(2)}) collective-permute-start(f32[24,1024]{1,0:T(8,128)S(1)} %get-tuple-element.20), channel_id=1, source_target_pairs={{0,2},{1,3},{2,0},{3,1},{4,6},{5,7},{6,4},{7,5},{8,10},{9,11},{10,... | collective-permute-start | bytes 294920 | tf_op jit(solution)/shard_map/ppermute | solution.py:229
  17.2 12.3 %collective-permute-start.6 = (f32[24,1024]{1,0:T(8,128)S(1)}, f32[24,1024]{1,0:T(8,128)S(1)}, u32[]{:S(2)}, u32[]{:S(2)}) collective-permute-start(f32[24,1024]{1,0:T(8,128)S(1)} %get-tuple-element.19), channel_id=1, source_target_pairs={{0,3},{1,0},{2,1},{3,2},{4,7},{5,4},{6,5},{7,6},{8,11},{9,8},{10,9... | collective-permute-start | bytes 294920 | tf_op jit(solution)/shard_map/ppermute | solution.py:229
  18.6 17.7 %copy-start.2 = (f32[1,512]{1,0:T(1,128)S(1)}, f32[1,512]{1,0:T(1,128)}, u32[]{:S(2)}) copy-start(f32[1,512]{1,0:T(1,128)} %param.16) | copy-start | bytes 6148
  20.3 10.3 %collective-permute-start.10 = (f32[24,1024]{1,0:T(8,128)S(1)}, f32[24,1024]{1,0:T(8,128)S(1)}, u32[]{:S(2)}, u32[]{:S(2)}) collective-permute-start(f32[24,1024]{1,0:T(8,128)S(1)} %get-tuple-element.23), channel_id=1, source_target_pairs={{0,2},{1,3},{2,0},{3,1},{4,6},{5,7},{6,4},{7,5},{8,10},{9,11},{10,... | collective-permute-start | bytes 294920 | tf_op jit(solution)/shard_map/ppermute | solution.py:229
  26.4 5.6 %collective-permute-start.11 = (f32[24,1024]{1,0:T(8,128)S(1)}, f32[24,1024]{1,0:T(8,128)S(1)}, u32[]{:S(2)}, u32[]{:S(2)}) collective-permute-start(f32[24,1024]{1,0:T(8,128)S(1)} %get-tuple-element.22), channel_id=1, source_target_pairs={{0,3},{1,0},{2,1},{3,2},{4,7},{5,4},{6,5},{7,6},{8,11},{9,8},{10,9... | collective-permute-start | bytes 294920 | tf_op jit(solution)/shard_map/ppermute | solution.py:229
  29.5 6.4 %collective-permute-start.9 = (f32[24,1024]{1,0:T(8,128)S(1)}, f32[24,1024]{1,0:T(8,128)S(1)}, u32[]{:S(2)}, u32[]{:S(2)}) collective-permute-start(f32[24,1024]{1,0:T(8,128)S(1)} %get-tuple-element.21), channel_id=1, source_target_pairs={{0,1},{1,2},{2,3},{3,0},{4,5},{5,6},{6,7},{7,4},{8,9},{9,10},{10,1... | collective-permute-start | bytes 294920 | tf_op jit(solution)/shard_map/ppermute | solution.py:229
  36.3 5.9 %collective-permute-start.13 = (bf16[2,24,1024]{2,1,0:T(8,128)(2,1)S(1)}, bf16[2,24,1024]{2,1,0:T(8,128)(2,1)S(1)}, u32[]{:S(2)}, u32[]{:S(2)}) collective-permute-start(bf16[2,24,1024]{2,1,0:T(8,128)(2,1)S(1)} %bitcast.155), channel_id=1, source_target_pairs={{0,2},{1,3},{2,0},{3,1},{4,6},{5,7},{6,4},{7,5},{8,10},{9,11},{10,... | collective-permute-start | bytes 294920 | tf_op jit(solution)/shard_map/ppermute | solution.py:188
  36.7 6.6 %collective-permute-start.12 = (bf16[2,24,1024]{2,1,0:T(8,128)(2,1)S(1)}, bf16[2,24,1024]{2,1,0:T(8,128)(2,1)S(1)}, u32[]{:S(2)}, u32[]{:S(2)}) collective-permute-start(bf16[2,24,1024]{2,1,0:T(8,128)(2,1)S(1)} %bitcast.156), channel_id=1, source_target_pairs={{0,1},{1,0},{2,3},{3,2},{4,5},{5,4},{6,7},{7,6},{8,9},{9,8},{10,11... | collective-permute-start | bytes 294920 | tf_op jit(solution)/shard_map/ppermute | solution.py:189
  42.2 4.6 %collective-permute-start.14 = (bf16[2,24,1024]{2,1,0:T(8,128)(2,1)S(1)}, bf16[2,24,1024]{2,1,0:T(8,128)(2,1)S(1)}, u32[]{:S(2)}, u32[]{:S(2)}) collective-permute-start(bf16[2,24,1024]{2,1,0:T(8,128)(2,1)S(1)} %collective-permute-done.13), channel_id=1, source_target_pairs={{0,1},{1,0},{2,3},{3,2},{4,5},{5,4},{6,7},{7,6},{8,9},{9,8},{10,11... | collective-permute-start | bytes 294920 | tf_op jit(solution)/shard_map/ppermute | solution.py:189
  48.3 19.9 %collective-permute-start.16 = (bf16[192,1024]{1,0:T(8,128)(2,1)S(1)}, bf16[192,1024]{1,0:T(8,128)(2,1)S(1)}, u32[]{:S(2)}, u32[]{:S(2)}) collective-permute-start(bf16[192,1024]{1,0:T(8,128)(2,1)S(1)} %bitcast.134), channel_id=1, source_target_pairs={{0,8},{4,12},{8,0},{12,4},{1,9},{5,13},{9,1},{13,5},{2,10},{6,14},... | collective-permute-start | bytes 1179656 | tf_op jit(solution)/shard_map/ppermute | solution.py:188
  49.9 17.7 %collective-permute-start.2 = (f32[4128]{0:T(1024)S(1)}, f32[4128]{0:T(1024)S(1)}, u32[]{:S(2)}, u32[]{:S(2)}) collective-permute-start(f32[4128]{0:T(1024)S(1)} %collective-permute-done.1), channel_id=1, source_target_pairs={{0,4},{4,0},{8,12},{12,8},{1,5},{5,1},{9,13},{13,9},{2,6},{6,2},{1... | collective-permute-start | bytes 49544 | tf_op jit(solution)/shard_map/ppermute | solution.py:189
  61.4 10.1 %copy-start.1 = (f32[2,8,64,96]{3,2,1,0:T(8,128)}, f32[2,8,64,96]{3,2,1,0:T(8,128)S(1)}, u32[]{:S(2)}) copy-start(f32[2,8,64,96]{3,2,1,0:T(8,128)S(1)} %tile.4) | copy-start | bytes 1179652
  67.6 2.0 %collective-permute-start.15 = (bf16[192,1024]{1,0:T(8,128)(2,1)S(1)}, bf16[192,1024]{1,0:T(8,128)(2,1)S(1)}, u32[]{:S(2)}, u32[]{:S(2)}) collective-permute-start(bf16[192,1024]{1,0:T(8,128)(2,1)S(1)} %bitcast.135), channel_id=1, source_target_pairs={{0,4},{4,0},{8,12},{12,8},{1,5},{5,1},{9,13},{13,9},{2,6},{6,2},{1... | collective-permute-start | bytes 1179656 | tf_op jit(solution)/shard_map/ppermute | solution.py:189
  68.2 1.9 %collective-permute-start.17 = (bf16[192,1024]{1,0:T(8,128)(2,1)S(1)}, bf16[192,1024]{1,0:T(8,128)(2,1)S(1)}, u32[]{:S(2)}, u32[]{:S(2)}) collective-permute-start(bf16[192,1024]{1,0:T(8,128)(2,1)S(1)} %collective-permute-done.16), channel_id=1, source_target_pairs={{0,4},{4,0},{8,12},{12,8},{1,5},{5,1},{9,13},{13,9},{2,6},{6,2},{1... | collective-permute-start | bytes 1179656 | tf_op jit(solution)/shard_map/ppermute | solution.py:189
  80.7 6.6 %collective-permute-start.18 = (bf16[48,1024]{1,0:T(8,128)(2,1)S(1)}, bf16[48,1024]{1,0:T(8,128)(2,1)S(1)}, u32[]{:S(2)}, u32[]{:S(2)}) collective-permute-start(bf16[48,1024]{1,0:T(8,128)(2,1)S(1)} %pad_maximum_fusion.6), channel_id=1, source_target_pairs={{0,1},{1,2},{2,3},{3,0},{4,5},{5,6},{6,7},{7,4},{8,9},{9,10},{10,1... | collective-permute-start | bytes 294920 | tf_op jit(solution)/shard_map/ppermute | solution.py:350
  80.8 8.4 %collective-permute-start.19 = (bf16[48,1024]{1,0:T(8,128)(2,1)S(1)}, bf16[48,1024]{1,0:T(8,128)(2,1)S(1)}, u32[]{:S(2)}, u32[]{:S(2)}) collective-permute-start(bf16[48,1024]{1,0:T(8,128)(2,1)S(1)} %pad_maximum_fusion.7), channel_id=1, source_target_pairs={{0,2},{1,3},{2,0},{3,1},{4,6},{5,7},{6,4},{7,5},{8,10},{9,11},{10,... | collective-permute-start | bytes 294920 | tf_op jit(solution)/shard_map/ppermute | solution.py:350
  83.5 6.1 %collective-permute-start.20 = (bf16[48,1024]{1,0:T(8,128)(2,1)S(1)}, bf16[48,1024]{1,0:T(8,128)(2,1)S(1)}, u32[]{:S(2)}, u32[]{:S(2)}) collective-permute-start(bf16[48,1024]{1,0:T(8,128)(2,1)S(1)} %pad_maximum_fusion.8), channel_id=1, source_target_pairs={{0,3},{1,0},{2,1},{3,2},{4,7},{5,4},{6,5},{7,6},{8,11},{9,8},{10,9... | collective-permute-start | bytes 294920 | tf_op jit(solution)/shard_map/ppermute | solution.py:350
  90.0 6.3 %collective-permute-start.22 = (bf16[2,24,1024]{2,1,0:T(8,128)(2,1)S(1)}, bf16[2,24,1024]{2,1,0:T(8,128)(2,1)S(1)}, u32[]{:S(2)}, u32[]{:S(2)}) collective-permute-start(bf16[2,24,1024]{2,1,0:T(8,128)(2,1)S(1)} %pad_maximum_fusion.9), channel_id=1, source_target_pairs={{0,2},{1,3},{2,0},{3,1},{4,6},{5,7},{6,4},{7,5},{8,10},{9,11},{10,... | collective-permute-start | bytes 294920 | tf_op jit(solution)/shard_map/ppermute | solution.py:188
  92.9 7.6 %collective-permute-start.21 = (bf16[2,24,1024]{2,1,0:T(8,128)(2,1)S(1)}, bf16[2,24,1024]{2,1,0:T(8,128)(2,1)S(1)}, u32[]{:S(2)}, u32[]{:S(2)}) collective-permute-start(bf16[2,24,1024]{2,1,0:T(8,128)(2,1)S(1)} %pad_maximum_fusion.9), channel_id=1, source_target_pairs={{0,1},{1,0},{2,3},{3,2},{4,5},{5,4},{6,7},{7,6},{8,9},{9,8},{10,11... | collective-permute-start | bytes 294920 | tf_op jit(solution)/shard_map/ppermute | solution.py:189
  96.4 6.8 %collective-permute-start.23 = (bf16[2,24,1024]{2,1,0:T(8,128)(2,1)S(1)}, bf16[2,24,1024]{2,1,0:T(8,128)(2,1)S(1)}, u32[]{:S(2)}, u32[]{:S(2)}) collective-permute-start(bf16[2,24,1024]{2,1,0:T(8,128)(2,1)S(1)} %collective-permute-done.22), channel_id=1, source_target_pairs={{0,1},{1,0},{2,3},{3,2},{4,5},{5,4},{6,7},{7,6},{8,9},{9,8},{10,11... | collective-permute-start | bytes 294920 | tf_op jit(solution)/shard_map/ppermute | solution.py:189
  108.4 1.8 %collective-permute-start.24 = (bf16[2,2,24,2048]{3,2,1,0:T(8,128)(2,1)S(1)}, bf16[2,2,24,2048]{3,2,1,0:T(8,128)(2,1)S(1)}, u32[]{:S(2)}, u32[]{:S(2)}) collective-permute-start(bf16[2,2,24,2048]{3,2,1,0:T(8,128)(2,1)S(1)} %pad_maximum_fusion.3), channel_id=1, source_target_pairs={{0,4},{4,0},{8,12},{12,8},{1,5},{5,1},{9,13},{13,9},{2,6},{6,2},{1... | collective-permute-start | bytes 1179656 | tf_op jit(solution)/shard_map/ppermute | solution.py:216
  110.3 10.6 %collective-permute-start.25 = (bf16[2,24,2048]{2,1,0:T(8,128)(2,1)S(1)}, bf16[2,24,2048]{2,1,0:T(8,128)(2,1)S(1)}, u32[]{:S(2)}, u32[]{:S(2)}) collective-permute-start(bf16[2,24,2048]{2,1,0:T(8,128)(2,1)S(1)} %fusion.9), channel_id=1, source_target_pairs={{0,8},{4,12},{8,0},{12,4},{1,9},{5,13},{9,1},{13,5},{2,10},{6,14},... | collective-permute-start | bytes 589832 | tf_op jit(solution)/shard_map/ppermute | solution.py:220

commit v14 on v10

--- a/solution.py
+++ b/solution.py
@@ -338,13 +338,21 @@
     raw_grad_rows = jnp.concatenate([key_portion, grad_rows[:, key_width:]], axis=1).astype(
         jnp.bfloat16
     )
-    raw_grad = to_natural(raw_grad_rows)
     owned = image_count // section_count
-    raw_grad = (
-        raw_grad.reshape(micro_count, section_count, owned, 2 * key_width)
-        .transpose(1, 0, 2, 3)
-        .reshape(total_rows, 2 * key_width)
-    )
+    if phased:
+        raw_blocks = in_order(raw_grad_rows.reshape(2, owned, pair_width), "shard")
+        raw_grad = jnp.take(
+            raw_blocks.reshape(2 * shard_count, owned, pair_width),
+            natural.T.reshape(-1),
+            axis=0,
+        ).reshape(total_rows, pair_width)
+    else:
+        raw_grad = to_natural(raw_grad_rows)
+        raw_grad = (
+            raw_grad.reshape(micro_count, section_count, owned, 2 * key_width)
+            .transpose(1, 0, 2, 3)
+            .reshape(total_rows, 2 * key_width)
+        )
     image_part = lax.dot_general(
         raw_grad, weights, (((1,), (1,)), ((), ())), preferred_element_type=jnp.float32
     )

time: 113 us -> 113 us (level)
  no operation moved by 1% of the time
where the time goes in v14:
time: 113 us
  waiting for transfers between devices  42.8 us (38%)
  starting transfers between devices  38.6 us (34%)
  Pallas kernels  8.22 us (7%)
  local copies, waits for them, and re-layouts  7.69 us (7%)
  matrix products  7.55 us (7%)
  other arithmetic  6.62 us (6%)
    ppermute x9, starting transfers between devices, scatter_blocks(): lax.ppermute(part, axis, [(i, (i + d) % count) for i in range(count)])  19.1 us
    ppermute x9, waiting for transfers between devices, scatter_blocks(): lax.ppermute(part, axis, [(i, (i + d) % count) for i in range(count)])  14.8 us
    ppermute x5, waiting for transfers between devices, gather_blocks(): across = lax.ppermute(block, axis, [(i, i ^ 2) for i in range(count)])  13.5 us
    pallas_call x1, Pallas kernels, attention_layers(): pl.pallas_call(functools.partial(attention_kernel, head_count=head_count,...  8.22 us
    ppermute x5, waiting for transfers between devices, gather_blocks(): lax.ppermute(across, axis, partner)  6.61 us
    ppermute x1, starting transfers between devices, scatter_blocks(): back = lax.ppermute(theirs, axis, [(i, i ^ 2) for i in range(count)])  6.32 us
    ppermute x5, starting transfers between devices, gather_blocks(): across = lax.ppermute(block, axis, [(i, i ^ 2) for i in range(count)])  6.29 us
    ppermute x1, waiting for transfers between devices, scatter_blocks(): back = lax.ppermute(theirs, axis, [(i, i ^ 2) for i in range(count)])  5.2 us
  transfers between devices with their start and end apart: 26, of which 16 were waited for; matrix products, arithmetic and copies ran while one was open for 11% of the time, Pallas kernels for 0%

profile of v14, /device:TPU:0, one launch (start us, length us, event | category | flops | bytes accessed | tf_op | source)
XLA Modules:
  0.0 112.7 jit_solution(4417376239955567694)
XLA Ops:
  1.1 2.6 %collective-permute-start.7 = (bf16[2,24,2048]{2,1,0:T(8,128)(2,1)}, bf16[2,24,2048]{2,1,0:T(8,128)(2,1)S(1)}, u32[]{:S(2)}, u32[]{:S(2)}) collective-permute-start(bf16[2,24,2048]{2,1,0:T(8,128)(2,1)} %param.13), channel_id=1, source_target_pairs={{0,8},{4,12},{8,0},{12,4},{1,9},{5,13},{9,1},{13,5},{2,10},{6,14},... | collective-permute-start | bytes 589832 | tf_op jit(solution)/shard_map/ppermute | solution.py:188
  7.7 2.0 %collective-permute-done.7 = bf16[2,24,2048]{2,1,0:T(8,128)(2,1)S(1)} collective-permute-done((bf16[2,24,2048]{2,1,0:T(8,128)(2,1)}, bf16[2,24,2048]{2,1,0:T(8,128)(2,1)S(1)}, u32[]{:S(2)}, u32[]{:S(2)}) %collective-permute-start.7) | collective-permute-done | bytes 196640 | tf_op jit(solution)/shard_map/ppermute | solution.py:188
  9.6 3.0 %fusion.2 = f32[4,24,1024]{2,1,0:T(8,128)S(1)} fusion(bf16[4,24,2048]{2,1,0:T(8,128)(2,1)S(1)} %bitcast.118, bf16[1,2048,1024]{2,1,0:T(8,128)(2,1)} %param.14), kind=kOutput, calls=%fused_computation.7 | convolution fusion | flops 402653184 | bytes 4980736 | tf_op jit(solution)/shard_map/dot_general | solution.py:273
  12.7 1.9 %collective-permute-start.4 = (f32[24,1024]{1,0:T(8,128)S(1)}, f32[24,1024]{1,0:T(8,128)S(1)}, u32[]{:S(2)}, u32[]{:S(2)}) collective-permute-start(f32[24,1024]{1,0:T(8,128)S(1)} %get-tuple-element.13), channel_id=1, source_target_pairs={{0,1},{1,2},{2,3},{3,0},{4,5},{5,6},{6,7},{7,4},{8,9},{9,10},{10,1... | collective-permute-start | bytes 294920 | tf_op jit(solution)/shard_map/ppermute | solution.py:229
  14.6 2.6 %collective-permute-start.5 = (f32[24,1024]{1,0:T(8,128)S(1)}, f32[24,1024]{1,0:T(8,128)S(1)}, u32[]{:S(2)}, u32[]{:S(2)}) collective-permute-start(f32[24,1024]{1,0:T(8,128)S(1)} %get-tuple-element.15), channel_id=1, source_target_pairs={{0,2},{1,3},{2,0},{3,1},{4,6},{5,7},{6,4},{7,5},{8,10},{9,11},{10,... | collective-permute-start | bytes 294920 | tf_op jit(solution)/shard_map/ppermute | solution.py:229
  17.2 1.4 %collective-permute-start.6 = (f32[24,1024]{1,0:T(8,128)S(1)}, f32[24,1024]{1,0:T(8,128)S(1)}, u32[]{:S(2)}, u32[]{:S(2)}) collective-permute-start(f32[24,1024]{1,0:T(8,128)S(1)} %get-tuple-element.14), channel_id=1, source_target_pairs={{0,3},{1,0},{2,1},{3,2},{4,7},{5,4},{6,5},{7,6},{8,11},{9,8},{10,9... | collective-permute-start | bytes 294920 | tf_op jit(solution)/shard_map/ppermute | solution.py:229
  20.3 6.1 %collective-permute-start.10 = (f32[24,1024]{1,0:T(8,128)S(1)}, f32[24,1024]{1,0:T(8,128)S(1)}, u32[]{:S(2)}, u32[]{:S(2)}) collective-permute-start(f32[24,1024]{1,0:T(8,128)S(1)} %get-tuple-element.18), channel_id=1, source_target_pairs={{0,2},{1,3},{2,0},{3,1},{4,6},{5,7},{6,4},{7,5},{8,10},{9,11},{10,... | collective-permute-start | bytes 294920 | tf_op jit(solution)/shard_map/ppermute | solution.py:229
  26.4 3.0 %collective-permute-start.11 = (f32[24,1024]{1,0:T(8,128)S(1)}, f32[24,1024]{1,0:T(8,128)S(1)}, u32[]{:S(2)}, u32[]{:S(2)}) collective-permute-start(f32[24,1024]{1,0:T(8,128)S(1)} %get-tuple-element.17), channel_id=1, source_target_pairs={{0,3},{1,0},{2,1},{3,2},{4,7},{5,4},{6,5},{7,6},{8,11},{9,8},{10,9... | collective-permute-start | bytes 294920 | tf_op jit(solution)/shard_map/ppermute | solution.py:229
  29.5 1.2 %collective-permute-done.10 = f32[24,1024]{1,0:T(8,128)S(1)} collective-permute-done((f32[24,1024]{1,0:T(8,128)S(1)}, f32[24,1024]{1,0:T(8,128)S(1)}, u32[]{:S(2)}, u32[]{:S(2)}) %collective-permute-start.10) | collective-permute-done | bytes 98336 | tf_op jit(solution)/shard_map/ppermute | solution.py:229
  30.7 1.4 %collective-permute-done.11 = f32[24,1024]{1,0:T(8,128)S(1)} collective-permute-done((f32[24,1024]{1,0:T(8,128)S(1)}, f32[24,1024]{1,0:T(8,128)S(1)}, u32[]{:S(2)}, u32[]{:S(2)}) %collective-permute-start.11) | collective-permute-done | bytes 98336 | tf_op jit(solution)/shard_map/ppermute | solution.py:229
  32.1 3.8 %collective-permute-done.9 = f32[24,1024]{1,0:T(8,128)S(1)} collective-permute-done((f32[24,1024]{1,0:T(8,128)S(1)}, f32[24,1024]{1,0:T(8,128)S(1)}, u32[]{:S(2)}, u32[]{:S(2)}) %collective-permute-start.9) | collective-permute-done | bytes 98336 | tf_op jit(solution)/shard_map/ppermute | solution.py:229
  37.5 4.7 %collective-permute-done.13 = bf16[2,24,1024]{2,1,0:T(8,128)(2,1)S(1)} collective-permute-done((bf16[2,24,1024]{2,1,0:T(8,128)(2,1)S(1)}, bf16[2,24,1024]{2,1,0:T(8,128)(2,1)S(1)}, u32[]{:S(2)}, u32[]{:S(2)}) %collective-permute-start.13) | collective-permute-done | bytes 98336 | tf_op jit(solution)/shard_map/ppermute | solution.py:188
  42.2 1.0 collective-permute-done.12
  43.2 3.6 %collective-permute-done.14 = bf16[2,24,1024]{2,1,0:T(8,128)(2,1)S(1)} collective-permute-done((bf16[2,24,1024]{2,1,0:T(8,128)(2,1)S(1)}, bf16[2,24,1024]{2,1,0:T(8,128)(2,1)S(1)}, u32[]{:S(2)}, u32[]{:S(2)}) %collective-permute-start.14) | collective-permute-done | bytes 98336 | tf_op jit(solution)/shard_map/ppermute | solution.py:189
  48.3 1.6 %collective-permute-start.16 = (bf16[192,1024]{1,0:T(8,128)(2,1)S(1)}, bf16[192,1024]{1,0:T(8,128)(2,1)S(1)}, u32[]{:S(2)}, u32[]{:S(2)}) collective-permute-start(bf16[192,1024]{1,0:T(8,128)(2,1)S(1)} %bitcast.120), channel_id=1, source_target_pairs={{0,8},{4,12},{8,0},{12,4},{1,9},{5,13},{9,1},{13,5},{2,10},{6,14},... | collective-permute-start | bytes 1179656 | tf_op jit(solution)/shard_map/ppermute | solution.py:188
  52.3 3.9 %collective-permute-done.16 = bf16[192,1024]{1,0:T(8,128)(2,1)S(1)} collective-permute-done((bf16[192,1024]{1,0:T(8,128)(2,1)S(1)}, bf16[192,1024]{1,0:T(8,128)(2,1)S(1)}, u32[]{:S(2)}, u32[]{:S(2)}) %collective-permute-start.16) | collective-permute-done | bytes 393248 | tf_op jit(solution)/shard_map/ppermute | solution.py:188
  57.9 1.4 %pad_maximum_fusion.keyval_ref = bf16[4,2,96,1024]{3,2,1,0:T(8,128)(2,1)} fusion(bf16[1,2,96,1024]{3,2,1,0:T(8,128)(2,1)S(1)} %bitcast.141, bf16[1,2,96,1024]{3,2,1,0:T(8,128)(2,1)S(1)} %bitcast.138, bf16[1,2,96,1024]{3,2,1,0:T(8,128)(2,1)S(1)} %bitcast.140, bf16[1,2,96,1024]{3,2,1,0:T(8,128)(2,1)S(1)} %bitcast.122), kind=kLoop, calls=%fused_computation.12 | loop fusion | flops 2359296 | bytes 3145728 | tf_op jit(solution)/shard_map/stack | solution.py:190
  59.3 8.2 %shard_map.104 = (f32[2,64,4096]{2,1,0:T(8,128)}, bf16[2,96,1024]{2,1,0:T(8,128)(2,1)}) custom-call(s32[1]{0:T(128)} %bitcast.section_ref, s32[4]{0:T(128)} %iota_xor_fusion.slots_ref, f32[4,32]{1,0:T(4,128)} %maximum_tanh_fusion.gates_ref, bf16[2,64,4096]{2,1,0:T(8,128)(2,1)} %queries_ref.1, bf16[4,2,96,1024]{3,2,1,0:T(8,128)(2,1)} %pad_maximum_fusion.keyval_ref, ...), custom_call_target="tpu_custom_call" | custom-call | flops 1409286144 | bytes 6815744 | tf_op jit(solution)/shard_map/pallas_call | solution.py:139
  67.5 1.6 %gather_fusion.2 = bf16[8,24,1024]{2,1,0:T(8,128)(2,1)S(1)} fusion(bf16[8,24,1024]{2,1,0:T(8,128)(2,1)} %bitcast.146, s32[1024]{0:T(1024)S(1)} %pad_clamp_fusion.1), kind=kCustom, calls=%fused_computation.3.clone | custom fusion | bytes 786464 | tf_op jit(solution)/shard_map/jit(_take)/gather | solution.py:295
  70.2 1.6 %collective-permute-start.19 = (bf16[48,1024]{1,0:T(8,128)(2,1)S(1)}, bf16[48,1024]{1,0:T(8,128)(2,1)S(1)}, u32[]{:S(2)}, u32[]{:S(2)}) collective-permute-start(bf16[48,1024]{1,0:T(8,128)(2,1)S(1)} %get-tuple-element.12), channel_id=1, source_target_pairs={{0,2},{1,3},{2,0},{3,1},{4,6},{5,7},{6,4},{7,5},{8,10},{9,11},{10,... | collective-permute-start | bytes 294920 | tf_op jit(solution)/shard_map/ppermute | solution.py:229
  71.8 1.5 %collective-permute-start.20 = (bf16[48,1024]{1,0:T(8,128)(2,1)S(1)}, bf16[48,1024]{1,0:T(8,128)(2,1)S(1)}, u32[]{:S(2)}, u32[]{:S(2)}) collective-permute-start(bf16[48,1024]{1,0:T(8,128)(2,1)S(1)} %get-tuple-element.11), channel_id=1, source_target_pairs={{0,3},{1,0},{2,1},{3,2},{4,7},{5,4},{6,5},{7,6},{8,11},{9,8},{10,9... | collective-permute-start | bytes 294920 | tf_op jit(solution)/shard_map/ppermute | solution.py:229
  73.3 2.5 %collective-permute-done.18 = bf16[48,1024]{1,0:T(8,128)(2,1)S(1)} collective-permute-done((bf16[48,1024]{1,0:T(8,128)(2,1)S(1)}, bf16[48,1024]{1,0:T(8,128)(2,1)S(1)}, u32[]{:S(2)}, u32[]{:S(2)}) %collective-permute-start.18) | collective-permute-done | bytes 98336 | tf_op jit(solution)/shard_map/ppermute | solution.py:229
  75.8 5.1 %collective-permute-done.19 = bf16[48,1024]{1,0:T(8,128)(2,1)S(1)} collective-permute-done((bf16[48,1024]{1,0:T(8,128)(2,1)S(1)}, bf16[48,1024]{1,0:T(8,128)(2,1)S(1)}, u32[]{:S(2)}, u32[]{:S(2)}) %collective-permute-start.19) | collective-permute-done | bytes 98336 | tf_op jit(solution)/shard_map/ppermute | solution.py:229
  81.3 1.7 %collective-permute-start.22 = (bf16[2,24,1024]{2,1,0:T(8,128)(2,1)S(1)}, bf16[2,24,1024]{2,1,0:T(8,128)(2,1)S(1)}, u32[]{:S(2)}, u32[]{:S(2)}) collective-permute-start(bf16[2,24,1024]{2,1,0:T(8,128)(2,1)S(1)} %pad_maximum_fusion.6), channel_id=1, source_target_pairs={{0,2},{1,3},{2,0},{3,1},{4,6},{5,7},{6,4},{7,5},{8,10},{9,11},{10,... | collective-permute-start | bytes 294920 | tf_op jit(solution)/shard_map/ppermute | solution.py:188
  83.1 1.3 %collective-permute-start.21 = (bf16[2,24,1024]{2,1,0:T(8,128)(2,1)S(1)}, bf16[2,24,1024]{2,1,0:T(8,128)(2,1)S(1)}, u32[]{:S(2)}, u32[]{:S(2)}) collective-permute-start(bf16[2,24,1024]{2,1,0:T(8,128)(2,1)S(1)} %pad_maximum_fusion.6), channel_id=1, source_target_pairs={{0,1},{1,0},{2,3},{3,2},{4,5},{5,4},{6,7},{7,6},{8,9},{9,8},{10,11... | collective-permute-start | bytes 294920 | tf_op jit(solution)/shard_map/ppermute | solution.py:189
  84.3 2.9 %collective-permute-done.22 = bf16[2,24,1024]{2,1,0:T(8,128)(2,1)S(1)} collective-permute-done((bf16[2,24,1024]{2,1,0:T(8,128)(2,1)S(1)}, bf16[2,24,1024]{2,1,0:T(8,128)(2,1)S(1)}, u32[]{:S(2)}, u32[]{:S(2)}) %collective-permute-start.22) | collective-permute-done | bytes 98336 | tf_op jit(solution)/shard_map/ppermute | solution.py:188
  87.2 3.4 %collective-permute-start.23 = (bf16[2,24,1024]{2,1,0:T(8,128)(2,1)S(1)}, bf16[2,24,1024]{2,1,0:T(8,128)(2,1)S(1)}, u32[]{:S(2)}, u32[]{:S(2)}) collective-permute-start(bf16[2,24,1024]{2,1,0:T(8,128)(2,1)S(1)} %collective-permute-done.22), channel_id=1, source_target_pairs={{0,1},{1,0},{2,3},{3,2},{4,5},{5,4},{6,7},{7,6},{8,9},{9,8},{10,11... | collective-permute-start | bytes 294920 | tf_op jit(solution)/shard_map/ppermute | solution.py:189
  90.6 2.6 %collective-permute-done.23 = bf16[2,24,1024]{2,1,0:T(8,128)(2,1)S(1)} collective-permute-done((bf16[2,24,1024]{2,1,0:T(8,128)(2,1)S(1)}, bf16[2,24,1024]{2,1,0:T(8,128)(2,1)S(1)}, u32[]{:S(2)}, u32[]{:S(2)}) %collective-permute-start.23) | collective-permute-done | bytes 98336 | tf_op jit(solution)/shard_map/ppermute | solution.py:189
  94.6 3.7 %fusion.6 = bf16[192,2048]{1,0:T(8,128)(2,1)S(1)} fusion(bf16[192,1024]{1,0:T(8,128)(2,1)S(1)} %bitcast.127, bf16[1,2048,1024]{2,1,0:T(8,128)(2,1)} %param.14), kind=kOutput, calls=%fused_computation.11 | convolution fusion | flops 805699584 | bytes 5373952 | tf_op jit(solution)/shard_map/dot_general | solution.py:356
  98.6 1.7 %collective-permute-done.24 = bf16[2,2,24,2048]{3,2,1,0:T(8,128)(2,1)S(1)} collective-permute-done((bf16[2,2,24,2048]{3,2,1,0:T(8,128)(2,1)S(1)}, bf16[2,2,24,2048]{3,2,1,0:T(8,128)(2,1)S(1)}, u32[]{:S(2)}, u32[]{:S(2)}) %collective-permute-start.24) | collective-permute-done | bytes 393248 | tf_op jit(solution)/shard_map/ppermute | solution.py:216
  100.3 6.3 %collective-permute-start.25 = (bf16[2,24,2048]{2,1,0:T(8,128)(2,1)S(1)}, bf16[2,24,2048]{2,1,0:T(8,128)(2,1)S(1)}, u32[]{:S(2)}, u32[]{:S(2)}) collective-permute-start(bf16[2,24,2048]{2,1,0:T(8,128)(2,1)S(1)} %fusion.9), channel_id=1, source_target_pairs={{0,8},{4,12},{8,0},{12,4},{1,9},{5,13},{9,1},{13,5},{2,10},{6,14},... | collective-permute-start | bytes 589832 | tf_op jit(solution)/shard_map/ppermute | solution.py:220
  106.6 5.2 %collective-permute-done.25 = bf16[2,24,2048]{2,1,0:T(8,128)(2,1)S(1)} collective-permute-done((bf16[2,24,2048]{2,1,0:T(8,128)(2,1)S(1)}, bf16[2,24,2048]{2,1,0:T(8,128)(2,1)S(1)}, u32[]{:S(2)}, u32[]{:S(2)}) %collective-permute-start.25) | collective-permute-done | bytes 196640 | tf_op jit(solution)/shard_map/ppermute | solution.py:220
  (107 shorter events, 17.2 us)
Async XLA Ops:
  0.6 6.0 %collective-permute-start.3 = (bf16[2,24,2048]{2,1,0:T(8,128)(2,1)}, bf16[2,24,2048]{2,1,0:T(8,128)(2,1)S(1)}, u32[]{:S(2)}, u32[]{:S(2)}) collective-permute-start(bf16[2,24,2048]{2,1,0:T(8,128)(2,1)} %param.13), channel_id=1, source_target_pairs={{0,4},{4,0},{8,12},{12,8},{1,5},{5,1},{9,13},{13,9},{2,6},{6,2},{1... | collective-permute-start | bytes 589832 | tf_op jit(solution)/shard_map/ppermute | solution.py:189
  1.1 8.5 %collective-permute-start.7 = (bf16[2,24,2048]{2,1,0:T(8,128)(2,1)}, bf16[2,24,2048]{2,1,0:T(8,128)(2,1)S(1)}, u32[]{:S(2)}, u32[]{:S(2)}) collective-permute-start(bf16[2,24,2048]{2,1,0:T(8,128)(2,1)} %param.13), channel_id=1, source_target_pairs={{0,8},{4,12},{8,0},{12,4},{1,9},{5,13},{9,1},{13,5},{2,10},{6,14},... | collective-permute-start | bytes 589832 | tf_op jit(solution)/shard_map/ppermute | solution.py:188
  5.1 44.7 %collective-permute-start.1 = (f32[4128]{0:T(1024)S(1)}, f32[4128]{0:T(1024)S(1)}, u32[]{:S(2)}, u32[]{:S(2)}) collective-permute-start(f32[4128]{0:T(1024)S(1)} %reduce), channel_id=1, source_target_pairs={{0,8},{4,12},{8,0},{12,4},{1,9},{5,13},{9,1},{13,5},{2,10},{6,14},... | collective-permute-start | bytes 49544 | tf_op jit(solution)/shard_map/ppermute | solution.py:188
  5.2 46.4 %collective-permute-start = (f32[4128]{0:T(1024)S(1)}, f32[4128]{0:T(1024)S(1)}, u32[]{:S(2)}, u32[]{:S(2)}) collective-permute-start(f32[4128]{0:T(1024)S(1)} %reduce), channel_id=1, source_target_pairs={{0,4},{4,0},{8,12},{12,8},{1,5},{5,1},{9,13},{13,9},{2,6},{6,2},{1... | collective-permute-start | bytes 49544 | tf_op jit(solution)/shard_map/ppermute | solution.py:189
  7.6 11.0 %copy-start = (bf16[1,2048,1024]{2,1,0:T(8,128)(2,1)S(1)}, bf16[1,2048,1024]{2,1,0:T(8,128)(2,1)}, u32[]{:S(2)}) copy-start(bf16[1,2048,1024]{2,1,0:T(8,128)(2,1)} %param.14) | copy-start | bytes 12582916
  9.6 7.5 %collective-permute-start.8 = (bf16[2,24,2048]{2,1,0:T(8,128)(2,1)S(1)}, bf16[2,24,2048]{2,1,0:T(8,128)(2,1)S(1)}, u32[]{:S(2)}, u32[]{:S(2)}) collective-permute-start(bf16[2,24,2048]{2,1,0:T(8,128)(2,1)S(1)} %collective-permute-done.7), channel_id=1, source_target_pairs={{0,4},{4,0},{8,12},{12,8},{1,5},{5,1},{9,13},{13,9},{2,6},{6,2},{1... | collective-permute-start | bytes 589832 | tf_op jit(solution)/shard_map/ppermute | solution.py:189
  12.7 7.7 %collective-permute-start.4 = (f32[24,1024]{1,0:T(8,128)S(1)}, f32[24,1024]{1,0:T(8,128)S(1)}, u32[]{:S(2)}, u32[]{:S(2)}) collective-permute-start(f32[24,1024]{1,0:T(8,128)S(1)} %get-tuple-element.13), channel_id=1, source_target_pairs={{0,1},{1,2},{2,3},{3,0},{4,5},{5,6},{6,7},{7,4},{8,9},{9,10},{10,1... | collective-permute-start | bytes 294920 | tf_op jit(solution)/shard_map/ppermute | solution.py:229
  14.6 11.9 %collective-permute-start.5 = (f32[24,1024]{1,0:T(8,128)S(1)}, f32[24,1024]{1,0:T(8,128)S(1)}, u32[]{:S(2)}, u32[]{:S(2)}) collective-permute-start(f32[24,1024]{1,0:T(8,128)S(1)} %get-tuple-element.15), channel_id=1, source_target_pairs={{0,2},{1,3},{2,0},{3,1},{4,6},{5,7},{6,4},{7,5},{8,10},{9,11},{10,... | collective-permute-start | bytes 294920 | tf_op jit(solution)/shard_map/ppermute | solution.py:229
  17.2 12.3 %collective-permute-start.6 = (f32[24,1024]{1,0:T(8,128)S(1)}, f32[24,1024]{1,0:T(8,128)S(1)}, u32[]{:S(2)}, u32[]{:S(2)}) collective-permute-start(f32[24,1024]{1,0:T(8,128)S(1)} %get-tuple-element.14), channel_id=1, source_target_pairs={{0,3},{1,0},{2,1},{3,2},{4,7},{5,4},{6,5},{7,6},{8,11},{9,8},{10,9... | collective-permute-start | bytes 294920 | tf_op jit(solution)/shard_map/ppermute | solution.py:229
  18.6 17.7 %copy-start.2 = (f32[1,512]{1,0:T(1,128)S(1)}, f32[1,512]{1,0:T(1,128)}, u32[]{:S(2)}) copy-start(f32[1,512]{1,0:T(1,128)} %param.16) | copy-start | bytes 6148
  20.3 10.3 %collective-permute-start.10 = (f32[24,1024]{1,0:T(8,128)S(1)}, f32[24,1024]{1,0:T(8,128)S(1)}, u32[]{:S(2)}, u32[]{:S(2)}) collective-permute-start(f32[24,1024]{1,0:T(8,128)S(1)} %get-tuple-element.18), channel_id=1, source_target_pairs={{0,2},{1,3},{2,0},{3,1},{4,6},{5,7},{6,4},{7,5},{8,10},{9,11},{10,... | collective-permute-start | bytes 294920 | tf_op jit(solution)/shard_map/ppermute | solution.py:229
  26.4 5.6 %collective-permute-start.11 = (f32[24,1024]{1,0:T(8,128)S(1)}, f32[24,1024]{1,0:T(8,128)S(1)}, u32[]{:S(2)}, u32[]{:S(2)}) collective-permute-start(f32[24,1024]{1,0:T(8,128)S(1)} %get-tuple-element.17), channel_id=1, source_target_pairs={{0,3},{1,0},{2,1},{3,2},{4,7},{5,4},{6,5},{7,6},{8,11},{9,8},{10,9... | collective-permute-start | bytes 294920 | tf_op jit(solution)/shard_map/ppermute | solution.py:229
  29.5 6.4 %collective-permute-start.9 = (f32[24,1024]{1,0:T(8,128)S(1)}, f32[24,1024]{1,0:T(8,128)S(1)}, u32[]{:S(2)}, u32[]{:S(2)}) collective-permute-start(f32[24,1024]{1,0:T(8,128)S(1)} %get-tuple-element.16), channel_id=1, source_target_pairs={{0,1},{1,2},{2,3},{3,0},{4,5},{5,6},{6,7},{7,4},{8,9},{9,10},{10,1... | collective-permute-start | bytes 294920 | tf_op jit(solution)/shard_map/ppermute | solution.py:229
  36.3 5.9 %collective-permute-start.13 = (bf16[2,24,1024]{2,1,0:T(8,128)(2,1)S(1)}, bf16[2,24,1024]{2,1,0:T(8,128)(2,1)S(1)}, u32[]{:S(2)}, u32[]{:S(2)}) collective-permute-start(bf16[2,24,1024]{2,1,0:T(8,128)(2,1)S(1)} %bitcast.142), channel_id=1, source_target_pairs={{0,2},{1,3},{2,0},{3,1},{4,6},{5,7},{6,4},{7,5},{8,10},{9,11},{10,... | collective-permute-start | bytes 294920 | tf_op jit(solution)/shard_map/ppermute | solution.py:188
  36.7 6.6 %collective-permute-start.12 = (bf16[2,24,1024]{2,1,0:T(8,128)(2,1)S(1)}, bf16[2,24,1024]{2,1,0:T(8,128)(2,1)S(1)}, u32[]{:S(2)}, u32[]{:S(2)}) collective-permute-start(bf16[2,24,1024]{2,1,0:T(8,128)(2,1)S(1)} %bitcast.143), channel_id=1, source_target_pairs={{0,1},{1,0},{2,3},{3,2},{4,5},{5,4},{6,7},{7,6},{8,9},{9,8},{10,11... | collective-permute-start | bytes 294920 | tf_op jit(solution)/shard_map/ppermute | solution.py:189
  42.2 4.6 %collective-permute-start.14 = (bf16[2,24,1024]{2,1,0:T(8,128)(2,1)S(1)}, bf16[2,24,1024]{2,1,0:T(8,128)(2,1)S(1)}, u32[]{:S(2)}, u32[]{:S(2)}) collective-permute-start(bf16[2,24,1024]{2,1,0:T(8,128)(2,1)S(1)} %collective-permute-done.13), channel_id=1, source_target_pairs={{0,1},{1,0},{2,3},{3,2},{4,5},{5,4},{6,7},{7,6},{8,9},{9,8},{10,11... | collective-permute-start | bytes 294920 | tf_op jit(solution)/shard_map/ppermute | solution.py:189
  48.3 7.9 %collective-permute-start.16 = (bf16[192,1024]{1,0:T(8,128)(2,1)S(1)}, bf16[192,1024]{1,0:T(8,128)(2,1)S(1)}, u32[]{:S(2)}, u32[]{:S(2)}) collective-permute-start(bf16[192,1024]{1,0:T(8,128)(2,1)S(1)} %bitcast.120), channel_id=1, source_target_pairs={{0,8},{4,12},{8,0},{12,4},{1,9},{5,13},{9,1},{13,5},{2,10},{6,14},... | collective-permute-start | bytes 1179656 | tf_op jit(solution)/shard_map/ppermute | solution.py:188
  49.9 1.8 %collective-permute-start.2 = (f32[4128]{0:T(1024)S(1)}, f32[4128]{0:T(1024)S(1)}, u32[]{:S(2)}, u32[]{:S(2)}) collective-permute-start(f32[4128]{0:T(1024)S(1)} %collective-permute-done.1), channel_id=1, source_target_pairs={{0,4},{4,0},{8,12},{12,8},{1,5},{5,1},{9,13},{13,9},{2,6},{6,2},{1... | collective-permute-start | bytes 49544 | tf_op jit(solution)/shard_map/ppermute | solution.py:189
  50.6 8.7 %copy-start.1 = (f32[2,8,64,96]{3,2,1,0:T(8,128)}, f32[2,8,64,96]{3,2,1,0:T(8,128)S(1)}, u32[]{:S(2)}) copy-start(f32[2,8,64,96]{3,2,1,0:T(8,128)S(1)} %tile.4) | copy-start | bytes 1179652
  51.7 5.8 %collective-permute-start.15 = (bf16[192,1024]{1,0:T(8,128)(2,1)S(1)}, bf16[192,1024]{1,0:T(8,128)(2,1)S(1)}, u32[]{:S(2)}, u32[]{:S(2)}) collective-permute-start(bf16[192,1024]{1,0:T(8,128)(2,1)S(1)} %bitcast.121), channel_id=1, source_target_pairs={{0,4},{4,0},{8,12},{12,8},{1,5},{5,1},{9,13},{13,9},{2,6},{6,2},{1... | collective-permute-start | bytes 1179656 | tf_op jit(solution)/shard_map/ppermute | solution.py:189
  56.2 1.7 %collective-permute-start.17 = (bf16[192,1024]{1,0:T(8,128)(2,1)S(1)}, bf16[192,1024]{1,0:T(8,128)(2,1)S(1)}, u32[]{:S(2)}, u32[]{:S(2)}) collective-permute-start(bf16[192,1024]{1,0:T(8,128)(2,1)S(1)} %collective-permute-done.16), channel_id=1, source_target_pairs={{0,4},{4,0},{8,12},{12,8},{1,5},{5,1},{9,13},{13,9},{2,6},{6,2},{1... | collective-permute-start | bytes 1179656 | tf_op jit(solution)/shard_map/ppermute | solution.py:189
  69.2 6.6 %collective-permute-start.18 = (bf16[48,1024]{1,0:T(8,128)(2,1)S(1)}, bf16[48,1024]{1,0:T(8,128)(2,1)S(1)}, u32[]{:S(2)}, u32[]{:S(2)}) collective-permute-start(bf16[48,1024]{1,0:T(8,128)(2,1)S(1)} %get-tuple-element.10), channel_id=1, source_target_pairs={{0,1},{1,2},{2,3},{3,0},{4,5},{5,6},{6,7},{7,4},{8,9},{9,10},{10,1... | collective-permute-start | bytes 294920 | tf_op jit(solution)/shard_map/ppermute | solution.py:229
  70.2 10.7 %collective-permute-start.19 = (bf16[48,1024]{1,0:T(8,128)(2,1)S(1)}, bf16[48,1024]{1,0:T(8,128)(2,1)S(1)}, u32[]{:S(2)}, u32[]{:S(2)}) collective-permute-start(bf16[48,1024]{1,0:T(8,128)(2,1)S(1)} %get-tuple-element.12), channel_id=1, source_target_pairs={{0,2},{1,3},{2,0},{3,1},{4,6},{5,7},{6,4},{7,5},{8,10},{9,11},{10,... | collective-permute-start | bytes 294920 | tf_op jit(solution)/shard_map/ppermute | solution.py:229
  71.8 9.0 %collective-permute-start.20 = (bf16[48,1024]{1,0:T(8,128)(2,1)S(1)}, bf16[48,1024]{1,0:T(8,128)(2,1)S(1)}, u32[]{:S(2)}, u32[]{:S(2)}) collective-permute-start(bf16[48,1024]{1,0:T(8,128)(2,1)S(1)} %get-tuple-element.11), channel_id=1, source_target_pairs={{0,3},{1,0},{2,1},{3,2},{4,7},{5,4},{6,5},{7,6},{8,11},{9,8},{10,9... | collective-permute-start | bytes 294920 | tf_op jit(solution)/shard_map/ppermute | solution.py:229
  81.3 5.9 %collective-permute-start.22 = (bf16[2,24,1024]{2,1,0:T(8,128)(2,1)S(1)}, bf16[2,24,1024]{2,1,0:T(8,128)(2,1)S(1)}, u32[]{:S(2)}, u32[]{:S(2)}) collective-permute-start(bf16[2,24,1024]{2,1,0:T(8,128)(2,1)S(1)} %pad_maximum_fusion.6), channel_id=1, source_target_pairs={{0,2},{1,3},{2,0},{3,1},{4,6},{5,7},{6,4},{7,5},{8,10},{9,11},{10,... | collective-permute-start | bytes 294920 | tf_op jit(solution)/shard_map/ppermute | solution.py:188
  83.1 7.6 %collective-permute-start.21 = (bf16[2,24,1024]{2,1,0:T(8,128)(2,1)S(1)}, bf16[2,24,1024]{2,1,0:T(8,128)(2,1)S(1)}, u32[]{:S(2)}, u32[]{:S(2)}) collective-permute-start(bf16[2,24,1024]{2,1,0:T(8,128)(2,1)S(1)} %pad_maximum_fusion.6), channel_id=1, source_target_pairs={{0,1},{1,0},{2,3},{3,2},{4,5},{5,4},{6,7},{7,6},{8,9},{9,8},{10,11... | collective-permute-start | bytes 294920 | tf_op jit(solution)/shard_map/ppermute | solution.py:189
  87.2 6.0 %collective-permute-start.23 = (bf16[2,24,1024]{2,1,0:T(8,128)(2,1)S(1)}, bf16[2,24,1024]{2,1,0:T(8,128)(2,1)S(1)}, u32[]{:S(2)}, u32[]{:S(2)}) collective-permute-start(bf16[2,24,1024]{2,1,0:T(8,128)(2,1)S(1)} %collective-permute-done.22), channel_id=1, source_target_pairs={{0,1},{1,0},{2,3},{3,2},{4,5},{5,4},{6,7},{7,6},{8,9},{9,8},{10,11... | collective-permute-start | bytes 294920 | tf_op jit(solution)/shard_map/ppermute | solution.py:189
  98.5 1.8 %collective-permute-start.24 = (bf16[2,2,24,2048]{3,2,1,0:T(8,128)(2,1)S(1)}, bf16[2,2,24,2048]{3,2,1,0:T(8,128)(2,1)S(1)}, u32[]{:S(2)}, u32[]{:S(2)}) collective-permute-start(bf16[2,2,24,2048]{3,2,1,0:T(8,128)(2,1)S(1)} %pad_maximum_fusion.3), channel_id=1, source_target_pairs={{0,4},{4,0},{8,12},{12,8},{1,5},{5,1},{9,13},{13,9},{2,6},{6,2},{1... | collective-permute-start | bytes 1179656 | tf_op jit(solution)/shard_map/ppermute | solution.py:216
  100.3 11.5 %collective-permute-start.25 = (bf16[2,24,2048]{2,1,0:T(8,128)(2,1)S(1)}, bf16[2,24,2048]{2,1,0:T(8,128)(2,1)S(1)}, u32[]{:S(2)}, u32[]{:S(2)}) collective-permute-start(bf16[2,24,2048]{2,1,0:T(8,128)(2,1)S(1)} %fusion.9), channel_id=1, source_target_pairs={{0,8},{4,12},{8,0},{12,4},{1,9},{5,13},{9,1},{13,5},{2,10},{6,14},... | collective-permute-start | bytes 589832 | tf_op jit(solution)/shard_map/ppermute | solution.py:220

commit v15 on v10

--- a/solution.py
+++ b/solution.py
@@ -177,7 +177,7 @@
     )
 
 
-def gather_blocks(block, axis):
+def gather_blocks(block, axis, below_only=False):
     count = lax.axis_size(axis)
     index = lax.axis_index(axis)
     positions = jnp.arange(count, dtype=jnp.int32)
@@ -185,8 +185,14 @@
         return lax.all_gather(block, axis, axis=0, tiled=False), positions
     if count == 4:
         partner = [(i, i ^ 1) for i in range(count)]
-        across = lax.ppermute(block, axis, [(i, i ^ 2) for i in range(count)])
-        received = [block, lax.ppermute(block, axis, partner), across, lax.ppermute(across, axis, partner)]
+        across_pairs = [(i, i ^ 2) for i in range(count)]
+        forward = partner
+        if below_only:
+            partner = [(i, j) for i, j in partner if i < j]
+            across_pairs = [(i, j) for i, j in across_pairs if i < j]
+            forward = [(i, j) for i, j in forward if i ^ 2 < j]
+        across = lax.ppermute(block, axis, across_pairs)
+        received = [block, lax.ppermute(block, axis, partner), across, lax.ppermute(across, axis, forward)]
         return jnp.stack(received), lax.bitwise_xor(index, positions)
     received = [block] + [
         lax.ppermute(block, axis, [(i, (i + d) % count) for i in range(count)])
@@ -253,7 +259,7 @@
     weights = keyval_weight[0]
 
     layer_params, layer_slots = gather_blocks(
-        jnp.concatenate([query_gain, gate_logit], axis=1)[0], "section"
+        jnp.concatenate([query_gain, gate_logit], axis=1)[0], "section", True
     )
     gains_all = layer_params[:, : query_gain.shape[1]]
     gates_all = layer_params[:, query_gain.shape[1] :]
@@ -318,7 +324,7 @@
         [key_rows.astype(jnp.bfloat16), raw_rows[:, key_width:].astype(jnp.bfloat16)], axis=1
     )
     keyval_own = to_natural(keyval_rows)
-    keyval_all, _ = gather_blocks(keyval_own, "section")
+    keyval_all, _ = gather_blocks(keyval_own, "section", True)
 
     same_document = text_document[:, :, None] == image_document[:, None, :]
     leaving, grad_local = attention_layers(

time: 113 us -> 117 us (1.035)
  starting transfers between devices: 38.6 us -> 46.6 us
  waiting for transfers between devices: 43 us -> 38.5 us
    ppermute x1, starting transfers between devices: 6.31 us -> 10.5 us  [scatter_blocks(): back = lax.ppermute(theirs, axis, [(i, i ^ 2) for i in range(count)])]
    ppermute x10, waiting for transfers between devices: 20.2 us -> 16.2 us  [the longest x5 9.68 us: gather_blocks(): across = lax.ppermute(block, axis, across_pairs)]
    ppermute x5, starting transfers between devices: 3.43 us -> 6.9 us  [gather_blocks(): lax.ppermute(block, axis, partner)]
  transfers between devices with their start and end apart: 26 -> 26, of which waited for: 16 -> 14; matrix products, arithmetic and copies ran while one was open for 11% -> 11% of each run, Pallas kernels for 0% -> 0%
where the time goes in v15:
time: 117 us; the launch traced here: 116 us
  starting transfers between devices  46.6 us (40%)
  waiting for transfers between devices  38.5 us (33%)
  Pallas kernels  8.22 us (7%)
  matrix products  7.69 us (7%)
  local copies, waits for them, and re-layouts  7.64 us (7%)
  other arithmetic  6.56 us (6%)
  between operations  1.25 us (1%)
    ppermute x9, starting transfers between devices, scatter_blocks(): lax.ppermute(part, axis, [(i, (i + d) % count) for i in range(count)])  19.2 us
    ppermute x9, waiting for transfers between devices, scatter_blocks(): lax.ppermute(part, axis, [(i, (i + d) % count) for i in range(count)])  14.1 us
    ppermute x1, starting transfers between devices, scatter_blocks(): back = lax.ppermute(theirs, axis, [(i, i ^ 2) for i in range(count)])  10.5 us
    ppermute x5, waiting for transfers between devices, gather_blocks(): across = lax.ppermute(block, axis, across_pairs)  9.68 us
    pallas_call x1, Pallas kernels, attention_layers(): pl.pallas_call(functools.partial(attention_kernel, head_count=head_count,...  8.22 us
    ppermute x5, starting transfers between devices, gather_blocks(): across = lax.ppermute(block, axis, across_pairs)  7.18 us
    ppermute x5, starting transfers between devices, gather_blocks(): lax.ppermute(block, axis, partner)  6.9 us
    ppermute x5, waiting for transfers between devices, gather_blocks(): lax.ppermute(across, axis, forward)  6.5 us
  transfers between devices with their start and end apart: 26, of which 14 were waited for; matrix products, arithmetic and copies ran while one was open for 11% of the time, Pallas kernels for 0%

profile of v15, /device:TPU:0, one launch (start us, length us, event | category | flops | bytes accessed | tf_op | source)
XLA Modules:
  0.0 116.5 jit_solution(12692977239453390481)
XLA Ops:
  1.1 2.6 %collective-permute-start.7 = (bf16[2,24,2048]{2,1,0:T(8,128)(2,1)}, bf16[2,24,2048]{2,1,0:T(8,128)(2,1)S(1)}, u32[]{:S(2)}, u32[]{:S(2)}) collective-permute-start(bf16[2,24,2048]{2,1,0:T(8,128)(2,1)} %param.13), channel_id=1, source_target_pairs={{0,8},{4,12},{8,0},{12,4},{1,9},{5,13},{9,1},{13,5},{2,10},{6,14},... | collective-permute-start | bytes 589832 | tf_op jit(solution)/shard_map/ppermute | solution.py:194
  5.1 1.9 %collective-permute-start.1 = (f32[4128]{0:T(1024)S(1)}, f32[4128]{0:T(1024)S(1)}, u32[]{:S(2)}, u32[]{:S(2)}) collective-permute-start(f32[4128]{0:T(1024)S(1)} %reduce), channel_id=1, source_target_pairs={{0,8},{4,12},{1,9},{5,13},{2,10},{6,14},{3,11},{7,15},{16,24},{20,... | collective-permute-start | bytes 49544 | tf_op jit(solution)/shard_map/ppermute | solution.py:194
  7.1 2.1 %collective-permute-start = (f32[4128]{0:T(1024)S(1)}, f32[4128]{0:T(1024)S(1)}, u32[]{:S(2)}, u32[]{:S(2)}) collective-permute-start(f32[4128]{0:T(1024)S(1)} %reduce), channel_id=1, source_target_pairs={{0,4},{8,12},{1,5},{9,13},{2,6},{10,14},{3,7},{11,15},{16,20},{24,... | collective-permute-start | bytes 49544 | tf_op jit(solution)/shard_map/ppermute | solution.py:195
  11.5 3.1 %fusion.2 = f32[4,24,1024]{2,1,0:T(8,128)S(1)} fusion(bf16[4,24,2048]{2,1,0:T(8,128)(2,1)S(1)} %bitcast.121, bf16[1,2048,1024]{2,1,0:T(8,128)(2,1)} %param.14), kind=kOutput, calls=%fused_computation.7 | convolution fusion | flops 402653184 | bytes 4980736 | tf_op jit(solution)/shard_map/dot_general | solution.py:279
  14.7 1.9 %collective-permute-start.4 = (f32[24,1024]{1,0:T(8,128)S(1)}, f32[24,1024]{1,0:T(8,128)S(1)}, u32[]{:S(2)}, u32[]{:S(2)}) collective-permute-start(f32[24,1024]{1,0:T(8,128)S(1)} %get-tuple-element.13), channel_id=1, source_target_pairs={{0,1},{1,2},{2,3},{3,0},{4,5},{5,6},{6,7},{7,4},{8,9},{9,10},{10,1... | collective-permute-start | bytes 294920 | tf_op jit(solution)/shard_map/ppermute | solution.py:235
  16.6 2.6 %collective-permute-start.5 = (f32[24,1024]{1,0:T(8,128)S(1)}, f32[24,1024]{1,0:T(8,128)S(1)}, u32[]{:S(2)}, u32[]{:S(2)}) collective-permute-start(f32[24,1024]{1,0:T(8,128)S(1)} %get-tuple-element.15), channel_id=1, source_target_pairs={{0,2},{1,3},{2,0},{3,1},{4,6},{5,7},{6,4},{7,5},{8,10},{9,11},{10,... | collective-permute-start | bytes 294920 | tf_op jit(solution)/shard_map/ppermute | solution.py:235
  19.1 1.4 %collective-permute-start.6 = (f32[24,1024]{1,0:T(8,128)S(1)}, f32[24,1024]{1,0:T(8,128)S(1)}, u32[]{:S(2)}, u32[]{:S(2)}) collective-permute-start(f32[24,1024]{1,0:T(8,128)S(1)} %get-tuple-element.14), channel_id=1, source_target_pairs={{0,3},{1,0},{2,1},{3,2},{4,7},{5,4},{6,5},{7,6},{8,11},{9,8},{10,9... | collective-permute-start | bytes 294920 | tf_op jit(solution)/shard_map/ppermute | solution.py:235
  22.3 6.1 %collective-permute-start.10 = (f32[24,1024]{1,0:T(8,128)S(1)}, f32[24,1024]{1,0:T(8,128)S(1)}, u32[]{:S(2)}, u32[]{:S(2)}) collective-permute-start(f32[24,1024]{1,0:T(8,128)S(1)} %get-tuple-element.18), channel_id=1, source_target_pairs={{0,2},{1,3},{2,0},{3,1},{4,6},{5,7},{6,4},{7,5},{8,10},{9,11},{10,... | collective-permute-start | bytes 294920 | tf_op jit(solution)/shard_map/ppermute | solution.py:235
  28.4 3.0 %collective-permute-start.11 = (f32[24,1024]{1,0:T(8,128)S(1)}, f32[24,1024]{1,0:T(8,128)S(1)}, u32[]{:S(2)}, u32[]{:S(2)}) collective-permute-start(f32[24,1024]{1,0:T(8,128)S(1)} %get-tuple-element.17), channel_id=1, source_target_pairs={{0,3},{1,0},{2,1},{3,2},{4,7},{5,4},{6,5},{7,6},{8,11},{9,8},{10,9... | collective-permute-start | bytes 294920 | tf_op jit(solution)/shard_map/ppermute | solution.py:235
  32.6 1.3 %collective-permute-done.11 = f32[24,1024]{1,0:T(8,128)S(1)} collective-permute-done((f32[24,1024]{1,0:T(8,128)S(1)}, f32[24,1024]{1,0:T(8,128)S(1)}, u32[]{:S(2)}, u32[]{:S(2)}) %collective-permute-start.11) | collective-permute-done | bytes 98336 | tf_op jit(solution)/shard_map/ppermute | solution.py:235
  33.9 4.0 %collective-permute-done.9 = f32[24,1024]{1,0:T(8,128)S(1)} collective-permute-done((f32[24,1024]{1,0:T(8,128)S(1)}, f32[24,1024]{1,0:T(8,128)S(1)}, u32[]{:S(2)}, u32[]{:S(2)}) %collective-permute-start.9) | collective-permute-done | bytes 98336 | tf_op jit(solution)/shard_map/ppermute | solution.py:235
  39.3 4.8 %collective-permute-done.13 = bf16[2,24,1024]{2,1,0:T(8,128)(2,1)S(1)} collective-permute-done((bf16[2,24,1024]{2,1,0:T(8,128)(2,1)S(1)}, bf16[2,24,1024]{2,1,0:T(8,128)(2,1)S(1)}, u32[]{:S(2)}, u32[]{:S(2)}) %collective-permute-start.13) | collective-permute-done | bytes 98336 | tf_op jit(solution)/shard_map/ppermute | solution.py:194
  44.1 1.3 %collective-permute-done.12 = bf16[2,24,1024]{2,1,0:T(8,128)(2,1)S(1)} collective-permute-done((bf16[2,24,1024]{2,1,0:T(8,128)(2,1)S(1)}, bf16[2,24,1024]{2,1,0:T(8,128)(2,1)S(1)}, u32[]{:S(2)}, u32[]{:S(2)}) %collective-permute-start.12) | collective-permute-done | bytes 98336 | tf_op jit(solution)/shard_map/ppermute | solution.py:195
  45.4 3.3 %collective-permute-done.14 = bf16[2,24,1024]{2,1,0:T(8,128)(2,1)S(1)} collective-permute-done((bf16[2,24,1024]{2,1,0:T(8,128)(2,1)S(1)}, bf16[2,24,1024]{2,1,0:T(8,128)(2,1)S(1)}, u32[]{:S(2)}, u32[]{:S(2)}) %collective-permute-start.14) | collective-permute-done | bytes 98336 | tf_op jit(solution)/shard_map/ppermute | solution.py:195
  50.2 1.6 %collective-permute-start.16 = (bf16[192,1024]{1,0:T(8,128)(2,1)S(1)}, bf16[192,1024]{1,0:T(8,128)(2,1)S(1)}, u32[]{:S(2)}, u32[]{:S(2)}) collective-permute-start(bf16[192,1024]{1,0:T(8,128)(2,1)S(1)} %bitcast.123), channel_id=1, source_target_pairs={{0,8},{4,12},{1,9},{5,13},{2,10},{6,14},{3,11},{7,15},{16,24},{20,... | collective-permute-start | bytes 1179656 | tf_op jit(solution)/shard_map/ppermute | solution.py:194
  54.1 1.3 %collective-permute-start.15 = (bf16[192,1024]{1,0:T(8,128)(2,1)S(1)}, bf16[192,1024]{1,0:T(8,128)(2,1)S(1)}, u32[]{:S(2)}, u32[]{:S(2)}) collective-permute-start(bf16[192,1024]{1,0:T(8,128)(2,1)S(1)} %bitcast.124), channel_id=1, source_target_pairs={{0,4},{8,12},{1,5},{9,13},{2,6},{10,14},{3,7},{11,15},{16,20},{24,... | collective-permute-start | bytes 1179656 | tf_op jit(solution)/shard_map/ppermute | solution.py:195
  55.4 1.9 %collective-permute-done.16 = bf16[192,1024]{1,0:T(8,128)(2,1)S(1)} collective-permute-done((bf16[192,1024]{1,0:T(8,128)(2,1)S(1)}, bf16[192,1024]{1,0:T(8,128)(2,1)S(1)}, u32[]{:S(2)}, u32[]{:S(2)}) %collective-permute-start.16) | collective-permute-done | bytes 393248 | tf_op jit(solution)/shard_map/ppermute | solution.py:194
  59.3 1.4 %pad_maximum_fusion.keyval_ref = bf16[4,2,96,1024]{3,2,1,0:T(8,128)(2,1)} fusion(bf16[1,2,96,1024]{3,2,1,0:T(8,128)(2,1)S(1)} %bitcast.145, bf16[1,2,96,1024]{3,2,1,0:T(8,128)(2,1)S(1)} %bitcast.142, bf16[1,2,96,1024]{3,2,1,0:T(8,128)(2,1)S(1)} %bitcast.144, bf16[1,2,96,1024]{3,2,1,0:T(8,128)(2,1)S(1)} %bitcast.125), kind=kLoop, calls=%fused_computation.12 | loop fusion | flops 2359296 | bytes 3145728 | tf_op jit(solution)/shard_map/stack | solution.py:196
  60.7 8.2 %shard_map.104 = (f32[2,64,4096]{2,1,0:T(8,128)}, bf16[2,96,1024]{2,1,0:T(8,128)(2,1)}) custom-call(s32[1]{0:T(128)} %bitcast.section_ref, s32[4]{0:T(128)} %iota_xor_fusion.slots_ref, f32[4,32]{1,0:T(4,128)} %maximum_tanh_fusion.gates_ref, bf16[2,64,4096]{2,1,0:T(8,128)(2,1)} %queries_ref.1, bf16[4,2,96,1024]{3,2,1,0:T(8,128)(2,1)} %pad_maximum_fusion.keyval_ref, ...), custom_call_target="tpu_custom_call" | custom-call | flops 1409286144 | bytes 6815744 | tf_op jit(solution)/shard_map/pallas_call | solution.py:139
  68.9 1.6 %gather_fusion.2 = bf16[8,24,1024]{2,1,0:T(8,128)(2,1)S(1)} fusion(bf16[8,24,1024]{2,1,0:T(8,128)(2,1)} %bitcast.150, s32[1024]{0:T(1024)S(1)} %pad_clamp_fusion), kind=kCustom, calls=%fused_computation.3.clone | custom fusion | bytes 786464 | tf_op jit(solution)/shard_map/jit(_take)/gather | solution.py:301
  71.5 1.8 %collective-permute-start.19 = (bf16[48,1024]{1,0:T(8,128)(2,1)S(1)}, bf16[48,1024]{1,0:T(8,128)(2,1)S(1)}, u32[]{:S(2)}, u32[]{:S(2)}) collective-permute-start(bf16[48,1024]{1,0:T(8,128)(2,1)S(1)} %get-tuple-element.12), channel_id=1, source_target_pairs={{0,2},{1,3},{2,0},{3,1},{4,6},{5,7},{6,4},{7,5},{8,10},{9,11},{10,... | collective-permute-start | bytes 294920 | tf_op jit(solution)/shard_map/ppermute | solution.py:235
  73.2 1.6 %collective-permute-start.20 = (bf16[48,1024]{1,0:T(8,128)(2,1)S(1)}, bf16[48,1024]{1,0:T(8,128)(2,1)S(1)}, u32[]{:S(2)}, u32[]{:S(2)}) collective-permute-start(bf16[48,1024]{1,0:T(8,128)(2,1)S(1)} %get-tuple-element.11), channel_id=1, source_target_pairs={{0,3},{1,0},{2,1},{3,2},{4,7},{5,4},{6,5},{7,6},{8,11},{9,8},{10,9... | collective-permute-start | bytes 294920 | tf_op jit(solution)/shard_map/ppermute | solution.py:235
  74.8 3.4 %collective-permute-done.18 = bf16[48,1024]{1,0:T(8,128)(2,1)S(1)} collective-permute-done((bf16[48,1024]{1,0:T(8,128)(2,1)S(1)}, bf16[48,1024]{1,0:T(8,128)(2,1)S(1)}, u32[]{:S(2)}, u32[]{:S(2)}) %collective-permute-start.18) | collective-permute-done | bytes 98336 | tf_op jit(solution)/shard_map/ppermute | solution.py:235
  78.2 3.5 %collective-permute-done.19 = bf16[48,1024]{1,0:T(8,128)(2,1)S(1)} collective-permute-done((bf16[48,1024]{1,0:T(8,128)(2,1)S(1)}, bf16[48,1024]{1,0:T(8,128)(2,1)S(1)}, u32[]{:S(2)}, u32[]{:S(2)}) %collective-permute-start.19) | collective-permute-done | bytes 98336 | tf_op jit(solution)/shard_map/ppermute | solution.py:235
  82.9 2.3 %collective-permute-start.21 = (bf16[2,24,1024]{2,1,0:T(8,128)(2,1)S(1)}, bf16[2,24,1024]{2,1,0:T(8,128)(2,1)S(1)}, u32[]{:S(2)}, u32[]{:S(2)}) collective-permute-start(bf16[2,24,1024]{2,1,0:T(8,128)(2,1)S(1)} %pad_maximum_fusion.6), channel_id=1, source_target_pairs={{0,1},{1,0},{2,3},{3,2},{4,5},{5,4},{6,7},{7,6},{8,9},{9,8},{10,11... | collective-permute-start | bytes 294920 | tf_op jit(solution)/shard_map/ppermute | solution.py:195
  85.2 3.0 %collective-permute-done.22 = bf16[2,24,1024]{2,1,0:T(8,128)(2,1)S(1)} collective-permute-done((bf16[2,24,1024]{2,1,0:T(8,128)(2,1)S(1)}, bf16[2,24,1024]{2,1,0:T(8,128)(2,1)S(1)}, u32[]{:S(2)}, u32[]{:S(2)}) %collective-permute-start.22) | collective-permute-done | bytes 98336 | tf_op jit(solution)/shard_map/ppermute | solution.py:194
  88.3 1.4 %collective-permute-start.23 = (bf16[2,24,1024]{2,1,0:T(8,128)(2,1)S(1)}, bf16[2,24,1024]{2,1,0:T(8,128)(2,1)S(1)}, u32[]{:S(2)}, u32[]{:S(2)}) collective-permute-start(bf16[2,24,1024]{2,1,0:T(8,128)(2,1)S(1)} %collective-permute-done.22), channel_id=1, source_target_pairs={{0,1},{1,0},{2,3},{3,2},{4,5},{5,4},{6,7},{7,6},{8,9},{9,8},{10,11... | collective-permute-start | bytes 294920 | tf_op jit(solution)/shard_map/ppermute | solution.py:195
  89.7 3.2 %collective-permute-done.23 = bf16[2,24,1024]{2,1,0:T(8,128)(2,1)S(1)} collective-permute-done((bf16[2,24,1024]{2,1,0:T(8,128)(2,1)S(1)}, bf16[2,24,1024]{2,1,0:T(8,128)(2,1)S(1)}, u32[]{:S(2)}, u32[]{:S(2)}) %collective-permute-start.23) | collective-permute-done | bytes 98336 | tf_op jit(solution)/shard_map/ppermute | solution.py:195
  94.3 3.7 %fusion.6 = bf16[192,2048]{1,0:T(8,128)(2,1)S(1)} fusion(bf16[192,1024]{1,0:T(8,128)(2,1)S(1)} %bitcast.131, bf16[1,2048,1024]{2,1,0:T(8,128)(2,1)} %param.14), kind=kOutput, calls=%fused_computation.11 | convolution fusion | flops 805699584 | bytes 5373952 | tf_op jit(solution)/shard_map/dot_general | solution.py:354
  98.3 1.7 %collective-permute-done.24 = bf16[2,2,24,2048]{3,2,1,0:T(8,128)(2,1)S(1)} collective-permute-done((bf16[2,2,24,2048]{3,2,1,0:T(8,128)(2,1)S(1)}, bf16[2,2,24,2048]{3,2,1,0:T(8,128)(2,1)S(1)}, u32[]{:S(2)}, u32[]{:S(2)}) %collective-permute-start.24) | collective-permute-done | bytes 393248 | tf_op jit(solution)/shard_map/ppermute | solution.py:222
  100.0 10.5 %collective-permute-start.25 = (bf16[2,24,2048]{2,1,0:T(8,128)(2,1)S(1)}, bf16[2,24,2048]{2,1,0:T(8,128)(2,1)S(1)}, u32[]{:S(2)}, u32[]{:S(2)}) collective-permute-start(bf16[2,24,2048]{2,1,0:T(8,128)(2,1)S(1)} %fusion.9), channel_id=1, source_target_pairs={{0,8},{4,12},{8,0},{12,4},{1,9},{5,13},{9,1},{13,5},{2,10},{6,14},... | collective-permute-start | bytes 589832 | tf_op jit(solution)/shard_map/ppermute | solution.py:226
  110.5 5.2 %collective-permute-done.25 = bf16[2,24,2048]{2,1,0:T(8,128)(2,1)S(1)} collective-permute-done((bf16[2,24,2048]{2,1,0:T(8,128)(2,1)S(1)}, bf16[2,24,2048]{2,1,0:T(8,128)(2,1)S(1)}, u32[]{:S(2)}, u32[]{:S(2)}) %collective-permute-start.25) | collective-permute-done | bytes 196640 | tf_op jit(solution)/shard_map/ppermute | solution.py:226
  (104 shorter events, 18.7 us)
Async XLA Ops:
  0.6 9.7 %collective-permute-start.3 = (bf16[2,24,2048]{2,1,0:T(8,128)(2,1)}, bf16[2,24,2048]{2,1,0:T(8,128)(2,1)S(1)}, u32[]{:S(2)}, u32[]{:S(2)}) collective-permute-start(bf16[2,24,2048]{2,1,0:T(8,128)(2,1)} %param.13), channel_id=1, source_target_pairs={{0,4},{4,0},{8,12},{12,8},{1,5},{5,1},{9,13},{13,9},{2,6},{6,2},{1... | collective-permute-start | bytes 589832 | tf_op jit(solution)/shard_map/ppermute | solution.py:195
  1.1 10.3 %collective-permute-start.7 = (bf16[2,24,2048]{2,1,0:T(8,128)(2,1)}, bf16[2,24,2048]{2,1,0:T(8,128)(2,1)S(1)}, u32[]{:S(2)}, u32[]{:S(2)}) collective-permute-start(bf16[2,24,2048]{2,1,0:T(8,128)(2,1)} %param.13), channel_id=1, source_target_pairs={{0,8},{4,12},{8,0},{12,4},{1,9},{5,13},{9,1},{13,5},{2,10},{6,14},... | collective-permute-start | bytes 589832 | tf_op jit(solution)/shard_map/ppermute | solution.py:194
  5.1 46.7 %collective-permute-start.1 = (f32[4128]{0:T(1024)S(1)}, f32[4128]{0:T(1024)S(1)}, u32[]{:S(2)}, u32[]{:S(2)}) collective-permute-start(f32[4128]{0:T(1024)S(1)} %reduce), channel_id=1, source_target_pairs={{0,8},{4,12},{1,9},{5,13},{2,10},{6,14},{3,11},{7,15},{16,24},{20,... | collective-permute-start | bytes 49544 | tf_op jit(solution)/shard_map/ppermute | solution.py:194
  7.1 46.9 %collective-permute-start = (f32[4128]{0:T(1024)S(1)}, f32[4128]{0:T(1024)S(1)}, u32[]{:S(2)}, u32[]{:S(2)}) collective-permute-start(f32[4128]{0:T(1024)S(1)} %reduce), channel_id=1, source_target_pairs={{0,4},{8,12},{1,5},{9,13},{2,6},{10,14},{3,7},{11,15},{16,20},{24,... | collective-permute-start | bytes 49544 | tf_op jit(solution)/shard_map/ppermute | solution.py:195
  11.4 9.2 %copy-start = (bf16[1,2048,1024]{2,1,0:T(8,128)(2,1)S(1)}, bf16[1,2048,1024]{2,1,0:T(8,128)(2,1)}, u32[]{:S(2)}) copy-start(bf16[1,2048,1024]{2,1,0:T(8,128)(2,1)} %param.14) | copy-start | bytes 12582916
  11.4 7.7 %collective-permute-start.8 = (bf16[2,24,2048]{2,1,0:T(8,128)(2,1)S(1)}, bf16[2,24,2048]{2,1,0:T(8,128)(2,1)S(1)}, u32[]{:S(2)}, u32[]{:S(2)}) collective-permute-start(bf16[2,24,2048]{2,1,0:T(8,128)(2,1)S(1)} %collective-permute-done.7), channel_id=1, source_target_pairs={{0,4},{4,0},{8,12},{12,8},{1,5},{5,1},{9,13},{13,9},{2,6},{6,2},{1... | collective-permute-start | bytes 589832 | tf_op jit(solution)/shard_map/ppermute | solution.py:195
  14.7 7.6 %collective-permute-start.4 = (f32[24,1024]{1,0:T(8,128)S(1)}, f32[24,1024]{1,0:T(8,128)S(1)}, u32[]{:S(2)}, u32[]{:S(2)}) collective-permute-start(f32[24,1024]{1,0:T(8,128)S(1)} %get-tuple-element.13), channel_id=1, source_target_pairs={{0,1},{1,2},{2,3},{3,0},{4,5},{5,6},{6,7},{7,4},{8,9},{9,10},{10,1... | collective-permute-start | bytes 294920 | tf_op jit(solution)/shard_map/ppermute | solution.py:235
  16.6 11.8 %collective-permute-start.5 = (f32[24,1024]{1,0:T(8,128)S(1)}, f32[24,1024]{1,0:T(8,128)S(1)}, u32[]{:S(2)}, u32[]{:S(2)}) collective-permute-start(f32[24,1024]{1,0:T(8,128)S(1)} %get-tuple-element.15), channel_id=1, source_target_pairs={{0,2},{1,3},{2,0},{3,1},{4,6},{5,7},{6,4},{7,5},{8,10},{9,11},{10,... | collective-permute-start | bytes 294920 | tf_op jit(solution)/shard_map/ppermute | solution.py:235
  19.1 12.3 %collective-permute-start.6 = (f32[24,1024]{1,0:T(8,128)S(1)}, f32[24,1024]{1,0:T(8,128)S(1)}, u32[]{:S(2)}, u32[]{:S(2)}) collective-permute-start(f32[24,1024]{1,0:T(8,128)S(1)} %get-tuple-element.14), channel_id=1, source_target_pairs={{0,3},{1,0},{2,1},{3,2},{4,7},{5,4},{6,5},{7,6},{8,11},{9,8},{10,9... | collective-permute-start | bytes 294920 | tf_op jit(solution)/shard_map/ppermute | solution.py:235
  20.6 17.7 %copy-start.2 = (f32[1,512]{1,0:T(1,128)S(1)}, f32[1,512]{1,0:T(1,128)}, u32[]{:S(2)}) copy-start(f32[1,512]{1,0:T(1,128)} %param.16) | copy-start | bytes 6148
  22.3 10.2 %collective-permute-start.10 = (f32[24,1024]{1,0:T(8,128)S(1)}, f32[24,1024]{1,0:T(8,128)S(1)}, u32[]{:S(2)}, u32[]{:S(2)}) collective-permute-start(f32[24,1024]{1,0:T(8,128)S(1)} %get-tuple-element.18), channel_id=1, source_target_pairs={{0,2},{1,3},{2,0},{3,1},{4,6},{5,7},{6,4},{7,5},{8,10},{9,11},{10,... | collective-permute-start | bytes 294920 | tf_op jit(solution)/shard_map/ppermute | solution.py:235
  28.4 5.4 %collective-permute-start.11 = (f32[24,1024]{1,0:T(8,128)S(1)}, f32[24,1024]{1,0:T(8,128)S(1)}, u32[]{:S(2)}, u32[]{:S(2)}) collective-permute-start(f32[24,1024]{1,0:T(8,128)S(1)} %get-tuple-element.17), channel_id=1, source_target_pairs={{0,3},{1,0},{2,1},{3,2},{4,7},{5,4},{6,5},{7,6},{8,11},{9,8},{10,9... | collective-permute-start | bytes 294920 | tf_op jit(solution)/shard_map/ppermute | solution.py:235
  31.4 6.4 %collective-permute-start.9 = (f32[24,1024]{1,0:T(8,128)S(1)}, f32[24,1024]{1,0:T(8,128)S(1)}, u32[]{:S(2)}, u32[]{:S(2)}) collective-permute-start(f32[24,1024]{1,0:T(8,128)S(1)} %get-tuple-element.16), channel_id=1, source_target_pairs={{0,1},{1,2},{2,3},{3,0},{4,5},{5,6},{6,7},{7,4},{8,9},{9,10},{10,1... | collective-permute-start | bytes 294920 | tf_op jit(solution)/shard_map/ppermute | solution.py:235
  38.3 5.8 %collective-permute-start.13 = (bf16[2,24,1024]{2,1,0:T(8,128)(2,1)S(1)}, bf16[2,24,1024]{2,1,0:T(8,128)(2,1)S(1)}, u32[]{:S(2)}, u32[]{:S(2)}) collective-permute-start(bf16[2,24,1024]{2,1,0:T(8,128)(2,1)S(1)} %bitcast.146), channel_id=1, source_target_pairs={{0,2},{1,3},{2,0},{3,1},{4,6},{5,7},{6,4},{7,5},{8,10},{9,11},{10,... | collective-permute-start | bytes 294920 | tf_op jit(solution)/shard_map/ppermute | solution.py:194
  38.7 6.7 %collective-permute-start.12 = (bf16[2,24,1024]{2,1,0:T(8,128)(2,1)S(1)}, bf16[2,24,1024]{2,1,0:T(8,128)(2,1)S(1)}, u32[]{:S(2)}, u32[]{:S(2)}) collective-permute-start(bf16[2,24,1024]{2,1,0:T(8,128)(2,1)S(1)} %bitcast.147), channel_id=1, source_target_pairs={{0,1},{1,0},{2,3},{3,2},{4,5},{5,4},{6,7},{7,6},{8,9},{9,8},{10,11... | collective-permute-start | bytes 294920 | tf_op jit(solution)/shard_map/ppermute | solution.py:195
  44.1 4.6 %collective-permute-start.14 = (bf16[2,24,1024]{2,1,0:T(8,128)(2,1)S(1)}, bf16[2,24,1024]{2,1,0:T(8,128)(2,1)S(1)}, u32[]{:S(2)}, u32[]{:S(2)}) collective-permute-start(bf16[2,24,1024]{2,1,0:T(8,128)(2,1)S(1)} %collective-permute-done.13), channel_id=1, source_target_pairs={{0,1},{1,0},{2,3},{3,2},{4,5},{5,4},{6,7},{7,6},{8,9},{9,8},{10,11... | collective-permute-start | bytes 294920 | tf_op jit(solution)/shard_map/ppermute | solution.py:195
  50.2 7.1 %collective-permute-start.16 = (bf16[192,1024]{1,0:T(8,128)(2,1)S(1)}, bf16[192,1024]{1,0:T(8,128)(2,1)S(1)}, u32[]{:S(2)}, u32[]{:S(2)}) collective-permute-start(bf16[192,1024]{1,0:T(8,128)(2,1)S(1)} %bitcast.123), channel_id=1, source_target_pairs={{0,8},{4,12},{1,9},{5,13},{2,10},{6,14},{3,11},{7,15},{16,24},{20,... | collective-permute-start | bytes 1179656 | tf_op jit(solution)/shard_map/ppermute | solution.py:194
  51.8 2.2 %collective-permute-start.2 = (f32[4128]{0:T(1024)S(1)}, f32[4128]{0:T(1024)S(1)}, u32[]{:S(2)}, u32[]{:S(2)}) collective-permute-start(f32[4128]{0:T(1024)S(1)} %collective-permute-done.1), channel_id=1, source_target_pairs={{8,12},{12,8},{9,13},{13,9},{10,14},{14,10},{11,15},{15,11},{24,28... | collective-permute-start | bytes 49544 | tf_op jit(solution)/shard_map/ppermute | solution.py:195
  53.0 7.6 %copy-start.1 = (f32[2,8,64,96]{3,2,1,0:T(8,128)}, f32[2,8,64,96]{3,2,1,0:T(8,128)S(1)}, u32[]{:S(2)}) copy-start(f32[2,8,64,96]{3,2,1,0:T(8,128)S(1)} %tile.4) | copy-start | bytes 1179652
  54.1 5.2 %collective-permute-start.15 = (bf16[192,1024]{1,0:T(8,128)(2,1)S(1)}, bf16[192,1024]{1,0:T(8,128)(2,1)S(1)}, u32[]{:S(2)}, u32[]{:S(2)}) collective-permute-start(bf16[192,1024]{1,0:T(8,128)(2,1)S(1)} %bitcast.124), channel_id=1, source_target_pairs={{0,4},{8,12},{1,5},{9,13},{2,6},{10,14},{3,7},{11,15},{16,20},{24,... | collective-permute-start | bytes 1179656 | tf_op jit(solution)/shard_map/ppermute | solution.py:195
  57.3 2.0 %collective-permute-start.17 = (bf16[192,1024]{1,0:T(8,128)(2,1)S(1)}, bf16[192,1024]{1,0:T(8,128)(2,1)S(1)}, u32[]{:S(2)}, u32[]{:S(2)}) collective-permute-start(bf16[192,1024]{1,0:T(8,128)(2,1)S(1)} %collective-permute-done.16), channel_id=1, source_target_pairs={{8,12},{12,8},{9,13},{13,9},{10,14},{14,10},{11,15},{15,11},{24,28... | collective-permute-start | bytes 1179656 | tf_op jit(solution)/shard_map/ppermute | solution.py:195
  70.6 7.6 %collective-permute-start.18 = (bf16[48,1024]{1,0:T(8,128)(2,1)S(1)}, bf16[48,1024]{1,0:T(8,128)(2,1)S(1)}, u32[]{:S(2)}, u32[]{:S(2)}) collective-permute-start(bf16[48,1024]{1,0:T(8,128)(2,1)S(1)} %get-tuple-element.10), channel_id=1, source_target_pairs={{0,1},{1,2},{2,3},{3,0},{4,5},{5,6},{6,7},{7,4},{8,9},{9,10},{10,1... | collective-permute-start | bytes 294920 | tf_op jit(solution)/shard_map/ppermute | solution.py:235
  71.5 10.2 %collective-permute-start.19 = (bf16[48,1024]{1,0:T(8,128)(2,1)S(1)}, bf16[48,1024]{1,0:T(8,128)(2,1)S(1)}, u32[]{:S(2)}, u32[]{:S(2)}) collective-permute-start(bf16[48,1024]{1,0:T(8,128)(2,1)S(1)} %get-tuple-element.12), channel_id=1, source_target_pairs={{0,2},{1,3},{2,0},{3,1},{4,6},{5,7},{6,4},{7,5},{8,10},{9,11},{10,... | collective-permute-start | bytes 294920 | tf_op jit(solution)/shard_map/ppermute | solution.py:235
  73.2 8.5 %collective-permute-start.20 = (bf16[48,1024]{1,0:T(8,128)(2,1)S(1)}, bf16[48,1024]{1,0:T(8,128)(2,1)S(1)}, u32[]{:S(2)}, u32[]{:S(2)}) collective-permute-start(bf16[48,1024]{1,0:T(8,128)(2,1)S(1)} %get-tuple-element.11), channel_id=1, source_target_pairs={{0,3},{1,0},{2,1},{3,2},{4,7},{5,4},{6,5},{7,6},{8,11},{9,8},{10,9... | collective-permute-start | bytes 294920 | tf_op jit(solution)/shard_map/ppermute | solution.py:235
  82.2 6.1 %collective-permute-start.22 = (bf16[2,24,1024]{2,1,0:T(8,128)(2,1)S(1)}, bf16[2,24,1024]{2,1,0:T(8,128)(2,1)S(1)}, u32[]{:S(2)}, u32[]{:S(2)}) collective-permute-start(bf16[2,24,1024]{2,1,0:T(8,128)(2,1)S(1)} %pad_maximum_fusion.6), channel_id=1, source_target_pairs={{0,2},{1,3},{2,0},{3,1},{4,6},{5,7},{6,4},{7,5},{8,10},{9,11},{10,... | collective-permute-start | bytes 294920 | tf_op jit(solution)/shard_map/ppermute | solution.py:194
  82.9 6.8 %collective-permute-start.21 = (bf16[2,24,1024]{2,1,0:T(8,128)(2,1)S(1)}, bf16[2,24,1024]{2,1,0:T(8,128)(2,1)S(1)}, u32[]{:S(2)}, u32[]{:S(2)}) collective-permute-start(bf16[2,24,1024]{2,1,0:T(8,128)(2,1)S(1)} %pad_maximum_fusion.6), channel_id=1, source_target_pairs={{0,1},{1,0},{2,3},{3,2},{4,5},{5,4},{6,7},{7,6},{8,9},{9,8},{10,11... | collective-permute-start | bytes 294920 | tf_op jit(solution)/shard_map/ppermute | solution.py:195
  88.3 4.6 %collective-permute-start.23 = (bf16[2,24,1024]{2,1,0:T(8,128)(2,1)S(1)}, bf16[2,24,1024]{2,1,0:T(8,128)(2,1)S(1)}, u32[]{:S(2)}, u32[]{:S(2)}) collective-permute-start(bf16[2,24,1024]{2,1,0:T(8,128)(2,1)S(1)} %collective-permute-done.22), channel_id=1, source_target_pairs={{0,1},{1,0},{2,3},{3,2},{4,5},{5,4},{6,7},{7,6},{8,9},{9,8},{10,11... | collective-permute-start | bytes 294920 | tf_op jit(solution)/shard_map/ppermute | solution.py:195
  98.2 1.8 %collective-permute-start.24 = (bf16[2,2,24,2048]{3,2,1,0:T(8,128)(2,1)S(1)}, bf16[2,2,24,2048]{3,2,1,0:T(8,128)(2,1)S(1)}, u32[]{:S(2)}, u32[]{:S(2)}) collective-permute-start(bf16[2,2,24,2048]{3,2,1,0:T(8,128)(2,1)S(1)} %pad_maximum_fusion.3), channel_id=1, source_target_pairs={{0,4},{4,0},{8,12},{12,8},{1,5},{5,1},{9,13},{13,9},{2,6},{6,2},{1... | collective-permute-start | bytes 1179656 | tf_op jit(solution)/shard_map/ppermute | solution.py:222
  100.0 15.7 %collective-permute-start.25 = (bf16[2,24,2048]{2,1,0:T(8,128)(2,1)S(1)}, bf16[2,24,2048]{2,1,0:T(8,128)(2,1)S(1)}, u32[]{:S(2)}, u32[]{:S(2)}) collective-permute-start(bf16[2,24,2048]{2,1,0:T(8,128)(2,1)S(1)} %fusion.9), channel_id=1, source_target_pairs={{0,8},{4,12},{8,0},{12,4},{1,9},{5,13},{9,1},{13,5},{2,10},{6,14},... | collective-permute-start | bytes 589832 | tf_op jit(solution)/shard_map/ppermute | solution.py:226

commit v16 on v10

--- a/solution.py
+++ b/solution.py
@@ -41,6 +41,7 @@
     cot_ref,
     out_ref,
     grad_ref,
+    query_scratch,
     *,
     head_count,
     keyval_heads,
@@ -66,11 +67,11 @@
             parts.append((x * lax.rsqrt(mean_square + epsilon) * gain).astype(jnp.bfloat16))
         return jnp.concatenate(parts, axis=0)
 
-    def forward(layer):
+    def forward(layer, saved=False):
         slot = slots_ref[layer]
         same = mask_ref[...] > 0.5
         for k in range(keyval_heads):
-            query = queries_of(slot, k)
+            query = query_scratch[k] if saved else queries_of(slot, k)
             key = keyval_ref[slot, :, head_cols(k)]
             value = keyval_ref[slot, :, pl.ds(key_width + k * head_dim, head_dim)]
             scores = lax.dot_general(
@@ -97,6 +98,7 @@
     own = slots_ref[section]
     for k in range(keyval_heads):
         query = queries_of(own, k)
+        query_scratch[k] = query
         key = keyval_ref[own, :, head_cols(k)]
         value = keyval_ref[own, :, pl.ds(key_width + k * head_dim, head_dim)]
         scores_t = lax.dot_general(
@@ -120,7 +122,7 @@
         grad_ref[:, head_cols(k)] = key_grad.astype(grad_ref.dtype)
         grad_ref[:, pl.ds(key_width + k * head_dim, head_dim)] = value_grad.astype(grad_ref.dtype)
 
-    forward(section)
+    forward(section, saved=True)
 
 
 def attention_layers(
@@ -158,6 +160,9 @@
             jax.ShapeDtypeStruct((micro_count, token_count, query_width), jnp.float32),
             jax.ShapeDtypeStruct((micro_count, image_count, pair_width), jnp.bfloat16),
         ],
+        scratch_shapes=[
+            pltpu.VMEM((keyval_heads, groups * token_count, head_dim), jnp.bfloat16)
+        ],
         compiler_params=pltpu.CompilerParams(dimension_semantics=("arbitrary",)),
         cost_estimate=pl.CostEstimate(
             flops=flops,

time: 113 us -> 113 us (level)
  no operation moved by 1% of the time
where the time goes in v16:
time: 113 us
  waiting for transfers between devices  43 us (38%)
  starting transfers between devices  38.7 us (34%)
  Pallas kernels  8.19 us (7%)
  local copies, waits for them, and re-layouts  7.63 us (7%)
  matrix products  7.55 us (7%)
  other arithmetic  6.55 us (6%)
    ppermute x9, starting transfers between devices, scatter_blocks(): lax.ppermute(part, axis, [(i, (i + d) % count) for i in range(count)])  19.1 us
    ppermute x9, waiting for transfers between devices, scatter_blocks(): lax.ppermute(part, axis, [(i, (i + d) % count) for i in range(count)])  14.8 us
    ppermute x5, waiting for transfers between devices, gather_blocks(): across = lax.ppermute(block, axis, [(i, i ^ 2) for i in range(count)])  13.6 us
    pallas_call x1, Pallas kernels, attention_layers(): pl.pallas_call(functools.partial(attention_kernel, head_count=head_count,...  8.19 us
    ppermute x5, waiting for transfers between devices, gather_blocks(): lax.ppermute(across, axis, partner)  6.58 us
    ppermute x1, starting transfers between devices, scatter_blocks(): back = lax.ppermute(theirs, axis, [(i, i ^ 2) for i in range(count)])  6.33 us
    ppermute x5, starting transfers between devices, gather_blocks(): across = lax.ppermute(block, axis, [(i, i ^ 2) for i in range(count)])  6.29 us
    ppermute x1, waiting for transfers between devices, scatter_blocks(): back = lax.ppermute(theirs, axis, [(i, i ^ 2) for i in range(count)])  5.2 us
  transfers between devices with their start and end apart: 26, of which 16 were waited for; matrix products, arithmetic and copies ran while one was open for 11% of the time, Pallas kernels for 0%

profile of v16, /device:TPU:0, one launch (start us, length us, event | category | flops | bytes accessed | tf_op | source)
XLA Modules:
  0.0 112.7 jit_solution(9929721510624161179)
XLA Ops:
  1.1 2.6 %collective-permute-start.7 = (bf16[2,24,2048]{2,1,0:T(8,128)(2,1)}, bf16[2,24,2048]{2,1,0:T(8,128)(2,1)S(1)}, u32[]{:S(2)}, u32[]{:S(2)}) collective-permute-start(bf16[2,24,2048]{2,1,0:T(8,128)(2,1)} %param.13), channel_id=1, source_target_pairs={{0,8},{4,12},{8,0},{12,4},{1,9},{5,13},{9,1},{13,5},{2,10},{6,14},... | collective-permute-start | bytes 589832 | tf_op jit(solution)/shard_map/ppermute | solution.py:193
  7.7 2.0 %collective-permute-done.7 = bf16[2,24,2048]{2,1,0:T(8,128)(2,1)S(1)} collective-permute-done((bf16[2,24,2048]{2,1,0:T(8,128)(2,1)}, bf16[2,24,2048]{2,1,0:T(8,128)(2,1)S(1)}, u32[]{:S(2)}, u32[]{:S(2)}) %collective-permute-start.7) | collective-permute-done | bytes 196640 | tf_op jit(solution)/shard_map/ppermute | solution.py:193
  9.6 3.0 %fusion.2 = f32[4,24,1024]{2,1,0:T(8,128)S(1)} fusion(bf16[4,24,2048]{2,1,0:T(8,128)(2,1)S(1)} %bitcast.121, bf16[1,2048,1024]{2,1,0:T(8,128)(2,1)} %param.14), kind=kOutput, calls=%fused_computation.7 | convolution fusion | flops 402653184 | bytes 4980736 | tf_op jit(solution)/shard_map/dot_general | solution.py:278
  12.7 1.9 %collective-permute-start.4 = (f32[24,1024]{1,0:T(8,128)S(1)}, f32[24,1024]{1,0:T(8,128)S(1)}, u32[]{:S(2)}, u32[]{:S(2)}) collective-permute-start(f32[24,1024]{1,0:T(8,128)S(1)} %get-tuple-element.13), channel_id=1, source_target_pairs={{0,1},{1,2},{2,3},{3,0},{4,5},{5,6},{6,7},{7,4},{8,9},{9,10},{10,1... | collective-permute-start | bytes 294920 | tf_op jit(solution)/shard_map/ppermute | solution.py:234
  14.6 2.6 %collective-permute-start.5 = (f32[24,1024]{1,0:T(8,128)S(1)}, f32[24,1024]{1,0:T(8,128)S(1)}, u32[]{:S(2)}, u32[]{:S(2)}) collective-permute-start(f32[24,1024]{1,0:T(8,128)S(1)} %get-tuple-element.15), channel_id=1, source_target_pairs={{0,2},{1,3},{2,0},{3,1},{4,6},{5,7},{6,4},{7,5},{8,10},{9,11},{10,... | collective-permute-start | bytes 294920 | tf_op jit(solution)/shard_map/ppermute | solution.py:234
  17.2 1.4 %collective-permute-start.6 = (f32[24,1024]{1,0:T(8,128)S(1)}, f32[24,1024]{1,0:T(8,128)S(1)}, u32[]{:S(2)}, u32[]{:S(2)}) collective-permute-start(f32[24,1024]{1,0:T(8,128)S(1)} %get-tuple-element.14), channel_id=1, source_target_pairs={{0,3},{1,0},{2,1},{3,2},{4,7},{5,4},{6,5},{7,6},{8,11},{9,8},{10,9... | collective-permute-start | bytes 294920 | tf_op jit(solution)/shard_map/ppermute | solution.py:234
  20.3 6.1 %collective-permute-start.10 = (f32[24,1024]{1,0:T(8,128)S(1)}, f32[24,1024]{1,0:T(8,128)S(1)}, u32[]{:S(2)}, u32[]{:S(2)}) collective-permute-start(f32[24,1024]{1,0:T(8,128)S(1)} %get-tuple-element.18), channel_id=1, source_target_pairs={{0,2},{1,3},{2,0},{3,1},{4,6},{5,7},{6,4},{7,5},{8,10},{9,11},{10,... | collective-permute-start | bytes 294920 | tf_op jit(solution)/shard_map/ppermute | solution.py:234
  26.4 3.0 %collective-permute-start.11 = (f32[24,1024]{1,0:T(8,128)S(1)}, f32[24,1024]{1,0:T(8,128)S(1)}, u32[]{:S(2)}, u32[]{:S(2)}) collective-permute-start(f32[24,1024]{1,0:T(8,128)S(1)} %get-tuple-element.17), channel_id=1, source_target_pairs={{0,3},{1,0},{2,1},{3,2},{4,7},{5,4},{6,5},{7,6},{8,11},{9,8},{10,9... | collective-permute-start | bytes 294920 | tf_op jit(solution)/shard_map/ppermute | solution.py:234
  29.5 1.2 %collective-permute-done.10 = f32[24,1024]{1,0:T(8,128)S(1)} collective-permute-done((f32[24,1024]{1,0:T(8,128)S(1)}, f32[24,1024]{1,0:T(8,128)S(1)}, u32[]{:S(2)}, u32[]{:S(2)}) %collective-permute-start.10) | collective-permute-done | bytes 98336 | tf_op jit(solution)/shard_map/ppermute | solution.py:234
  30.7 1.4 %collective-permute-done.11 = f32[24,1024]{1,0:T(8,128)S(1)} collective-permute-done((f32[24,1024]{1,0:T(8,128)S(1)}, f32[24,1024]{1,0:T(8,128)S(1)}, u32[]{:S(2)}, u32[]{:S(2)}) %collective-permute-start.11) | collective-permute-done | bytes 98336 | tf_op jit(solution)/shard_map/ppermute | solution.py:234
  32.1 3.8 %collective-permute-done.9 = f32[24,1024]{1,0:T(8,128)S(1)} collective-permute-done((f32[24,1024]{1,0:T(8,128)S(1)}, f32[24,1024]{1,0:T(8,128)S(1)}, u32[]{:S(2)}, u32[]{:S(2)}) %collective-permute-start.9) | collective-permute-done | bytes 98336 | tf_op jit(solution)/shard_map/ppermute | solution.py:234
  37.5 4.7 %collective-permute-done.13 = bf16[2,24,1024]{2,1,0:T(8,128)(2,1)S(1)} collective-permute-done((bf16[2,24,1024]{2,1,0:T(8,128)(2,1)S(1)}, bf16[2,24,1024]{2,1,0:T(8,128)(2,1)S(1)}, u32[]{:S(2)}, u32[]{:S(2)}) %collective-permute-start.13) | collective-permute-done | bytes 98336 | tf_op jit(solution)/shard_map/ppermute | solution.py:193
  42.2 1.0 collective-permute-done.12
  43.2 3.6 %collective-permute-done.14 = bf16[2,24,1024]{2,1,0:T(8,128)(2,1)S(1)} collective-permute-done((bf16[2,24,1024]{2,1,0:T(8,128)(2,1)S(1)}, bf16[2,24,1024]{2,1,0:T(8,128)(2,1)S(1)}, u32[]{:S(2)}, u32[]{:S(2)}) %collective-permute-start.14) | collective-permute-done | bytes 98336 | tf_op jit(solution)/shard_map/ppermute | solution.py:194
  48.3 1.6 %collective-permute-start.16 = (bf16[192,1024]{1,0:T(8,128)(2,1)S(1)}, bf16[192,1024]{1,0:T(8,128)(2,1)S(1)}, u32[]{:S(2)}, u32[]{:S(2)}) collective-permute-start(bf16[192,1024]{1,0:T(8,128)(2,1)S(1)} %bitcast.123), channel_id=1, source_target_pairs={{0,8},{4,12},{8,0},{12,4},{1,9},{5,13},{9,1},{13,5},{2,10},{6,14},... | collective-permute-start | bytes 1179656 | tf_op jit(solution)/shard_map/ppermute | solution.py:193
  52.1 4.1 %collective-permute-done.16 = bf16[192,1024]{1,0:T(8,128)(2,1)S(1)} collective-permute-done((bf16[192,1024]{1,0:T(8,128)(2,1)S(1)}, bf16[192,1024]{1,0:T(8,128)(2,1)S(1)}, u32[]{:S(2)}, u32[]{:S(2)}) %collective-permute-start.16) | collective-permute-done | bytes 393248 | tf_op jit(solution)/shard_map/ppermute | solution.py:193
  57.9 1.4 %pad_maximum_fusion.keyval_ref = bf16[4,2,96,1024]{3,2,1,0:T(8,128)(2,1)} fusion(bf16[1,2,96,1024]{3,2,1,0:T(8,128)(2,1)S(1)} %bitcast.145, bf16[1,2,96,1024]{3,2,1,0:T(8,128)(2,1)S(1)} %bitcast.142, bf16[1,2,96,1024]{3,2,1,0:T(8,128)(2,1)S(1)} %bitcast.144, bf16[1,2,96,1024]{3,2,1,0:T(8,128)(2,1)S(1)} %bitcast.125), kind=kLoop, calls=%fused_computation.12 | loop fusion | flops 2359296 | bytes 3145728 | tf_op jit(solution)/shard_map/stack | solution.py:195
  59.3 8.2 %shard_map.104 = (f32[2,64,4096]{2,1,0:T(8,128)}, bf16[2,96,1024]{2,1,0:T(8,128)(2,1)}) custom-call(s32[1]{0:T(128)} %bitcast.section_ref, s32[4]{0:T(128)} %iota_xor_fusion.slots_ref, f32[4,32]{1,0:T(4,128)} %maximum_tanh_fusion.gates_ref, bf16[2,64,4096]{2,1,0:T(8,128)(2,1)} %queries_ref.1, bf16[4,2,96,1024]{3,2,1,0:T(8,128)(2,1)} %pad_maximum_fusion.keyval_ref, ...), custom_call_target="tpu_custom_call" | custom-call | flops 1409286144 | bytes 6815744 | tf_op jit(solution)/shard_map/pallas_call | solution.py:141
  67.5 1.6 %gather_fusion.2 = bf16[8,24,1024]{2,1,0:T(8,128)(2,1)S(1)} fusion(bf16[8,24,1024]{2,1,0:T(8,128)(2,1)} %bitcast.150, s32[1024]{0:T(1024)S(1)} %pad_clamp_fusion), kind=kCustom, calls=%fused_computation.3.clone | custom fusion | bytes 786464 | tf_op jit(solution)/shard_map/jit(_take)/gather | solution.py:300
  70.2 1.7 %collective-permute-start.19 = (bf16[48,1024]{1,0:T(8,128)(2,1)S(1)}, bf16[48,1024]{1,0:T(8,128)(2,1)S(1)}, u32[]{:S(2)}, u32[]{:S(2)}) collective-permute-start(bf16[48,1024]{1,0:T(8,128)(2,1)S(1)} %get-tuple-element.12), channel_id=1, source_target_pairs={{0,2},{1,3},{2,0},{3,1},{4,6},{5,7},{6,4},{7,5},{8,10},{9,11},{10,... | collective-permute-start | bytes 294920 | tf_op jit(solution)/shard_map/ppermute | solution.py:234
  71.8 1.5 %collective-permute-start.20 = (bf16[48,1024]{1,0:T(8,128)(2,1)S(1)}, bf16[48,1024]{1,0:T(8,128)(2,1)S(1)}, u32[]{:S(2)}, u32[]{:S(2)}) collective-permute-start(bf16[48,1024]{1,0:T(8,128)(2,1)S(1)} %get-tuple-element.11), channel_id=1, source_target_pairs={{0,3},{1,0},{2,1},{3,2},{4,7},{5,4},{6,5},{7,6},{8,11},{9,8},{10,9... | collective-permute-start | bytes 294920 | tf_op jit(solution)/shard_map/ppermute | solution.py:234
  73.3 2.5 %collective-permute-done.18 = bf16[48,1024]{1,0:T(8,128)(2,1)S(1)} collective-permute-done((bf16[48,1024]{1,0:T(8,128)(2,1)S(1)}, bf16[48,1024]{1,0:T(8,128)(2,1)S(1)}, u32[]{:S(2)}, u32[]{:S(2)}) %collective-permute-start.18) | collective-permute-done | bytes 98336 | tf_op jit(solution)/shard_map/ppermute | solution.py:234
  75.8 5.1 %collective-permute-done.19 = bf16[48,1024]{1,0:T(8,128)(2,1)S(1)} collective-permute-done((bf16[48,1024]{1,0:T(8,128)(2,1)S(1)}, bf16[48,1024]{1,0:T(8,128)(2,1)S(1)}, u32[]{:S(2)}, u32[]{:S(2)}) %collective-permute-start.19) | collective-permute-done | bytes 98336 | tf_op jit(solution)/shard_map/ppermute | solution.py:234
  81.3 1.7 %collective-permute-start.22 = (bf16[2,24,1024]{2,1,0:T(8,128)(2,1)S(1)}, bf16[2,24,1024]{2,1,0:T(8,128)(2,1)S(1)}, u32[]{:S(2)}, u32[]{:S(2)}) collective-permute-start(bf16[2,24,1024]{2,1,0:T(8,128)(2,1)S(1)} %pad_maximum_fusion.6), channel_id=1, source_target_pairs={{0,2},{1,3},{2,0},{3,1},{4,6},{5,7},{6,4},{7,5},{8,10},{9,11},{10,... | collective-permute-start | bytes 294920 | tf_op jit(solution)/shard_map/ppermute | solution.py:193
  83.0 1.3 %collective-permute-start.21 = (bf16[2,24,1024]{2,1,0:T(8,128)(2,1)S(1)}, bf16[2,24,1024]{2,1,0:T(8,128)(2,1)S(1)}, u32[]{:S(2)}, u32[]{:S(2)}) collective-permute-start(bf16[2,24,1024]{2,1,0:T(8,128)(2,1)S(1)} %pad_maximum_fusion.6), channel_id=1, source_target_pairs={{0,1},{1,0},{2,3},{3,2},{4,5},{5,4},{6,7},{7,6},{8,9},{9,8},{10,11... | collective-permute-start | bytes 294920 | tf_op jit(solution)/shard_map/ppermute | solution.py:194
  84.3 2.9 %collective-permute-done.22 = bf16[2,24,1024]{2,1,0:T(8,128)(2,1)S(1)} collective-permute-done((bf16[2,24,1024]{2,1,0:T(8,128)(2,1)S(1)}, bf16[2,24,1024]{2,1,0:T(8,128)(2,1)S(1)}, u32[]{:S(2)}, u32[]{:S(2)}) %collective-permute-start.22) | collective-permute-done | bytes 98336 | tf_op jit(solution)/shard_map/ppermute | solution.py:193
  87.2 3.4 %collective-permute-start.23 = (bf16[2,24,1024]{2,1,0:T(8,128)(2,1)S(1)}, bf16[2,24,1024]{2,1,0:T(8,128)(2,1)S(1)}, u32[]{:S(2)}, u32[]{:S(2)}) collective-permute-start(bf16[2,24,1024]{2,1,0:T(8,128)(2,1)S(1)} %collective-permute-done.22), channel_id=1, source_target_pairs={{0,1},{1,0},{2,3},{3,2},{4,5},{5,4},{6,7},{7,6},{8,9},{9,8},{10,11... | collective-permute-start | bytes 294920 | tf_op jit(solution)/shard_map/ppermute | solution.py:194
  90.6 2.6 %collective-permute-done.23 = bf16[2,24,1024]{2,1,0:T(8,128)(2,1)S(1)} collective-permute-done((bf16[2,24,1024]{2,1,0:T(8,128)(2,1)S(1)}, bf16[2,24,1024]{2,1,0:T(8,128)(2,1)S(1)}, u32[]{:S(2)}, u32[]{:S(2)}) %collective-permute-start.23) | collective-permute-done | bytes 98336 | tf_op jit(solution)/shard_map/ppermute | solution.py:194
  94.6 3.7 %fusion.6 = bf16[192,2048]{1,0:T(8,128)(2,1)S(1)} fusion(bf16[192,1024]{1,0:T(8,128)(2,1)S(1)} %bitcast.131, bf16[1,2048,1024]{2,1,0:T(8,128)(2,1)} %param.14), kind=kOutput, calls=%fused_computation.11 | convolution fusion | flops 805699584 | bytes 5373952 | tf_op jit(solution)/shard_map/dot_general | solution.py:353
  98.6 1.7 %collective-permute-done.24 = bf16[2,2,24,2048]{3,2,1,0:T(8,128)(2,1)S(1)} collective-permute-done((bf16[2,2,24,2048]{3,2,1,0:T(8,128)(2,1)S(1)}, bf16[2,2,24,2048]{3,2,1,0:T(8,128)(2,1)S(1)}, u32[]{:S(2)}, u32[]{:S(2)}) %collective-permute-start.24) | collective-permute-done | bytes 393248 | tf_op jit(solution)/shard_map/ppermute | solution.py:221
  100.3 6.3 %collective-permute-start.25 = (bf16[2,24,2048]{2,1,0:T(8,128)(2,1)S(1)}, bf16[2,24,2048]{2,1,0:T(8,128)(2,1)S(1)}, u32[]{:S(2)}, u32[]{:S(2)}) collective-permute-start(bf16[2,24,2048]{2,1,0:T(8,128)(2,1)S(1)} %fusion.9), channel_id=1, source_target_pairs={{0,8},{4,12},{8,0},{12,4},{1,9},{5,13},{9,1},{13,5},{2,10},{6,14},... | collective-permute-start | bytes 589832 | tf_op jit(solution)/shard_map/ppermute | solution.py:225
  106.6 5.2 %collective-permute-done.25 = bf16[2,24,2048]{2,1,0:T(8,128)(2,1)S(1)} collective-permute-done((bf16[2,24,2048]{2,1,0:T(8,128)(2,1)S(1)}, bf16[2,24,2048]{2,1,0:T(8,128)(2,1)S(1)}, u32[]{:S(2)}, u32[]{:S(2)}) %collective-permute-start.25) | collective-permute-done | bytes 196640 | tf_op jit(solution)/shard_map/ppermute | solution.py:225
  (104 shorter events, 17.1 us)
Async XLA Ops:
  0.6 6.0 %collective-permute-start.3 = (bf16[2,24,2048]{2,1,0:T(8,128)(2,1)}, bf16[2,24,2048]{2,1,0:T(8,128)(2,1)S(1)}, u32[]{:S(2)}, u32[]{:S(2)}) collective-permute-start(bf16[2,24,2048]{2,1,0:T(8,128)(2,1)} %param.13), channel_id=1, source_target_pairs={{0,4},{4,0},{8,12},{12,8},{1,5},{5,1},{9,13},{13,9},{2,6},{6,2},{1... | collective-permute-start | bytes 589832 | tf_op jit(solution)/shard_map/ppermute | solution.py:194
  1.1 8.5 %collective-permute-start.7 = (bf16[2,24,2048]{2,1,0:T(8,128)(2,1)}, bf16[2,24,2048]{2,1,0:T(8,128)(2,1)S(1)}, u32[]{:S(2)}, u32[]{:S(2)}) collective-permute-start(bf16[2,24,2048]{2,1,0:T(8,128)(2,1)} %param.13), channel_id=1, source_target_pairs={{0,8},{4,12},{8,0},{12,4},{1,9},{5,13},{9,1},{13,5},{2,10},{6,14},... | collective-permute-start | bytes 589832 | tf_op jit(solution)/shard_map/ppermute | solution.py:193
  5.1 44.7 %collective-permute-start.1 = (f32[4128]{0:T(1024)S(1)}, f32[4128]{0:T(1024)S(1)}, u32[]{:S(2)}, u32[]{:S(2)}) collective-permute-start(f32[4128]{0:T(1024)S(1)} %reduce), channel_id=1, source_target_pairs={{0,8},{4,12},{8,0},{12,4},{1,9},{5,13},{9,1},{13,5},{2,10},{6,14},... | collective-permute-start | bytes 49544 | tf_op jit(solution)/shard_map/ppermute | solution.py:193
  5.2 46.2 %collective-permute-start = (f32[4128]{0:T(1024)S(1)}, f32[4128]{0:T(1024)S(1)}, u32[]{:S(2)}, u32[]{:S(2)}) collective-permute-start(f32[4128]{0:T(1024)S(1)} %reduce), channel_id=1, source_target_pairs={{0,4},{4,0},{8,12},{12,8},{1,5},{5,1},{9,13},{13,9},{2,6},{6,2},{1... | collective-permute-start | bytes 49544 | tf_op jit(solution)/shard_map/ppermute | solution.py:194
  7.6 11.0 %copy-start = (bf16[1,2048,1024]{2,1,0:T(8,128)(2,1)S(1)}, bf16[1,2048,1024]{2,1,0:T(8,128)(2,1)}, u32[]{:S(2)}) copy-start(bf16[1,2048,1024]{2,1,0:T(8,128)(2,1)} %param.14) | copy-start | bytes 12582916
  9.6 7.5 %collective-permute-start.8 = (bf16[2,24,2048]{2,1,0:T(8,128)(2,1)S(1)}, bf16[2,24,2048]{2,1,0:T(8,128)(2,1)S(1)}, u32[]{:S(2)}, u32[]{:S(2)}) collective-permute-start(bf16[2,24,2048]{2,1,0:T(8,128)(2,1)S(1)} %collective-permute-done.7), channel_id=1, source_target_pairs={{0,4},{4,0},{8,12},{12,8},{1,5},{5,1},{9,13},{13,9},{2,6},{6,2},{1... | collective-permute-start | bytes 589832 | tf_op jit(solution)/shard_map/ppermute | solution.py:194
  12.7 7.7 %collective-permute-start.4 = (f32[24,1024]{1,0:T(8,128)S(1)}, f32[24,1024]{1,0:T(8,128)S(1)}, u32[]{:S(2)}, u32[]{:S(2)}) collective-permute-start(f32[24,1024]{1,0:T(8,128)S(1)} %get-tuple-element.13), channel_id=1, source_target_pairs={{0,1},{1,2},{2,3},{3,0},{4,5},{5,6},{6,7},{7,4},{8,9},{9,10},{10,1... | collective-permute-start | bytes 294920 | tf_op jit(solution)/shard_map/ppermute | solution.py:234
  14.6 11.9 %collective-permute-start.5 = (f32[24,1024]{1,0:T(8,128)S(1)}, f32[24,1024]{1,0:T(8,128)S(1)}, u32[]{:S(2)}, u32[]{:S(2)}) collective-permute-start(f32[24,1024]{1,0:T(8,128)S(1)} %get-tuple-element.15), channel_id=1, source_target_pairs={{0,2},{1,3},{2,0},{3,1},{4,6},{5,7},{6,4},{7,5},{8,10},{9,11},{10,... | collective-permute-start | bytes 294920 | tf_op jit(solution)/shard_map/ppermute | solution.py:234
  17.2 12.3 %collective-permute-start.6 = (f32[24,1024]{1,0:T(8,128)S(1)}, f32[24,1024]{1,0:T(8,128)S(1)}, u32[]{:S(2)}, u32[]{:S(2)}) collective-permute-start(f32[24,1024]{1,0:T(8,128)S(1)} %get-tuple-element.14), channel_id=1, source_target_pairs={{0,3},{1,0},{2,1},{3,2},{4,7},{5,4},{6,5},{7,6},{8,11},{9,8},{10,9... | collective-permute-start | bytes 294920 | tf_op jit(solution)/shard_map/ppermute | solution.py:234
  18.6 17.7 %copy-start.2 = (f32[1,512]{1,0:T(1,128)S(1)}, f32[1,512]{1,0:T(1,128)}, u32[]{:S(2)}) copy-start(f32[1,512]{1,0:T(1,128)} %param.16) | copy-start | bytes 6148
  20.3 10.3 %collective-permute-start.10 = (f32[24,1024]{1,0:T(8,128)S(1)}, f32[24,1024]{1,0:T(8,128)S(1)}, u32[]{:S(2)}, u32[]{:S(2)}) collective-permute-start(f32[24,1024]{1,0:T(8,128)S(1)} %get-tuple-element.18), channel_id=1, source_target_pairs={{0,2},{1,3},{2,0},{3,1},{4,6},{5,7},{6,4},{7,5},{8,10},{9,11},{10,... | collective-permute-start | bytes 294920 | tf_op jit(solution)/shard_map/ppermute | solution.py:234
  26.4 5.6 %collective-permute-start.11 = (f32[24,1024]{1,0:T(8,128)S(1)}, f32[24,1024]{1,0:T(8,128)S(1)}, u32[]{:S(2)}, u32[]{:S(2)}) collective-permute-start(f32[24,1024]{1,0:T(8,128)S(1)} %get-tuple-element.17), channel_id=1, source_target_pairs={{0,3},{1,0},{2,1},{3,2},{4,7},{5,4},{6,5},{7,6},{8,11},{9,8},{10,9... | collective-permute-start | bytes 294920 | tf_op jit(solution)/shard_map/ppermute | solution.py:234
  29.5 6.4 %collective-permute-start.9 = (f32[24,1024]{1,0:T(8,128)S(1)}, f32[24,1024]{1,0:T(8,128)S(1)}, u32[]{:S(2)}, u32[]{:S(2)}) collective-permute-start(f32[24,1024]{1,0:T(8,128)S(1)} %get-tuple-element.16), channel_id=1, source_target_pairs={{0,1},{1,2},{2,3},{3,0},{4,5},{5,6},{6,7},{7,4},{8,9},{9,10},{10,1... | collective-permute-start | bytes 294920 | tf_op jit(solution)/shard_map/ppermute | solution.py:234
  36.3 5.9 %collective-permute-start.13 = (bf16[2,24,1024]{2,1,0:T(8,128)(2,1)S(1)}, bf16[2,24,1024]{2,1,0:T(8,128)(2,1)S(1)}, u32[]{:S(2)}, u32[]{:S(2)}) collective-permute-start(bf16[2,24,1024]{2,1,0:T(8,128)(2,1)S(1)} %bitcast.146), channel_id=1, source_target_pairs={{0,2},{1,3},{2,0},{3,1},{4,6},{5,7},{6,4},{7,5},{8,10},{9,11},{10,... | collective-permute-start | bytes 294920 | tf_op jit(solution)/shard_map/ppermute | solution.py:193
  36.7 6.6 %collective-permute-start.12 = (bf16[2,24,1024]{2,1,0:T(8,128)(2,1)S(1)}, bf16[2,24,1024]{2,1,0:T(8,128)(2,1)S(1)}, u32[]{:S(2)}, u32[]{:S(2)}) collective-permute-start(bf16[2,24,1024]{2,1,0:T(8,128)(2,1)S(1)} %bitcast.147), channel_id=1, source_target_pairs={{0,1},{1,0},{2,3},{3,2},{4,5},{5,4},{6,7},{7,6},{8,9},{9,8},{10,11... | collective-permute-start | bytes 294920 | tf_op jit(solution)/shard_map/ppermute | solution.py:194
  42.2 4.6 %collective-permute-start.14 = (bf16[2,24,1024]{2,1,0:T(8,128)(2,1)S(1)}, bf16[2,24,1024]{2,1,0:T(8,128)(2,1)S(1)}, u32[]{:S(2)}, u32[]{:S(2)}) collective-permute-start(bf16[2,24,1024]{2,1,0:T(8,128)(2,1)S(1)} %collective-permute-done.13), channel_id=1, source_target_pairs={{0,1},{1,0},{2,3},{3,2},{4,5},{5,4},{6,7},{7,6},{8,9},{9,8},{10,11... | collective-permute-start | bytes 294920 | tf_op jit(solution)/shard_map/ppermute | solution.py:194
  48.3 7.9 %collective-permute-start.16 = (bf16[192,1024]{1,0:T(8,128)(2,1)S(1)}, bf16[192,1024]{1,0:T(8,128)(2,1)S(1)}, u32[]{:S(2)}, u32[]{:S(2)}) collective-permute-start(bf16[192,1024]{1,0:T(8,128)(2,1)S(1)} %bitcast.123), channel_id=1, source_target_pairs={{0,8},{4,12},{8,0},{12,4},{1,9},{5,13},{9,1},{13,5},{2,10},{6,14},... | collective-permute-start | bytes 1179656 | tf_op jit(solution)/shard_map/ppermute | solution.py:193
  49.9 1.6 %collective-permute-start.2 = (f32[4128]{0:T(1024)S(1)}, f32[4128]{0:T(1024)S(1)}, u32[]{:S(2)}, u32[]{:S(2)}) collective-permute-start(f32[4128]{0:T(1024)S(1)} %collective-permute-done.1), channel_id=1, source_target_pairs={{0,4},{4,0},{8,12},{12,8},{1,5},{5,1},{9,13},{13,9},{2,6},{6,2},{1... | collective-permute-start | bytes 49544 | tf_op jit(solution)/shard_map/ppermute | solution.py:194
  50.5 8.8 %copy-start.1 = (f32[2,8,64,96]{3,2,1,0:T(8,128)}, f32[2,8,64,96]{3,2,1,0:T(8,128)S(1)}, u32[]{:S(2)}) copy-start(f32[2,8,64,96]{3,2,1,0:T(8,128)S(1)} %tile.4) | copy-start | bytes 1179652
  51.5 6.0 %collective-permute-start.15 = (bf16[192,1024]{1,0:T(8,128)(2,1)S(1)}, bf16[192,1024]{1,0:T(8,128)(2,1)S(1)}, u32[]{:S(2)}, u32[]{:S(2)}) collective-permute-start(bf16[192,1024]{1,0:T(8,128)(2,1)S(1)} %bitcast.124), channel_id=1, source_target_pairs={{0,4},{4,0},{8,12},{12,8},{1,5},{5,1},{9,13},{13,9},{2,6},{6,2},{1... | collective-permute-start | bytes 1179656 | tf_op jit(solution)/shard_map/ppermute | solution.py:194
  56.2 1.7 %collective-permute-start.17 = (bf16[192,1024]{1,0:T(8,128)(2,1)S(1)}, bf16[192,1024]{1,0:T(8,128)(2,1)S(1)}, u32[]{:S(2)}, u32[]{:S(2)}) collective-permute-start(bf16[192,1024]{1,0:T(8,128)(2,1)S(1)} %collective-permute-done.16), channel_id=1, source_target_pairs={{0,4},{4,0},{8,12},{12,8},{1,5},{5,1},{9,13},{13,9},{2,6},{6,2},{1... | collective-permute-start | bytes 1179656 | tf_op jit(solution)/shard_map/ppermute | solution.py:194
  69.2 6.6 %collective-permute-start.18 = (bf16[48,1024]{1,0:T(8,128)(2,1)S(1)}, bf16[48,1024]{1,0:T(8,128)(2,1)S(1)}, u32[]{:S(2)}, u32[]{:S(2)}) collective-permute-start(bf16[48,1024]{1,0:T(8,128)(2,1)S(1)} %get-tuple-element.10), channel_id=1, source_target_pairs={{0,1},{1,2},{2,3},{3,0},{4,5},{5,6},{6,7},{7,4},{8,9},{9,10},{10,1... | collective-permute-start | bytes 294920 | tf_op jit(solution)/shard_map/ppermute | solution.py:234
  70.2 10.7 %collective-permute-start.19 = (bf16[48,1024]{1,0:T(8,128)(2,1)S(1)}, bf16[48,1024]{1,0:T(8,128)(2,1)S(1)}, u32[]{:S(2)}, u32[]{:S(2)}) collective-permute-start(bf16[48,1024]{1,0:T(8,128)(2,1)S(1)} %get-tuple-element.12), channel_id=1, source_target_pairs={{0,2},{1,3},{2,0},{3,1},{4,6},{5,7},{6,4},{7,5},{8,10},{9,11},{10,... | collective-permute-start | bytes 294920 | tf_op jit(solution)/shard_map/ppermute | solution.py:234
  71.8 9.0 %collective-permute-start.20 = (bf16[48,1024]{1,0:T(8,128)(2,1)S(1)}, bf16[48,1024]{1,0:T(8,128)(2,1)S(1)}, u32[]{:S(2)}, u32[]{:S(2)}) collective-permute-start(bf16[48,1024]{1,0:T(8,128)(2,1)S(1)} %get-tuple-element.11), channel_id=1, source_target_pairs={{0,3},{1,0},{2,1},{3,2},{4,7},{5,4},{6,5},{7,6},{8,11},{9,8},{10,9... | collective-permute-start | bytes 294920 | tf_op jit(solution)/shard_map/ppermute | solution.py:234
  81.3 5.9 %collective-permute-start.22 = (bf16[2,24,1024]{2,1,0:T(8,128)(2,1)S(1)}, bf16[2,24,1024]{2,1,0:T(8,128)(2,1)S(1)}, u32[]{:S(2)}, u32[]{:S(2)}) collective-permute-start(bf16[2,24,1024]{2,1,0:T(8,128)(2,1)S(1)} %pad_maximum_fusion.6), channel_id=1, source_target_pairs={{0,2},{1,3},{2,0},{3,1},{4,6},{5,7},{6,4},{7,5},{8,10},{9,11},{10,... | collective-permute-start | bytes 294920 | tf_op jit(solution)/shard_map/ppermute | solution.py:193
  83.0 7.6 %collective-permute-start.21 = (bf16[2,24,1024]{2,1,0:T(8,128)(2,1)S(1)}, bf16[2,24,1024]{2,1,0:T(8,128)(2,1)S(1)}, u32[]{:S(2)}, u32[]{:S(2)}) collective-permute-start(bf16[2,24,1024]{2,1,0:T(8,128)(2,1)S(1)} %pad_maximum_fusion.6), channel_id=1, source_target_pairs={{0,1},{1,0},{2,3},{3,2},{4,5},{5,4},{6,7},{7,6},{8,9},{9,8},{10,11... | collective-permute-start | bytes 294920 | tf_op jit(solution)/shard_map/ppermute | solution.py:194
  87.2 6.0 %collective-permute-start.23 = (bf16[2,24,1024]{2,1,0:T(8,128)(2,1)S(1)}, bf16[2,24,1024]{2,1,0:T(8,128)(2,1)S(1)}, u32[]{:S(2)}, u32[]{:S(2)}) collective-permute-start(bf16[2,24,1024]{2,1,0:T(8,128)(2,1)S(1)} %collective-permute-done.22), channel_id=1, source_target_pairs={{0,1},{1,0},{2,3},{3,2},{4,5},{5,4},{6,7},{7,6},{8,9},{9,8},{10,11... | collective-permute-start | bytes 294920 | tf_op jit(solution)/shard_map/ppermute | solution.py:194
  98.5 1.8 %collective-permute-start.24 = (bf16[2,2,24,2048]{3,2,1,0:T(8,128)(2,1)S(1)}, bf16[2,2,24,2048]{3,2,1,0:T(8,128)(2,1)S(1)}, u32[]{:S(2)}, u32[]{:S(2)}) collective-permute-start(bf16[2,2,24,2048]{3,2,1,0:T(8,128)(2,1)S(1)} %pad_maximum_fusion.3), channel_id=1, source_target_pairs={{0,4},{4,0},{8,12},{12,8},{1,5},{5,1},{9,13},{13,9},{2,6},{6,2},{1... | collective-permute-start | bytes 1179656 | tf_op jit(solution)/shard_map/ppermute | solution.py:221
  100.3 11.5 %collective-permute-start.25 = (bf16[2,24,2048]{2,1,0:T(8,128)(2,1)S(1)}, bf16[2,24,2048]{2,1,0:T(8,128)(2,1)S(1)}, u32[]{:S(2)}, u32[]{:S(2)}) collective-permute-start(bf16[2,24,2048]{2,1,0:T(8,128)(2,1)S(1)} %fusion.9), channel_id=1, source_target_pairs={{0,8},{4,12},{8,0},{12,4},{1,9},{5,13},{9,1},{13,5},{2,10},{6,14},... | collective-permute-start | bytes 589832 | tf_op jit(solution)/shard_map/ppermute | solution.py:225

commit v17 on v10

--- a/solution.py
+++ b/solution.py
@@ -68,15 +68,14 @@
 
     def forward(layer):
         slot = slots_ref[layer]
-        same = mask_ref[...] > 0.5
+        bias = mask_ref[...]
         for k in range(keyval_heads):
             query = queries_of(slot, k)
             key = keyval_ref[slot, :, head_cols(k)]
             value = keyval_ref[slot, :, pl.ds(key_width + k * head_dim, head_dim)]
             scores = lax.dot_general(
                 query, key, (((1,), (1,)), ((), ())), preferred_element_type=jnp.float32
-            ) * scale
-            scores = jnp.where(same, scores, -jnp.inf)
+            ) * scale + bias
             powered = jnp.exp(scores - jnp.max(scores, axis=-1, keepdims=True))
             probs = powered * (1.0 / jnp.sum(powered, axis=-1, keepdims=True))
             attended = jnp.dot(
@@ -93,7 +92,7 @@
 
     lax.fori_loop(0, section, layer_step, 0)
 
-    same_t = mask_t_ref[...] > 0.5
+    bias_t = mask_t_ref[...]
     own = slots_ref[section]
     for k in range(keyval_heads):
         query = queries_of(own, k)
@@ -101,8 +100,7 @@
         value = keyval_ref[own, :, pl.ds(key_width + k * head_dim, head_dim)]
         scores_t = lax.dot_general(
             key, query, (((1,), (1,)), ((), ())), preferred_element_type=jnp.float32
-        ) * scale
-        scores_t = jnp.where(same_t, scores_t, -jnp.inf)
+        ) * scale + bias_t
         powered = jnp.exp(scores_t - jnp.max(scores_t, axis=0, keepdims=True))
         probs_t = powered * (1.0 / jnp.sum(powered, axis=0, keepdims=True))
         upstream = jnp.concatenate(
@@ -132,7 +130,8 @@
     head_dim = query_width // head_count
     keyval_heads = pair_width // 2 // head_dim
     groups = head_count // keyval_heads
-    mask = jnp.tile(same_document.astype(jnp.float32), (1, groups, 1))
+    bias = jnp.where(same_document, 0.0, -jnp.inf).astype(jnp.float32)
+    mask = jnp.tile(bias, (1, groups, 1))
     mask_t = jnp.swapaxes(mask, 1, 2)
     smem = pl.BlockSpec(memory_space=pltpu.SMEM)
     flops = 2 * micro_count * (layer_count + 3) * head_count * token_count * image_count * head_dim * 2

time: 113 us -> 113 us (level)
  no operation moved by 1% of the time
where the time goes in v17:
time: 113 us
  waiting for transfers between devices  43 us (38%)
  starting transfers between devices  38.6 us (34%)
  Pallas kernels  8.2 us (7%)
  local copies, waits for them, and re-layouts  7.63 us (7%)
  matrix products  7.54 us (7%)
  other arithmetic  6.55 us (6%)
    ppermute x9, starting transfers between devices, scatter_blocks(): lax.ppermute(part, axis, [(i, (i + d) % count) for i in range(count)])  19.1 us
    ppermute x9, waiting for transfers between devices, scatter_blocks(): lax.ppermute(part, axis, [(i, (i + d) % count) for i in range(count)])  14.8 us
    ppermute x5, waiting for transfers between devices, gather_blocks(): across = lax.ppermute(block, axis, [(i, i ^ 2) for i in range(count)])  13.7 us
    pallas_call x1, Pallas kernels, attention_layers(): pl.pallas_call(functools.partial(attention_kernel, head_count=head_count,...  8.2 us
    ppermute x5, waiting for transfers between devices, gather_blocks(): lax.ppermute(across, axis, partner)  6.58 us
    ppermute x1, starting transfers between devices, scatter_blocks(): back = lax.ppermute(theirs, axis, [(i, i ^ 2) for i in range(count)])  6.29 us
    ppermute x5, starting transfers between devices, gather_blocks(): across = lax.ppermute(block, axis, [(i, i ^ 2) for i in range(count)])  6.29 us
    ppermute x1, waiting for transfers between devices, scatter_blocks(): back = lax.ppermute(theirs, axis, [(i, i ^ 2) for i in range(count)])  5.2 us
  transfers between devices with their start and end apart: 26, of which 16 were waited for; matrix products, arithmetic and copies ran while one was open for 11% of the time, Pallas kernels for 0%

profile of v17, /device:TPU:0, one launch (start us, length us, event | category | flops | bytes accessed | tf_op | source)
XLA Modules:
  0.0 112.6 jit_solution(6841537553680017301)
XLA Ops:
  1.1 2.6 %collective-permute-start.7 = (bf16[2,24,2048]{2,1,0:T(8,128)(2,1)}, bf16[2,24,2048]{2,1,0:T(8,128)(2,1)S(1)}, u32[]{:S(2)}, u32[]{:S(2)}) collective-permute-start(bf16[2,24,2048]{2,1,0:T(8,128)(2,1)} %param.13), channel_id=1, source_target_pairs={{0,8},{4,12},{8,0},{12,4},{1,9},{5,13},{9,1},{13,5},{2,10},{6,14},... | collective-permute-start | bytes 589832 | tf_op jit(solution)/shard_map/ppermute | solution.py:187
  7.7 2.0 %collective-permute-done.7 = bf16[2,24,2048]{2,1,0:T(8,128)(2,1)S(1)} collective-permute-done((bf16[2,24,2048]{2,1,0:T(8,128)(2,1)}, bf16[2,24,2048]{2,1,0:T(8,128)(2,1)S(1)}, u32[]{:S(2)}, u32[]{:S(2)}) %collective-permute-start.7) | collective-permute-done | bytes 196640 | tf_op jit(solution)/shard_map/ppermute | solution.py:187
  9.6 3.0 %fusion.2 = f32[4,24,1024]{2,1,0:T(8,128)S(1)} fusion(bf16[4,24,2048]{2,1,0:T(8,128)(2,1)S(1)} %bitcast.121, bf16[1,2048,1024]{2,1,0:T(8,128)(2,1)} %param.14), kind=kOutput, calls=%fused_computation.7 | convolution fusion | flops 402653184 | bytes 4980736 | tf_op jit(solution)/shard_map/dot_general | solution.py:272
  12.7 1.9 %collective-permute-start.4 = (f32[24,1024]{1,0:T(8,128)S(1)}, f32[24,1024]{1,0:T(8,128)S(1)}, u32[]{:S(2)}, u32[]{:S(2)}) collective-permute-start(f32[24,1024]{1,0:T(8,128)S(1)} %get-tuple-element.13), channel_id=1, source_target_pairs={{0,1},{1,2},{2,3},{3,0},{4,5},{5,6},{6,7},{7,4},{8,9},{9,10},{10,1... | collective-permute-start | bytes 294920 | tf_op jit(solution)/shard_map/ppermute | solution.py:228
  14.6 2.6 %collective-permute-start.5 = (f32[24,1024]{1,0:T(8,128)S(1)}, f32[24,1024]{1,0:T(8,128)S(1)}, u32[]{:S(2)}, u32[]{:S(2)}) collective-permute-start(f32[24,1024]{1,0:T(8,128)S(1)} %get-tuple-element.15), channel_id=1, source_target_pairs={{0,2},{1,3},{2,0},{3,1},{4,6},{5,7},{6,4},{7,5},{8,10},{9,11},{10,... | collective-permute-start | bytes 294920 | tf_op jit(solution)/shard_map/ppermute | solution.py:228
  17.2 1.4 %collective-permute-start.6 = (f32[24,1024]{1,0:T(8,128)S(1)}, f32[24,1024]{1,0:T(8,128)S(1)}, u32[]{:S(2)}, u32[]{:S(2)}) collective-permute-start(f32[24,1024]{1,0:T(8,128)S(1)} %get-tuple-element.14), channel_id=1, source_target_pairs={{0,3},{1,0},{2,1},{3,2},{4,7},{5,4},{6,5},{7,6},{8,11},{9,8},{10,9... | collective-permute-start | bytes 294920 | tf_op jit(solution)/shard_map/ppermute | solution.py:228
  20.3 6.1 %collective-permute-start.10 = (f32[24,1024]{1,0:T(8,128)S(1)}, f32[24,1024]{1,0:T(8,128)S(1)}, u32[]{:S(2)}, u32[]{:S(2)}) collective-permute-start(f32[24,1024]{1,0:T(8,128)S(1)} %get-tuple-element.18), channel_id=1, source_target_pairs={{0,2},{1,3},{2,0},{3,1},{4,6},{5,7},{6,4},{7,5},{8,10},{9,11},{10,... | collective-permute-start | bytes 294920 | tf_op jit(solution)/shard_map/ppermute | solution.py:228
  26.4 3.0 %collective-permute-start.11 = (f32[24,1024]{1,0:T(8,128)S(1)}, f32[24,1024]{1,0:T(8,128)S(1)}, u32[]{:S(2)}, u32[]{:S(2)}) collective-permute-start(f32[24,1024]{1,0:T(8,128)S(1)} %get-tuple-element.17), channel_id=1, source_target_pairs={{0,3},{1,0},{2,1},{3,2},{4,7},{5,4},{6,5},{7,6},{8,11},{9,8},{10,9... | collective-permute-start | bytes 294920 | tf_op jit(solution)/shard_map/ppermute | solution.py:228
  29.5 1.2 %collective-permute-done.10 = f32[24,1024]{1,0:T(8,128)S(1)} collective-permute-done((f32[24,1024]{1,0:T(8,128)S(1)}, f32[24,1024]{1,0:T(8,128)S(1)}, u32[]{:S(2)}, u32[]{:S(2)}) %collective-permute-start.10) | collective-permute-done | bytes 98336 | tf_op jit(solution)/shard_map/ppermute | solution.py:228
  30.7 1.4 %collective-permute-done.11 = f32[24,1024]{1,0:T(8,128)S(1)} collective-permute-done((f32[24,1024]{1,0:T(8,128)S(1)}, f32[24,1024]{1,0:T(8,128)S(1)}, u32[]{:S(2)}, u32[]{:S(2)}) %collective-permute-start.11) | collective-permute-done | bytes 98336 | tf_op jit(solution)/shard_map/ppermute | solution.py:228
  32.1 3.8 %collective-permute-done.9 = f32[24,1024]{1,0:T(8,128)S(1)} collective-permute-done((f32[24,1024]{1,0:T(8,128)S(1)}, f32[24,1024]{1,0:T(8,128)S(1)}, u32[]{:S(2)}, u32[]{:S(2)}) %collective-permute-start.9) | collective-permute-done | bytes 98336 | tf_op jit(solution)/shard_map/ppermute | solution.py:228
  37.5 4.7 %collective-permute-done.13 = bf16[2,24,1024]{2,1,0:T(8,128)(2,1)S(1)} collective-permute-done((bf16[2,24,1024]{2,1,0:T(8,128)(2,1)S(1)}, bf16[2,24,1024]{2,1,0:T(8,128)(2,1)S(1)}, u32[]{:S(2)}, u32[]{:S(2)}) %collective-permute-start.13) | collective-permute-done | bytes 98336 | tf_op jit(solution)/shard_map/ppermute | solution.py:187
  42.2 1.0 collective-permute-done.12
  43.2 3.6 %collective-permute-done.14 = bf16[2,24,1024]{2,1,0:T(8,128)(2,1)S(1)} collective-permute-done((bf16[2,24,1024]{2,1,0:T(8,128)(2,1)S(1)}, bf16[2,24,1024]{2,1,0:T(8,128)(2,1)S(1)}, u32[]{:S(2)}, u32[]{:S(2)}) %collective-permute-start.14) | collective-permute-done | bytes 98336 | tf_op jit(solution)/shard_map/ppermute | solution.py:188
  48.3 1.6 %collective-permute-start.16 = (bf16[192,1024]{1,0:T(8,128)(2,1)S(1)}, bf16[192,1024]{1,0:T(8,128)(2,1)S(1)}, u32[]{:S(2)}, u32[]{:S(2)}) collective-permute-start(bf16[192,1024]{1,0:T(8,128)(2,1)S(1)} %bitcast.123), channel_id=1, source_target_pairs={{0,8},{4,12},{8,0},{12,4},{1,9},{5,13},{9,1},{13,5},{2,10},{6,14},... | collective-permute-start | bytes 1179656 | tf_op jit(solution)/shard_map/ppermute | solution.py:187
  52.1 4.1 %collective-permute-done.16 = bf16[192,1024]{1,0:T(8,128)(2,1)S(1)} collective-permute-done((bf16[192,1024]{1,0:T(8,128)(2,1)S(1)}, bf16[192,1024]{1,0:T(8,128)(2,1)S(1)}, u32[]{:S(2)}, u32[]{:S(2)}) %collective-permute-start.16) | collective-permute-done | bytes 393248 | tf_op jit(solution)/shard_map/ppermute | solution.py:187
  57.9 1.4 %pad_maximum_fusion.keyval_ref = bf16[4,2,96,1024]{3,2,1,0:T(8,128)(2,1)} fusion(bf16[1,2,96,1024]{3,2,1,0:T(8,128)(2,1)S(1)} %bitcast.145, bf16[1,2,96,1024]{3,2,1,0:T(8,128)(2,1)S(1)} %bitcast.142, bf16[1,2,96,1024]{3,2,1,0:T(8,128)(2,1)S(1)} %bitcast.144, bf16[1,2,96,1024]{3,2,1,0:T(8,128)(2,1)S(1)} %bitcast.125), kind=kLoop, calls=%fused_computation.12 | loop fusion | flops 2359296 | bytes 3145728 | tf_op jit(solution)/shard_map/stack | solution.py:189
  59.3 8.2 %shard_map.104 = (f32[2,64,4096]{2,1,0:T(8,128)}, bf16[2,96,1024]{2,1,0:T(8,128)(2,1)}) custom-call(s32[1]{0:T(128)} %bitcast.section_ref, s32[4]{0:T(128)} %iota_xor_fusion.slots_ref, f32[4,32]{1,0:T(4,128)} %maximum_tanh_fusion.gates_ref, bf16[2,64,4096]{2,1,0:T(8,128)(2,1)} %queries_ref.1, bf16[4,2,96,1024]{3,2,1,0:T(8,128)(2,1)} %pad_maximum_fusion.keyval_ref, ...), custom_call_target="tpu_custom_call" | custom-call | flops 1409286144 | bytes 6815744 | tf_op jit(solution)/shard_map/pallas_call | solution.py:138
  67.5 1.6 %gather_fusion.2 = bf16[8,24,1024]{2,1,0:T(8,128)(2,1)S(1)} fusion(bf16[8,24,1024]{2,1,0:T(8,128)(2,1)} %bitcast.150, s32[1024]{0:T(1024)S(1)} %pad_clamp_fusion), kind=kCustom, calls=%fused_computation.3.clone | custom fusion | bytes 786464 | tf_op jit(solution)/shard_map/jit(_take)/gather | solution.py:294
  70.2 1.7 %collective-permute-start.19 = (bf16[48,1024]{1,0:T(8,128)(2,1)S(1)}, bf16[48,1024]{1,0:T(8,128)(2,1)S(1)}, u32[]{:S(2)}, u32[]{:S(2)}) collective-permute-start(bf16[48,1024]{1,0:T(8,128)(2,1)S(1)} %get-tuple-element.12), channel_id=1, source_target_pairs={{0,2},{1,3},{2,0},{3,1},{4,6},{5,7},{6,4},{7,5},{8,10},{9,11},{10,... | collective-permute-start | bytes 294920 | tf_op jit(solution)/shard_map/ppermute | solution.py:228
  71.8 1.5 %collective-permute-start.20 = (bf16[48,1024]{1,0:T(8,128)(2,1)S(1)}, bf16[48,1024]{1,0:T(8,128)(2,1)S(1)}, u32[]{:S(2)}, u32[]{:S(2)}) collective-permute-start(bf16[48,1024]{1,0:T(8,128)(2,1)S(1)} %get-tuple-element.11), channel_id=1, source_target_pairs={{0,3},{1,0},{2,1},{3,2},{4,7},{5,4},{6,5},{7,6},{8,11},{9,8},{10,9... | collective-permute-start | bytes 294920 | tf_op jit(solution)/shard_map/ppermute | solution.py:228
  73.3 2.5 %collective-permute-done.18 = bf16[48,1024]{1,0:T(8,128)(2,1)S(1)} collective-permute-done((bf16[48,1024]{1,0:T(8,128)(2,1)S(1)}, bf16[48,1024]{1,0:T(8,128)(2,1)S(1)}, u32[]{:S(2)}, u32[]{:S(2)}) %collective-permute-start.18) | collective-permute-done | bytes 98336 | tf_op jit(solution)/shard_map/ppermute | solution.py:228
  75.8 5.1 %collective-permute-done.19 = bf16[48,1024]{1,0:T(8,128)(2,1)S(1)} collective-permute-done((bf16[48,1024]{1,0:T(8,128)(2,1)S(1)}, bf16[48,1024]{1,0:T(8,128)(2,1)S(1)}, u32[]{:S(2)}, u32[]{:S(2)}) %collective-permute-start.19) | collective-permute-done | bytes 98336 | tf_op jit(solution)/shard_map/ppermute | solution.py:228
  81.3 1.7 %collective-permute-start.22 = (bf16[2,24,1024]{2,1,0:T(8,128)(2,1)S(1)}, bf16[2,24,1024]{2,1,0:T(8,128)(2,1)S(1)}, u32[]{:S(2)}, u32[]{:S(2)}) collective-permute-start(bf16[2,24,1024]{2,1,0:T(8,128)(2,1)S(1)} %pad_maximum_fusion.6), channel_id=1, source_target_pairs={{0,2},{1,3},{2,0},{3,1},{4,6},{5,7},{6,4},{7,5},{8,10},{9,11},{10,... | collective-permute-start | bytes 294920 | tf_op jit(solution)/shard_map/ppermute | solution.py:187
  83.0 1.3 %collective-permute-start.21 = (bf16[2,24,1024]{2,1,0:T(8,128)(2,1)S(1)}, bf16[2,24,1024]{2,1,0:T(8,128)(2,1)S(1)}, u32[]{:S(2)}, u32[]{:S(2)}) collective-permute-start(bf16[2,24,1024]{2,1,0:T(8,128)(2,1)S(1)} %pad_maximum_fusion.6), channel_id=1, source_target_pairs={{0,1},{1,0},{2,3},{3,2},{4,5},{5,4},{6,7},{7,6},{8,9},{9,8},{10,11... | collective-permute-start | bytes 294920 | tf_op jit(solution)/shard_map/ppermute | solution.py:188
  84.3 2.9 %collective-permute-done.22 = bf16[2,24,1024]{2,1,0:T(8,128)(2,1)S(1)} collective-permute-done((bf16[2,24,1024]{2,1,0:T(8,128)(2,1)S(1)}, bf16[2,24,1024]{2,1,0:T(8,128)(2,1)S(1)}, u32[]{:S(2)}, u32[]{:S(2)}) %collective-permute-start.22) | collective-permute-done | bytes 98336 | tf_op jit(solution)/shard_map/ppermute | solution.py:187
  87.2 3.4 %collective-permute-start.23 = (bf16[2,24,1024]{2,1,0:T(8,128)(2,1)S(1)}, bf16[2,24,1024]{2,1,0:T(8,128)(2,1)S(1)}, u32[]{:S(2)}, u32[]{:S(2)}) collective-permute-start(bf16[2,24,1024]{2,1,0:T(8,128)(2,1)S(1)} %collective-permute-done.22), channel_id=1, source_target_pairs={{0,1},{1,0},{2,3},{3,2},{4,5},{5,4},{6,7},{7,6},{8,9},{9,8},{10,11... | collective-permute-start | bytes 294920 | tf_op jit(solution)/shard_map/ppermute | solution.py:188
  90.6 2.6 %collective-permute-done.23 = bf16[2,24,1024]{2,1,0:T(8,128)(2,1)S(1)} collective-permute-done((bf16[2,24,1024]{2,1,0:T(8,128)(2,1)S(1)}, bf16[2,24,1024]{2,1,0:T(8,128)(2,1)S(1)}, u32[]{:S(2)}, u32[]{:S(2)}) %collective-permute-start.23) | collective-permute-done | bytes 98336 | tf_op jit(solution)/shard_map/ppermute | solution.py:188
  94.6 3.7 %fusion.6 = bf16[192,2048]{1,0:T(8,128)(2,1)S(1)} fusion(bf16[192,1024]{1,0:T(8,128)(2,1)S(1)} %bitcast.131, bf16[1,2048,1024]{2,1,0:T(8,128)(2,1)} %param.14), kind=kOutput, calls=%fused_computation.11 | convolution fusion | flops 805699584 | bytes 5373952 | tf_op jit(solution)/shard_map/dot_general | solution.py:347
  98.6 1.7 %collective-permute-done.24 = bf16[2,2,24,2048]{3,2,1,0:T(8,128)(2,1)S(1)} collective-permute-done((bf16[2,2,24,2048]{3,2,1,0:T(8,128)(2,1)S(1)}, bf16[2,2,24,2048]{3,2,1,0:T(8,128)(2,1)S(1)}, u32[]{:S(2)}, u32[]{:S(2)}) %collective-permute-start.24) | collective-permute-done | bytes 393248 | tf_op jit(solution)/shard_map/ppermute | solution.py:215
  100.3 6.3 %collective-permute-start.25 = (bf16[2,24,2048]{2,1,0:T(8,128)(2,1)S(1)}, bf16[2,24,2048]{2,1,0:T(8,128)(2,1)S(1)}, u32[]{:S(2)}, u32[]{:S(2)}) collective-permute-start(bf16[2,24,2048]{2,1,0:T(8,128)(2,1)S(1)} %fusion.9), channel_id=1, source_target_pairs={{0,8},{4,12},{8,0},{12,4},{1,9},{5,13},{9,1},{13,5},{2,10},{6,14},... | collective-permute-start | bytes 589832 | tf_op jit(solution)/shard_map/ppermute | solution.py:219
  106.6 5.2 %collective-permute-done.25 = bf16[2,24,2048]{2,1,0:T(8,128)(2,1)S(1)} collective-permute-done((bf16[2,24,2048]{2,1,0:T(8,128)(2,1)S(1)}, bf16[2,24,2048]{2,1,0:T(8,128)(2,1)S(1)}, u32[]{:S(2)}, u32[]{:S(2)}) %collective-permute-start.25) | collective-permute-done | bytes 196640 | tf_op jit(solution)/shard_map/ppermute | solution.py:219
  (104 shorter events, 17.1 us)
Async XLA Ops:
  0.6 6.0 %collective-permute-start.3 = (bf16[2,24,2048]{2,1,0:T(8,128)(2,1)}, bf16[2,24,2048]{2,1,0:T(8,128)(2,1)S(1)}, u32[]{:S(2)}, u32[]{:S(2)}) collective-permute-start(bf16[2,24,2048]{2,1,0:T(8,128)(2,1)} %param.13), channel_id=1, source_target_pairs={{0,4},{4,0},{8,12},{12,8},{1,5},{5,1},{9,13},{13,9},{2,6},{6,2},{1... | collective-permute-start | bytes 589832 | tf_op jit(solution)/shard_map/ppermute | solution.py:188
  1.1 8.5 %collective-permute-start.7 = (bf16[2,24,2048]{2,1,0:T(8,128)(2,1)}, bf16[2,24,2048]{2,1,0:T(8,128)(2,1)S(1)}, u32[]{:S(2)}, u32[]{:S(2)}) collective-permute-start(bf16[2,24,2048]{2,1,0:T(8,128)(2,1)} %param.13), channel_id=1, source_target_pairs={{0,8},{4,12},{8,0},{12,4},{1,9},{5,13},{9,1},{13,5},{2,10},{6,14},... | collective-permute-start | bytes 589832 | tf_op jit(solution)/shard_map/ppermute | solution.py:187
  5.1 44.7 %collective-permute-start.1 = (f32[4128]{0:T(1024)S(1)}, f32[4128]{0:T(1024)S(1)}, u32[]{:S(2)}, u32[]{:S(2)}) collective-permute-start(f32[4128]{0:T(1024)S(1)} %reduce), channel_id=1, source_target_pairs={{0,8},{4,12},{8,0},{12,4},{1,9},{5,13},{9,1},{13,5},{2,10},{6,14},... | collective-permute-start | bytes 49544 | tf_op jit(solution)/shard_map/ppermute | solution.py:187
  5.2 46.2 %collective-permute-start = (f32[4128]{0:T(1024)S(1)}, f32[4128]{0:T(1024)S(1)}, u32[]{:S(2)}, u32[]{:S(2)}) collective-permute-start(f32[4128]{0:T(1024)S(1)} %reduce), channel_id=1, source_target_pairs={{0,4},{4,0},{8,12},{12,8},{1,5},{5,1},{9,13},{13,9},{2,6},{6,2},{1... | collective-permute-start | bytes 49544 | tf_op jit(solution)/shard_map/ppermute | solution.py:188
  7.6 11.0 %copy-start = (bf16[1,2048,1024]{2,1,0:T(8,128)(2,1)S(1)}, bf16[1,2048,1024]{2,1,0:T(8,128)(2,1)}, u32[]{:S(2)}) copy-start(bf16[1,2048,1024]{2,1,0:T(8,128)(2,1)} %param.14) | copy-start | bytes 12582916
  9.6 7.5 %collective-permute-start.8 = (bf16[2,24,2048]{2,1,0:T(8,128)(2,1)S(1)}, bf16[2,24,2048]{2,1,0:T(8,128)(2,1)S(1)}, u32[]{:S(2)}, u32[]{:S(2)}) collective-permute-start(bf16[2,24,2048]{2,1,0:T(8,128)(2,1)S(1)} %collective-permute-done.7), channel_id=1, source_target_pairs={{0,4},{4,0},{8,12},{12,8},{1,5},{5,1},{9,13},{13,9},{2,6},{6,2},{1... | collective-permute-start | bytes 589832 | tf_op jit(solution)/shard_map/ppermute | solution.py:188
  12.7 7.7 %collective-permute-start.4 = (f32[24,1024]{1,0:T(8,128)S(1)}, f32[24,1024]{1,0:T(8,128)S(1)}, u32[]{:S(2)}, u32[]{:S(2)}) collective-permute-start(f32[24,1024]{1,0:T(8,128)S(1)} %get-tuple-element.13), channel_id=1, source_target_pairs={{0,1},{1,2},{2,3},{3,0},{4,5},{5,6},{6,7},{7,4},{8,9},{9,10},{10,1... | collective-permute-start | bytes 294920 | tf_op jit(solution)/shard_map/ppermute | solution.py:228
  14.6 11.9 %collective-permute-start.5 = (f32[24,1024]{1,0:T(8,128)S(1)}, f32[24,1024]{1,0:T(8,128)S(1)}, u32[]{:S(2)}, u32[]{:S(2)}) collective-permute-start(f32[24,1024]{1,0:T(8,128)S(1)} %get-tuple-element.15), channel_id=1, source_target_pairs={{0,2},{1,3},{2,0},{3,1},{4,6},{5,7},{6,4},{7,5},{8,10},{9,11},{10,... | collective-permute-start | bytes 294920 | tf_op jit(solution)/shard_map/ppermute | solution.py:228
  17.2 12.3 %collective-permute-start.6 = (f32[24,1024]{1,0:T(8,128)S(1)}, f32[24,1024]{1,0:T(8,128)S(1)}, u32[]{:S(2)}, u32[]{:S(2)}) collective-permute-start(f32[24,1024]{1,0:T(8,128)S(1)} %get-tuple-element.14), channel_id=1, source_target_pairs={{0,3},{1,0},{2,1},{3,2},{4,7},{5,4},{6,5},{7,6},{8,11},{9,8},{10,9... | collective-permute-start | bytes 294920 | tf_op jit(solution)/shard_map/ppermute | solution.py:228
  18.6 17.7 %copy-start.2 = (f32[1,512]{1,0:T(1,128)S(1)}, f32[1,512]{1,0:T(1,128)}, u32[]{:S(2)}) copy-start(f32[1,512]{1,0:T(1,128)} %param.16) | copy-start | bytes 6148
  20.3 10.3 %collective-permute-start.10 = (f32[24,1024]{1,0:T(8,128)S(1)}, f32[24,1024]{1,0:T(8,128)S(1)}, u32[]{:S(2)}, u32[]{:S(2)}) collective-permute-start(f32[24,1024]{1,0:T(8,128)S(1)} %get-tuple-element.18), channel_id=1, source_target_pairs={{0,2},{1,3},{2,0},{3,1},{4,6},{5,7},{6,4},{7,5},{8,10},{9,11},{10,... | collective-permute-start | bytes 294920 | tf_op jit(solution)/shard_map/ppermute | solution.py:228
  26.4 5.6 %collective-permute-start.11 = (f32[24,1024]{1,0:T(8,128)S(1)}, f32[24,1024]{1,0:T(8,128)S(1)}, u32[]{:S(2)}, u32[]{:S(2)}) collective-permute-start(f32[24,1024]{1,0:T(8,128)S(1)} %get-tuple-element.17), channel_id=1, source_target_pairs={{0,3},{1,0},{2,1},{3,2},{4,7},{5,4},{6,5},{7,6},{8,11},{9,8},{10,9... | collective-permute-start | bytes 294920 | tf_op jit(solution)/shard_map/ppermute | solution.py:228
  29.5 6.4 %collective-permute-start.9 = (f32[24,1024]{1,0:T(8,128)S(1)}, f32[24,1024]{1,0:T(8,128)S(1)}, u32[]{:S(2)}, u32[]{:S(2)}) collective-permute-start(f32[24,1024]{1,0:T(8,128)S(1)} %get-tuple-element.16), channel_id=1, source_target_pairs={{0,1},{1,2},{2,3},{3,0},{4,5},{5,6},{6,7},{7,4},{8,9},{9,10},{10,1... | collective-permute-start | bytes 294920 | tf_op jit(solution)/shard_map/ppermute | solution.py:228
  36.3 5.9 %collective-permute-start.13 = (bf16[2,24,1024]{2,1,0:T(8,128)(2,1)S(1)}, bf16[2,24,1024]{2,1,0:T(8,128)(2,1)S(1)}, u32[]{:S(2)}, u32[]{:S(2)}) collective-permute-start(bf16[2,24,1024]{2,1,0:T(8,128)(2,1)S(1)} %bitcast.146), channel_id=1, source_target_pairs={{0,2},{1,3},{2,0},{3,1},{4,6},{5,7},{6,4},{7,5},{8,10},{9,11},{10,... | collective-permute-start | bytes 294920 | tf_op jit(solution)/shard_map/ppermute | solution.py:187
  36.7 6.6 %collective-permute-start.12 = (bf16[2,24,1024]{2,1,0:T(8,128)(2,1)S(1)}, bf16[2,24,1024]{2,1,0:T(8,128)(2,1)S(1)}, u32[]{:S(2)}, u32[]{:S(2)}) collective-permute-start(bf16[2,24,1024]{2,1,0:T(8,128)(2,1)S(1)} %bitcast.147), channel_id=1, source_target_pairs={{0,1},{1,0},{2,3},{3,2},{4,5},{5,4},{6,7},{7,6},{8,9},{9,8},{10,11... | collective-permute-start | bytes 294920 | tf_op jit(solution)/shard_map/ppermute | solution.py:188
  42.2 4.6 %collective-permute-start.14 = (bf16[2,24,1024]{2,1,0:T(8,128)(2,1)S(1)}, bf16[2,24,1024]{2,1,0:T(8,128)(2,1)S(1)}, u32[]{:S(2)}, u32[]{:S(2)}) collective-permute-start(bf16[2,24,1024]{2,1,0:T(8,128)(2,1)S(1)} %collective-permute-done.13), channel_id=1, source_target_pairs={{0,1},{1,0},{2,3},{3,2},{4,5},{5,4},{6,7},{7,6},{8,9},{9,8},{10,11... | collective-permute-start | bytes 294920 | tf_op jit(solution)/shard_map/ppermute | solution.py:188
  48.3 7.9 %collective-permute-start.16 = (bf16[192,1024]{1,0:T(8,128)(2,1)S(1)}, bf16[192,1024]{1,0:T(8,128)(2,1)S(1)}, u32[]{:S(2)}, u32[]{:S(2)}) collective-permute-start(bf16[192,1024]{1,0:T(8,128)(2,1)S(1)} %bitcast.123), channel_id=1, source_target_pairs={{0,8},{4,12},{8,0},{12,4},{1,9},{5,13},{9,1},{13,5},{2,10},{6,14},... | collective-permute-start | bytes 1179656 | tf_op jit(solution)/shard_map/ppermute | solution.py:187
  49.9 1.6 %collective-permute-start.2 = (f32[4128]{0:T(1024)S(1)}, f32[4128]{0:T(1024)S(1)}, u32[]{:S(2)}, u32[]{:S(2)}) collective-permute-start(f32[4128]{0:T(1024)S(1)} %collective-permute-done.1), channel_id=1, source_target_pairs={{0,4},{4,0},{8,12},{12,8},{1,5},{5,1},{9,13},{13,9},{2,6},{6,2},{1... | collective-permute-start | bytes 49544 | tf_op jit(solution)/shard_map/ppermute | solution.py:188
  50.5 8.8 %copy-start.1 = (f32[2,8,64,96]{3,2,1,0:T(8,128)}, f32[2,8,64,96]{3,2,1,0:T(8,128)S(1)}, u32[]{:S(2)}) copy-start(f32[2,8,64,96]{3,2,1,0:T(8,128)S(1)} %tile.4) | copy-start | bytes 1179652
  51.5 6.0 %collective-permute-start.15 = (bf16[192,1024]{1,0:T(8,128)(2,1)S(1)}, bf16[192,1024]{1,0:T(8,128)(2,1)S(1)}, u32[]{:S(2)}, u32[]{:S(2)}) collective-permute-start(bf16[192,1024]{1,0:T(8,128)(2,1)S(1)} %bitcast.124), channel_id=1, source_target_pairs={{0,4},{4,0},{8,12},{12,8},{1,5},{5,1},{9,13},{13,9},{2,6},{6,2},{1... | collective-permute-start | bytes 1179656 | tf_op jit(solution)/shard_map/ppermute | solution.py:188
  56.2 1.7 %collective-permute-start.17 = (bf16[192,1024]{1,0:T(8,128)(2,1)S(1)}, bf16[192,1024]{1,0:T(8,128)(2,1)S(1)}, u32[]{:S(2)}, u32[]{:S(2)}) collective-permute-start(bf16[192,1024]{1,0:T(8,128)(2,1)S(1)} %collective-permute-done.16), channel_id=1, source_target_pairs={{0,4},{4,0},{8,12},{12,8},{1,5},{5,1},{9,13},{13,9},{2,6},{6,2},{1... | collective-permute-start | bytes 1179656 | tf_op jit(solution)/shard_map/ppermute | solution.py:188
  69.2 6.6 %collective-permute-start.18 = (bf16[48,1024]{1,0:T(8,128)(2,1)S(1)}, bf16[48,1024]{1,0:T(8,128)(2,1)S(1)}, u32[]{:S(2)}, u32[]{:S(2)}) collective-permute-start(bf16[48,1024]{1,0:T(8,128)(2,1)S(1)} %get-tuple-element.10), channel_id=1, source_target_pairs={{0,1},{1,2},{2,3},{3,0},{4,5},{5,6},{6,7},{7,4},{8,9},{9,10},{10,1... | collective-permute-start | bytes 294920 | tf_op jit(solution)/shard_map/ppermute | solution.py:228
  70.2 10.7 %collective-permute-start.19 = (bf16[48,1024]{1,0:T(8,128)(2,1)S(1)}, bf16[48,1024]{1,0:T(8,128)(2,1)S(1)}, u32[]{:S(2)}, u32[]{:S(2)}) collective-permute-start(bf16[48,1024]{1,0:T(8,128)(2,1)S(1)} %get-tuple-element.12), channel_id=1, source_target_pairs={{0,2},{1,3},{2,0},{3,1},{4,6},{5,7},{6,4},{7,5},{8,10},{9,11},{10,... | collective-permute-start | bytes 294920 | tf_op jit(solution)/shard_map/ppermute | solution.py:228
  71.8 9.0 %collective-permute-start.20 = (bf16[48,1024]{1,0:T(8,128)(2,1)S(1)}, bf16[48,1024]{1,0:T(8,128)(2,1)S(1)}, u32[]{:S(2)}, u32[]{:S(2)}) collective-permute-start(bf16[48,1024]{1,0:T(8,128)(2,1)S(1)} %get-tuple-element.11), channel_id=1, source_target_pairs={{0,3},{1,0},{2,1},{3,2},{4,7},{5,4},{6,5},{7,6},{8,11},{9,8},{10,9... | collective-permute-start | bytes 294920 | tf_op jit(solution)/shard_map/ppermute | solution.py:228
  81.3 5.9 %collective-permute-start.22 = (bf16[2,24,1024]{2,1,0:T(8,128)(2,1)S(1)}, bf16[2,24,1024]{2,1,0:T(8,128)(2,1)S(1)}, u32[]{:S(2)}, u32[]{:S(2)}) collective-permute-start(bf16[2,24,1024]{2,1,0:T(8,128)(2,1)S(1)} %pad_maximum_fusion.6), channel_id=1, source_target_pairs={{0,2},{1,3},{2,0},{3,1},{4,6},{5,7},{6,4},{7,5},{8,10},{9,11},{10,... | collective-permute-start | bytes 294920 | tf_op jit(solution)/shard_map/ppermute | solution.py:187
  83.0 7.6 %collective-permute-start.21 = (bf16[2,24,1024]{2,1,0:T(8,128)(2,1)S(1)}, bf16[2,24,1024]{2,1,0:T(8,128)(2,1)S(1)}, u32[]{:S(2)}, u32[]{:S(2)}) collective-permute-start(bf16[2,24,1024]{2,1,0:T(8,128)(2,1)S(1)} %pad_maximum_fusion.6), channel_id=1, source_target_pairs={{0,1},{1,0},{2,3},{3,2},{4,5},{5,4},{6,7},{7,6},{8,9},{9,8},{10,11... | collective-permute-start | bytes 294920 | tf_op jit(solution)/shard_map/ppermute | solution.py:188
  87.2 6.0 %collective-permute-start.23 = (bf16[2,24,1024]{2,1,0:T(8,128)(2,1)S(1)}, bf16[2,24,1024]{2,1,0:T(8,128)(2,1)S(1)}, u32[]{:S(2)}, u32[]{:S(2)}) collective-permute-start(bf16[2,24,1024]{2,1,0:T(8,128)(2,1)S(1)} %collective-permute-done.22), channel_id=1, source_target_pairs={{0,1},{1,0},{2,3},{3,2},{4,5},{5,4},{6,7},{7,6},{8,9},{9,8},{10,11... | collective-permute-start | bytes 294920 | tf_op jit(solution)/shard_map/ppermute | solution.py:188
  98.5 1.8 %collective-permute-start.24 = (bf16[2,2,24,2048]{3,2,1,0:T(8,128)(2,1)S(1)}, bf16[2,2,24,2048]{3,2,1,0:T(8,128)(2,1)S(1)}, u32[]{:S(2)}, u32[]{:S(2)}) collective-permute-start(bf16[2,2,24,2048]{3,2,1,0:T(8,128)(2,1)S(1)} %pad_maximum_fusion.3), channel_id=1, source_target_pairs={{0,4},{4,0},{8,12},{12,8},{1,5},{5,1},{9,13},{13,9},{2,6},{6,2},{1... | collective-permute-start | bytes 1179656 | tf_op jit(solution)/shard_map/ppermute | solution.py:215
  100.3 11.5 %collective-permute-start.25 = (bf16[2,24,2048]{2,1,0:T(8,128)(2,1)S(1)}, bf16[2,24,2048]{2,1,0:T(8,128)(2,1)S(1)}, u32[]{:S(2)}, u32[]{:S(2)}) collective-permute-start(bf16[2,24,2048]{2,1,0:T(8,128)(2,1)S(1)} %fusion.9), channel_id=1, source_target_pairs={{0,8},{4,12},{8,0},{12,4},{1,9},{5,13},{9,1},{13,5},{2,10},{6,14},... | collective-permute-start | bytes 589832 | tf_op jit(solution)/shard_map/ppermute | solution.py:219
